TPU v7x, 32 devices: a whole 2x2x4 slice. The times are simulated.
32 devices in a mesh: groups: 2 (over y), tile: 4 (over z), dither: 2 (over x), band: 2 (over core).
Axes of the slice: x: 2, y: 2, z: 4, core: 2. Of those that a mesh axis runs over, the one named last changes fastest.
Arguments:
- spectra: bfloat16 [2048, 1024], P(('groups', 'tile'), 'band'), parts along dimension 0, may hold values from -6 to 6
- psf_blocks: bfloat16 [16, 128, 128], replicated, may hold values from -0.5 to 0.5
- observed: bfloat16 [4, 4096, 128], P(('groups', 'dither'), 'tile'), parts along dimension 0, may hold values from -6 to 6
- bad_mask: int32 [4, 4096, 128], P(('groups', 'dither'), 'tile'), parts along dimension 0, may hold values 0 or 1
- trace_tile: int32 [32768, 1], P(('groups', 'tile', 'dither', 'band')), parts along dimension 0, may hold values from 0 to 3; in each aligned block of 1024 rows (0 to 1023, 1024 to 2047, ...) at most 512 rows name the same one
- trace_slot: int32 [32768], P(('groups', 'tile', 'dither', 'band')), parts along dimension 0, may hold values from 0 to 1023
- trace_source: int32 [32768, 1], P(('groups', 'tile', 'dither', 'band')), parts along dimension 0, may hold values from 0 to 255; in each aligned block of 1024 rows (0 to 1023, 1024 to 2047, ...) at most 8 rows name the same one
- trace_block: int32 [32768], P(('groups', 'tile', 'dither', 'band')), parts along dimension 0, may hold values from 0 to 3
- psf_index: int32 [32768], P(('groups', 'tile', 'dither', 'band')), parts along dimension 0, may hold values from 0 to 15
Outputs:
- gradient: float32 [2048, 1024], P(('groups', 'tile', 'dither'), 'band'), parts along dimension 0
- residual: bfloat16 [4, 4096, 128], P(('groups', 'dither'), 'tile'), parts along dimension 0
There are 2 independent parts, one for each index of `groups`. A program takes and returns all parts, laid end to end along the dimension named above; an argument that names none is the same for every part. Nothing has to cross between parts.
Inputs may be any that keep to these rules, and one draw needn't show every extreme that they name: `trace_tile`: among the trace blocks of one sky region, dither and wavelength half, at most 512 name the same tile, and in every draw some tile is named by exactly 512 of them for some such group. `trace_source`: among the trace blocks of one sky region, dither and wavelength half, at most 8 name the same source, and in every draw some source is named by exactly 8 of them for some such group.
All inputs are finite; a program needn't handle non-finite values. No bound on the sum of `bad_mask` on one device may be relied on, other than what follows from the above.
Results may differ from a plain program's by a relative error of at most 0.006.
Values may be sent and summed in bfloat16 or wider, within the bound.
No kernel may reach another device: no remote copies, remote signals or barrier semaphores. Data moves between devices by JAX's collectives and lax.ppermute only.
A program may use at most 64 MiB of HBM per device.

v0:
```python
import math

import jax
import jax.numpy as jnp
from jax import lax
from jax.sharding import PartitionSpec as P


def in_blocks(worker, values, kinds):
    row_count = values.shape[0]
    block_size = math.gcd(row_count, 512)
    result = lax.map(
        worker,
        (
            values.reshape(row_count // block_size, block_size, values.shape[1]),
            kinds.reshape(row_count // block_size, block_size),
        ),
    )
    return result.reshape(row_count, result.shape[-1])


def through_table(values, kinds, psf_blocks):
    table_count, bin_count, pixel_count = psf_blocks.shape
    flat_table = psf_blocks.reshape(table_count * bin_count, pixel_count)

    def through_single(inputs):
        part_values, part_kinds = inputs
        chosen = (
            part_kinds[:, None, None] == jnp.arange(table_count, dtype=jnp.int32)[None, :, None]
        )
        spread = jnp.where(chosen, part_values[:, None, :], jnp.zeros((), jnp.bfloat16))
        spread = spread.reshape(part_values.shape[0], table_count * bin_count)
        return jnp.dot(spread, flat_table, preferred_element_type=jnp.float32)

    return in_blocks(through_single, values, kinds)


def back_through_table(values, kinds, psf_blocks):
    table_count, bin_count, pixel_count = psf_blocks.shape
    back_table = psf_blocks.transpose(2, 0, 1).reshape(pixel_count, table_count * bin_count)

    def back_single(inputs):
        part_values, part_kinds = inputs
        product = jnp.dot(part_values, back_table, preferred_element_type=jnp.float32)
        product = product.reshape(part_values.shape[0], table_count, bin_count)
        chosen = (
            part_kinds[:, None, None] == jnp.arange(table_count, dtype=jnp.int32)[None, :, None]
        )
        return jnp.sum(jnp.where(chosen, product, 0.0), axis=1)

    return in_blocks(back_single, values, kinds)


def slot_positions(target, group_count):
    member = (target[:, None] == jnp.arange(group_count, dtype=jnp.int32)[None, :]).astype(
        jnp.int32
    )
    return jnp.sum((jnp.cumsum(member, axis=0) - 1) * member, axis=1)


def per_device(
    spectra,
    psf_blocks,
    observed,
    bad_mask,
    trace_tile,
    trace_slot,
    trace_source,
    trace_block,
    psf_index,
):
    tile_count = lax.axis_size("tile")
    entry_count = trace_slot.shape[0]
    capacity = 2 * entry_count // tile_count
    table_count, bin_count, pixel_count = psf_blocks.shape
    source_count = spectra.shape[0]
    block_count = spectra.shape[1] // bin_count
    slot_count = observed.shape[1]
    target = trace_tile[:, 0]
    source_local = trace_source[:, 0]
    position = slot_positions(target, tile_count)
    spec_rows = source_local * block_count + trace_block
    spec_values = spectra.reshape(source_count * block_count, bin_count)[spec_rows]
    send_slots = jnp.zeros((tile_count, capacity), jnp.int32).at[target, position].set(trace_slot)
    send_values = (
        jnp.zeros((tile_count, capacity, bin_count), jnp.bfloat16)
        .at[target, position]
        .set(spec_values)
    )
    send_kinds = jnp.zeros((tile_count, capacity), jnp.int32).at[target, position].set(psf_index)
    got_values, got_slots, got_kinds = (
        lax.all_to_all(send_values, "tile", split_axis=0, concat_axis=0, tiled=True),
        lax.all_to_all(send_slots, "tile", split_axis=0, concat_axis=0, tiled=True),
        lax.all_to_all(send_kinds, "tile", split_axis=0, concat_axis=0, tiled=True),
    )
    flat_kinds = got_kinds.reshape(tile_count * capacity)
    flat_traces = through_table(
        got_values.reshape(tile_count * capacity, bin_count), flat_kinds, psf_blocks
    ).astype(jnp.bfloat16)
    flat_slots = got_slots.reshape(tile_count * capacity)
    partial_value = jax.ops.segment_sum(flat_traces.astype(jnp.float32), flat_slots, slot_count)
    model_image = lax.psum(partial_value, "band")
    residual = (
        bad_mask[0].astype(jnp.float32) * (model_image - observed[0].astype(jnp.float32))
    ).astype(jnp.bfloat16)
    under_rows = residual[flat_slots]
    owner_terms = back_through_table(under_rows, flat_kinds, psf_blocks)
    returned = lax.all_to_all(
        owner_terms.reshape(tile_count, capacity, bin_count).astype(jnp.bfloat16),
        "tile",
        split_axis=0,
        concat_axis=0,
        tiled=True,
    ).astype(jnp.float32)
    grad_terms = returned[target, position]
    local_grad = jax.ops.segment_sum(grad_terms, spec_rows, source_count * block_count)
    local_grad = local_grad.reshape(source_count, block_count * bin_count)
    gradient = lax.psum_scatter(local_grad, "dither", scatter_dimension=0, tiled=True)
    return (gradient, residual[None])


def solution(mesh):
    in_specs = (
        P(("groups", "tile"), "band"),
        P(),
        P(("groups", "dither"), "tile", None),
        P(("groups", "dither"), "tile", None),
        P(("groups", "tile", "dither", "band"), None),
        P(("groups", "tile", "dither", "band")),
        P(("groups", "tile", "dither", "band"), None),
        P(("groups", "tile", "dither", "band")),
        P(("groups", "tile", "dither", "band")),
    )
    out_specs = (P(("groups", "tile", "dither"), "band"), P(("groups", "dither"), "tile", None))
    return jax.shard_map(
        per_device, mesh=mesh, in_specs=in_specs, out_specs=out_specs, check_vma=False
    )
```

profile of v0, /device:TPU:0, one launch (start us, length us, event | category | flops | bytes accessed | tf_op | source)
XLA Modules:
  0.0 171.7 jit_solution(7300409605480088494)
XLA Ops:
  7.9 1.1 reduce-window.6
  11.7 0.8 and_reduce_fusion
  13.8 5.0 %scatter_custom_fusion.2 = s32[2048]{0:T(1024)} fusion(s32[1024]{0:T(1024)S(1)} %get-tuple-element.83, s32[1024]{0:T(1024)} %param.21, s32[]{:T(128)} %copy.45), kind=kCustom, calls=%fused_computation.57 | custom fusion | bytes 8704
  18.9 6.3 %all-to-all-start = ((s32[4,1,512]{2,1,0:T(1,128)}), s32[4,1,512]{2,1,0:T(1,128)S(1)}, u32[]{:S(2)}, u32[]{:S(2)}) async-start(s32[4,1,512]{2,1,0:T(1,128)} %bitcast.14), calls=%async_computation | async-start | bytes 16384 | tf_op jit(solution)/shard_map/all_to_all | solution.py:94
  25.2 1.1 reshape.162
  26.3 7.0 %scatter_custom_fusion.4 = bf16[2048,128]{1,0:T(8,128)(2,1)} fusion(s32[1024]{0:T(1024)S(1)} %get-tuple-element.83, bf16[1024,128]{1,0:T(8,128)(2,1)S(1)} %reshape.162, s32[1024]{0:T(1024)S(1)} %get-tuple-element.78, bf16[]{:T(256)} %constant.45.clone.1), kind=kCustom, calls=%fused_computation.31 | custom fusion | bytes 524290
  33.4 5.1 %all-to-all-start.2 = ((bf16[4,512,128]{2,1,0:T(8,128)(2,1)}), bf16[4,512,128]{2,1,0:T(8,128)(2,1)S(1)}, u32[]{:S(2)}, u32[]{:S(2)}) async-start(bf16[4,512,128]{2,1,0:T(8,128)(2,1)} %bitcast.18), calls=%async_computation.2 | async-start | bytes 1048576 | tf_op jit(solution)/shard_map/all_to_all | solution.py:92
  38.5 5.0 %scatter_custom_fusion.3 = s32[2048]{0:T(1024)} fusion(s32[1024]{0:T(1024)S(1)} %get-tuple-element.83, s32[1024]{0:T(1024)} %param.18, s32[]{:T(128)} %copy.45), kind=kCustom, calls=%fused_computation.55 | custom fusion | bytes 8704
  43.5 8.9 %all-to-all-done.2 = bf16[4,512,128]{2,1,0:T(8,128)(2,1)S(1)} async-done(((bf16[4,512,128]{2,1,0:T(8,128)(2,1)}), bf16[4,512,128]{2,1,0:T(8,128)(2,1)S(1)}, u32[]{:S(2)}, u32[]{:S(2)}) %all-to-all-start.2) | async-done | bytes 524320 | tf_op jit(solution)/shard_map/all_to_all | solution.py:92
  52.4 3.2 %all-to-all-start.1 = ((s32[4,1,512]{2,1,0:T(1,128)}), s32[4,1,512]{2,1,0:T(1,128)S(1)}, u32[]{:S(2)}, u32[]{:S(2)}) async-start(s32[4,1,512]{2,1,0:T(1,128)} %bitcast.16), calls=%async_computation.1 | async-start | bytes 16384 | tf_op jit(solution)/shard_map/all_to_all | solution.py:93
  55.8 14.7 %while.20 = (s32[]{:T(128)}, bf16[4,512,128]{2,1,0:T(8,128)(2,1)S(1)}, s32[4,512]{1,0:T(4,128)S(1)}, bf16[4,512,128]{2,1,0:T(8,128)(2,1)S(1)}, bf16[2048,128]{1,0:T(8,128)(2,1)S(1)}, /*index=5*/s32[]{:T(128)}) while((s32[]{:T(128)}, bf16[4,512,128]{2,1,0:T(8,128)(2,1)S(1)}, s32[4,512]{1,0:T(4,128)S(1)}, bf16[4,512,128]{2,1,0:T(8,128)(2,1)S(1)}, ...), condition=%wide.region_7.8_spmd, body=%wide.region_6.7_spmd.sunk | while | flops 269492224 | bytes 5396561 | solution.py:12
  56.0 2.7 %broadcast_select_fusion.3 = bf16[512,16,128]{2,1,0:T(8,128)(2,1)S(1)} fusion(pred[512,16]{1,0:T(8,128)(4,1)S(1)} %iota_compare_fusion.6, bf16[512,128]{1,0:T(8,128)(2,1)S(1)} %dynamic-slice_bitcast_fusion.2), kind=kLoop, calls=%fused_computation.11.clone.1 | loop fusion | flops 1048576 | bytes 2236416 | tf_op jit(solution)/shard_map/while/body/eval_jaxpr/jit(_where)/select_n | solution.py:31
  58.7 0.8 fusion.40
  59.7 2.7 %broadcast_select_fusion.3 = bf16[512,16,128]{2,1,0:T(8,128)(2,1)S(1)} fusion(pred[512,16]{1,0:T(8,128)(4,1)S(1)} %iota_compare_fusion.6, bf16[512,128]{1,0:T(8,128)(2,1)S(1)} %dynamic-slice_bitcast_fusion.2), kind=kLoop, calls=%fused_computation.11.clone.1 | loop fusion | flops 1048576 | bytes 2236416 | tf_op jit(solution)/shard_map/while/body/eval_jaxpr/jit(_where)/select_n | solution.py:31
  62.4 0.8 fusion.40
  63.3 2.7 %broadcast_select_fusion.3 = bf16[512,16,128]{2,1,0:T(8,128)(2,1)S(1)} fusion(pred[512,16]{1,0:T(8,128)(4,1)S(1)} %iota_compare_fusion.6, bf16[512,128]{1,0:T(8,128)(2,1)S(1)} %dynamic-slice_bitcast_fusion.2), kind=kLoop, calls=%fused_computation.11.clone.1 | loop fusion | flops 1048576 | bytes 2236416 | tf_op jit(solution)/shard_map/while/body/eval_jaxpr/jit(_where)/select_n | solution.py:31
  66.0 0.8 fusion.40
  67.0 2.7 %broadcast_select_fusion.3 = bf16[512,16,128]{2,1,0:T(8,128)(2,1)S(1)} fusion(pred[512,16]{1,0:T(8,128)(4,1)S(1)} %iota_compare_fusion.6, bf16[512,128]{1,0:T(8,128)(2,1)S(1)} %dynamic-slice_bitcast_fusion.2), kind=kLoop, calls=%fused_computation.11.clone.1 | loop fusion | flops 1048576 | bytes 2236416 | tf_op jit(solution)/shard_map/while/body/eval_jaxpr/jit(_where)/select_n | solution.py:31
  69.7 0.8 fusion.40
  70.5 14.4 %scatter_custom_fusion = f32[1024,128]{1,0:T(8,128)} fusion(s32[2048]{0:T(1024)S(1)} %bitcast.100, bf16[2048,128]{1,0:T(8,128)(2,1)S(1)} %bitcast.93, f32[]{:T(128)} %constant.24.clone.1), kind=kCustom, calls=%fused_computation.24 | custom fusion | flops 524288 | bytes 1048580 | tf_op jit(solution)/shard_map/scatter-add | solution.py:101
  85.0 20.0 %all-reduce.2.cloned.1.call-done = f32[1024,128]{1,0:T(8,128)} async-done(((f32[1024,128]{1,0:T(8,128)}), f32[1024,128]{1,0:T(8,128)}) %all-reduce.2.cloned.1.call-update) | async-done | bytes 524304 | tf_op jit(solution)/shard_map/psum | solution.py:102
  105.0 1.1 fusion.15
  106.2 6.2 %gather_fusion = bf16[2048,128]{1,0:T(8,128)(2,1)S(1)} fusion(bf16[1024,128]{1,0:T(8,128)(2,1)S(1)} %fusion.15, s32[2048]{0:T(1024)S(1)} %broadcast_clamp_fusion), kind=kCustom, calls=%fused_computation.1 | custom fusion | bytes 1056768 | tf_op jit(solution)/shard_map/gather | solution.py:106
  112.5 6.5 %while.21 = (s32[]{:T(128)}, bf16[4,512,128]{2,1,0:T(8,128)(2,1)S(1)}, s32[4,512]{1,0:T(4,128)S(1)}, bf16[4,512,128]{2,1,0:T(8,128)(2,1)S(1)}, bf16[128,2048]{0,1:T(8,128)(2,1)S(1)}, /*index=5*/s32[]{:T(128)}) while((s32[]{:T(128)}, bf16[4,512,128]{2,1,0:T(8,128)(2,1)S(1)}, s32[4,512]{1,0:T(4,128)S(1)}, ...), condition=%wide.region_12.13_spmd, body=%wide.region_10.12_spmd.sunk | while | flops 270475264 | bytes 1071185 | solution.py:12
  112.5 1.5 select_reduce_fusion.2
  114.1 1.5 select_reduce_fusion.2
  115.8 1.5 select_reduce_fusion.2
  117.4 1.5 select_reduce_fusion.2
  119.0 19.6 %all_to_all.31 = bf16[4,512,128]{2,1,0:T(8,128)(2,1)S(1)} all-to-all(bf16[4,512,128]{2,1,0:T(8,128)(2,1)S(1)} %get-tuple-element.57), channel_id=1, replica_groups=mesh['groups'=2,'tile'=4,'dither'=2,'band'=2] {'tile'}, dimensions={0} | all-to-all | bytes 1048576 | tf_op jit(solution)/shard_map/all_to_all | solution.py:108
  138.7 11.6 %scatter_custom_fusion.1 = f32[1024,128]{1,0:T(8,128)S(1)} fusion(s32[1024]{0:T(1024)S(1)} %get-tuple-element.79, f32[4,512,128]{2,1,0:T(8,128)S(1)} %convert_element_type.46, s32[1024]{0:T(1024)S(1)} %bitcast.106, f32[]{:T(128)} %constant.24.clone.1), kind=kCustom, calls=%fused_computation.29 | custom fusion | flops 131072 | bytes 524292 | tf_op jit(solution)/shard_map/scatter-add | solution.py:116
  150.3 0.9 reshape.166
  151.2 13.7 %reduce-scatter.2.cloned.1.call-done = f32[128,512]{1,0:T(8,128)} async-done(((f32[256,512]{1,0:T(8,128)}), f32[128,512]{1,0:T(8,128)}) %reduce-scatter.2.cloned.1.call-update) | async-done | bytes 262160 | tf_op jit(solution)/shard_map/reduce_scatter | solution.py:118
  (53 shorter events, 5.9 us)
Async XLA Ops:
  7.2 48.6 %copy-start.3 = (bf16[16,128,128]{2,1,0:T(8,128)(2,1)S(1)}, bf16[16,128,128]{2,1,0:T(8,128)(2,1)}, u32[]{:S(2)}) copy-start(bf16[16,128,128]{2,1,0:T(8,128)(2,1)} %param.14) | copy-start | bytes 1572868
  18.9 14.5 %all-to-all-start = ((s32[4,1,512]{2,1,0:T(1,128)}), s32[4,1,512]{2,1,0:T(1,128)S(1)}, u32[]{:S(2)}, u32[]{:S(2)}) async-start(s32[4,1,512]{2,1,0:T(1,128)} %bitcast.14), calls=%async_computation | async-start | bytes 16384 | tf_op jit(solution)/shard_map/all_to_all | solution.py:94
  33.4 19.0 %all-to-all-start.2 = ((bf16[4,512,128]{2,1,0:T(8,128)(2,1)}), bf16[4,512,128]{2,1,0:T(8,128)(2,1)S(1)}, u32[]{:S(2)}, u32[]{:S(2)}) async-start(bf16[4,512,128]{2,1,0:T(8,128)(2,1)} %bitcast.18), calls=%async_computation.2 | async-start | bytes 1048576 | tf_op jit(solution)/shard_map/all_to_all | solution.py:92
  52.4 18.1 %all-to-all-start.1 = ((s32[4,1,512]{2,1,0:T(1,128)}), s32[4,1,512]{2,1,0:T(1,128)S(1)}, u32[]{:S(2)}, u32[]{:S(2)}) async-start(s32[4,1,512]{2,1,0:T(1,128)} %bitcast.16), calls=%async_computation.1 | async-start | bytes 16384 | tf_op jit(solution)/shard_map/all_to_all | solution.py:93
  55.6 49.4 %all-reduce.2.cloned.1.call-start = ((), (), s32[]{:S(2)}) async-start(), calls=%async_computation.5 | async-start | bytes 1048576 | tf_op jit(solution)/shard_map/psum | solution.py:102
  55.8 49.3 %copy-start.1 = (s32[1,1024,128]{2,1,0:T(8,128)S(1)}, s32[1,1024,128]{2,1,0:T(8,128)}, u32[]{:S(2)}) copy-start(s32[1,1024,128]{2,1,0:T(8,128)} %param.16) | copy-start | bytes 1572868
  55.8 49.3 %copy-start.2 = (bf16[1,1024,128]{2,1,0:T(8,128)(2,1)S(1)}, bf16[1,1024,128]{2,1,0:T(8,128)(2,1)}, u32[]{:S(2)}) copy-start(bf16[1,1024,128]{2,1,0:T(8,128)(2,1)} %param.15) | copy-start | bytes 786436
  84.9 80.0 %reduce-scatter.2.cloned.1.call-start = ((), (), s32[]{:S(2)}) async-start(), calls=%async_computation.6 | async-start | bytes 786432 | tf_op jit(solution)/shard_map/reduce_scatter | solution.py:118
  106.2 6.2 %copy-start = (bf16[1024,128]{1,0:T(8,128)(2,1)}, bf16[1024,128]{1,0:T(8,128)(2,1)S(1)}, u32[]{:S(2)}) copy-start(bf16[1024,128]{1,0:T(8,128)(2,1)S(1)} %fusion.15) | copy-start | bytes 786436
Sparse Core Ops, SparseCore 0:
  85.0 19.9 all-reduce.1
  151.3 13.5 reduce-scatter.1
where the time goes:
time: 172 us
  other arithmetic  45 us (26%)
  waiting for transfers between devices  42.7 us (25%)
  local copies, waits for them, and re-layouts  25.9 us (15%)
  blocking collectives  19.6 us (11%)
  starting transfers between devices  14.7 us (9%)
  between operations  14.2 us (8%)
  matrix products  9.27 us (5%)
    psum x1, waiting for transfers between devices, per_device(): model_image = lax.psum(partial_value, 'band')  20 us
    all_to_all x1, blocking collectives, per_device(): lax.all_to_all(owner_terms.reshape(tile_count, capacity, bin_count).astyp...  19.6 us
    unnamed x12, local copies, waits for them, and re-layouts  17.2 us
    scatter-add x1, other arithmetic, per_device(): jax.ops.segment_sum(flat_traces.astype(jnp.float32), flat_slots, slot_count)  14.4 us
    reduce_scatter x1, waiting for transfers between devices, per_device(): lax.psum_scatter(local_grad, 'dither', scatter_dimension=0, tiled=True)  13.7 us
    scatter-add x1, other arithmetic, per_device(): jax.ops.segment_sum(grad_terms, spec_rows, source_count * block_count)  11.6 us
    select_n x4, other arithmetic, through_single(): jnp.where(chosen, part_values[:, None, :], jnp.zeros((), jnp.bfloat16))  10.8 us
    all_to_all x1, waiting for transfers between devices, per_device(): lax.all_to_all(send_values, 'tile', split_axis=0, concat_axis=0, tiled=True)  8.89 us
  transfers between devices with their start and end apart: 5, of which 3 were waited for; matrix products, arithmetic and copies ran while one was open for 16% of the time, Pallas kernels for 0%

commit v1 on v0

v1 whole, which is shorter than its diff:
```python
import jax
import jax.numpy as jnp
from jax import lax
from jax.sharding import PartitionSpec as P


def one_hot_rows(index, width):
    return (index[:, None] == jnp.arange(width, dtype=jnp.int32)[None, :]).astype(jnp.bfloat16)


def select_dot(selector, values, precision=None):
    return jnp.dot(selector, values, preferred_element_type=jnp.float32, precision=precision)


def select_dot_t(selector, values, precision=None):
    return lax.dot_general(
        selector,
        values,
        (((0,), (0,)), ((), ())),
        preferred_element_type=jnp.float32,
        precision=precision,
    )


def spread_by_kind(values, kinds, table_count):
    chosen = kinds[:, None, None] == jnp.arange(table_count, dtype=jnp.int32)[None, :, None]
    spread = jnp.where(chosen, values[:, None, :], jnp.zeros((), values.dtype))
    return spread.reshape(values.shape[0], table_count * values.shape[1])


def swap_add(value, axis):
    count = lax.axis_size(axis)
    if count == 2:
        return value + lax.ppermute(value, axis, [(0, 1), (1, 0)])
    return lax.psum(value, axis)


def per_device(
    spectra,
    psf_blocks,
    observed,
    bad_mask,
    trace_tile,
    trace_slot,
    trace_source,
    trace_block,
    psf_index,
):
    tile_count = lax.axis_size("tile")
    dither_count = lax.axis_size("dither")
    entry_count = trace_slot.shape[0]
    capacity = 2 * entry_count // tile_count
    table_count, bin_count, pixel_count = psf_blocks.shape
    source_count = spectra.shape[0]
    block_count = spectra.shape[1] // bin_count
    row_count = source_count * block_count
    slot_count = observed.shape[1]
    send_count = tile_count * capacity

    target = trace_tile[:, 0]
    kinds = psf_index
    spec_rows = trace_source[:, 0] * block_count + trace_block
    member = (target[:, None] == jnp.arange(tile_count, dtype=jnp.int32)[None, :]).astype(jnp.int32)
    position = jnp.sum((jnp.cumsum(member, axis=0) - 1) * member, axis=1)
    dest = target * capacity + position

    gather_spec = one_hot_rows(spec_rows, row_count)
    spec_values = select_dot(gather_spec, spectra.reshape(row_count, bin_count)).astype(jnp.bfloat16)
    psf_flat = psf_blocks.reshape(table_count * bin_count, pixel_count)
    traces = select_dot(spread_by_kind(spec_values, kinds, table_count), psf_flat).astype(jnp.bfloat16)
    place = one_hot_rows(dest, send_count)
    send_traces = select_dot_t(place, traces).astype(jnp.bfloat16)
    slot_parts = jnp.stack([trace_slot // 256, trace_slot % 256], axis=1).astype(jnp.bfloat16)
    send_slots = select_dot_t(place, slot_parts).astype(jnp.bfloat16)
    code_rows = -(-2 * capacity // pixel_count)
    send_slots = send_slots.reshape(tile_count, 2 * capacity)
    send_slots = jnp.pad(send_slots, ((0, 0), (0, code_rows * pixel_count - 2 * capacity)))
    send = jnp.concatenate(
        [
            send_traces.reshape(tile_count, capacity, pixel_count),
            send_slots.reshape(tile_count, code_rows, pixel_count),
        ],
        axis=1,
    )
    got = lax.all_to_all(send, "tile", split_axis=0, concat_axis=0, tiled=True)
    got_traces = got[:, :capacity].reshape(send_count, pixel_count)
    got_codes = got[:, capacity:].reshape(tile_count, code_rows * pixel_count)[:, : 2 * capacity]
    got_codes = got_codes.astype(jnp.int32).reshape(send_count, 2)
    got_slots = got_codes[:, 0] * 256 + got_codes[:, 1]

    at_slot = one_hot_rows(got_slots, slot_count)
    partial_value = select_dot_t(at_slot, got_traces)
    model_image = swap_add(partial_value, "band")
    residual = (
        bad_mask[0].astype(jnp.float32) * (model_image - observed[0].astype(jnp.float32))
    ).astype(jnp.bfloat16)

    under_rows = select_dot(at_slot, residual).astype(jnp.bfloat16)
    returned = lax.all_to_all(
        under_rows.reshape(tile_count, capacity, pixel_count),
        "tile",
        split_axis=0,
        concat_axis=0,
        tiled=True,
    )
    entry_rows = select_dot(place, returned.reshape(send_count, pixel_count)).astype(jnp.bfloat16)
    back_table = psf_blocks.transpose(0, 2, 1).reshape(table_count * pixel_count, bin_count)
    terms = select_dot(spread_by_kind(entry_rows, kinds, table_count), back_table)
    local_grad = select_dot_t(gather_spec, terms, precision=lax.Precision.HIGHEST)
    local_grad = local_grad.reshape(source_count, block_count * bin_count)

    if dither_count == 2:
        dither = lax.axis_index("dither")
        halves = local_grad.reshape(2, source_count // 2, block_count * bin_count)
        mine = jnp.where(dither == 0, halves[0], halves[1])
        theirs = jnp.where(dither == 0, halves[1], halves[0])
        gradient = mine + lax.ppermute(theirs, "dither", [(0, 1), (1, 0)])
    else:
        gradient = lax.psum_scatter(local_grad, "dither", scatter_dimension=0, tiled=True)
    return (gradient, residual[None])


def solution(mesh):
    in_specs = (
        P(("groups", "tile"), "band"),
        P(),
        P(("groups", "dither"), "tile", None),
        P(("groups", "dither"), "tile", None),
        P(("groups", "tile", "dither", "band"), None),
        P(("groups", "tile", "dither", "band")),
        P(("groups", "tile", "dither", "band"), None),
        P(("groups", "tile", "dither", "band")),
        P(("groups", "tile", "dither", "band")),
    )
    out_specs = (P(("groups", "tile", "dither"), "band"), P(("groups", "dither"), "tile", None))
    return jax.shard_map(
        per_device, mesh=mesh, in_specs=in_specs, out_specs=out_specs, check_vma=False
    )
```

time: 172 us -> 93.5 us (0.54)
  other arithmetic: 45 us -> 19.6 us
  local copies, waits for them, and re-layouts: 25.9 us -> 3.47 us
  waiting for transfers between devices: 42.7 us -> 22.9 us
  between operations: 14.2 us -> 0.82 us
  matrix products: 9.27 us -> 20.4 us
  starting transfers between devices: 14.7 us -> 5.09 us
    scatter-add x2 -> x0, other arithmetic: 26 us -> none  [the longest x1 14.4 us: per_device(): jax.ops.segment_sum(flat_traces.astype(jnp.float32), flat_slots, slot_count)]
    psum x1 -> x0, waiting for transfers between devices: 20 us -> none  [per_device(): model_image = lax.psum(partial_value, 'band')]
    unnamed x12 -> x10, local copies, waits for them, and re-layouts: 17.2 us -> 0.03 us
    reduce_scatter x1 -> x0, waiting for transfers between devices: 13.7 us -> none  [per_device(): lax.psum_scatter(local_grad, 'dither', scatter_dimension=0, tiled=True)]
    all_to_all x3 -> x1, starting transfers between devices: 14.7 us -> 3.47 us  [per_device(): lax.all_to_all(under_rows.reshape(tile_count, capacity, pixel_count), 'ti...]
    dot_general x8, matrix products: 9.27 us -> 20.4 us  [the longest x4 14.4 us: select_dot_t(): lax.dot_general(selector, values, (((0,), (0,)), ((), ())), preferred_ele...]
    ppermute x0 -> x2, waiting for transfers between devices: none -> 7.88 us  [the longest x1 5.98 us: per_device(): gradient = mine + lax.ppermute(theirs, 'dither', [(0, 1), (1, 0)])]
    gather x1 -> x0, local copies, waits for them, and re-layouts: 6.18 us -> none  [per_device(): under_rows = residual[flat_slots]]
  transfers between devices with their start and end apart: 5 -> 3, of which waited for: 3 -> 3; matrix products, arithmetic and copies ran while one was open for 16% -> 0% of each run, Pallas kernels for 0% -> 0%
where the time goes in v1:
time: 93.5 us; the launch traced here: 93 us
  waiting for transfers between devices  22.9 us (24%)
  blocking collectives  20.8 us (22%)
  matrix products  20.4 us (22%)
  other arithmetic  19.6 us (21%)
  starting transfers between devices  5.09 us (5%)
  local copies, waits for them, and re-layouts  3.47 us (4%)
    all_to_all x1, blocking collectives, per_device(): got = lax.all_to_all(send, 'tile', split_axis=0, concat_axis=0, tiled=True)  20.8 us
    all_to_all x1, waiting for transfers between devices, per_device(): lax.all_to_all(under_rows.reshape(tile_count, capacity, pixel_count), 'ti...  15 us
    dot_general x4, matrix products, select_dot_t(): lax.dot_general(selector, values, (((0,), (0,)), ((), ())), preferred_ele...  14.4 us
    select_n x2, other arithmetic, spread_by_kind(): spread = jnp.where(chosen, values[:, None, :], jnp.zeros((), values.dtype))  12.2 us
    ppermute x1, waiting for transfers between devices, per_device(): gradient = mine + lax.ppermute(theirs, 'dither', [(0, 1), (1, 0)])  5.98 us
    dot_general x4, matrix products, select_dot(): jnp.dot(selector, values, preferred_element_type=jnp.float32, precision=p...  5.95 us
    all_to_all x1, starting transfers between devices, per_device(): lax.all_to_all(under_rows.reshape(tile_count, capacity, pixel_count), 'ti...  3.47 us
    another operation x3, other arithmetic  2.01 us
  transfers between devices with their start and end apart: 3, of which 3 were waited for; matrix products, arithmetic and copies ran while one was open for 0% of the time, Pallas kernels for 0%

profile of v1, /device:TPU:0, one launch (start us, length us, event | category | flops | bytes accessed | tf_op | source)
XLA Modules:
  0.0 93.0 jit_solution(7331927244630696524)
XLA Ops:
  0.7 0.8 fusion.40
  1.4 1.1 %reduce-window.6 = s32[4,8,128]{2,1,0:T(8,128)S(1)} reduce-window(s32[4,8,128]{2,1,0:T(8,128)S(1)} %fusion.40, s32[]{:T(128)} %constant.37.clone.1), window={size=1x1x128 pad=0_0x0_0x127_0}, to_apply=%region_0.0 | reduce-window | flops 520192 | bytes 32772 | tf_op jit(solution)/shard_map/reduce-window
  2.5 0.2 slice_reduce_fusion
  2.8 0.2 reduce-window.9
  3.0 0.7 fusion.39
  3.7 0.7 multiply_add_fusion
  4.4 0.7 broadcast_multiply_fusion
  5.1 1.1 %reshape.94 = bf16[1024,128]{1,0:T(8,128)(2,1)S(1)} reshape(bf16[256,512]{1,0:T(8,128)(2,1)} %param.9) | data formatting | bytes 524288 | tf_op jit(solution)/shard_map/reshape | solution.py:68
  6.2 0.9 iota_compare_fusion.20
  7.1 0.7 fusion.41
  7.8 1.5 %fusion.18 = bf16[2048,2]{0,1:T(2,128)(2,1)S(1)} fusion(s32[1024]{0:T(1024)S(1)} %bitcast.56, bf16[1024,1]{0,1:T(2,128)(2,1)S(1)} %stack.13, bf16[1024,1]{0,1:T(2,128)(2,1)S(1)} %stack.12), kind=kOutput, calls=%fused_computation.23 | convolution fusion | flops 10498048 | bytes 16384 | tf_op jit(solution)/shard_map/dot_general | solution.py:16
  9.4 0.3 copy.11
  9.7 0.7 reshape.96
  10.4 0.8 fusion.30
  11.2 6.7 %broadcast_select_fusion.1 = bf16[1024,16,128]{2,1,0:T(8,128)(2,1)} fusion(pred[1024,16]{1,0:T(8,128)(4,1)S(1)} %iota_compare_fusion.20, bf16[1024,128]{1,0:T(8,128)(2,1)S(1)} %fusion.30), kind=kLoop, calls=%fused_computation.20 | loop fusion | flops 2097152 | bytes 4472832 | tf_op jit(solution)/shard_map/jit(_where)/select_n | solution.py:27
  17.9 6.6 %fusion.16 = bf16[2048,128]{1,0:T(8,128)(2,1)S(1)} fusion(s32[1024]{0:T(1024)S(1)} %bitcast.57, bf16[16,128,128]{2,1,0:T(8,128)(2,1)S(1)} %copy-done, bf16[1024,16,128]{2,1,0:T(8,128)(2,1)} %broadcast_select_fusion.1), kind=kOutput, calls=%fused_computation.21 | convolution fusion | flops 1076232192 | bytes 5246976 | tf_op jit(solution)/shard_map/dot_general | solution.py:16
  24.5 20.8 %all_to_all.10 = bf16[4,520,128]{2,1,0:T(8,128)(2,1)S(1)} all-to-all(bf16[4,520,128]{2,1,0:T(8,128)(2,1)S(1)} %pad_maximum_fusion), channel_id=1, replica_groups=mesh['groups'=2,'tile'=4,'dither'=2,'band'=2] {'tile'}, dimensions={0} | all-to-all | bytes 1064960 | tf_op jit(solution)/shard_map/all_to_all | solution.py:85
  45.3 1.0 %reshape.100 = s32[2048,2]{1,0:T(8,128)S(1)} reshape(s32[4,8,128]{2,1,0:T(8,128)S(1)} %slice_convert_fusion) | data formatting | bytes 32768 | tf_op jit(solution)/shard_map/convert_element_type | solution.py:88
  46.4 0.6 fusion.32
  47.1 2.7 %fusion.1 = f32[1024,128]{1,0:T(8,128)S(1)} fusion(bf16[2048,128]{1,0:T(8,128)(2,1)S(1)} %bitcast.49, s32[2048]{0:T(1024)S(1)} %fusion.32), kind=kOutput, calls=%fused_computation.2 | convolution fusion | flops 538968064 | bytes 1056768 | tf_op jit(solution)/shard_map/dot_general | solution.py:16
  49.8 1.9 %collective-permute-done = f32[1024,128]{1,0:T(8,128)S(1)} collective-permute-done((f32[1024,128]{1,0:T(8,128)S(1)}, f32[1024,128]{1,0:T(8,128)S(1)}, u32[]{:S(2)}, u32[]{:S(2)}) %collective-permute-start) | collective-permute-done | bytes 524320 | tf_op jit(solution)/shard_map/ppermute | solution.py:34
  51.7 0.1 fusion.36
  51.9 2.4 %fusion.17 = bf16[2048,128]{1,0:T(8,128)(2,1)} fusion(bf16[1024,128]{1,0:T(8,128)(2,1)S(1)} %fusion.36, s32[2048]{0:T(1024)S(1)} %fusion.32), kind=kOutput, calls=%fused_computation.22 | convolution fusion | flops 539230208 | bytes 794624 | tf_op jit(solution)/shard_map/dot_general | solution.py:12
  54.3 3.5 %all-to-all-start.1 = ((bf16[4,512,128]{2,1,0:T(8,128)(2,1)}), bf16[4,512,128]{2,1,0:T(8,128)(2,1)S(1)}, u32[]{:S(2)}, u32[]{:S(2)}) async-start(bf16[4,512,128]{2,1,0:T(8,128)(2,1)} %bitcast.11), calls=%async_computation.1 | async-start | bytes 1048576 | tf_op jit(solution)/shard_map/all_to_all | solution.py:99
  57.8 15.0 %all-to-all-done.1 = bf16[4,512,128]{2,1,0:T(8,128)(2,1)S(1)} async-done(((bf16[4,512,128]{2,1,0:T(8,128)(2,1)}), bf16[4,512,128]{2,1,0:T(8,128)(2,1)S(1)}, u32[]{:S(2)}, u32[]{:S(2)}) %all-to-all-start.1) | async-done | bytes 524320 | tf_op jit(solution)/shard_map/all_to_all | solution.py:99
  72.8 1.5 %fusion.31 = bf16[1024,128]{1,0:T(8,128)(2,1)S(1)} fusion(bf16[2048,128]{1,0:T(8,128)(2,1)S(1)} %bitcast.47, s32[1024]{0:T(1024)S(1)} %bitcast.58), kind=kOutput, calls=%fused_computation.30 | convolution fusion | flops 539099136 | bytes 790528 | tf_op jit(solution)/shard_map/dot_general | solution.py:12
  74.3 5.5 %broadcast_select_fusion = bf16[1024,16,128]{2,1,0:T(8,128)(2,1)S(1)} fusion(pred[1024,16]{1,0:T(8,128)(4,1)S(1)} %iota_compare_fusion.20, bf16[1024,128]{1,0:T(8,128)(2,1)S(1)} %fusion.31), kind=kLoop, calls=%fused_computation.19 | loop fusion | flops 2097152 | bytes 4472832 | tf_op jit(solution)/shard_map/jit(_where)/select_n | solution.py:27
  79.8 1.3 %fusion.24 = f32[1024,128]{1,0:T(8,128)S(1)} fusion(bf16[1024,16,128]{2,1,0:T(8,128)(2,1)S(1)} %broadcast_select_fusion, bf16[16,128,128]{2,1,0:T(8,128)(2,1)S(1)} %copy-done), kind=kOutput, calls=%fused_computation.27 | convolution fusion | flops 536870912 | bytes 5242880 | tf_op jit(solution)/shard_map/dot_general | solution.py:12
  81.0 3.6 %fusion.14 = f32[1024,128]{1,0:T(8,128)S(1)} fusion(f32[1024,128]{1,0:T(8,128)S(1)} %fusion.24, s32[1024]{0:T(1024)S(1)} %add.27), kind=kOutput, calls=%fused_computation.17 | convolution fusion | flops 1611661312 | bytes 1052672 | tf_op jit(solution)/shard_map/dot_general | solution.py:16
  84.7 1.6 %collective-permute-start.1 = (f32[128,512]{1,0:T(8,128)S(1)}, f32[128,512]{1,0:T(8,128)S(1)}, u32[]{:S(2)}, u32[]{:S(2)}) collective-permute-start(f32[128,512]{1,0:T(8,128)S(1)} %select_n.45), channel_id=1, source_target_pairs={{0,2},{2,0},{1,3},{3,1},{4,6},{6,4},{5,7},{7,5},{8,10},{10,8},{9,1... | collective-permute-start | bytes 786440 | tf_op jit(solution)/shard_map/ppermute | solution.py:117
  86.3 6.0 %collective-permute-done.1 = f32[128,512]{1,0:T(8,128)S(1)} collective-permute-done((f32[128,512]{1,0:T(8,128)S(1)}, f32[128,512]{1,0:T(8,128)S(1)}, u32[]{:S(2)}, u32[]{:S(2)}) %collective-permute-start.1) | collective-permute-done | bytes 262176 | tf_op jit(solution)/shard_map/ppermute | solution.py:117
  92.3 0.7 add.32
  (21 shorter events, 0.4 us)
Async XLA Ops:
  0.6 17.3 %copy-start = (bf16[16,128,128]{2,1,0:T(8,128)(2,1)S(1)}, bf16[16,128,128]{2,1,0:T(8,128)(2,1)}, u32[]{:S(2)}) copy-start(bf16[16,128,128]{2,1,0:T(8,128)(2,1)} %param.10) | copy-start | bytes 1572868
  0.6 9.7 %copy-start.4 = (s32[1024]{0:T(1024)S(1)}, s32[1024]{0:T(1024)}, u32[]{:S(2)}) copy-start(s32[1024]{0:T(1024)} %param.16) | copy-start | bytes 12292
  46.3 5.4 %copy-start.1 = (s32[1,1024,128]{2,1,0:T(8,128)S(1)}, s32[1,1024,128]{2,1,0:T(8,128)}, u32[]{:S(2)}) copy-start(s32[1,1024,128]{2,1,0:T(8,128)} %param.12) | copy-start | bytes 1572868
  46.4 5.4 %copy-start.2 = (bf16[1,1024,128]{2,1,0:T(8,128)(2,1)S(1)}, bf16[1,1024,128]{2,1,0:T(8,128)(2,1)}, u32[]{:S(2)}) copy-start(bf16[1,1024,128]{2,1,0:T(8,128)(2,1)} %param.11) | copy-start | bytes 786436
  49.8 2.0 %collective-permute-start = (f32[1024,128]{1,0:T(8,128)S(1)}, f32[1024,128]{1,0:T(8,128)S(1)}, u32[]{:S(2)}, u32[]{:S(2)}) collective-permute-start(f32[1024,128]{1,0:T(8,128)S(1)} %fusion.1), channel_id=1, source_target_pairs={{0,1},{1,0},{2,3},{3,2},{4,5},{5,4},{6,7},{7,6},{8,9},{9,8},{10,11... | collective-permute-start | bytes 1572872 | tf_op jit(solution)/shard_map/ppermute | solution.py:34
  51.9 22.4 %copy-start.3 = (bf16[1024,128]{1,0:T(8,128)(2,1)}, bf16[1024,128]{1,0:T(8,128)(2,1)S(1)}, u32[]{:S(2)}) copy-start(bf16[1024,128]{1,0:T(8,128)(2,1)S(1)} %fusion.36) | copy-start | bytes 786436
  54.3 18.5 %all-to-all-start.1 = ((bf16[4,512,128]{2,1,0:T(8,128)(2,1)}), bf16[4,512,128]{2,1,0:T(8,128)(2,1)S(1)}, u32[]{:S(2)}, u32[]{:S(2)}) async-start(bf16[4,512,128]{2,1,0:T(8,128)(2,1)} %bitcast.11), calls=%async_computation.1 | async-start | bytes 1048576 | tf_op jit(solution)/shard_map/all_to_all | solution.py:99
  84.7 7.6 %collective-permute-start.1 = (f32[128,512]{1,0:T(8,128)S(1)}, f32[128,512]{1,0:T(8,128)S(1)}, u32[]{:S(2)}, u32[]{:S(2)}) collective-permute-start(f32[128,512]{1,0:T(8,128)S(1)} %select_n.45), channel_id=1, source_target_pairs={{0,2},{2,0},{1,3},{3,1},{4,6},{6,4},{5,7},{7,5},{8,10},{10,8},{9,1... | collective-permute-start | bytes 786440 | tf_op jit(solution)/shard_map/ppermute | solution.py:117

commit v2 on v1

--- a/solution.py
+++ b/solution.py
@@ -35,6 +35,15 @@
     return lax.psum(value, axis)
 
 
+def exchange(blocks, axis, direction):
+    count = lax.axis_size(axis)
+    moved = [blocks[0]]
+    for step in range(1, count):
+        pairs = [(j, (j + direction * step) % count) for j in range(count)]
+        moved.append(lax.ppermute(blocks[step], axis, pairs))
+    return jnp.stack(moved)
+
+
 def per_device(
     spectra,
     psf_blocks,
@@ -62,7 +71,8 @@
     spec_rows = trace_source[:, 0] * block_count + trace_block
     member = (target[:, None] == jnp.arange(tile_count, dtype=jnp.int32)[None, :]).astype(jnp.int32)
     position = jnp.sum((jnp.cumsum(member, axis=0) - 1) * member, axis=1)
-    dest = target * capacity + position
+    shift = (target - lax.axis_index("tile")) % tile_count
+    dest = shift * capacity + position
 
     gather_spec = one_hot_rows(spec_rows, row_count)
     spec_values = select_dot(gather_spec, spectra.reshape(row_count, bin_count)).astype(jnp.bfloat16)
@@ -82,7 +92,7 @@
         ],
         axis=1,
     )
-    got = lax.all_to_all(send, "tile", split_axis=0, concat_axis=0, tiled=True)
+    got = exchange(send, "tile", 1)
     got_traces = got[:, :capacity].reshape(send_count, pixel_count)
     got_codes = got[:, capacity:].reshape(tile_count, code_rows * pixel_count)[:, : 2 * capacity]
     got_codes = got_codes.astype(jnp.int32).reshape(send_count, 2)
@@ -96,17 +106,13 @@
     ).astype(jnp.bfloat16)
 
     under_rows = select_dot(at_slot, residual).astype(jnp.bfloat16)
-    returned = lax.all_to_all(
-        under_rows.reshape(tile_count, capacity, pixel_count),
-        "tile",
-        split_axis=0,
-        concat_axis=0,
-        tiled=True,
-    )
+    returned = exchange(under_rows.reshape(tile_count, capacity, pixel_count), "tile", -1)
     entry_rows = select_dot(place, returned.reshape(send_count, pixel_count)).astype(jnp.bfloat16)
     back_table = psf_blocks.transpose(0, 2, 1).reshape(table_count * pixel_count, bin_count)
     terms = select_dot(spread_by_kind(entry_rows, kinds, table_count), back_table)
-    local_grad = select_dot_t(gather_spec, terms, precision=lax.Precision.HIGHEST)
+    terms_hi = terms.astype(jnp.bfloat16)
+    terms_lo = (terms - terms_hi.astype(jnp.float32)).astype(jnp.bfloat16)
+    local_grad = select_dot_t(gather_spec, terms_hi) + select_dot_t(gather_spec, terms_lo)
     local_grad = local_grad.reshape(source_count, block_count * bin_count)
 
     if dither_count == 2:

time: 93.5 us -> 69.5 us (0.74)
  blocking collectives: 20.8 us -> 0 us
  other arithmetic: 19.6 us -> 7.34 us
  starting transfers between devices: 5.09 us -> 11.6 us
  waiting for transfers between devices: 22.9 us -> 27.3 us
  matrix products: 20.4 us -> 18.2 us
    all_to_all x1 -> x0, blocking collectives: 20.8 us -> none  [per_device(): got = lax.all_to_all(send, 'tile', split_axis=0, concat_axis=0, tiled=True)]
    ppermute x0 -> x6, waiting for transfers between devices: none -> 20.2 us  [exchange(): moved.append(lax.ppermute(blocks[step], axis, pairs))]
    all_to_all x1 -> x0, waiting for transfers between devices: 15 us -> none  [per_device(): lax.all_to_all(under_rows.reshape(tile_count, capacity, pixel_count), 'ti...]
    select_n x2 -> x0, other arithmetic: 12.2 us -> none  [spread_by_kind(): spread = jnp.where(chosen, values[:, None, :], jnp.zeros((), values.dtype))]
    ppermute x0 -> x6, starting transfers between devices: none -> 9.99 us  [exchange(): moved.append(lax.ppermute(blocks[step], axis, pairs))]
    all_to_all x1 -> x0, starting transfers between devices: 3.47 us -> none  [per_device(): lax.all_to_all(under_rows.reshape(tile_count, capacity, pixel_count), 'ti...]
    dot_general x4 -> x5, matrix products: 14.4 us -> 11.8 us  [select_dot_t(): lax.dot_general(selector, values, (((0,), (0,)), ((), ())), preferred_ele...]
    another operation x3 -> x5, other arithmetic: 2.01 us -> 2.12 us
  transfers between devices with their start and end apart: 3 -> 8, of which waited for: 3 -> 7; matrix products, arithmetic and copies ran while one was open for 0% -> 0% of each run, Pallas kernels for 0% -> 0%
where the time goes in v2:
time: 69.5 us; the launch traced here: 68.8 us
  waiting for transfers between devices  27.3 us (39%)
  matrix products  18.2 us (26%)
  starting transfers between devices  11.6 us (17%)
  other arithmetic  7.34 us (11%)
  local copies, waits for them, and re-layouts  3.48 us (5%)
  between operations  0.83 us (1%)
    ppermute x6, waiting for transfers between devices, exchange(): moved.append(lax.ppermute(blocks[step], axis, pairs))  20.2 us
    dot_general x5, matrix products, select_dot_t(): lax.dot_general(selector, values, (((0,), (0,)), ((), ())), preferred_ele...  11.8 us
    ppermute x6, starting transfers between devices, exchange(): moved.append(lax.ppermute(blocks[step], axis, pairs))  9.99 us
    dot_general x4, matrix products, select_dot(): jnp.dot(selector, values, preferred_element_type=jnp.float32, precision=p...  6.35 us
    ppermute x1, waiting for transfers between devices, per_device(): gradient = mine + lax.ppermute(theirs, 'dither', [(0, 1), (1, 0)])  5.21 us
    another operation x3, other arithmetic  2.01 us
    ppermute x1, waiting for transfers between devices, swap_add(): return value + lax.ppermute(value, axis, [(0, 1), (1, 0)])  1.89 us
    ppermute x1, starting transfers between devices, per_device(): gradient = mine + lax.ppermute(theirs, 'dither', [(0, 1), (1, 0)])  1.56 us
  transfers between devices with their start and end apart: 8, of which 7 were waited for; matrix products, arithmetic and copies ran while one was open for 0% of the time, Pallas kernels for 0%

profile of v2, /device:TPU:0, one launch (start us, length us, event | category | flops | bytes accessed | tf_op | source)
XLA Modules:
  0.0 68.8 jit_solution(9919537958768766031)
XLA Ops:
  0.7 0.7 %broadcast_multiply_fusion = s32[1024,1]{0,1:T(1,128)S(1)} fusion(s32[1024,1]{0,1:T(1,128)} %param.15), kind=kLoop, calls=%fused_computation.97 | loop fusion | flops 1024 | bytes 8192 | tf_op jit(solution)/shard_map/mul | solution.py:71
  1.4 0.7 %fusion.58 = (bf16[1024]{0:T(1024)(128)(2,1)S(1)}, bf16[1024]{0:T(1024)(128)(2,1)S(1)}) fusion(s32[1024]{0:T(1024)} %param.14), kind=kLoop, calls=%fused_computation.86 | loop fusion | flops 21504 | bytes 8192 | tf_op jit(solution)/shard_map/convert.5
  2.1 0.7 %iota_compare_fusion.23 = pred[1024,16]{0,1:T(8,128)(4,1)S(1)} fusion(s32[1024]{0:T(1024)} %param.17), kind=kLoop, calls=%fused_computation.68 | loop fusion | flops 16384 | bytes 20480 | tf_op jit(solution)/shard_map/eq | solution.py:26
  2.8 0.7 %fusion.57 = s32[4,8,128]{2,1,0:T(8,128)S(1)} fusion(s32[8,128]{1,0:T(8,128)} %bitcast.72), kind=kLoop, calls=%fused_computation.78 | loop fusion | flops 8192 | bytes 20480 | tf_op jit(solution)/shard_map/convert_element_type | solution.py:72
  3.5 1.1 %reduce-window.6 = s32[4,8,128]{2,1,0:T(8,128)S(1)} reduce-window(s32[4,8,128]{2,1,0:T(8,128)S(1)} %fusion.57, s32[]{:T(128)} %constant.49.clone.1), window={size=1x1x128 pad=0_0x0_0x127_0}, to_apply=%region_0.0 | reduce-window | flops 520192 | bytes 32772 | tf_op jit(solution)/shard_map/reduce-window
  5.1 1.1 %reshape.99 = bf16[1024,128]{1,0:T(8,128)(2,1)S(1)} reshape(bf16[256,512]{1,0:T(8,128)(2,1)} %param.9) | data formatting | bytes 524288 | tf_op jit(solution)/shard_map/reshape | solution.py:78
  6.2 0.7 %fusion.56 = s32[1024]{0:T(1024)S(1)} fusion(s32[1,4,8,128]{3,2,1,0:T(8,128)S(1)} %add_bitcast_fusion, s32[1024]{0:T(1024)} %bitcast.73), kind=kLoop, calls=%fused_computation.73 | loop fusion | flops 11264 | bytes 24576 | tf_op jit(solution)/shard_map/reduce_sum | solution.py:73
  7.0 0.7 %fusion.61 = s32[1024,1]{0,1:T(1,128)S(1)} fusion(s32[1024,1]{0,1:T(1,128)S(1)} %bitcast.75, s32[1024,1]{0,1:T(1,128)} %param.13, s32[]{:T(128)S(6)} %axis_index.28), kind=kLoop, calls=%fused_computation.89 | loop fusion | flops 14336 | bytes 12292 | tf_op jit(solution)/shard_map/add | solution.py:75
  7.7 1.5 %fusion.21 = bf16[2048,2]{0,1:T(2,128)(2,1)S(1)} fusion(s32[1024]{0:T(1024)S(1)} %bitcast.77, bf16[1024,1]{0,1:T(2,128)(2,1)S(1)} %stack.37, bf16[1024,1]{0,1:T(2,128)(2,1)S(1)} %stack.36), kind=kOutput, calls=%fused_computation.24 | convolution fusion | flops 10498048 | bytes 16384 | tf_op jit(solution)/shard_map/dot_general | solution.py:16
  10.2 0.8 %fusion.39 = bf16[1024,128]{1,0:T(8,128)(2,1)S(1)} fusion(bf16[1024,128]{1,0:T(8,128)(2,1)S(1)} %reshape.99, s32[1024]{0:T(1024)S(1)} %add.35), kind=kOutput, calls=%fused_computation.36 | convolution fusion | flops 269615104 | bytes 528384 | tf_op jit(solution)/shard_map/dot_general | solution.py:12
  11.0 4.8 %fusion.19 = bf16[2048,128]{1,0:T(8,128)(2,1)S(1)} fusion(s32[1024]{0:T(1024)S(1)} %bitcast.78, bf16[16,128,128]{2,1,0:T(8,128)(2,1)S(1)} %copy-done, pred[1024,16]{0,1:T(8,128)(4,1)S(1)} %iota_compare_fusion.23, bf16[1024,128]{1,0:T(8,128)(2,1)S(1)} %fusion.39), kind=kOutput, calls=%fused_computation.22 | convolution fusion | flops 1078329344 | bytes 1331200 | tf_op jit(solution)/shard_map/dot_general | solution.py:16
  15.8 3.1 %collective-permute-start = (bf16[520,128]{1,0:T(8,128)(2,1)S(1)}, bf16[520,128]{1,0:T(8,128)(2,1)S(1)}, u32[]{:S(2)}, u32[]{:S(2)}) collective-permute-start(bf16[520,128]{1,0:T(8,128)(2,1)S(1)} %get-tuple-element.3), channel_id=1, source_target_pairs={{0,4},{4,8},{8,12},{12,0},{1,5},{5,9},{9,13},{13,1},{2,6},{6,10},{... | collective-permute-start | bytes 399368 | tf_op jit(solution)/shard_map/ppermute | solution.py:43
  18.9 2.3 %collective-permute-start.2 = (bf16[520,128]{1,0:T(8,128)(2,1)S(1)}, bf16[520,128]{1,0:T(8,128)(2,1)S(1)}, u32[]{:S(2)}, u32[]{:S(2)}) collective-permute-start(bf16[520,128]{1,0:T(8,128)(2,1)S(1)} %get-tuple-element.4), channel_id=1, source_target_pairs={{0,12},{4,0},{8,4},{12,8},{1,13},{5,1},{9,5},{13,9},{2,14},{6,2},{... | collective-permute-start | bytes 399368 | tf_op jit(solution)/shard_map/ppermute | solution.py:43
  21.2 0.8 %collective-permute-start.1 = (bf16[520,128]{1,0:T(8,128)(2,1)S(1)}, bf16[520,128]{1,0:T(8,128)(2,1)S(1)}, u32[]{:S(2)}, u32[]{:S(2)}) collective-permute-start(bf16[520,128]{1,0:T(8,128)(2,1)S(1)} %get-tuple-element.5), channel_id=1, source_target_pairs={{0,8},{4,12},{8,0},{12,4},{1,9},{5,13},{9,1},{13,5},{2,10},{6,14},... | collective-permute-start | bytes 399368 | tf_op jit(solution)/shard_map/ppermute | solution.py:43
  22.0 3.4 %collective-permute-done = bf16[520,128]{1,0:T(8,128)(2,1)S(1)} collective-permute-done((bf16[520,128]{1,0:T(8,128)(2,1)S(1)}, bf16[520,128]{1,0:T(8,128)(2,1)S(1)}, u32[]{:S(2)}, u32[]{:S(2)}) %collective-permute-start) | collective-permute-done | bytes 133152 | tf_op jit(solution)/shard_map/ppermute | solution.py:43
  25.3 1.4 %collective-permute-done.2 = bf16[520,128]{1,0:T(8,128)(2,1)S(1)} collective-permute-done((bf16[520,128]{1,0:T(8,128)(2,1)S(1)}, bf16[520,128]{1,0:T(8,128)(2,1)S(1)}, u32[]{:S(2)}, u32[]{:S(2)}) %collective-permute-start.2) | collective-permute-done | bytes 133152 | tf_op jit(solution)/shard_map/ppermute | solution.py:43
  26.8 6.3 %collective-permute-done.1 = bf16[520,128]{1,0:T(8,128)(2,1)S(1)} collective-permute-done((bf16[520,128]{1,0:T(8,128)(2,1)S(1)}, bf16[520,128]{1,0:T(8,128)(2,1)S(1)}, u32[]{:S(2)}, u32[]{:S(2)}) %collective-permute-start.1) | collective-permute-done | bytes 133152 | tf_op jit(solution)/shard_map/ppermute | solution.py:43
  33.1 1.0 %reshape.104 = s32[2048,2]{1,0:T(8,128)S(1)} reshape(s32[4,8,128]{2,1,0:T(8,128)S(1)} %maximum_convert_fusion) | data formatting | bytes 32768 | tf_op jit(solution)/shard_map/convert_element_type | solution.py:98
  34.8 2.7 %fusion.1 = f32[1024,128]{1,0:T(8,128)S(1)} fusion(bf16[2048,128]{1,0:T(8,128)(2,1)S(1)} %bitcast.65, s32[2048]{0:T(1024)S(1)} %fusion.41), kind=kOutput, calls=%fused_computation.2 | convolution fusion | flops 538968064 | bytes 1056768 | tf_op jit(solution)/shard_map/dot_general | solution.py:16
  37.5 1.9 %collective-permute-done.3 = f32[1024,128]{1,0:T(8,128)S(1)} collective-permute-done((f32[1024,128]{1,0:T(8,128)S(1)}, f32[1024,128]{1,0:T(8,128)S(1)}, u32[]{:S(2)}, u32[]{:S(2)}) %collective-permute-start.3) | collective-permute-done | bytes 524320 | tf_op jit(solution)/shard_map/ppermute | solution.py:34
  39.6 1.7 %fusion.20 = bf16[2048,128]{1,0:T(8,128)(2,1)S(1)} fusion(bf16[1024,128]{1,0:T(8,128)(2,1)S(1)} %fusion.45, s32[2048]{0:T(1024)S(1)} %fusion.41), kind=kOutput, calls=%fused_computation.23 | convolution fusion | flops 539230208 | bytes 794624 | tf_op jit(solution)/shard_map/dot_general | solution.py:12
  41.4 2.2 %collective-permute-start.5 = (bf16[512,128]{1,0:T(8,128)(2,1)S(1)}, bf16[512,128]{1,0:T(8,128)(2,1)S(1)}, u32[]{:S(2)}, u32[]{:S(2)}) collective-permute-start(bf16[512,128]{1,0:T(8,128)(2,1)S(1)} %get-tuple-element.10), channel_id=1, source_target_pairs={{0,8},{4,12},{8,0},{12,4},{1,9},{5,13},{9,1},{13,5},{2,10},{6,14},... | collective-permute-start | bytes 393224 | tf_op jit(solution)/shard_map/ppermute | solution.py:43
  43.6 1.6 %collective-permute-start.4 = (bf16[512,128]{1,0:T(8,128)(2,1)S(1)}, bf16[512,128]{1,0:T(8,128)(2,1)S(1)}, u32[]{:S(2)}, u32[]{:S(2)}) collective-permute-start(bf16[512,128]{1,0:T(8,128)(2,1)S(1)} %get-tuple-element.11), channel_id=1, source_target_pairs={{0,12},{4,0},{8,4},{12,8},{1,13},{5,1},{9,5},{13,9},{2,14},{6,2},{... | collective-permute-start | bytes 393224 | tf_op jit(solution)/shard_map/ppermute | solution.py:43
  45.2 4.5 %collective-permute-done.6 = bf16[512,128]{1,0:T(8,128)(2,1)S(1)} collective-permute-done((bf16[512,128]{1,0:T(8,128)(2,1)S(1)}, bf16[512,128]{1,0:T(8,128)(2,1)S(1)}, u32[]{:S(2)}, u32[]{:S(2)}) %collective-permute-start.6) | collective-permute-done | bytes 131104 | tf_op jit(solution)/shard_map/ppermute | solution.py:43
  49.7 4.7 %collective-permute-done.5 = bf16[512,128]{1,0:T(8,128)(2,1)S(1)} collective-permute-done((bf16[512,128]{1,0:T(8,128)(2,1)S(1)}, bf16[512,128]{1,0:T(8,128)(2,1)S(1)}, u32[]{:S(2)}, u32[]{:S(2)}) %collective-permute-start.5) | collective-permute-done | bytes 131104 | tf_op jit(solution)/shard_map/ppermute | solution.py:43
  54.4 1.5 %fusion.40 = bf16[1024,128]{1,0:T(8,128)(2,1)S(1)} fusion(bf16[2048,128]{1,0:T(8,128)(2,1)S(1)} %bitcast.67, s32[1024]{0:T(1024)S(1)} %bitcast.79), kind=kOutput, calls=%fused_computation.37 | convolution fusion | flops 539099136 | bytes 790528 | tf_op jit(solution)/shard_map/dot_general | solution.py:12
  55.9 2.3 %fusion.33 = f32[1024,128]{1,0:T(8,128)S(1)} fusion(pred[1024,16]{0,1:T(8,128)(4,1)S(1)} %iota_compare_fusion.23, bf16[1024,128]{1,0:T(8,128)(2,1)S(1)} %fusion.40, bf16[16,128,128]{2,1,0:T(8,128)(2,1)S(1)} %copy-done), kind=kOutput, calls=%fused_computation.34 | convolution fusion | flops 538968064 | bytes 1327104 | tf_op jit(solution)/shard_map/dot_general | solution.py:12
  58.3 1.4 %fusion.14 = f32[1024,128]{1,0:T(8,128)S(1)} fusion(s32[1024]{0:T(1024)S(1)} %add.35, f32[1024,128]{1,0:T(8,128)S(1)} %fusion.33), kind=kOutput, calls=%fused_computation.17 | convolution fusion | flops 270008320 | bytes 1052672 | tf_op jit(solution)/shard_map/dot_general | solution.py:16
  59.7 1.4 %fusion.29 = f32[1024,128]{1,0:T(8,128)S(1)} fusion(f32[1024,128]{1,0:T(8,128)S(1)} %fusion.14, s32[1024]{0:T(1024)S(1)} %add.35, f32[1024,128]{1,0:T(8,128)S(1)} %fusion.33), kind=kOutput, calls=%fused_computation.32 | convolution fusion | flops 269746176 | bytes 1576960 | tf_op jit(solution)/shard_map/dot_general | solution.py:16
  61.2 1.6 %collective-permute-start.7 = (f32[128,512]{1,0:T(8,128)S(1)}, f32[128,512]{1,0:T(8,128)S(1)}, u32[]{:S(2)}, u32[]{:S(2)}) collective-permute-start(f32[128,512]{1,0:T(8,128)S(1)} %select_n.51), channel_id=1, source_target_pairs={{0,2},{2,0},{1,3},{3,1},{4,6},{6,4},{5,7},{7,5},{8,10},{10,8},{9,1... | collective-permute-start | bytes 786440 | tf_op jit(solution)/shard_map/ppermute | solution.py:123
  62.8 5.2 %collective-permute-done.7 = f32[128,512]{1,0:T(8,128)S(1)} collective-permute-done((f32[128,512]{1,0:T(8,128)S(1)}, f32[128,512]{1,0:T(8,128)S(1)}, u32[]{:S(2)}, u32[]{:S(2)}) %collective-permute-start.7) | collective-permute-done | bytes 262176 | tf_op jit(solution)/shard_map/ppermute | solution.py:123
  68.0 0.7 %add.42 = f32[128,512]{1,0:T(8,128)} add(f32[128,512]{1,0:T(8,128)S(1)} %select_n.49, f32[128,512]{1,0:T(8,128)S(1)} %collective-permute-done.7) | non-fusion elementwise | flops 65536 | bytes 786432 | tf_op jit(solution)/shard_map/add | solution.py:123
  (31 shorter events, 2.7 us)
Async XLA Ops:
  0.6 10.4 %copy-start = (bf16[16,128,128]{2,1,0:T(8,128)(2,1)S(1)}, bf16[16,128,128]{2,1,0:T(8,128)(2,1)}, u32[]{:S(2)}) copy-start(bf16[16,128,128]{2,1,0:T(8,128)(2,1)} %param.10) | copy-start | bytes 1572868
  9.2 1.0 %copy-start.4 = (s32[1024]{0:T(1024)S(1)}, s32[1024]{0:T(1024)}, u32[]{:S(2)}) copy-start(s32[1024]{0:T(1024)} %param.16) | copy-start | bytes 12292
  15.8 9.5 %collective-permute-start = (bf16[520,128]{1,0:T(8,128)(2,1)S(1)}, bf16[520,128]{1,0:T(8,128)(2,1)S(1)}, u32[]{:S(2)}, u32[]{:S(2)}) collective-permute-start(bf16[520,128]{1,0:T(8,128)(2,1)S(1)} %get-tuple-element.3), channel_id=1, source_target_pairs={{0,4},{4,8},{8,12},{12,0},{1,5},{5,9},{9,13},{13,1},{2,6},{6,10},{... | collective-permute-start | bytes 399368 | tf_op jit(solution)/shard_map/ppermute | solution.py:43
  18.9 7.9 %collective-permute-start.2 = (bf16[520,128]{1,0:T(8,128)(2,1)S(1)}, bf16[520,128]{1,0:T(8,128)(2,1)S(1)}, u32[]{:S(2)}, u32[]{:S(2)}) collective-permute-start(bf16[520,128]{1,0:T(8,128)(2,1)S(1)} %get-tuple-element.4), channel_id=1, source_target_pairs={{0,12},{4,0},{8,4},{12,8},{1,13},{5,1},{9,5},{13,9},{2,14},{6,2},{... | collective-permute-start | bytes 399368 | tf_op jit(solution)/shard_map/ppermute | solution.py:43
  21.2 11.9 %collective-permute-start.1 = (bf16[520,128]{1,0:T(8,128)(2,1)S(1)}, bf16[520,128]{1,0:T(8,128)(2,1)S(1)}, u32[]{:S(2)}, u32[]{:S(2)}) collective-permute-start(bf16[520,128]{1,0:T(8,128)(2,1)S(1)} %get-tuple-element.5), channel_id=1, source_target_pairs={{0,8},{4,12},{8,0},{12,4},{1,9},{5,13},{9,1},{13,5},{2,10},{6,14},... | collective-permute-start | bytes 399368 | tf_op jit(solution)/shard_map/ppermute | solution.py:43
  34.7 4.7 %copy-start.1 = (s32[1,1024,128]{2,1,0:T(8,128)S(1)}, s32[1,1024,128]{2,1,0:T(8,128)}, u32[]{:S(2)}) copy-start(s32[1,1024,128]{2,1,0:T(8,128)} %param.12) | copy-start | bytes 1572868
  34.7 4.7 %copy-start.2 = (bf16[1,1024,128]{2,1,0:T(8,128)(2,1)S(1)}, bf16[1,1024,128]{2,1,0:T(8,128)(2,1)}, u32[]{:S(2)}) copy-start(bf16[1,1024,128]{2,1,0:T(8,128)(2,1)} %param.11) | copy-start | bytes 786436
  37.5 2.0 %collective-permute-start.3 = (f32[1024,128]{1,0:T(8,128)S(1)}, f32[1024,128]{1,0:T(8,128)S(1)}, u32[]{:S(2)}, u32[]{:S(2)}) collective-permute-start(f32[1024,128]{1,0:T(8,128)S(1)} %fusion.1), channel_id=1, source_target_pairs={{0,1},{1,0},{2,3},{3,2},{4,5},{5,4},{6,7},{7,6},{8,9},{9,8},{10,11... | collective-permute-start | bytes 1572872 | tf_op jit(solution)/shard_map/ppermute | solution.py:34
  39.6 1.7 %copy-start.3 = (bf16[1024,128]{1,0:T(8,128)(2,1)}, bf16[1024,128]{1,0:T(8,128)(2,1)S(1)}, u32[]{:S(2)}) copy-start(bf16[1024,128]{1,0:T(8,128)(2,1)S(1)} %fusion.45) | copy-start | bytes 786436
  41.3 8.3 %collective-permute-start.6 = (bf16[512,128]{1,0:T(8,128)(2,1)S(1)}, bf16[512,128]{1,0:T(8,128)(2,1)S(1)}, u32[]{:S(2)}, u32[]{:S(2)}) collective-permute-start(bf16[512,128]{1,0:T(8,128)(2,1)S(1)} %get-tuple-element.9), channel_id=1, source_target_pairs={{0,4},{4,8},{8,12},{12,0},{1,5},{5,9},{9,13},{13,1},{2,6},{6,10},{... | collective-permute-start | bytes 393224 | tf_op jit(solution)/shard_map/ppermute | solution.py:43
  41.4 12.9 %collective-permute-start.5 = (bf16[512,128]{1,0:T(8,128)(2,1)S(1)}, bf16[512,128]{1,0:T(8,128)(2,1)S(1)}, u32[]{:S(2)}, u32[]{:S(2)}) collective-permute-start(bf16[512,128]{1,0:T(8,128)(2,1)S(1)} %get-tuple-element.10), channel_id=1, source_target_pairs={{0,8},{4,12},{8,0},{12,4},{1,9},{5,13},{9,1},{13,5},{2,10},{6,14},... | collective-permute-start | bytes 393224 | tf_op jit(solution)/shard_map/ppermute | solution.py:43
  43.6 10.8 %collective-permute-start.4 = (bf16[512,128]{1,0:T(8,128)(2,1)S(1)}, bf16[512,128]{1,0:T(8,128)(2,1)S(1)}, u32[]{:S(2)}, u32[]{:S(2)}) collective-permute-start(bf16[512,128]{1,0:T(8,128)(2,1)S(1)} %get-tuple-element.11), channel_id=1, source_target_pairs={{0,12},{4,0},{8,4},{12,8},{1,13},{5,1},{9,5},{13,9},{2,14},{6,2},{... | collective-permute-start | bytes 393224 | tf_op jit(solution)/shard_map/ppermute | solution.py:43
  61.2 6.8 %collective-permute-start.7 = (f32[128,512]{1,0:T(8,128)S(1)}, f32[128,512]{1,0:T(8,128)S(1)}, u32[]{:S(2)}, u32[]{:S(2)}) collective-permute-start(f32[128,512]{1,0:T(8,128)S(1)} %select_n.51), channel_id=1, source_target_pairs={{0,2},{2,0},{1,3},{3,1},{4,6},{6,4},{5,7},{7,5},{8,10},{10,8},{9,1... | collective-permute-start | bytes 786440 | tf_op jit(solution)/shard_map/ppermute | solution.py:123

commit v3 on v2

--- a/solution.py
+++ b/solution.py
@@ -69,8 +69,11 @@
     target = trace_tile[:, 0]
     kinds = psf_index
     spec_rows = trace_source[:, 0] * block_count + trace_block
-    member = (target[:, None] == jnp.arange(tile_count, dtype=jnp.int32)[None, :]).astype(jnp.int32)
-    position = jnp.sum((jnp.cumsum(member, axis=0) - 1) * member, axis=1)
+    member = one_hot_rows(target, tile_count)
+    entry_ids = jnp.arange(entry_count, dtype=jnp.int32)
+    up_to = (entry_ids[None, :] <= entry_ids[:, None]).astype(jnp.bfloat16)
+    running = select_dot(up_to, member)
+    position = jnp.sum((running - 1.0) * member.astype(jnp.float32), axis=1).astype(jnp.int32)
     shift = (target - lax.axis_index("tile")) % tile_count
     dest = shift * capacity + position
 
@@ -110,18 +113,21 @@
     entry_rows = select_dot(place, returned.reshape(send_count, pixel_count)).astype(jnp.bfloat16)
     back_table = psf_blocks.transpose(0, 2, 1).reshape(table_count * pixel_count, bin_count)
     terms = select_dot(spread_by_kind(entry_rows, kinds, table_count), back_table)
-    terms_hi = terms.astype(jnp.bfloat16)
-    terms_lo = (terms - terms_hi.astype(jnp.float32)).astype(jnp.bfloat16)
-    local_grad = select_dot_t(gather_spec, terms_hi) + select_dot_t(gather_spec, terms_lo)
-    local_grad = local_grad.reshape(source_count, block_count * bin_count)
+    terms = terms.astype(jnp.bfloat16)
 
     if dither_count == 2:
         dither = lax.axis_index("dither")
-        halves = local_grad.reshape(2, source_count // 2, block_count * bin_count)
-        mine = jnp.where(dither == 0, halves[0], halves[1])
-        theirs = jnp.where(dither == 0, halves[1], halves[0])
-        gradient = mine + lax.ppermute(theirs, "dither", [(0, 1), (1, 0)])
+        half_rows = row_count // 2
+        own_start = dither * half_rows
+        their_rows = one_hot_rows(spec_rows - (half_rows - own_start), half_rows)
+        own_rows = one_hot_rows(spec_rows - own_start, half_rows)
+        theirs = select_dot_t(their_rows, terms).reshape(source_count // 2, block_count * bin_count)
+        sent = lax.ppermute(theirs, "dither", [(0, 1), (1, 0)])
+        mine = select_dot_t(own_rows, terms).reshape(source_count // 2, block_count * bin_count)
+        gradient = mine + sent
     else:
+        local_grad = select_dot_t(gather_spec, terms)
+        local_grad = local_grad.reshape(source_count, block_count * bin_count)
         gradient = lax.psum_scatter(local_grad, "dither", scatter_dimension=0, tiled=True)
     return (gradient, residual[None])
 

time: 69.5 us -> 62.9 us (0.905)
  other arithmetic: 7.34 us -> 2.49 us
  local copies, waits for them, and re-layouts: 3.48 us -> 2.32 us
  waiting for transfers between devices: 27.3 us -> 26.4 us
    another operation x3 -> x1, other arithmetic: 2.01 us -> 0.01 us
    dot_general x4 -> x5, matrix products: 6.35 us -> 7.82 us  [select_dot(): jnp.dot(selector, values, preferred_element_type=jnp.float32, precision=p...]
    dot_general x5, matrix products: 11.8 us -> 10.7 us  [select_dot_t(): lax.dot_general(selector, values, (((0,), (0,)), ((), ())), preferred_ele...]
    reshape x1, local copies, waits for them, and re-layouts: 1.12 us -> 0.16 us  [per_device(): spectra.reshape(row_count, bin_count)]
    ppermute x1, waiting for transfers between devices: 5.21 us -> 4.31 us  [per_device(): sent = lax.ppermute(theirs, 'dither', [(0, 1), (1, 0)])]
    reduce_sum x1 -> x0, other arithmetic: 0.7 us -> none  [per_device(): position = jnp.sum((jnp.cumsum(member, axis=0) - 1) * member, axis=1)]
  transfers between devices with their start and end apart: 8 -> 8, of which waited for: 7 -> 7; matrix products, arithmetic and copies ran while one was open for 0% -> 1% of each run, Pallas kernels for 0% -> 0%
where the time goes in v3:
time: 62.9 us; the launch traced here: 62.4 us
  waiting for transfers between devices  26.4 us (42%)
  matrix products  18.6 us (30%)
  starting transfers between devices  11.6 us (18%)
  other arithmetic  2.49 us (4%)
  local copies, waits for them, and re-layouts  2.32 us (4%)
  between operations  0.94 us (1%)
    ppermute x6, waiting for transfers between devices, exchange(): moved.append(lax.ppermute(blocks[step], axis, pairs))  20.2 us
    dot_general x5, matrix products, select_dot_t(): lax.dot_general(selector, values, (((0,), (0,)), ((), ())), preferred_ele...  10.7 us
    ppermute x6, starting transfers between devices, exchange(): moved.append(lax.ppermute(blocks[step], axis, pairs))  9.99 us
    dot_general x5, matrix products, select_dot(): jnp.dot(selector, values, preferred_element_type=jnp.float32, precision=p...  7.82 us
    ppermute x1, waiting for transfers between devices, per_device(): sent = lax.ppermute(theirs, 'dither', [(0, 1), (1, 0)])  4.31 us
    ppermute x1, waiting for transfers between devices, swap_add(): return value + lax.ppermute(value, axis, [(0, 1), (1, 0)])  1.89 us
    ppermute x1, starting transfers between devices, per_device(): sent = lax.ppermute(theirs, 'dither', [(0, 1), (1, 0)])  1.55 us
  transfers between devices with their start and end apart: 8, of which 7 were waited for; matrix products, arithmetic and copies ran while one was open for 1% of the time, Pallas kernels for 0%

profile of v3, /device:TPU:0, one launch (start us, length us, event | category | flops | bytes accessed | tf_op | source)
XLA Modules:
  0.0 62.4 jit_solution(12144780459659786770)
XLA Ops:
  0.7 0.8 %broadcast_multiply_fusion = s32[1024,1]{0,1:T(1,128)S(1)} fusion(s32[1024,1]{0,1:T(1,128)} %param.15), kind=kLoop, calls=%fused_computation.96 | loop fusion | flops 1024 | bytes 8192 | tf_op jit(solution)/shard_map/mul | solution.py:71
  1.5 1.2 %fusion.44 = f32[1024]{0:T(1024)S(1)} fusion(s32[1024]{0:T(1024)} %bitcast.62), kind=kOutput, calls=%fused_computation.42 | convolution fusion | flops 9464832 | bytes 8192 | tf_op jit(solution)/shard_map/dot_general | solution.py:12
  2.8 0.2 reshape.87
  3.0 1.5 %fusion.20 = bf16[2048,2]{0,1:T(2,128)(2,1)S(1)} fusion(s32[1024]{0:T(1024)S(1)} %bitcast.63, bf16[1024,1]{0,1:T(2,128)(2,1)S(1)} %stack.37, bf16[1024,1]{0,1:T(2,128)(2,1)S(1)} %stack.36), kind=kOutput, calls=%fused_computation.24 | convolution fusion | flops 10498048 | bytes 16384 | tf_op jit(solution)/shard_map/dot_general | solution.py:16
  4.5 0.3 copy.12
  4.9 0.7 %reshape.89 = bf16[4,8,128]{2,1,0:T(8,128)(2,1)S(1)} reshape(bf16[2048,2]{1,0:T(8,128)(2,1)S(1)} %copy.12) | data formatting | bytes 16384 | tf_op jit(solution)/shard_map/reshape | solution.py:94
  5.5 0.8 %fusion.40 = bf16[1024,128]{1,0:T(8,128)(2,1)S(1)} fusion(bf16[1024,128]{1,0:T(8,128)(2,1)S(1)} %reshape.87, s32[1024]{0:T(1024)S(1)} %get-tuple-element.3), kind=kOutput, calls=%fused_computation.38 | convolution fusion | flops 269615104 | bytes 528384 | tf_op jit(solution)/shard_map/dot_general | solution.py:12
  6.4 4.8 %fusion.18 = bf16[2048,128]{1,0:T(8,128)(2,1)S(1)} fusion(s32[1024]{0:T(1024)S(1)} %bitcast.64, bf16[16,128,128]{2,1,0:T(8,128)(2,1)S(1)} %copy-done, pred[1024,16]{0,1:T(8,128)(4,1)S(1)} %iota_compare_fusion.31, bf16[1024,128]{1,0:T(8,128)(2,1)S(1)} %fusion.40), kind=kOutput, calls=%fused_computation.22 | convolution fusion | flops 1078329344 | bytes 1331200 | tf_op jit(solution)/shard_map/dot_general | solution.py:16
  11.2 3.1 %collective-permute-start = (bf16[520,128]{1,0:T(8,128)(2,1)S(1)}, bf16[520,128]{1,0:T(8,128)(2,1)S(1)}, u32[]{:S(2)}, u32[]{:S(2)}) collective-permute-start(bf16[520,128]{1,0:T(8,128)(2,1)S(1)} %get-tuple-element.5), channel_id=1, source_target_pairs={{0,4},{4,8},{8,12},{12,0},{1,5},{5,9},{9,13},{13,1},{2,6},{6,10},{... | collective-permute-start | bytes 399368 | tf_op jit(solution)/shard_map/ppermute | solution.py:43
  14.3 2.3 %collective-permute-start.2 = (bf16[520,128]{1,0:T(8,128)(2,1)S(1)}, bf16[520,128]{1,0:T(8,128)(2,1)S(1)}, u32[]{:S(2)}, u32[]{:S(2)}) collective-permute-start(bf16[520,128]{1,0:T(8,128)(2,1)S(1)} %get-tuple-element.6), channel_id=1, source_target_pairs={{0,12},{4,0},{8,4},{12,8},{1,13},{5,1},{9,5},{13,9},{2,14},{6,2},{... | collective-permute-start | bytes 399368 | tf_op jit(solution)/shard_map/ppermute | solution.py:43
  16.5 0.8 %collective-permute-start.1 = (bf16[520,128]{1,0:T(8,128)(2,1)S(1)}, bf16[520,128]{1,0:T(8,128)(2,1)S(1)}, u32[]{:S(2)}, u32[]{:S(2)}) collective-permute-start(bf16[520,128]{1,0:T(8,128)(2,1)S(1)} %get-tuple-element.7), channel_id=1, source_target_pairs={{0,8},{4,12},{8,0},{12,4},{1,9},{5,13},{9,1},{13,5},{2,10},{6,14},... | collective-permute-start | bytes 399368 | tf_op jit(solution)/shard_map/ppermute | solution.py:43
  17.3 3.4 %collective-permute-done = bf16[520,128]{1,0:T(8,128)(2,1)S(1)} collective-permute-done((bf16[520,128]{1,0:T(8,128)(2,1)S(1)}, bf16[520,128]{1,0:T(8,128)(2,1)S(1)}, u32[]{:S(2)}, u32[]{:S(2)}) %collective-permute-start) | collective-permute-done | bytes 133152 | tf_op jit(solution)/shard_map/ppermute | solution.py:43
  20.7 1.4 %collective-permute-done.2 = bf16[520,128]{1,0:T(8,128)(2,1)S(1)} collective-permute-done((bf16[520,128]{1,0:T(8,128)(2,1)S(1)}, bf16[520,128]{1,0:T(8,128)(2,1)S(1)}, u32[]{:S(2)}, u32[]{:S(2)}) %collective-permute-start.2) | collective-permute-done | bytes 133152 | tf_op jit(solution)/shard_map/ppermute | solution.py:43
  22.1 6.3 %collective-permute-done.1 = bf16[520,128]{1,0:T(8,128)(2,1)S(1)} collective-permute-done((bf16[520,128]{1,0:T(8,128)(2,1)S(1)}, bf16[520,128]{1,0:T(8,128)(2,1)S(1)}, u32[]{:S(2)}, u32[]{:S(2)}) %collective-permute-start.1) | collective-permute-done | bytes 133152 | tf_op jit(solution)/shard_map/ppermute | solution.py:43
  28.4 1.0 %reshape.94 = s32[2048,2]{1,0:T(8,128)S(1)} reshape(s32[4,8,128]{2,1,0:T(8,128)S(1)} %maximum_convert_fusion) | data formatting | bytes 32768 | tf_op jit(solution)/shard_map/convert_element_type | solution.py:101
  29.5 0.6 %fusion.45 = s32[2048]{0:T(1024)S(1)} fusion(s32[2048,2]{1,0:T(8,128)S(1)} %reshape.94), kind=kLoop, calls=%fused_computation.44 | loop fusion | flops 4096 | bytes 24576 | tf_op jit(solution)/shard_map/add | solution.py:102
  30.1 2.7 %fusion.1 = f32[1024,128]{1,0:T(8,128)S(1)} fusion(bf16[2048,128]{1,0:T(8,128)(2,1)S(1)} %bitcast.53, s32[2048]{0:T(1024)S(1)} %fusion.45), kind=kOutput, calls=%fused_computation.2 | convolution fusion | flops 538968064 | bytes 1056768 | tf_op jit(solution)/shard_map/dot_general | solution.py:16
  32.8 0.1 collective-permute-start.3
  32.9 1.9 %collective-permute-done.3 = f32[1024,128]{1,0:T(8,128)S(1)} collective-permute-done((f32[1024,128]{1,0:T(8,128)S(1)}, f32[1024,128]{1,0:T(8,128)S(1)}, u32[]{:S(2)}, u32[]{:S(2)}) %collective-permute-start.3) | collective-permute-done | bytes 524320 | tf_op jit(solution)/shard_map/ppermute | solution.py:34
  34.8 0.1 fusion.51
  35.0 1.7 %fusion.19 = bf16[2048,128]{1,0:T(8,128)(2,1)S(1)} fusion(bf16[1024,128]{1,0:T(8,128)(2,1)S(1)} %fusion.51, s32[2048]{0:T(1024)S(1)} %fusion.45), kind=kOutput, calls=%fused_computation.23 | convolution fusion | flops 539230208 | bytes 794624 | tf_op jit(solution)/shard_map/dot_general | solution.py:12
  36.8 2.2 %collective-permute-start.5 = (bf16[512,128]{1,0:T(8,128)(2,1)S(1)}, bf16[512,128]{1,0:T(8,128)(2,1)S(1)}, u32[]{:S(2)}, u32[]{:S(2)}) collective-permute-start(bf16[512,128]{1,0:T(8,128)(2,1)S(1)} %get-tuple-element.10), channel_id=1, source_target_pairs={{0,8},{4,12},{8,0},{12,4},{1,9},{5,13},{9,1},{13,5},{2,10},{6,14},... | collective-permute-start | bytes 393224 | tf_op jit(solution)/shard_map/ppermute | solution.py:43
  39.0 1.6 %collective-permute-start.4 = (bf16[512,128]{1,0:T(8,128)(2,1)S(1)}, bf16[512,128]{1,0:T(8,128)(2,1)S(1)}, u32[]{:S(2)}, u32[]{:S(2)}) collective-permute-start(bf16[512,128]{1,0:T(8,128)(2,1)S(1)} %get-tuple-element.11), channel_id=1, source_target_pairs={{0,12},{4,0},{8,4},{12,8},{1,13},{5,1},{9,5},{13,9},{2,14},{6,2},{... | collective-permute-start | bytes 393224 | tf_op jit(solution)/shard_map/ppermute | solution.py:43
  40.6 4.5 %collective-permute-done.6 = bf16[512,128]{1,0:T(8,128)(2,1)S(1)} collective-permute-done((bf16[512,128]{1,0:T(8,128)(2,1)S(1)}, bf16[512,128]{1,0:T(8,128)(2,1)S(1)}, u32[]{:S(2)}, u32[]{:S(2)}) %collective-permute-start.6) | collective-permute-done | bytes 131104 | tf_op jit(solution)/shard_map/ppermute | solution.py:43
  45.0 4.7 %collective-permute-done.5 = bf16[512,128]{1,0:T(8,128)(2,1)S(1)} collective-permute-done((bf16[512,128]{1,0:T(8,128)(2,1)S(1)}, bf16[512,128]{1,0:T(8,128)(2,1)S(1)}, u32[]{:S(2)}, u32[]{:S(2)}) %collective-permute-start.5) | collective-permute-done | bytes 131104 | tf_op jit(solution)/shard_map/ppermute | solution.py:43
  49.8 1.5 %fusion.41 = bf16[1024,128]{1,0:T(8,128)(2,1)S(1)} fusion(bf16[2048,128]{1,0:T(8,128)(2,1)S(1)} %bitcast.55, s32[1024]{0:T(1024)S(1)} %bitcast.65), kind=kOutput, calls=%fused_computation.39 | convolution fusion | flops 539099136 | bytes 790528 | tf_op jit(solution)/shard_map/dot_general | solution.py:12
  51.3 2.6 %fusion.34 = bf16[1024,128]{1,0:T(8,128)(2,1)S(1)} fusion(pred[1024,16]{0,1:T(8,128)(4,1)S(1)} %iota_compare_fusion.31, bf16[1024,128]{1,0:T(8,128)(2,1)S(1)} %fusion.41, bf16[16,128,128]{2,1,0:T(8,128)(2,1)S(1)} %copy-done), kind=kOutput, calls=%fused_computation.36 | convolution fusion | flops 539099136 | bytes 1064960 | tf_op jit(solution)/shard_map/dot_general | solution.py:12
  53.9 0.9 %fusion.27 = f32[512,128]{1,0:T(8,128)S(1)} fusion(bf16[1024,128]{1,0:T(8,128)(2,1)S(1)} %fusion.34, s32[1024]{0:T(1024)S(1)} %get-tuple-element.2), kind=kOutput, calls=%fused_computation.33 | convolution fusion | flops 134742016 | bytes 528384 | tf_op jit(solution)/shard_map/dot_general | solution.py:16
  54.8 1.6 %collective-permute-start.7 = (f32[128,512]{1,0:T(8,128)S(1)}, f32[128,512]{1,0:T(8,128)S(1)}, u32[]{:S(2)}, u32[]{:S(2)}) collective-permute-start(f32[128,512]{1,0:T(8,128)S(1)} %reshape.93), channel_id=1, source_target_pairs={{0,2},{2,0},{1,3},{3,1},{4,6},{6,4},{5,7},{7,5},{8,10},{10,8},{9,1... | collective-permute-start | bytes 786440 | tf_op jit(solution)/shard_map/ppermute | solution.py:125
  56.4 0.9 %fusion.26 = f32[512,128]{1,0:T(8,128)S(1)} fusion(bf16[1024,128]{1,0:T(8,128)(2,1)S(1)} %fusion.34, s32[1024]{0:T(1024)S(1)} %broadcast_subtract_fusion.1), kind=kOutput, calls=%fused_computation.32 | convolution fusion | flops 134742016 | bytes 528384 | tf_op jit(solution)/shard_map/dot_general | solution.py:16
  57.3 4.3 %collective-permute-done.7 = f32[128,512]{1,0:T(8,128)S(1)} collective-permute-done((f32[128,512]{1,0:T(8,128)S(1)}, f32[128,512]{1,0:T(8,128)S(1)}, u32[]{:S(2)}, u32[]{:S(2)}) %collective-permute-start.7) | collective-permute-done | bytes 262176 | tf_op jit(solution)/shard_map/ppermute | solution.py:125
  61.6 0.7 %add.36 = f32[128,512]{1,0:T(8,128)} add(f32[128,512]{1,0:T(8,128)S(1)} %reshape.92, f32[128,512]{1,0:T(8,128)S(1)} %collective-permute-done.7) | non-fusion elementwise | flops 65536 | bytes 786432 | tf_op jit(solution)/shard_map/add | solution.py:127
  (35 shorter events, 0.5 us)
Async XLA Ops:
  0.6 5.7 %copy-start = (bf16[16,128,128]{2,1,0:T(8,128)(2,1)S(1)}, bf16[16,128,128]{2,1,0:T(8,128)(2,1)}, u32[]{:S(2)}) copy-start(bf16[16,128,128]{2,1,0:T(8,128)(2,1)} %param.10) | copy-start | bytes 1572868
  0.6 2.3 %copy-start.6 = (s32[1024,1]{0,1:T(1,128)S(1)}, s32[1024,1]{0,1:T(1,128)}, u32[]{:S(2)}) copy-start(s32[1024,1]{0,1:T(1,128)} %param.13) | copy-start | bytes 12292
  0.7 2.1 %copy-start.7 = (s32[1024]{0:T(1024)S(1)}, s32[1024]{0:T(1024)}, u32[]{:S(2)}) copy-start(s32[1024]{0:T(1024)} %param.14) | copy-start | bytes 12292
  0.7 2.1 %copy-start.5 = (s32[1024]{0:T(1024)S(1)}, s32[1024]{0:T(1024)}, u32[]{:S(2)}) copy-start(s32[1024]{0:T(1024)} %param.17) | copy-start | bytes 12292
  0.7 2.1 %copy-start.2 = (bf16[256,512]{1,0:T(8,128)(2,1)S(1)}, bf16[256,512]{1,0:T(8,128)(2,1)}, u32[]{:S(2)}) copy-start(bf16[256,512]{1,0:T(8,128)(2,1)} %param.9) | copy-start | bytes 786436
  4.5 1.0 %copy-start.8 = (s32[1024]{0:T(1024)S(1)}, s32[1024]{0:T(1024)}, u32[]{:S(2)}) copy-start(s32[1024]{0:T(1024)} %param.16) | copy-start | bytes 12292
  11.2 9.5 %collective-permute-start = (bf16[520,128]{1,0:T(8,128)(2,1)S(1)}, bf16[520,128]{1,0:T(8,128)(2,1)S(1)}, u32[]{:S(2)}, u32[]{:S(2)}) collective-permute-start(bf16[520,128]{1,0:T(8,128)(2,1)S(1)} %get-tuple-element.5), channel_id=1, source_target_pairs={{0,4},{4,8},{8,12},{12,0},{1,5},{5,9},{9,13},{13,1},{2,6},{6,10},{... | collective-permute-start | bytes 399368 | tf_op jit(solution)/shard_map/ppermute | solution.py:43
  14.3 7.9 %collective-permute-start.2 = (bf16[520,128]{1,0:T(8,128)(2,1)S(1)}, bf16[520,128]{1,0:T(8,128)(2,1)S(1)}, u32[]{:S(2)}, u32[]{:S(2)}) collective-permute-start(bf16[520,128]{1,0:T(8,128)(2,1)S(1)} %get-tuple-element.6), channel_id=1, source_target_pairs={{0,12},{4,0},{8,4},{12,8},{1,13},{5,1},{9,5},{13,9},{2,14},{6,2},{... | collective-permute-start | bytes 399368 | tf_op jit(solution)/shard_map/ppermute | solution.py:43
  16.5 11.9 %collective-permute-start.1 = (bf16[520,128]{1,0:T(8,128)(2,1)S(1)}, bf16[520,128]{1,0:T(8,128)(2,1)S(1)}, u32[]{:S(2)}, u32[]{:S(2)}) collective-permute-start(bf16[520,128]{1,0:T(8,128)(2,1)S(1)} %get-tuple-element.7), channel_id=1, source_target_pairs={{0,8},{4,12},{8,0},{12,4},{1,9},{5,13},{9,1},{13,5},{2,10},{6,14},... | collective-permute-start | bytes 399368 | tf_op jit(solution)/shard_map/ppermute | solution.py:43
  30.1 4.7 %copy-start.1 = (s32[1,1024,128]{2,1,0:T(8,128)S(1)}, s32[1,1024,128]{2,1,0:T(8,128)}, u32[]{:S(2)}) copy-start(s32[1,1024,128]{2,1,0:T(8,128)} %param.12) | copy-start | bytes 1572868
  30.1 4.7 %copy-start.3 = (bf16[1,1024,128]{2,1,0:T(8,128)(2,1)S(1)}, bf16[1,1024,128]{2,1,0:T(8,128)(2,1)}, u32[]{:S(2)}) copy-start(bf16[1,1024,128]{2,1,0:T(8,128)(2,1)} %param.11) | copy-start | bytes 786436
  32.8 2.0 %collective-permute-start.3 = (f32[1024,128]{1,0:T(8,128)S(1)}, f32[1024,128]{1,0:T(8,128)S(1)}, u32[]{:S(2)}, u32[]{:S(2)}) collective-permute-start(f32[1024,128]{1,0:T(8,128)S(1)} %fusion.1), channel_id=1, source_target_pairs={{0,1},{1,0},{2,3},{3,2},{4,5},{5,4},{6,7},{7,6},{8,9},{9,8},{10,11... | collective-permute-start | bytes 1572872 | tf_op jit(solution)/shard_map/ppermute | solution.py:34
  34.9 1.7 %copy-start.4 = (bf16[1024,128]{1,0:T(8,128)(2,1)}, bf16[1024,128]{1,0:T(8,128)(2,1)S(1)}, u32[]{:S(2)}) copy-start(bf16[1024,128]{1,0:T(8,128)(2,1)S(1)} %fusion.51) | copy-start | bytes 786436
  36.7 8.3 %collective-permute-start.6 = (bf16[512,128]{1,0:T(8,128)(2,1)S(1)}, bf16[512,128]{1,0:T(8,128)(2,1)S(1)}, u32[]{:S(2)}, u32[]{:S(2)}) collective-permute-start(bf16[512,128]{1,0:T(8,128)(2,1)S(1)} %get-tuple-element.9), channel_id=1, source_target_pairs={{0,4},{4,8},{8,12},{12,0},{1,5},{5,9},{9,13},{13,1},{2,6},{6,10},{... | collective-permute-start | bytes 393224 | tf_op jit(solution)/shard_map/ppermute | solution.py:43
  36.8 12.9 %collective-permute-start.5 = (bf16[512,128]{1,0:T(8,128)(2,1)S(1)}, bf16[512,128]{1,0:T(8,128)(2,1)S(1)}, u32[]{:S(2)}, u32[]{:S(2)}) collective-permute-start(bf16[512,128]{1,0:T(8,128)(2,1)S(1)} %get-tuple-element.10), channel_id=1, source_target_pairs={{0,8},{4,12},{8,0},{12,4},{1,9},{5,13},{9,1},{13,5},{2,10},{6,14},... | collective-permute-start | bytes 393224 | tf_op jit(solution)/shard_map/ppermute | solution.py:43
  39.0 10.8 %collective-permute-start.4 = (bf16[512,128]{1,0:T(8,128)(2,1)S(1)}, bf16[512,128]{1,0:T(8,128)(2,1)S(1)}, u32[]{:S(2)}, u32[]{:S(2)}) collective-permute-start(bf16[512,128]{1,0:T(8,128)(2,1)S(1)} %get-tuple-element.11), channel_id=1, source_target_pairs={{0,12},{4,0},{8,4},{12,8},{1,13},{5,1},{9,5},{13,9},{2,14},{6,2},{... | collective-permute-start | bytes 393224 | tf_op jit(solution)/shard_map/ppermute | solution.py:43
  54.8 6.8 %collective-permute-start.7 = (f32[128,512]{1,0:T(8,128)S(1)}, f32[128,512]{1,0:T(8,128)S(1)}, u32[]{:S(2)}, u32[]{:S(2)}) collective-permute-start(f32[128,512]{1,0:T(8,128)S(1)} %reshape.93), channel_id=1, source_target_pairs={{0,2},{2,0},{1,3},{3,1},{4,6},{6,4},{5,7},{7,5},{8,10},{10,8},{9,1... | collective-permute-start | bytes 786440 | tf_op jit(solution)/shard_map/ppermute | solution.py:125

commit v4 on v3

--- a/solution.py
+++ b/solution.py
@@ -41,7 +41,7 @@
     for step in range(1, count):
         pairs = [(j, (j + direction * step) % count) for j in range(count)]
         moved.append(lax.ppermute(blocks[step], axis, pairs))
-    return jnp.stack(moved)
+    return moved
 
 
 def per_device(
@@ -81,36 +81,33 @@
     spec_values = select_dot(gather_spec, spectra.reshape(row_count, bin_count)).astype(jnp.bfloat16)
     psf_flat = psf_blocks.reshape(table_count * bin_count, pixel_count)
     traces = select_dot(spread_by_kind(spec_values, kinds, table_count), psf_flat).astype(jnp.bfloat16)
-    place = one_hot_rows(dest, send_count)
-    send_traces = select_dot_t(place, traces).astype(jnp.bfloat16)
     slot_parts = jnp.stack([trace_slot // 256, trace_slot % 256], axis=1).astype(jnp.bfloat16)
-    send_slots = select_dot_t(place, slot_parts).astype(jnp.bfloat16)
     code_rows = -(-2 * capacity // pixel_count)
-    send_slots = send_slots.reshape(tile_count, 2 * capacity)
-    send_slots = jnp.pad(send_slots, ((0, 0), (0, code_rows * pixel_count - 2 * capacity)))
-    send = jnp.concatenate(
-        [
-            send_traces.reshape(tile_count, capacity, pixel_count),
-            send_slots.reshape(tile_count, code_rows, pixel_count),
-        ],
-        axis=1,
-    )
+    places = [one_hot_rows(dest - step * capacity, capacity) for step in range(tile_count)]
+    send = []
+    for step in range(tile_count):
+        codes = select_dot_t(slot_parts, places[step]).astype(jnp.bfloat16).reshape(2 * capacity)
+        codes = jnp.pad(codes, (0, code_rows * pixel_count - 2 * capacity))
+        block = select_dot_t(places[step], traces).astype(jnp.bfloat16)
+        send.append(jnp.concatenate([block, codes.reshape(code_rows, pixel_count)], axis=0))
     got = exchange(send, "tile", 1)
-    got_traces = got[:, :capacity].reshape(send_count, pixel_count)
-    got_codes = got[:, capacity:].reshape(tile_count, code_rows * pixel_count)[:, : 2 * capacity]
-    got_codes = got_codes.astype(jnp.int32).reshape(send_count, 2)
-    got_slots = got_codes[:, 0] * 256 + got_codes[:, 1]
+    got_traces = [block[:capacity] for block in got]
+    got_slots = []
+    for block in got:
+        codes = block[capacity:].reshape(code_rows * pixel_count)[: 2 * capacity]
+        codes = codes.astype(jnp.int32).reshape(2, capacity)
+        got_slots.append(codes[0] * 256 + codes[1])
 
-    at_slot = one_hot_rows(got_slots, slot_count)
-    partial_value = select_dot_t(at_slot, got_traces)
+    at_slot = [one_hot_rows(slots, slot_count) for slots in got_slots]
+    partial_value = sum(select_dot_t(a, b) for a, b in zip(at_slot, got_traces))
     model_image = swap_add(partial_value, "band")
     residual = (
         bad_mask[0].astype(jnp.float32) * (model_image - observed[0].astype(jnp.float32))
     ).astype(jnp.bfloat16)
 
-    under_rows = select_dot(at_slot, residual).astype(jnp.bfloat16)
-    returned = exchange(under_rows.reshape(tile_count, capacity, pixel_count), "tile", -1)
-    entry_rows = select_dot(place, returned.reshape(send_count, pixel_count)).astype(jnp.bfloat16)
+    under_rows = [select_dot(a, residual).astype(jnp.bfloat16) for a in at_slot]
+    returned = exchange(under_rows, "tile", -1)
+    entry_rows = sum(select_dot(p, r) for p, r in zip(places, returned)).astype(jnp.bfloat16)
     back_table = psf_blocks.transpose(0, 2, 1).reshape(table_count * pixel_count, bin_count)
     terms = select_dot(spread_by_kind(entry_rows, kinds, table_count), back_table)
     terms = terms.astype(jnp.bfloat16)
@@ -122,9 +119,9 @@
         their_rows = one_hot_rows(spec_rows - (half_rows - own_start), half_rows)
         own_rows = one_hot_rows(spec_rows - own_start, half_rows)
         theirs = select_dot_t(their_rows, terms).reshape(source_count // 2, block_count * bin_count)
-        sent = lax.ppermute(theirs, "dither", [(0, 1), (1, 0)])
+        sent = lax.ppermute(theirs.astype(jnp.bfloat16), "dither", [(0, 1), (1, 0)])
         mine = select_dot_t(own_rows, terms).reshape(source_count // 2, block_count * bin_count)
-        gradient = mine + sent
+        gradient = mine + sent.astype(jnp.float32)
     else:
         local_grad = select_dot_t(gather_spec, terms)
         local_grad = local_grad.reshape(source_count, block_count * bin_count)

time: 62.9 us -> 56.7 us (0.901)
  waiting for transfers between devices: 26.4 us -> 18.3 us
  matrix products: 18.6 us -> 22.4 us
  local copies, waits for them, and re-layouts: 2.32 us -> 0.67 us
  other arithmetic: 2.49 us -> 1.76 us
  starting transfers between devices: 11.6 us -> 12.3 us
    ppermute x6, waiting for transfers between devices: 20.2 us -> 13.9 us  [exchange(): moved.append(lax.ppermute(blocks[step], axis, pairs))]
    dot_general x5 -> x11, matrix products: 7.82 us -> 12 us  [select_dot(): jnp.dot(selector, values, preferred_element_type=jnp.float32, precision=p...]
    ppermute x1, waiting for transfers between devices: 4.31 us -> 2.55 us  [per_device(): sent = lax.ppermute(theirs.astype(jnp.bfloat16), 'dither', [(0, 1), (1, 0)])]
    convert_element_type x2 -> x1, local copies, waits for them, and re-layouts: 1.32 us -> 0.09 us  [per_device(): sent = lax.ppermute(theirs.astype(jnp.bfloat16), 'dither', [(0, 1), (1, 0)])]
    ppermute x6, starting transfers between devices: 9.99 us -> 10.7 us  [exchange(): moved.append(lax.ppermute(blocks[step], axis, pairs))]
    reshape x2 -> x3, local copies, waits for them, and re-layouts: 0.7 us -> 0.04 us  [per_device(): codes.reshape(code_rows, pixel_count)]
    add x3 -> x5, other arithmetic: 1.4 us -> 0.76 us  [the longest x1 0.73 us: per_device(): gradient = mine + sent.astype(jnp.float32)]
    dot_general x5 -> x13, matrix products: 10.7 us -> 10.4 us  [select_dot_t(): lax.dot_general(selector, values, (((0,), (0,)), ((), ())), preferred_ele...]
  transfers between devices with their start and end apart: 8 -> 8, of which waited for: 7 -> 6; matrix products, arithmetic and copies ran while one was open for 1% -> 14% of each run, Pallas kernels for 0% -> 0%
where the time goes in v4:
time: 56.7 us; the launch traced here: 56.4 us
  matrix products  22.4 us (40%)
  waiting for transfers between devices  18.3 us (32%)
  starting transfers between devices  12.3 us (22%)
  other arithmetic  1.76 us (3%)
  between operations  1.02 us (2%)
  local copies, waits for them, and re-layouts  0.67 us (1%)
    ppermute x6, waiting for transfers between devices, exchange(): moved.append(lax.ppermute(blocks[step], axis, pairs))  13.9 us
    dot_general x11, matrix products, select_dot(): jnp.dot(selector, values, preferred_element_type=jnp.float32, precision=p...  12 us
    ppermute x6, starting transfers between devices, exchange(): moved.append(lax.ppermute(blocks[step], axis, pairs))  10.7 us
    dot_general x13, matrix products, select_dot_t(): lax.dot_general(selector, values, (((0,), (0,)), ((), ())), preferred_ele...  10.4 us
    ppermute x1, waiting for transfers between devices, per_device(): sent = lax.ppermute(theirs.astype(jnp.bfloat16), 'dither', [(0, 1), (1, 0)])  2.55 us
    ppermute x1, waiting for transfers between devices, swap_add(): return value + lax.ppermute(value, axis, [(0, 1), (1, 0)])  1.89 us
    ppermute x1, starting transfers between devices, per_device(): sent = lax.ppermute(theirs.astype(jnp.bfloat16), 'dither', [(0, 1), (1, 0)])  1.56 us
  transfers between devices with their start and end apart: 8, of which 6 were waited for; matrix products, arithmetic and copies ran while one was open for 14% of the time, Pallas kernels for 0%

profile of v4, /device:TPU:0, one launch (start us, length us, event | category | flops | bytes accessed | tf_op | source)
XLA Modules:
  0.0 56.4 jit_solution(5676786110672479001)
XLA Ops:
  0.7 0.7 %broadcast_multiply_fusion = s32[1024,1]{0,1:T(1,128)S(1)} fusion(s32[1024,1]{0,1:T(1,128)} %param.15), kind=kLoop, calls=%fused_computation.143 | loop fusion | flops 1024 | bytes 8192 | tf_op jit(solution)/shard_map/mul | solution.py:71
  1.4 1.3 %fusion.66 = f32[1024]{0:T(1024)S(1)} fusion(s32[1024]{0:T(1024)} %bitcast.65), kind=kOutput, calls=%fused_computation.70 | convolution fusion | flops 9464832 | bytes 8192 | tf_op jit(solution)/shard_map/dot_general | solution.py:12
  3.8 0.8 %fusion.54 = bf16[1024,128]{1,0:T(8,128)(2,1)S(1)} fusion(bf16[1024,128]{1,0:T(8,128)(2,1)S(1)} %reshape.145, s32[1024]{0:T(1024)S(1)} %get-tuple-element.3), kind=kOutput, calls=%fused_computation.58 | convolution fusion | flops 269615104 | bytes 528384 | tf_op jit(solution)/shard_map/dot_general | solution.py:12
  4.7 3.0 %fusion.51 = bf16[1024,128]{1,0:T(8,128)(2,1)S(1)} fusion(bf16[16,128,128]{2,1,0:T(8,128)(2,1)S(1)} %copy-done, pred[1024,16]{0,1:T(8,128)(4,1)S(1)} %iota_compare_fusion.90, bf16[1024,128]{1,0:T(8,128)(2,1)S(1)} %fusion.54), kind=kOutput, calls=%fused_computation.57 | convolution fusion | flops 539099136 | bytes 1064960 | tf_op jit(solution)/shard_map/dot_general | solution.py:12
  7.7 0.9 %fusion.58 = bf16[512,128]{1,0:T(8,128)(2,1)S(1)} fusion(bf16[1024,128]{1,0:T(8,128)(2,1)S(1)} %fusion.51, s32[1024]{0:T(1024)S(1)} %bitcast.52), kind=kOutput, calls=%fused_computation.62 | convolution fusion | flops 134807552 | bytes 397312 | tf_op jit(solution)/shard_map/dot_general | solution.py:16
  8.6 3.1 %collective-permute-start = (bf16[520,128]{1,0:T(8,128)(2,1)S(1)}, bf16[520,128]{1,0:T(8,128)(2,1)S(1)}, u32[]{:S(2)}, u32[]{:S(2)}) collective-permute-start(bf16[520,128]{1,0:T(8,128)(2,1)S(1)} %pad_maximum_fusion), channel_id=1, source_target_pairs={{0,4},{4,8},{8,12},{12,0},{1,5},{5,9},{9,13},{13,1},{2,6},{6,10},{... | collective-permute-start | bytes 399368 | tf_op jit(solution)/shard_map/ppermute | solution.py:43
  12.2 0.9 %fusion.60 = bf16[512,128]{1,0:T(8,128)(2,1)S(1)} fusion(bf16[1024,128]{1,0:T(8,128)(2,1)S(1)} %fusion.51, s32[1024]{0:T(1024)S(1)} %bitcast.60), kind=kOutput, calls=%fused_computation.64 | convolution fusion | flops 134807552 | bytes 397312 | tf_op jit(solution)/shard_map/dot_general | solution.py:16
  13.1 2.7 %collective-permute-start.1 = (bf16[520,128]{1,0:T(8,128)(2,1)S(1)}, bf16[520,128]{1,0:T(8,128)(2,1)S(1)}, u32[]{:S(2)}, u32[]{:S(2)}) collective-permute-start(bf16[520,128]{1,0:T(8,128)(2,1)S(1)} %pad_maximum_fusion.1), channel_id=1, source_target_pairs={{0,8},{4,12},{8,0},{12,4},{1,9},{5,13},{9,1},{13,5},{2,10},{6,14},... | collective-permute-start | bytes 399368 | tf_op jit(solution)/shard_map/ppermute | solution.py:43
  16.2 0.9 %fusion.62 = bf16[512,128]{1,0:T(8,128)(2,1)S(1)} fusion(bf16[1024,128]{1,0:T(8,128)(2,1)S(1)} %fusion.51, s32[1024]{0:T(1024)S(1)} %bitcast.63), kind=kOutput, calls=%fused_computation.66 | convolution fusion | flops 134807552 | bytes 397312 | tf_op jit(solution)/shard_map/dot_general | solution.py:16
  17.2 1.4 %collective-permute-start.2 = (bf16[520,128]{1,0:T(8,128)(2,1)S(1)}, bf16[520,128]{1,0:T(8,128)(2,1)S(1)}, u32[]{:S(2)}, u32[]{:S(2)}) collective-permute-start(bf16[520,128]{1,0:T(8,128)(2,1)S(1)} %pad_maximum_fusion.2), channel_id=1, source_target_pairs={{0,12},{4,0},{8,4},{12,8},{1,13},{5,1},{9,5},{13,9},{2,14},{6,2},{... | collective-permute-start | bytes 399368 | tf_op jit(solution)/shard_map/ppermute | solution.py:43
  19.1 1.5 %fusion.29 = f32[1024,128]{1,0:T(8,128)S(1)} fusion(bf16[1024,128]{1,0:T(8,128)(2,1)S(1)} %fusion.51, s32[512]{0:T(512)S(1)} %bitcast.66, s32[1024]{0:T(1024)S(1)} %bitcast.55), kind=kOutput, calls=%fused_computation.39 | convolution fusion | flops 269549568 | bytes 792576 | tf_op jit(solution)/shard_map/dot_general | solution.py:16
  20.7 2.4 %collective-permute-done.1 = bf16[520,128]{1,0:T(8,128)(2,1)S(1)} collective-permute-done((bf16[520,128]{1,0:T(8,128)(2,1)S(1)}, bf16[520,128]{1,0:T(8,128)(2,1)S(1)}, u32[]{:S(2)}, u32[]{:S(2)}) %collective-permute-start.1) | collective-permute-done | bytes 133152 | tf_op jit(solution)/shard_map/ppermute | solution.py:43
  23.1 1.5 %collective-permute-done.2 = bf16[520,128]{1,0:T(8,128)(2,1)S(1)} collective-permute-done((bf16[520,128]{1,0:T(8,128)(2,1)S(1)}, bf16[520,128]{1,0:T(8,128)(2,1)S(1)}, u32[]{:S(2)}, u32[]{:S(2)}) %collective-permute-start.2) | collective-permute-done | bytes 133152 | tf_op jit(solution)/shard_map/ppermute | solution.py:43
  24.6 0.8 %fusion.10 = f32[1024,128]{1,0:T(8,128)S(1)} fusion(s32[512]{0:T(512)S(1)} %add_bitcast_fusion, bf16[520,128]{1,0:T(8,128)(2,1)S(1)} %collective-permute-done.2), kind=kOutput, calls=%fused_computation.14 | convolution fusion | flops 134742016 | bytes 657408 | tf_op jit(solution)/shard_map/dot_general | solution.py:16
  25.5 0.8 %fusion.15 = f32[1024,128]{1,0:T(8,128)S(1)} fusion(s32[512]{0:T(512)S(1)} %add_bitcast_fusion.1, bf16[520,128]{1,0:T(8,128)(2,1)S(1)} %collective-permute-done.1), kind=kOutput, calls=%fused_computation.21 | convolution fusion | flops 134742016 | bytes 657408 | tf_op jit(solution)/shard_map/dot_general | solution.py:16
  26.3 0.8 %fusion.44 = f32[1024,128]{1,0:T(8,128)S(1)} fusion(f32[1024,128]{1,0:T(8,128)S(1)} %fusion.10, f32[1024,128]{1,0:T(8,128)S(1)} %fusion.15, f32[1024,128]{1,0:T(8,128)S(1)} %fusion.29, s32[512]{0:T(512)S(1)} %add_bitcast_fusion.2, bf16[520,128]{1,0:T(8,128)(2,1)S(1)} %collective-permute-done), kind=kOutput, calls=%fused_computation.52 | convolution fusion | flops 135135232 | bytes 2230272 | tf_op jit(solution)/shard_map/dot_general | solution.py:16
  27.2 1.9 %collective-permute-done.3 = f32[1024,128]{1,0:T(8,128)S(1)} collective-permute-done((f32[1024,128]{1,0:T(8,128)S(1)}, f32[1024,128]{1,0:T(8,128)S(1)}, u32[]{:S(2)}, u32[]{:S(2)}) %collective-permute-start.3) | collective-permute-done | bytes 524320 | tf_op jit(solution)/shard_map/ppermute | solution.py:34
  29.3 0.5 fusion.63
  29.8 0.5 fusion.61
  30.3 0.5 fusion.59
  30.8 2.9 %collective-permute-start.4 = (bf16[512,128]{1,0:T(8,128)(2,1)S(1)}, bf16[512,128]{1,0:T(8,128)(2,1)S(1)}, u32[]{:S(2)}, u32[]{:S(2)}) collective-permute-start(bf16[512,128]{1,0:T(8,128)(2,1)S(1)} %fusion.59), channel_id=1, source_target_pairs={{0,12},{4,0},{8,4},{12,8},{1,13},{5,1},{9,5},{13,9},{2,14},{6,2},{... | collective-permute-start | bytes 393224 | tf_op jit(solution)/shard_map/ppermute | solution.py:43
  34.3 1.3 %fusion.30 = f32[1024,128]{1,0:T(8,128)S(1)} fusion(bf16[1024,128]{1,0:T(8,128)(2,1)S(1)} %fusion.97, s32[512]{0:T(512)S(1)} %bitcast.67, s32[1024]{0:T(1024)S(1)} %bitcast.56), kind=kOutput, calls=%fused_computation.41 | convolution fusion | flops 269549568 | bytes 792576 | tf_op jit(solution)/shard_map/dot_general | solution.py:12
  35.6 7.6 %collective-permute-done.6 = bf16[512,128]{1,0:T(8,128)(2,1)S(1)} collective-permute-done((bf16[512,128]{1,0:T(8,128)(2,1)S(1)}, bf16[512,128]{1,0:T(8,128)(2,1)S(1)}, u32[]{:S(2)}, u32[]{:S(2)}) %collective-permute-start.6) | collective-permute-done | bytes 131104 | tf_op jit(solution)/shard_map/ppermute | solution.py:43
  43.2 0.5 fusion.11
  43.7 2.3 %collective-permute-done.5 = bf16[512,128]{1,0:T(8,128)(2,1)S(1)} collective-permute-done((bf16[512,128]{1,0:T(8,128)(2,1)S(1)}, bf16[512,128]{1,0:T(8,128)(2,1)S(1)}, u32[]{:S(2)}, u32[]{:S(2)}) %collective-permute-start.5) | collective-permute-done | bytes 131104 | tf_op jit(solution)/shard_map/ppermute | solution.py:43
  46.5 0.5 fusion.47
  47.1 2.6 %fusion.48 = bf16[1024,128]{1,0:T(8,128)(2,1)S(1)} fusion(pred[1024,16]{0,1:T(8,128)(4,1)S(1)} %iota_compare_fusion.90, bf16[1024,128]{1,0:T(8,128)(2,1)S(1)} %fusion.47, bf16[16,128,128]{2,1,0:T(8,128)(2,1)S(1)} %copy-done), kind=kOutput, calls=%fused_computation.56 | convolution fusion | flops 539099136 | bytes 1064960 | tf_op jit(solution)/shard_map/dot_general | solution.py:12
  49.7 0.9 %fusion.55 = bf16[512,128]{1,0:T(8,128)(2,1)S(1)} fusion(bf16[1024,128]{1,0:T(8,128)(2,1)S(1)} %fusion.48, s32[1024]{0:T(1024)S(1)} %get-tuple-element.2), kind=kOutput, calls=%fused_computation.59 | convolution fusion | flops 134807552 | bytes 397312 | tf_op jit(solution)/shard_map/dot_general | solution.py:16
  50.7 1.6 %collective-permute-start.7 = (bf16[128,512]{1,0:T(8,128)(2,1)S(1)}, bf16[128,512]{1,0:T(8,128)(2,1)S(1)}, u32[]{:S(2)}, u32[]{:S(2)}) collective-permute-start(bf16[128,512]{1,0:T(8,128)(2,1)S(1)} %convert_element_type.153), channel_id=1, source_target_pairs={{0,2},{2,0},{1,3},{3,1},{4,6},{6,4},{5,7},{7,5},{8,10},{10,8},{9,1... | collective-permute-start | bytes 393224 | tf_op jit(solution)/shard_map/ppermute | solution.py:122
  52.2 0.9 %fusion.33 = f32[512,128]{1,0:T(8,128)S(1)} fusion(bf16[1024,128]{1,0:T(8,128)(2,1)S(1)} %fusion.48, s32[1024]{0:T(1024)S(1)} %broadcast_subtract_fusion.1), kind=kOutput, calls=%fused_computation.45 | convolution fusion | flops 134742016 | bytes 528384 | tf_op jit(solution)/shard_map/dot_general | solution.py:16
  53.1 2.5 %collective-permute-done.7 = bf16[128,512]{1,0:T(8,128)(2,1)S(1)} collective-permute-done((bf16[128,512]{1,0:T(8,128)(2,1)S(1)}, bf16[128,512]{1,0:T(8,128)(2,1)S(1)}, u32[]{:S(2)}, u32[]{:S(2)}) %collective-permute-start.7) | collective-permute-done | bytes 131104 | tf_op jit(solution)/shard_map/ppermute | solution.py:122
  55.7 0.7 %convert_add_fusion = f32[128,512]{1,0:T(8,128)} fusion(f32[128,512]{1,0:T(8,128)S(1)} %reshape.149, bf16[128,512]{1,0:T(8,128)(2,1)S(1)} %collective-permute-done.7), kind=kLoop, calls=%fused_computation.102 | loop fusion | flops 131072 | bytes 655360 | tf_op jit(solution)/shard_map/add | solution.py:124
  (55 shorter events, 4.1 us)
Async XLA Ops:
  0.6 4.1 %copy-start = (bf16[16,128,128]{2,1,0:T(8,128)(2,1)S(1)}, bf16[16,128,128]{2,1,0:T(8,128)(2,1)}, u32[]{:S(2)}) copy-start(bf16[16,128,128]{2,1,0:T(8,128)(2,1)} %param.10) | copy-start | bytes 1572868
  1.4 1.3 %copy-start.6 = (s32[1024]{0:T(1024)S(1)}, s32[1024]{0:T(1024)}, u32[]{:S(2)}) copy-start(s32[1024]{0:T(1024)} %param.14) | copy-start | bytes 12292
  1.4 1.4 %copy-start.7 = (s32[1024,1]{0,1:T(1,128)S(1)}, s32[1024,1]{0,1:T(1,128)}, u32[]{:S(2)}) copy-start(s32[1024,1]{0,1:T(1,128)} %param.13) | copy-start | bytes 12292
  2.7 0.7 %copy-start.5 = (s32[1024]{0:T(1024)S(1)}, s32[1024]{0:T(1024)}, u32[]{:S(2)}) copy-start(s32[1024]{0:T(1024)} %param.17) | copy-start | bytes 12292
  2.7 1.0 %copy-start.2 = (bf16[256,512]{1,0:T(8,128)(2,1)S(1)}, bf16[256,512]{1,0:T(8,128)(2,1)}, u32[]{:S(2)}) copy-start(bf16[256,512]{1,0:T(8,128)(2,1)} %param.9) | copy-start | bytes 786436
  2.8 1.0 %copy-start.8 = (s32[1024]{0:T(1024)S(1)}, s32[1024]{0:T(1024)}, u32[]{:S(2)}) copy-start(s32[1024]{0:T(1024)} %param.16) | copy-start | bytes 12292
  8.6 12.0 %collective-permute-start = (bf16[520,128]{1,0:T(8,128)(2,1)S(1)}, bf16[520,128]{1,0:T(8,128)(2,1)S(1)}, u32[]{:S(2)}, u32[]{:S(2)}) collective-permute-start(bf16[520,128]{1,0:T(8,128)(2,1)S(1)} %pad_maximum_fusion), channel_id=1, source_target_pairs={{0,4},{4,8},{8,12},{12,0},{1,5},{5,9},{9,13},{13,1},{2,6},{6,10},{... | collective-permute-start | bytes 399368 | tf_op jit(solution)/shard_map/ppermute | solution.py:43
  13.1 10.0 %collective-permute-start.1 = (bf16[520,128]{1,0:T(8,128)(2,1)S(1)}, bf16[520,128]{1,0:T(8,128)(2,1)S(1)}, u32[]{:S(2)}, u32[]{:S(2)}) collective-permute-start(bf16[520,128]{1,0:T(8,128)(2,1)S(1)} %pad_maximum_fusion.1), channel_id=1, source_target_pairs={{0,8},{4,12},{8,0},{12,4},{1,9},{5,13},{9,1},{13,5},{2,10},{6,14},... | collective-permute-start | bytes 399368 | tf_op jit(solution)/shard_map/ppermute | solution.py:43
  17.2 7.5 %collective-permute-start.2 = (bf16[520,128]{1,0:T(8,128)(2,1)S(1)}, bf16[520,128]{1,0:T(8,128)(2,1)S(1)}, u32[]{:S(2)}, u32[]{:S(2)}) collective-permute-start(bf16[520,128]{1,0:T(8,128)(2,1)S(1)} %pad_maximum_fusion.2), channel_id=1, source_target_pairs={{0,12},{4,0},{8,4},{12,8},{1,13},{5,1},{9,5},{13,9},{2,14},{6,2},{... | collective-permute-start | bytes 399368 | tf_op jit(solution)/shard_map/ppermute | solution.py:43
  26.3 2.8 %copy-start.1 = (s32[1,1024,128]{2,1,0:T(8,128)S(1)}, s32[1,1024,128]{2,1,0:T(8,128)}, u32[]{:S(2)}) copy-start(s32[1,1024,128]{2,1,0:T(8,128)} %param.12) | copy-start | bytes 1572868
  26.3 2.8 %copy-start.3 = (bf16[1,1024,128]{2,1,0:T(8,128)(2,1)S(1)}, bf16[1,1024,128]{2,1,0:T(8,128)(2,1)}, u32[]{:S(2)}) copy-start(bf16[1,1024,128]{2,1,0:T(8,128)(2,1)} %param.11) | copy-start | bytes 786436
  27.2 2.0 %collective-permute-start.3 = (f32[1024,128]{1,0:T(8,128)S(1)}, f32[1024,128]{1,0:T(8,128)S(1)}, u32[]{:S(2)}, u32[]{:S(2)}) collective-permute-start(f32[1024,128]{1,0:T(8,128)S(1)} %fusion.44), channel_id=1, source_target_pairs={{0,1},{1,0},{2,3},{3,2},{4,5},{5,4},{6,7},{7,6},{8,9},{9,8},{10,11... | collective-permute-start | bytes 1572872 | tf_op jit(solution)/shard_map/ppermute | solution.py:34
  29.2 5.1 %copy-start.4 = (bf16[1024,128]{1,0:T(8,128)(2,1)}, bf16[1024,128]{1,0:T(8,128)(2,1)S(1)}, u32[]{:S(2)}) copy-start(bf16[1024,128]{1,0:T(8,128)(2,1)S(1)} %fusion.97) | copy-start | bytes 786436
  30.8 15.7 %collective-permute-start.4 = (bf16[512,128]{1,0:T(8,128)(2,1)S(1)}, bf16[512,128]{1,0:T(8,128)(2,1)S(1)}, u32[]{:S(2)}, u32[]{:S(2)}) collective-permute-start(bf16[512,128]{1,0:T(8,128)(2,1)S(1)} %fusion.59), channel_id=1, source_target_pairs={{0,12},{4,0},{8,4},{12,8},{1,13},{5,1},{9,5},{13,9},{2,14},{6,2},{... | collective-permute-start | bytes 393224 | tf_op jit(solution)/shard_map/ppermute | solution.py:43
  33.7 12.3 %collective-permute-start.5 = (bf16[512,128]{1,0:T(8,128)(2,1)S(1)}, bf16[512,128]{1,0:T(8,128)(2,1)S(1)}, u32[]{:S(2)}, u32[]{:S(2)}) collective-permute-start(bf16[512,128]{1,0:T(8,128)(2,1)S(1)} %fusion.61), channel_id=1, source_target_pairs={{0,8},{4,12},{8,0},{12,4},{1,9},{5,13},{9,1},{13,5},{2,10},{6,14},... | collective-permute-start | bytes 393224 | tf_op jit(solution)/shard_map/ppermute | solution.py:43
  34.1 9.1 %collective-permute-start.6 = (bf16[512,128]{1,0:T(8,128)(2,1)S(1)}, bf16[512,128]{1,0:T(8,128)(2,1)S(1)}, u32[]{:S(2)}, u32[]{:S(2)}) collective-permute-start(bf16[512,128]{1,0:T(8,128)(2,1)S(1)} %fusion.63), channel_id=1, source_target_pairs={{0,4},{4,8},{8,12},{12,0},{1,5},{5,9},{9,13},{13,1},{2,6},{6,10},{... | collective-permute-start | bytes 393224 | tf_op jit(solution)/shard_map/ppermute | solution.py:43
  50.7 5.0 %collective-permute-start.7 = (bf16[128,512]{1,0:T(8,128)(2,1)S(1)}, bf16[128,512]{1,0:T(8,128)(2,1)S(1)}, u32[]{:S(2)}, u32[]{:S(2)}) collective-permute-start(bf16[128,512]{1,0:T(8,128)(2,1)S(1)} %convert_element_type.153), channel_id=1, source_target_pairs={{0,2},{2,0},{1,3},{3,1},{4,6},{6,4},{5,7},{7,5},{8,10},{10,8},{9,1... | collective-permute-start | bytes 393224 | tf_op jit(solution)/shard_map/ppermute | solution.py:122

commit v5 on v4

--- a/solution.py
+++ b/solution.py
@@ -1,3 +1,5 @@
+import math
+
 import jax
 import jax.numpy as jnp
 from jax import lax
@@ -70,9 +72,17 @@
     kinds = psf_index
     spec_rows = trace_source[:, 0] * block_count + trace_block
     member = one_hot_rows(target, tile_count)
-    entry_ids = jnp.arange(entry_count, dtype=jnp.int32)
-    up_to = (entry_ids[None, :] <= entry_ids[:, None]).astype(jnp.bfloat16)
-    running = select_dot(up_to, member)
+    chunk = math.gcd(entry_count, 128)
+    chunk_ids = jnp.arange(chunk, dtype=jnp.int32)
+    up_to = (chunk_ids[None, :] <= chunk_ids[:, None]).astype(jnp.bfloat16)
+    within = jnp.einsum(
+        "ij,cjt->cit",
+        up_to,
+        member.reshape(entry_count // chunk, chunk, tile_count),
+        preferred_element_type=jnp.float32,
+    )
+    totals = within[:, -1, :]
+    running = (within + (jnp.cumsum(totals, axis=0) - totals)[:, None, :]).reshape(entry_count, tile_count)
     position = jnp.sum((running - 1.0) * member.astype(jnp.float32), axis=1).astype(jnp.int32)
     shift = (target - lax.axis_index("tile")) % tile_count
     dest = shift * capacity + position
@@ -84,12 +94,15 @@
     slot_parts = jnp.stack([trace_slot // 256, trace_slot % 256], axis=1).astype(jnp.bfloat16)
     code_rows = -(-2 * capacity // pixel_count)
     places = [one_hot_rows(dest - step * capacity, capacity) for step in range(tile_count)]
+    with_codes = jnp.concatenate([traces, slot_parts], axis=1)
     send = []
     for step in range(tile_count):
-        codes = select_dot_t(slot_parts, places[step]).astype(jnp.bfloat16).reshape(2 * capacity)
+        placed = select_dot_t(places[step], with_codes).astype(jnp.bfloat16)
+        codes = placed[:, pixel_count:].T.reshape(2 * capacity)
         codes = jnp.pad(codes, (0, code_rows * pixel_count - 2 * capacity))
-        block = select_dot_t(places[step], traces).astype(jnp.bfloat16)
-        send.append(jnp.concatenate([block, codes.reshape(code_rows, pixel_count)], axis=0))
+        send.append(
+            jnp.concatenate([placed[:, :pixel_count], codes.reshape(code_rows, pixel_count)], axis=0)
+        )
     got = exchange(send, "tile", 1)
     got_traces = [block[:capacity] for block in got]
     got_slots = []

time: 56.7 us -> 59.7 us (1.053)
  matrix products: 22.4 us -> 20 us
  other arithmetic: 1.76 us -> 4.11 us
  local copies, waits for them, and re-layouts: 0.67 us -> 1.8 us
  waiting for transfers between devices: 18.3 us -> 19.3 us
  starting transfers between devices: 12.3 us -> 13.2 us
    dot_general x13 -> x10, matrix products: 10.4 us -> 7.46 us  [select_dot_t(): lax.dot_general(selector, values, (((0,), (0,)), ((), ())), preferred_ele...]
    ppermute x6, waiting for transfers between devices: 13.9 us -> 14.9 us  [exchange(): moved.append(lax.ppermute(blocks[step], axis, pairs))]
    reshape x1, local copies, waits for them, and re-layouts: 0.16 us -> 1.11 us  [per_device(): spectra.reshape(row_count, bin_count)]
    ppermute x6, starting transfers between devices: 10.7 us -> 11.5 us  [exchange(): moved.append(lax.ppermute(blocks[step], axis, pairs))]
    dot_general x0 -> x1, matrix products: none -> 0.82 us  [per_device(): jnp.einsum('ij,cjt->cit', up_to, member.reshape(entry_count // chunk, chu...]
    reduce_sum x0 -> x1, other arithmetic: none -> 0.77 us  [per_device(): jnp.sum((running - 1.0) * member.astype(jnp.float32), axis=1)]
    eq x1, other arithmetic: 0.01 us -> 0.72 us  [spread_by_kind(): kinds[:, None, None]]
    another operation x2, other arithmetic: 0.03 us -> 0.73 us  [the longest x1 0.02 us: per_device(): jnp.stack([trace_slot // 256, trace_slot % 256], axis=1)]
  transfers between devices with their start and end apart: 8 -> 8, of which waited for: 6 -> 6; matrix products, arithmetic and copies ran while one was open for 14% -> 10% of each run, Pallas kernels for 0% -> 0%
where the time goes in v5:
time: 59.7 us; the launch traced here: 59.4 us
  matrix products  20 us (34%)
  waiting for transfers between devices  19.3 us (32%)
  starting transfers between devices  13.2 us (22%)
  other arithmetic  4.11 us (7%)
  local copies, waits for them, and re-layouts  1.8 us (3%)
  between operations  1.03 us (2%)
    ppermute x6, waiting for transfers between devices, exchange(): moved.append(lax.ppermute(blocks[step], axis, pairs))  14.9 us
    dot_general x10, matrix products, select_dot(): jnp.dot(selector, values, preferred_element_type=jnp.float32, precision=p...  11.7 us
    ppermute x6, starting transfers between devices, exchange(): moved.append(lax.ppermute(blocks[step], axis, pairs))  11.5 us
    dot_general x10, matrix products, select_dot_t(): lax.dot_general(selector, values, (((0,), (0,)), ((), ())), preferred_ele...  7.46 us
    ppermute x1, waiting for transfers between devices, per_device(): sent = lax.ppermute(theirs.astype(jnp.bfloat16), 'dither', [(0, 1), (1, 0)])  2.55 us
    ppermute x1, waiting for transfers between devices, swap_add(): return value + lax.ppermute(value, axis, [(0, 1), (1, 0)])  1.89 us
    ppermute x1, starting transfers between devices, per_device(): sent = lax.ppermute(theirs.astype(jnp.bfloat16), 'dither', [(0, 1), (1, 0)])  1.56 us
  transfers between devices with their start and end apart: 8, of which 6 were waited for; matrix products, arithmetic and copies ran while one was open for 10% of the time, Pallas kernels for 0%

profile of v5, /device:TPU:0, one launch (start us, length us, event | category | flops | bytes accessed | tf_op | source)
XLA Modules:
  0.0 59.4 jit_solution(6090265990572038049)
XLA Ops:
  0.7 0.7 %broadcast_multiply_fusion = s32[1024,1]{0,1:T(1,128)S(1)} fusion(s32[1024,1]{0,1:T(1,128)} %param.15), kind=kLoop, calls=%fused_computation.136 | loop fusion | flops 1024 | bytes 8192 | tf_op jit(solution)/shard_map/mul | solution.py:73
  1.4 0.7 %fusion.91 = (bf16[1024]{0:T(1024)(128)(2,1)S(1)}, bf16[1024]{0:T(1024)(128)(2,1)S(1)}) fusion(s32[1024]{0:T(1024)} %param.14), kind=kLoop, calls=%fused_computation.114 | loop fusion | flops 21504 | bytes 8192 | tf_op jit(solution)/shard_map/convert.5
  2.1 0.8 %convolution_bitcast_fusion = f32[8,128,4]{1,0,2:T(8,128)S(1)} fusion(s32[8,128]{1,0:T(8,128)} %bitcast.56), kind=kOutput, calls=%fused_computation.62 | convolution fusion | flops 1069056 | bytes 20480 | tf_op jit(solution)/shard_map/ij,cjt->cit/dot_general | solution.py:78
  3.0 0.7 %iota_compare_fusion.57 = pred[1024,16]{0,1:T(8,128)(4,1)S(1)} fusion(s32[1024]{0:T(1024)} %param.17), kind=kLoop, calls=%fused_computation.99 | loop fusion | flops 16384 | bytes 20480 | tf_op jit(solution)/shard_map/eq | solution.py:28
  3.9 0.8 %multiply_reduce_fusion = f32[8,128]{1,0:T(8,128)S(1)} fusion(f32[8,128,4]{1,0,2:T(8,128)S(1)} %convolution_bitcast_fusion, f32[8,4]{0,1:T(4,128)S(1)} %subtract_reduce_fusion, s32[8,128]{1,0:T(8,128)} %bitcast.57), kind=kLoop, calls=%fused_computation.103 | loop fusion | flops 27648 | bytes 24704 | tf_op jit(solution)/shard_map/reduce_sum | solution.py:86
  4.7 1.1 %reshape.174 = bf16[1024,128]{1,0:T(8,128)(2,1)S(1)} reshape(bf16[256,512]{1,0:T(8,128)(2,1)} %param.9) | data formatting | bytes 524288 | tf_op jit(solution)/shard_map/reshape | solution.py:91
  5.9 0.8 %fusion.49 = bf16[1024,128]{1,0:T(8,128)(2,1)S(1)} fusion(bf16[1024,128]{1,0:T(8,128)(2,1)S(1)} %reshape.174, s32[1024]{0:T(1024)S(1)} %get-tuple-element.3), kind=kOutput, calls=%fused_computation.52 | convolution fusion | flops 269615104 | bytes 528384 | tf_op jit(solution)/shard_map/dot_general | solution.py:14
  6.8 3.9 %fusion.46 = bf16[1024,128]{0,1:T(8,128)(2,1)S(1)} fusion(bf16[16,128,128]{2,1,0:T(8,128)(2,1)S(1)} %copy-done, pred[1024,16]{0,1:T(8,128)(4,1)S(1)} %iota_compare_fusion.57, bf16[1024,128]{1,0:T(8,128)(2,1)S(1)} %fusion.49), kind=kOutput, calls=%fused_computation.51 | convolution fusion | flops 539099136 | bytes 1064960 | tf_op jit(solution)/shard_map/dot_general | solution.py:14
  10.7 0.7 %convolution_convert_fusion.2 = bf16[512,130]{1,0:T(8,128)(2,1)S(1)} fusion(s32[1024]{0:T(1024)S(1)} %bitcast.58, bf16[1024,1]{0,1:T(2,128)(2,1)S(1)} %stack.11, bf16[1024,1]{0,1:T(2,128)(2,1)S(1)} %stack.10, bf16[1024,128]{0,1:T(8,128)(2,1)S(1)} %fusion.46), kind=kOutput, calls=%fused_computation.55 | convolution fusion | flops 138228736 | bytes 403456 | tf_op jit(solution)/shard_map/dot_general | solution.py:18
  11.6 3.1 %collective-permute-start = (bf16[520,128]{1,0:T(8,128)(2,1)S(1)}, bf16[520,128]{1,0:T(8,128)(2,1)S(1)}, u32[]{:S(2)}, u32[]{:S(2)}) collective-permute-start(bf16[520,128]{1,0:T(8,128)(2,1)S(1)} %pad_maximum_fusion.1), channel_id=1, source_target_pairs={{0,4},{4,8},{8,12},{12,0},{1,5},{5,9},{9,13},{13,1},{2,6},{6,10},{... | collective-permute-start | bytes 399368 | tf_op jit(solution)/shard_map/ppermute | solution.py:45
  14.7 0.7 %convolution_convert_fusion.1 = bf16[512,130]{1,0:T(8,128)(2,1)S(1)} fusion(s32[1024]{0:T(1024)S(1)} %bitcast.64, bf16[1024,1]{0,1:T(2,128)(2,1)S(1)} %stack.11, bf16[1024,1]{0,1:T(2,128)(2,1)S(1)} %stack.10, bf16[1024,128]{0,1:T(8,128)(2,1)S(1)} %fusion.46), kind=kOutput, calls=%fused_computation.54 | convolution fusion | flops 138228736 | bytes 403456 | tf_op jit(solution)/shard_map/dot_general | solution.py:18
  15.6 2.6 %collective-permute-start.1 = (bf16[520,128]{1,0:T(8,128)(2,1)S(1)}, bf16[520,128]{1,0:T(8,128)(2,1)S(1)}, u32[]{:S(2)}, u32[]{:S(2)}) collective-permute-start(bf16[520,128]{1,0:T(8,128)(2,1)S(1)} %pad_maximum_fusion.2), channel_id=1, source_target_pairs={{0,8},{4,12},{8,0},{12,4},{1,9},{5,13},{9,1},{13,5},{2,10},{6,14},... | collective-permute-start | bytes 399368 | tf_op jit(solution)/shard_map/ppermute | solution.py:45
  18.2 0.7 %convolution_convert_fusion = bf16[512,130]{1,0:T(8,128)(2,1)S(1)} fusion(s32[1024]{0:T(1024)S(1)} %bitcast.66, bf16[1024,1]{0,1:T(2,128)(2,1)S(1)} %stack.11, bf16[1024,1]{0,1:T(2,128)(2,1)S(1)} %stack.10, bf16[1024,128]{0,1:T(8,128)(2,1)S(1)} %fusion.46), kind=kOutput, calls=%fused_computation.53 | convolution fusion | flops 138228736 | bytes 403456 | tf_op jit(solution)/shard_map/dot_general | solution.py:18
  19.1 1.4 %collective-permute-start.2 = (bf16[520,128]{1,0:T(8,128)(2,1)S(1)}, bf16[520,128]{1,0:T(8,128)(2,1)S(1)}, u32[]{:S(2)}, u32[]{:S(2)}) collective-permute-start(bf16[520,128]{1,0:T(8,128)(2,1)S(1)} %pad_maximum_fusion.3), channel_id=1, source_target_pairs={{0,12},{4,0},{8,4},{12,8},{1,13},{5,1},{9,5},{13,9},{2,14},{6,2},{... | collective-permute-start | bytes 399368 | tf_op jit(solution)/shard_map/ppermute | solution.py:45
  20.5 0.5 fusion.50
  21.1 0.6 fusion.56
  21.7 4.4 %collective-permute-done.1 = bf16[520,128]{1,0:T(8,128)(2,1)S(1)} collective-permute-done((bf16[520,128]{1,0:T(8,128)(2,1)S(1)}, bf16[520,128]{1,0:T(8,128)(2,1)S(1)}, u32[]{:S(2)}, u32[]{:S(2)}) %collective-permute-start.1) | collective-permute-done | bytes 133152 | tf_op jit(solution)/shard_map/ppermute | solution.py:45
  26.1 0.6 %collective-permute-done.2 = bf16[520,128]{1,0:T(8,128)(2,1)S(1)} collective-permute-done((bf16[520,128]{1,0:T(8,128)(2,1)S(1)}, bf16[520,128]{1,0:T(8,128)(2,1)S(1)}, u32[]{:S(2)}, u32[]{:S(2)}) %collective-permute-start.2) | collective-permute-done | bytes 133152 | tf_op jit(solution)/shard_map/ppermute | solution.py:45
  26.7 0.8 %fusion.9 = f32[1024,128]{1,0:T(8,128)S(1)} fusion(s32[512]{0:T(512)S(1)} %add_bitcast_fusion, bf16[520,128]{1,0:T(8,128)(2,1)S(1)} %collective-permute-done.2), kind=kOutput, calls=%fused_computation.12 | convolution fusion | flops 134742016 | bytes 657408 | tf_op jit(solution)/shard_map/dot_general | solution.py:18
  27.6 0.8 %fusion.13 = f32[1024,128]{1,0:T(8,128)S(1)} fusion(s32[512]{0:T(512)S(1)} %add_bitcast_fusion.1, bf16[520,128]{1,0:T(8,128)(2,1)S(1)} %collective-permute-done.1), kind=kOutput, calls=%fused_computation.18 | convolution fusion | flops 134742016 | bytes 657408 | tf_op jit(solution)/shard_map/dot_general | solution.py:18
  28.4 0.8 %fusion.39 = f32[1024,128]{1,0:T(8,128)S(1)} fusion(f32[1024,128]{1,0:T(8,128)S(1)} %fusion.9, f32[1024,128]{1,0:T(8,128)S(1)} %fusion.13, f32[1024,128]{1,0:T(8,128)S(1)} %fusion.56, s32[512]{0:T(512)S(1)} %add_bitcast_fusion.2, bf16[520,128]{1,0:T(8,128)(2,1)S(1)} %collective-permute-done), kind=kOutput, calls=%fused_computation.46 | convolution fusion | flops 135135232 | bytes 2230272 | tf_op jit(solution)/shard_map/dot_general | solution.py:18
  29.3 1.9 %collective-permute-done.3 = f32[1024,128]{1,0:T(8,128)S(1)} collective-permute-done((f32[1024,128]{1,0:T(8,128)S(1)}, f32[1024,128]{1,0:T(8,128)S(1)}, u32[]{:S(2)}, u32[]{:S(2)}) %collective-permute-start.3) | collective-permute-done | bytes 524320 | tf_op jit(solution)/shard_map/ppermute | solution.py:36
  32.9 3.8 %collective-permute-start.4 = (bf16[512,128]{1,0:T(8,128)(2,1)S(1)}, bf16[512,128]{1,0:T(8,128)(2,1)S(1)}, u32[]{:S(2)}, u32[]{:S(2)}) collective-permute-start(bf16[512,128]{1,0:T(8,128)(2,1)S(1)} %fusion.53), channel_id=1, source_target_pairs={{0,12},{4,0},{8,4},{12,8},{1,13},{5,1},{9,5},{13,9},{2,14},{6,2},{... | collective-permute-start | bytes 393224 | tf_op jit(solution)/shard_map/ppermute | solution.py:45
  37.3 1.3 %fusion.26 = f32[1024,128]{1,0:T(8,128)S(1)} fusion(bf16[1024,128]{1,0:T(8,128)(2,1)S(1)} %fusion.81, s32[512]{0:T(512)S(1)} %bitcast.69, s32[1024]{0:T(1024)S(1)} %bitcast.61), kind=kOutput, calls=%fused_computation.36 | convolution fusion | flops 269549568 | bytes 792576 | tf_op jit(solution)/shard_map/dot_general | solution.py:14
  38.6 7.6 %collective-permute-done.6 = bf16[512,128]{1,0:T(8,128)(2,1)S(1)} collective-permute-done((bf16[512,128]{1,0:T(8,128)(2,1)S(1)}, bf16[512,128]{1,0:T(8,128)(2,1)S(1)}, u32[]{:S(2)}, u32[]{:S(2)}) %collective-permute-start.6) | collective-permute-done | bytes 131104 | tf_op jit(solution)/shard_map/ppermute | solution.py:45
  46.7 2.3 %collective-permute-done.5 = bf16[512,128]{1,0:T(8,128)(2,1)S(1)} collective-permute-done((bf16[512,128]{1,0:T(8,128)(2,1)S(1)}, bf16[512,128]{1,0:T(8,128)(2,1)S(1)}, u32[]{:S(2)}, u32[]{:S(2)}) %collective-permute-start.5) | collective-permute-done | bytes 131104 | tf_op jit(solution)/shard_map/ppermute | solution.py:45
  50.1 2.6 %fusion.43 = bf16[1024,128]{1,0:T(8,128)(2,1)S(1)} fusion(pred[1024,16]{0,1:T(8,128)(4,1)S(1)} %iota_compare_fusion.57, bf16[1024,128]{1,0:T(8,128)(2,1)S(1)} %fusion.42, bf16[16,128,128]{2,1,0:T(8,128)(2,1)S(1)} %copy-done), kind=kOutput, calls=%fused_computation.50 | convolution fusion | flops 539099136 | bytes 1064960 | tf_op jit(solution)/shard_map/dot_general | solution.py:14
  52.7 0.9 %fusion.51 = bf16[512,128]{1,0:T(8,128)(2,1)S(1)} fusion(bf16[1024,128]{1,0:T(8,128)(2,1)S(1)} %fusion.43, s32[1024]{0:T(1024)S(1)} %get-tuple-element.2), kind=kOutput, calls=%fused_computation.57 | convolution fusion | flops 134807552 | bytes 397312 | tf_op jit(solution)/shard_map/dot_general | solution.py:18
  53.6 1.6 %collective-permute-start.7 = (bf16[128,512]{1,0:T(8,128)(2,1)S(1)}, bf16[128,512]{1,0:T(8,128)(2,1)S(1)}, u32[]{:S(2)}, u32[]{:S(2)}) collective-permute-start(bf16[128,512]{1,0:T(8,128)(2,1)S(1)} %convert_element_type.143), channel_id=1, source_target_pairs={{0,2},{2,0},{1,3},{3,1},{4,6},{6,4},{5,7},{7,5},{8,10},{10,8},{9,1... | collective-permute-start | bytes 393224 | tf_op jit(solution)/shard_map/ppermute | solution.py:135
  55.2 0.9 %fusion.28 = f32[512,128]{1,0:T(8,128)S(1)} fusion(bf16[1024,128]{1,0:T(8,128)(2,1)S(1)} %fusion.43, s32[1024]{0:T(1024)S(1)} %broadcast_subtract_fusion.1), kind=kOutput, calls=%fused_computation.39 | convolution fusion | flops 134742016 | bytes 528384 | tf_op jit(solution)/shard_map/dot_general | solution.py:18
  56.1 2.6 %collective-permute-done.7 = bf16[128,512]{1,0:T(8,128)(2,1)S(1)} collective-permute-done((bf16[128,512]{1,0:T(8,128)(2,1)S(1)}, bf16[128,512]{1,0:T(8,128)(2,1)S(1)}, u32[]{:S(2)}, u32[]{:S(2)}) %collective-permute-start.7) | collective-permute-done | bytes 131104 | tf_op jit(solution)/shard_map/ppermute | solution.py:135
  58.7 0.7 %convert_add_fusion = f32[128,512]{1,0:T(8,128)} fusion(f32[128,512]{1,0:T(8,128)S(1)} %reshape.178, bf16[128,512]{1,0:T(8,128)(2,1)S(1)} %collective-permute-done.7), kind=kLoop, calls=%fused_computation.87 | loop fusion | flops 131072 | bytes 655360 | tf_op jit(solution)/shard_map/add | solution.py:137
  (59 shorter events, 4.9 us)
Async XLA Ops:
  0.6 6.1 %copy-start = (bf16[16,128,128]{2,1,0:T(8,128)(2,1)S(1)}, bf16[16,128,128]{2,1,0:T(8,128)(2,1)}, u32[]{:S(2)}) copy-start(bf16[16,128,128]{2,1,0:T(8,128)(2,1)} %param.10) | copy-start | bytes 1572868
  0.6 5.2 %copy-start.4 = (s32[1024,1]{0,1:T(1,128)S(1)}, s32[1024,1]{0,1:T(1,128)}, u32[]{:S(2)}) copy-start(s32[1024,1]{0,1:T(1,128)} %param.13) | copy-start | bytes 12292
  0.7 5.2 %copy-start.5 = (s32[1024]{0:T(1024)S(1)}, s32[1024]{0:T(1024)}, u32[]{:S(2)}) copy-start(s32[1024]{0:T(1024)} %param.16) | copy-start | bytes 12292
  11.6 10.1 %collective-permute-start = (bf16[520,128]{1,0:T(8,128)(2,1)S(1)}, bf16[520,128]{1,0:T(8,128)(2,1)S(1)}, u32[]{:S(2)}, u32[]{:S(2)}) collective-permute-start(bf16[520,128]{1,0:T(8,128)(2,1)S(1)} %pad_maximum_fusion.1), channel_id=1, source_target_pairs={{0,4},{4,8},{8,12},{12,0},{1,5},{5,9},{9,13},{13,1},{2,6},{6,10},{... | collective-permute-start | bytes 399368 | tf_op jit(solution)/shard_map/ppermute | solution.py:45
  15.6 10.5 %collective-permute-start.1 = (bf16[520,128]{1,0:T(8,128)(2,1)S(1)}, bf16[520,128]{1,0:T(8,128)(2,1)S(1)}, u32[]{:S(2)}, u32[]{:S(2)}) collective-permute-start(bf16[520,128]{1,0:T(8,128)(2,1)S(1)} %pad_maximum_fusion.2), channel_id=1, source_target_pairs={{0,8},{4,12},{8,0},{12,4},{1,9},{5,13},{9,1},{13,5},{2,10},{6,14},... | collective-permute-start | bytes 399368 | tf_op jit(solution)/shard_map/ppermute | solution.py:45
  19.1 7.6 %collective-permute-start.2 = (bf16[520,128]{1,0:T(8,128)(2,1)S(1)}, bf16[520,128]{1,0:T(8,128)(2,1)S(1)}, u32[]{:S(2)}, u32[]{:S(2)}) collective-permute-start(bf16[520,128]{1,0:T(8,128)(2,1)S(1)} %pad_maximum_fusion.3), channel_id=1, source_target_pairs={{0,12},{4,0},{8,4},{12,8},{1,13},{5,1},{9,5},{13,9},{2,14},{6,2},{... | collective-permute-start | bytes 399368 | tf_op jit(solution)/shard_map/ppermute | solution.py:45
  28.4 2.8 %copy-start.1 = (s32[1,1024,128]{2,1,0:T(8,128)S(1)}, s32[1,1024,128]{2,1,0:T(8,128)}, u32[]{:S(2)}) copy-start(s32[1,1024,128]{2,1,0:T(8,128)} %param.12) | copy-start | bytes 1572868
  28.4 2.8 %copy-start.2 = (bf16[1,1024,128]{2,1,0:T(8,128)(2,1)S(1)}, bf16[1,1024,128]{2,1,0:T(8,128)(2,1)}, u32[]{:S(2)}) copy-start(bf16[1,1024,128]{2,1,0:T(8,128)(2,1)} %param.11) | copy-start | bytes 786436
  29.2 2.0 %collective-permute-start.3 = (f32[1024,128]{1,0:T(8,128)S(1)}, f32[1024,128]{1,0:T(8,128)S(1)}, u32[]{:S(2)}, u32[]{:S(2)}) collective-permute-start(f32[1024,128]{1,0:T(8,128)S(1)} %fusion.39), channel_id=1, source_target_pairs={{0,1},{1,0},{2,3},{3,2},{4,5},{5,4},{6,7},{7,6},{8,9},{9,8},{10,11... | collective-permute-start | bytes 1572872 | tf_op jit(solution)/shard_map/ppermute | solution.py:36
  31.3 6.0 %copy-start.3 = (bf16[1024,128]{1,0:T(8,128)(2,1)}, bf16[1024,128]{1,0:T(8,128)(2,1)S(1)}, u32[]{:S(2)}) copy-start(bf16[1024,128]{1,0:T(8,128)(2,1)S(1)} %fusion.81) | copy-start | bytes 786436
  32.9 16.6 %collective-permute-start.4 = (bf16[512,128]{1,0:T(8,128)(2,1)S(1)}, bf16[512,128]{1,0:T(8,128)(2,1)S(1)}, u32[]{:S(2)}, u32[]{:S(2)}) collective-permute-start(bf16[512,128]{1,0:T(8,128)(2,1)S(1)} %fusion.53), channel_id=1, source_target_pairs={{0,12},{4,0},{8,4},{12,8},{1,13},{5,1},{9,5},{13,9},{2,14},{6,2},{... | collective-permute-start | bytes 393224 | tf_op jit(solution)/shard_map/ppermute | solution.py:45
  36.7 12.4 %collective-permute-start.5 = (bf16[512,128]{1,0:T(8,128)(2,1)S(1)}, bf16[512,128]{1,0:T(8,128)(2,1)S(1)}, u32[]{:S(2)}, u32[]{:S(2)}) collective-permute-start(bf16[512,128]{1,0:T(8,128)(2,1)S(1)} %fusion.54), channel_id=1, source_target_pairs={{0,8},{4,12},{8,0},{12,4},{1,9},{5,13},{9,1},{13,5},{2,10},{6,14},... | collective-permute-start | bytes 393224 | tf_op jit(solution)/shard_map/ppermute | solution.py:45
  37.1 9.1 %collective-permute-start.6 = (bf16[512,128]{1,0:T(8,128)(2,1)S(1)}, bf16[512,128]{1,0:T(8,128)(2,1)S(1)}, u32[]{:S(2)}, u32[]{:S(2)}) collective-permute-start(bf16[512,128]{1,0:T(8,128)(2,1)S(1)} %fusion.55), channel_id=1, source_target_pairs={{0,4},{4,8},{8,12},{12,0},{1,5},{5,9},{9,13},{13,1},{2,6},{6,10},{... | collective-permute-start | bytes 393224 | tf_op jit(solution)/shard_map/ppermute | solution.py:45
  53.6 5.0 %collective-permute-start.7 = (bf16[128,512]{1,0:T(8,128)(2,1)S(1)}, bf16[128,512]{1,0:T(8,128)(2,1)S(1)}, u32[]{:S(2)}, u32[]{:S(2)}) collective-permute-start(bf16[128,512]{1,0:T(8,128)(2,1)S(1)} %convert_element_type.143), channel_id=1, source_target_pairs={{0,2},{2,0},{1,3},{3,1},{4,6},{6,4},{5,7},{7,5},{8,10},{10,8},{9,1... | collective-permute-start | bytes 393224 | tf_op jit(solution)/shard_map/ppermute | solution.py:135

commit v6 on v4

--- a/solution.py
+++ b/solution.py
@@ -84,12 +84,15 @@
     slot_parts = jnp.stack([trace_slot // 256, trace_slot % 256], axis=1).astype(jnp.bfloat16)
     code_rows = -(-2 * capacity // pixel_count)
     places = [one_hot_rows(dest - step * capacity, capacity) for step in range(tile_count)]
+    with_codes = jnp.concatenate([traces, slot_parts], axis=1)
     send = []
     for step in range(tile_count):
-        codes = select_dot_t(slot_parts, places[step]).astype(jnp.bfloat16).reshape(2 * capacity)
+        placed = select_dot_t(places[step], with_codes).astype(jnp.bfloat16)
+        codes = placed[:, pixel_count:].T.reshape(2 * capacity)
         codes = jnp.pad(codes, (0, code_rows * pixel_count - 2 * capacity))
-        block = select_dot_t(places[step], traces).astype(jnp.bfloat16)
-        send.append(jnp.concatenate([block, codes.reshape(code_rows, pixel_count)], axis=0))
+        send.append(
+            jnp.concatenate([placed[:, :pixel_count], codes.reshape(code_rows, pixel_count)], axis=0)
+        )
     got = exchange(send, "tile", 1)
     got_traces = [block[:capacity] for block in got]
     got_slots = []

time: 56.7 us -> 57.2 us (level)
  matrix products: 22.4 us -> 20.4 us
  waiting for transfers between devices: 18.3 us -> 19.3 us
  starting transfers between devices: 12.3 us -> 13.2 us
    dot_general x13 -> x10, matrix products: 10.4 us -> 7.46 us  [select_dot_t(): lax.dot_general(selector, values, (((0,), (0,)), ((), ())), preferred_ele...]
    ppermute x6, waiting for transfers between devices: 13.9 us -> 14.9 us  [exchange(): moved.append(lax.ppermute(blocks[step], axis, pairs))]
    ppermute x6, starting transfers between devices: 10.7 us -> 11.6 us  [exchange(): moved.append(lax.ppermute(blocks[step], axis, pairs))]
    dot_general x11, matrix products: 12 us -> 12.9 us  [select_dot(): jnp.dot(selector, values, preferred_element_type=jnp.float32, precision=p...]
  transfers between devices with their start and end apart: 8 -> 8, of which waited for: 6 -> 6; matrix products, arithmetic and copies ran while one was open for 14% -> 11% of each run, Pallas kernels for 0% -> 0%
where the time goes in v6:
time: 57.2 us; the launch traced here: 56.9 us
  matrix products  20.4 us (36%)
  waiting for transfers between devices  19.3 us (34%)
  starting transfers between devices  13.2 us (23%)
  other arithmetic  1.77 us (3%)
  local copies, waits for them, and re-layouts  1.17 us (2%)
  between operations  1.08 us (2%)
    ppermute x6, waiting for transfers between devices, exchange(): moved.append(lax.ppermute(blocks[step], axis, pairs))  14.9 us
    dot_general x11, matrix products, select_dot(): jnp.dot(selector, values, preferred_element_type=jnp.float32, precision=p...  12.9 us
    ppermute x6, starting transfers between devices, exchange(): moved.append(lax.ppermute(blocks[step], axis, pairs))  11.6 us
    dot_general x10, matrix products, select_dot_t(): lax.dot_general(selector, values, (((0,), (0,)), ((), ())), preferred_ele...  7.46 us
    ppermute x1, waiting for transfers between devices, per_device(): sent = lax.ppermute(theirs.astype(jnp.bfloat16), 'dither', [(0, 1), (1, 0)])  2.55 us
    ppermute x1, waiting for transfers between devices, swap_add(): return value + lax.ppermute(value, axis, [(0, 1), (1, 0)])  1.89 us
    ppermute x1, starting transfers between devices, per_device(): sent = lax.ppermute(theirs.astype(jnp.bfloat16), 'dither', [(0, 1), (1, 0)])  1.55 us
  transfers between devices with their start and end apart: 8, of which 6 were waited for; matrix products, arithmetic and copies ran while one was open for 11% of the time, Pallas kernels for 0%

profile of v6, /device:TPU:0, one launch (start us, length us, event | category | flops | bytes accessed | tf_op | source)
XLA Modules:
  0.0 56.9 jit_solution(9559518533639023507)
XLA Ops:
  0.7 0.7 %broadcast_multiply_fusion = s32[1024,1]{0,1:T(1,128)S(1)} fusion(s32[1024,1]{0,1:T(1,128)} %param.15), kind=kLoop, calls=%fused_computation.136 | loop fusion | flops 1024 | bytes 8192 | tf_op jit(solution)/shard_map/mul | solution.py:71
  1.4 1.2 %fusion.59 = f32[1024]{0:T(1024)S(1)} fusion(s32[1024]{0:T(1024)} %bitcast.61), kind=kOutput, calls=%fused_computation.66 | convolution fusion | flops 9464832 | bytes 8192 | tf_op jit(solution)/shard_map/dot_general | solution.py:12
  3.4 0.8 %fusion.50 = bf16[1024,128]{1,0:T(8,128)(2,1)S(1)} fusion(bf16[1024,128]{1,0:T(8,128)(2,1)S(1)} %reshape.145, s32[1024]{0:T(1024)S(1)} %get-tuple-element.3), kind=kOutput, calls=%fused_computation.54 | convolution fusion | flops 269615104 | bytes 528384 | tf_op jit(solution)/shard_map/dot_general | solution.py:12
  4.2 3.9 %fusion.47 = bf16[1024,128]{0,1:T(8,128)(2,1)S(1)} fusion(bf16[16,128,128]{2,1,0:T(8,128)(2,1)S(1)} %copy-done, pred[1024,16]{0,1:T(8,128)(4,1)S(1)} %iota_compare_fusion.64, bf16[1024,128]{1,0:T(8,128)(2,1)S(1)} %fusion.50), kind=kOutput, calls=%fused_computation.53 | convolution fusion | flops 539099136 | bytes 1064960 | tf_op jit(solution)/shard_map/dot_general | solution.py:12
  8.2 0.7 %convolution_convert_fusion.2 = bf16[512,130]{1,0:T(8,128)(2,1)S(1)} fusion(s32[1024]{0:T(1024)S(1)} %bitcast.51, bf16[1024,1]{0,1:T(2,128)(2,1)S(1)} %stack.11, bf16[1024,1]{0,1:T(2,128)(2,1)S(1)} %stack.10, bf16[1024,128]{0,1:T(8,128)(2,1)S(1)} %fusion.47), kind=kOutput, calls=%fused_computation.57 | convolution fusion | flops 138228736 | bytes 403456 | tf_op jit(solution)/shard_map/dot_general | solution.py:16
  9.1 3.1 %collective-permute-start = (bf16[520,128]{1,0:T(8,128)(2,1)S(1)}, bf16[520,128]{1,0:T(8,128)(2,1)S(1)}, u32[]{:S(2)}, u32[]{:S(2)}) collective-permute-start(bf16[520,128]{1,0:T(8,128)(2,1)S(1)} %pad_maximum_fusion.1), channel_id=1, source_target_pairs={{0,4},{4,8},{8,12},{12,0},{1,5},{5,9},{9,13},{13,1},{2,6},{6,10},{... | collective-permute-start | bytes 399368 | tf_op jit(solution)/shard_map/ppermute | solution.py:43
  12.2 0.7 %convolution_convert_fusion.1 = bf16[512,130]{1,0:T(8,128)(2,1)S(1)} fusion(s32[1024]{0:T(1024)S(1)} %bitcast.57, bf16[1024,1]{0,1:T(2,128)(2,1)S(1)} %stack.11, bf16[1024,1]{0,1:T(2,128)(2,1)S(1)} %stack.10, bf16[1024,128]{0,1:T(8,128)(2,1)S(1)} %fusion.47), kind=kOutput, calls=%fused_computation.56 | convolution fusion | flops 138228736 | bytes 403456 | tf_op jit(solution)/shard_map/dot_general | solution.py:16
  13.1 2.6 %collective-permute-start.1 = (bf16[520,128]{1,0:T(8,128)(2,1)S(1)}, bf16[520,128]{1,0:T(8,128)(2,1)S(1)}, u32[]{:S(2)}, u32[]{:S(2)}) collective-permute-start(bf16[520,128]{1,0:T(8,128)(2,1)S(1)} %pad_maximum_fusion.2), channel_id=1, source_target_pairs={{0,8},{4,12},{8,0},{12,4},{1,9},{5,13},{9,1},{13,5},{2,10},{6,14},... | collective-permute-start | bytes 399368 | tf_op jit(solution)/shard_map/ppermute | solution.py:43
  15.7 0.7 %convolution_convert_fusion = bf16[512,130]{1,0:T(8,128)(2,1)S(1)} fusion(s32[1024]{0:T(1024)S(1)} %bitcast.59, bf16[1024,1]{0,1:T(2,128)(2,1)S(1)} %stack.11, bf16[1024,1]{0,1:T(2,128)(2,1)S(1)} %stack.10, bf16[1024,128]{0,1:T(8,128)(2,1)S(1)} %fusion.47), kind=kOutput, calls=%fused_computation.55 | convolution fusion | flops 138228736 | bytes 403456 | tf_op jit(solution)/shard_map/dot_general | solution.py:16
  16.6 1.4 %collective-permute-start.2 = (bf16[520,128]{1,0:T(8,128)(2,1)S(1)}, bf16[520,128]{1,0:T(8,128)(2,1)S(1)}, u32[]{:S(2)}, u32[]{:S(2)}) collective-permute-start(bf16[520,128]{1,0:T(8,128)(2,1)S(1)} %pad_maximum_fusion.3), channel_id=1, source_target_pairs={{0,12},{4,0},{8,4},{12,8},{1,13},{5,1},{9,5},{13,9},{2,14},{6,2},{... | collective-permute-start | bytes 399368 | tf_op jit(solution)/shard_map/ppermute | solution.py:43
  18.0 0.5 fusion.51
  18.6 0.6 fusion.60
  19.2 4.4 %collective-permute-done.1 = bf16[520,128]{1,0:T(8,128)(2,1)S(1)} collective-permute-done((bf16[520,128]{1,0:T(8,128)(2,1)S(1)}, bf16[520,128]{1,0:T(8,128)(2,1)S(1)}, u32[]{:S(2)}, u32[]{:S(2)}) %collective-permute-start.1) | collective-permute-done | bytes 133152 | tf_op jit(solution)/shard_map/ppermute | solution.py:43
  23.6 0.6 %collective-permute-done.2 = bf16[520,128]{1,0:T(8,128)(2,1)S(1)} collective-permute-done((bf16[520,128]{1,0:T(8,128)(2,1)S(1)}, bf16[520,128]{1,0:T(8,128)(2,1)S(1)}, u32[]{:S(2)}, u32[]{:S(2)}) %collective-permute-start.2) | collective-permute-done | bytes 133152 | tf_op jit(solution)/shard_map/ppermute | solution.py:43
  24.2 0.8 %fusion.10 = f32[1024,128]{1,0:T(8,128)S(1)} fusion(s32[512]{0:T(512)S(1)} %add_bitcast_fusion, bf16[520,128]{1,0:T(8,128)(2,1)S(1)} %collective-permute-done.2), kind=kOutput, calls=%fused_computation.14 | convolution fusion | flops 134742016 | bytes 657408 | tf_op jit(solution)/shard_map/dot_general | solution.py:16
  25.0 0.8 %fusion.14 = f32[1024,128]{1,0:T(8,128)S(1)} fusion(s32[512]{0:T(512)S(1)} %add_bitcast_fusion.1, bf16[520,128]{1,0:T(8,128)(2,1)S(1)} %collective-permute-done.1), kind=kOutput, calls=%fused_computation.20 | convolution fusion | flops 134742016 | bytes 657408 | tf_op jit(solution)/shard_map/dot_general | solution.py:16
  25.9 0.8 %fusion.40 = f32[1024,128]{1,0:T(8,128)S(1)} fusion(f32[1024,128]{1,0:T(8,128)S(1)} %fusion.10, f32[1024,128]{1,0:T(8,128)S(1)} %fusion.14, f32[1024,128]{1,0:T(8,128)S(1)} %fusion.60, s32[512]{0:T(512)S(1)} %add_bitcast_fusion.2, bf16[520,128]{1,0:T(8,128)(2,1)S(1)} %collective-permute-done), kind=kOutput, calls=%fused_computation.48 | convolution fusion | flops 135135232 | bytes 2230272 | tf_op jit(solution)/shard_map/dot_general | solution.py:16
  26.8 1.9 %collective-permute-done.3 = f32[1024,128]{1,0:T(8,128)S(1)} collective-permute-done((f32[1024,128]{1,0:T(8,128)S(1)}, f32[1024,128]{1,0:T(8,128)S(1)}, u32[]{:S(2)}, u32[]{:S(2)}) %collective-permute-start.3) | collective-permute-done | bytes 524320 | tf_op jit(solution)/shard_map/ppermute | solution.py:34
  28.8 0.5 fusion.56
  29.4 0.5 fusion.55
  29.9 0.5 fusion.54
  30.4 3.8 %collective-permute-start.4 = (bf16[512,128]{1,0:T(8,128)(2,1)S(1)}, bf16[512,128]{1,0:T(8,128)(2,1)S(1)}, u32[]{:S(2)}, u32[]{:S(2)}) collective-permute-start(bf16[512,128]{1,0:T(8,128)(2,1)S(1)} %fusion.54), channel_id=1, source_target_pairs={{0,12},{4,0},{8,4},{12,8},{1,13},{5,1},{9,5},{13,9},{2,14},{6,2},{... | collective-permute-start | bytes 393224 | tf_op jit(solution)/shard_map/ppermute | solution.py:43
  34.8 1.3 %fusion.27 = f32[1024,128]{1,0:T(8,128)S(1)} fusion(bf16[1024,128]{1,0:T(8,128)(2,1)S(1)} %fusion.85, s32[512]{0:T(512)S(1)} %bitcast.63, s32[1024]{0:T(1024)S(1)} %bitcast.54), kind=kOutput, calls=%fused_computation.38 | convolution fusion | flops 269549568 | bytes 792576 | tf_op jit(solution)/shard_map/dot_general | solution.py:12
  36.1 7.6 %collective-permute-done.6 = bf16[512,128]{1,0:T(8,128)(2,1)S(1)} collective-permute-done((bf16[512,128]{1,0:T(8,128)(2,1)S(1)}, bf16[512,128]{1,0:T(8,128)(2,1)S(1)}, u32[]{:S(2)}, u32[]{:S(2)}) %collective-permute-start.6) | collective-permute-done | bytes 131104 | tf_op jit(solution)/shard_map/ppermute | solution.py:43
  44.2 2.3 %collective-permute-done.5 = bf16[512,128]{1,0:T(8,128)(2,1)S(1)} collective-permute-done((bf16[512,128]{1,0:T(8,128)(2,1)S(1)}, bf16[512,128]{1,0:T(8,128)(2,1)S(1)}, u32[]{:S(2)}, u32[]{:S(2)}) %collective-permute-start.5) | collective-permute-done | bytes 131104 | tf_op jit(solution)/shard_map/ppermute | solution.py:43
  47.0 0.5 fusion.43
  47.6 2.6 %fusion.44 = bf16[1024,128]{1,0:T(8,128)(2,1)S(1)} fusion(pred[1024,16]{0,1:T(8,128)(4,1)S(1)} %iota_compare_fusion.64, bf16[1024,128]{1,0:T(8,128)(2,1)S(1)} %fusion.43, bf16[16,128,128]{2,1,0:T(8,128)(2,1)S(1)} %copy-done), kind=kOutput, calls=%fused_computation.52 | convolution fusion | flops 539099136 | bytes 1064960 | tf_op jit(solution)/shard_map/dot_general | solution.py:12
  50.2 0.9 %fusion.52 = bf16[512,128]{1,0:T(8,128)(2,1)S(1)} fusion(bf16[1024,128]{1,0:T(8,128)(2,1)S(1)} %fusion.44, s32[1024]{0:T(1024)S(1)} %get-tuple-element.2), kind=kOutput, calls=%fused_computation.59 | convolution fusion | flops 134807552 | bytes 397312 | tf_op jit(solution)/shard_map/dot_general | solution.py:16
  51.1 1.6 %collective-permute-start.7 = (bf16[128,512]{1,0:T(8,128)(2,1)S(1)}, bf16[128,512]{1,0:T(8,128)(2,1)S(1)}, u32[]{:S(2)}, u32[]{:S(2)}) collective-permute-start(bf16[128,512]{1,0:T(8,128)(2,1)S(1)} %convert_element_type.141), channel_id=1, source_target_pairs={{0,2},{2,0},{1,3},{3,1},{4,6},{6,4},{5,7},{7,5},{8,10},{10,8},{9,1... | collective-permute-start | bytes 393224 | tf_op jit(solution)/shard_map/ppermute | solution.py:125
  52.7 0.9 %fusion.29 = f32[512,128]{1,0:T(8,128)S(1)} fusion(bf16[1024,128]{1,0:T(8,128)(2,1)S(1)} %fusion.44, s32[1024]{0:T(1024)S(1)} %broadcast_subtract_fusion.1), kind=kOutput, calls=%fused_computation.41 | convolution fusion | flops 134742016 | bytes 528384 | tf_op jit(solution)/shard_map/dot_general | solution.py:16
  53.6 2.5 %collective-permute-done.7 = bf16[128,512]{1,0:T(8,128)(2,1)S(1)} collective-permute-done((bf16[128,512]{1,0:T(8,128)(2,1)S(1)}, bf16[128,512]{1,0:T(8,128)(2,1)S(1)}, u32[]{:S(2)}, u32[]{:S(2)}) %collective-permute-start.7) | collective-permute-done | bytes 131104 | tf_op jit(solution)/shard_map/ppermute | solution.py:125
  56.2 0.7 %convert_add_fusion = f32[128,512]{1,0:T(8,128)} fusion(f32[128,512]{1,0:T(8,128)S(1)} %reshape.149, bf16[128,512]{1,0:T(8,128)(2,1)S(1)} %collective-permute-done.7), kind=kLoop, calls=%fused_computation.91 | loop fusion | flops 131072 | bytes 655360 | tf_op jit(solution)/shard_map/add | solution.py:127
  (61 shorter events, 3.2 us)
Async XLA Ops:
  0.6 3.6 %copy-start = (bf16[16,128,128]{2,1,0:T(8,128)(2,1)S(1)}, bf16[16,128,128]{2,1,0:T(8,128)(2,1)}, u32[]{:S(2)}) copy-start(bf16[16,128,128]{2,1,0:T(8,128)(2,1)} %param.10) | copy-start | bytes 1572868
  1.4 1.3 %copy-start.6 = (s32[1024]{0:T(1024)S(1)}, s32[1024]{0:T(1024)}, u32[]{:S(2)}) copy-start(s32[1024]{0:T(1024)} %param.14) | copy-start | bytes 12292
  1.4 1.3 %copy-start.5 = (s32[1024]{0:T(1024)S(1)}, s32[1024]{0:T(1024)}, u32[]{:S(2)}) copy-start(s32[1024]{0:T(1024)} %param.17) | copy-start | bytes 12292
  1.4 1.4 %copy-start.2 = (bf16[256,512]{1,0:T(8,128)(2,1)S(1)}, bf16[256,512]{1,0:T(8,128)(2,1)}, u32[]{:S(2)}) copy-start(bf16[256,512]{1,0:T(8,128)(2,1)} %param.9) | copy-start | bytes 786436
  2.7 0.7 %copy-start.7 = (s32[1024,1]{0,1:T(1,128)S(1)}, s32[1024,1]{0,1:T(1,128)}, u32[]{:S(2)}) copy-start(s32[1024,1]{0,1:T(1,128)} %param.13) | copy-start | bytes 12292
  2.7 0.7 %copy-start.8 = (s32[1024]{0:T(1024)S(1)}, s32[1024]{0:T(1024)}, u32[]{:S(2)}) copy-start(s32[1024]{0:T(1024)} %param.16) | copy-start | bytes 12292
  9.1 10.1 %collective-permute-start = (bf16[520,128]{1,0:T(8,128)(2,1)S(1)}, bf16[520,128]{1,0:T(8,128)(2,1)S(1)}, u32[]{:S(2)}, u32[]{:S(2)}) collective-permute-start(bf16[520,128]{1,0:T(8,128)(2,1)S(1)} %pad_maximum_fusion.1), channel_id=1, source_target_pairs={{0,4},{4,8},{8,12},{12,0},{1,5},{5,9},{9,13},{13,1},{2,6},{6,10},{... | collective-permute-start | bytes 399368 | tf_op jit(solution)/shard_map/ppermute | solution.py:43
  13.1 10.5 %collective-permute-start.1 = (bf16[520,128]{1,0:T(8,128)(2,1)S(1)}, bf16[520,128]{1,0:T(8,128)(2,1)S(1)}, u32[]{:S(2)}, u32[]{:S(2)}) collective-permute-start(bf16[520,128]{1,0:T(8,128)(2,1)S(1)} %pad_maximum_fusion.2), channel_id=1, source_target_pairs={{0,8},{4,12},{8,0},{12,4},{1,9},{5,13},{9,1},{13,5},{2,10},{6,14},... | collective-permute-start | bytes 399368 | tf_op jit(solution)/shard_map/ppermute | solution.py:43
  16.6 7.6 %collective-permute-start.2 = (bf16[520,128]{1,0:T(8,128)(2,1)S(1)}, bf16[520,128]{1,0:T(8,128)(2,1)S(1)}, u32[]{:S(2)}, u32[]{:S(2)}) collective-permute-start(bf16[520,128]{1,0:T(8,128)(2,1)S(1)} %pad_maximum_fusion.3), channel_id=1, source_target_pairs={{0,12},{4,0},{8,4},{12,8},{1,13},{5,1},{9,5},{13,9},{2,14},{6,2},{... | collective-permute-start | bytes 399368 | tf_op jit(solution)/shard_map/ppermute | solution.py:43
  25.9 2.8 %copy-start.1 = (s32[1,1024,128]{2,1,0:T(8,128)S(1)}, s32[1,1024,128]{2,1,0:T(8,128)}, u32[]{:S(2)}) copy-start(s32[1,1024,128]{2,1,0:T(8,128)} %param.12) | copy-start | bytes 1572868
  25.9 2.8 %copy-start.3 = (bf16[1,1024,128]{2,1,0:T(8,128)(2,1)S(1)}, bf16[1,1024,128]{2,1,0:T(8,128)(2,1)}, u32[]{:S(2)}) copy-start(bf16[1,1024,128]{2,1,0:T(8,128)(2,1)} %param.11) | copy-start | bytes 786436
  26.7 2.0 %collective-permute-start.3 = (f32[1024,128]{1,0:T(8,128)S(1)}, f32[1024,128]{1,0:T(8,128)S(1)}, u32[]{:S(2)}, u32[]{:S(2)}) collective-permute-start(f32[1024,128]{1,0:T(8,128)S(1)} %fusion.40), channel_id=1, source_target_pairs={{0,1},{1,0},{2,3},{3,2},{4,5},{5,4},{6,7},{7,6},{8,9},{9,8},{10,11... | collective-permute-start | bytes 1572872 | tf_op jit(solution)/shard_map/ppermute | solution.py:34
  28.8 6.0 %copy-start.4 = (bf16[1024,128]{1,0:T(8,128)(2,1)}, bf16[1024,128]{1,0:T(8,128)(2,1)S(1)}, u32[]{:S(2)}) copy-start(bf16[1024,128]{1,0:T(8,128)(2,1)S(1)} %fusion.85) | copy-start | bytes 786436
  30.4 16.6 %collective-permute-start.4 = (bf16[512,128]{1,0:T(8,128)(2,1)S(1)}, bf16[512,128]{1,0:T(8,128)(2,1)S(1)}, u32[]{:S(2)}, u32[]{:S(2)}) collective-permute-start(bf16[512,128]{1,0:T(8,128)(2,1)S(1)} %fusion.54), channel_id=1, source_target_pairs={{0,12},{4,0},{8,4},{12,8},{1,13},{5,1},{9,5},{13,9},{2,14},{6,2},{... | collective-permute-start | bytes 393224 | tf_op jit(solution)/shard_map/ppermute | solution.py:43
  34.2 12.4 %collective-permute-start.5 = (bf16[512,128]{1,0:T(8,128)(2,1)S(1)}, bf16[512,128]{1,0:T(8,128)(2,1)S(1)}, u32[]{:S(2)}, u32[]{:S(2)}) collective-permute-start(bf16[512,128]{1,0:T(8,128)(2,1)S(1)} %fusion.55), channel_id=1, source_target_pairs={{0,8},{4,12},{8,0},{12,4},{1,9},{5,13},{9,1},{13,5},{2,10},{6,14},... | collective-permute-start | bytes 393224 | tf_op jit(solution)/shard_map/ppermute | solution.py:43
  34.6 9.1 %collective-permute-start.6 = (bf16[512,128]{1,0:T(8,128)(2,1)S(1)}, bf16[512,128]{1,0:T(8,128)(2,1)S(1)}, u32[]{:S(2)}, u32[]{:S(2)}) collective-permute-start(bf16[512,128]{1,0:T(8,128)(2,1)S(1)} %fusion.56), channel_id=1, source_target_pairs={{0,4},{4,8},{8,12},{12,0},{1,5},{5,9},{9,13},{13,1},{2,6},{6,10},{... | collective-permute-start | bytes 393224 | tf_op jit(solution)/shard_map/ppermute | solution.py:43
  51.1 5.0 %collective-permute-start.7 = (bf16[128,512]{1,0:T(8,128)(2,1)S(1)}, bf16[128,512]{1,0:T(8,128)(2,1)S(1)}, u32[]{:S(2)}, u32[]{:S(2)}) collective-permute-start(bf16[128,512]{1,0:T(8,128)(2,1)S(1)} %convert_element_type.141), channel_id=1, source_target_pairs={{0,2},{2,0},{1,3},{3,1},{4,6},{6,4},{5,7},{7,5},{8,10},{10,8},{9,1... | collective-permute-start | bytes 393224 | tf_op jit(solution)/shard_map/ppermute | solution.py:125

commit v7 on v6

--- a/solution.py
+++ b/solution.py
@@ -1,3 +1,5 @@
+import functools
+
 import jax
 import jax.numpy as jnp
 from jax import lax
@@ -84,15 +86,28 @@
     slot_parts = jnp.stack([trace_slot // 256, trace_slot % 256], axis=1).astype(jnp.bfloat16)
     code_rows = -(-2 * capacity // pixel_count)
     places = [one_hot_rows(dest - step * capacity, capacity) for step in range(tile_count)]
-    with_codes = jnp.concatenate([traces, slot_parts], axis=1)
+    marked_rows = spec_rows + 1
+    local_parts = jnp.stack([marked_rows // 256, marked_rows % 256, kinds], axis=1).astype(jnp.bfloat16)
+    with_codes = jnp.concatenate([traces, slot_parts, local_parts], axis=1)
     send = []
+    block_rows = []
+    block_kinds = []
     for step in range(tile_count):
-        placed = select_dot_t(places[step], with_codes).astype(jnp.bfloat16)
-        codes = placed[:, pixel_count:].T.reshape(2 * capacity)
+        placed = select_dot_t(places[step], with_codes)
+        codes = placed[:, pixel_count : pixel_count + 2].astype(jnp.bfloat16).T.reshape(2 * capacity)
         codes = jnp.pad(codes, (0, code_rows * pixel_count - 2 * capacity))
         send.append(
-            jnp.concatenate([placed[:, :pixel_count], codes.reshape(code_rows, pixel_count)], axis=0)
+            jnp.concatenate(
+                [
+                    placed[:, :pixel_count].astype(jnp.bfloat16),
+                    codes.reshape(code_rows, pixel_count),
+                ],
+                axis=0,
+            )
         )
+        local = placed[:, pixel_count + 2 :].astype(jnp.int32)
+        block_rows.append(local[:, 0] * 256 + local[:, 1] - 1)
+        block_kinds.append(local[:, 2])
     got = exchange(send, "tile", 1)
     got_traces = [block[:capacity] for block in got]
     got_slots = []
@@ -110,24 +125,30 @@
 
     under_rows = [select_dot(a, residual).astype(jnp.bfloat16) for a in at_slot]
     returned = exchange(under_rows, "tile", -1)
-    entry_rows = sum(select_dot(p, r) for p, r in zip(places, returned)).astype(jnp.bfloat16)
     back_table = psf_blocks.transpose(0, 2, 1).reshape(table_count * pixel_count, bin_count)
-    terms = select_dot(spread_by_kind(entry_rows, kinds, table_count), back_table)
-    terms = terms.astype(jnp.bfloat16)
+    block_terms = [
+        select_dot(spread_by_kind(rows, kinds_here, table_count), back_table).astype(jnp.bfloat16)
+        for rows, kinds_here in zip(returned, block_kinds)
+    ]
+
+    def gathered(offset, width):
+        parts = [
+            select_dot_t(one_hot_rows(rows - offset, width), terms)
+            for rows, terms in zip(block_rows, block_terms)
+        ]
+        return functools.reduce(jnp.add, parts)
 
     if dither_count == 2:
         dither = lax.axis_index("dither")
         half_rows = row_count // 2
         own_start = dither * half_rows
-        their_rows = one_hot_rows(spec_rows - (half_rows - own_start), half_rows)
-        own_rows = one_hot_rows(spec_rows - own_start, half_rows)
-        theirs = select_dot_t(their_rows, terms).reshape(source_count // 2, block_count * bin_count)
+        theirs = gathered(half_rows - own_start, half_rows)
+        theirs = theirs.reshape(source_count // 2, block_count * bin_count)
         sent = lax.ppermute(theirs.astype(jnp.bfloat16), "dither", [(0, 1), (1, 0)])
-        mine = select_dot_t(own_rows, terms).reshape(source_count // 2, block_count * bin_count)
+        mine = gathered(own_start, half_rows).reshape(source_count // 2, block_count * bin_count)
         gradient = mine + sent.astype(jnp.float32)
     else:
-        local_grad = select_dot_t(gather_spec, terms)
-        local_grad = local_grad.reshape(source_count, block_count * bin_count)
+        local_grad = gathered(0, row_count).reshape(source_count, block_count * bin_count)
         gradient = lax.psum_scatter(local_grad, "dither", scatter_dimension=0, tiled=True)
     return (gradient, residual[None])
 

time: 57.2 us -> 60.2 us (1.052)
  matrix products: 20.4 us -> 23.7 us
  waiting for transfers between devices: 19.3 us -> 16.7 us
  other arithmetic: 1.77 us -> 3.97 us
    dot_general x10 -> x16, matrix products: 7.46 us -> 9.62 us  [select_dot_t(): lax.dot_general(selector, values, (((0,), (0,)), ((), ())), preferred_ele...]
    ppermute x6, waiting for transfers between devices: 14.9 us -> 13.1 us  [exchange(): moved.append(lax.ppermute(blocks[step], axis, pairs))]
    another operation x1 -> x4, other arithmetic: 0.01 us -> 1.47 us
    dot_general x11, matrix products: 12.9 us -> 14 us  [select_dot(): jnp.dot(selector, values, preferred_element_type=jnp.float32, precision=p...]
    ppermute x1, waiting for transfers between devices: 2.55 us -> 1.8 us  [per_device(): sent = lax.ppermute(theirs.astype(jnp.bfloat16), 'dither', [(0, 1), (1, 0)])]
    eq x1 -> x5, other arithmetic: 0.01 us -> 0.74 us  [spread_by_kind(): kinds[:, None, None]]
  transfers between devices with their start and end apart: 8 -> 8, of which waited for: 6 -> 4; matrix products, arithmetic and copies ran while one was open for 11% -> 19% of each run, Pallas kernels for 0% -> 0%
where the time goes in v7:
time: 60.2 us; the launch traced here: 59.9 us
  matrix products  23.7 us (39%)
  waiting for transfers between devices  16.7 us (28%)
  starting transfers between devices  12.9 us (21%)
  other arithmetic  3.97 us (7%)
  local copies, waits for them, and re-layouts  1.33 us (2%)
  between operations  1.32 us (2%)
    dot_general x11, matrix products, select_dot(): jnp.dot(selector, values, preferred_element_type=jnp.float32, precision=p...  14 us
    ppermute x6, waiting for transfers between devices, exchange(): moved.append(lax.ppermute(blocks[step], axis, pairs))  13.1 us
    ppermute x6, starting transfers between devices, exchange(): moved.append(lax.ppermute(blocks[step], axis, pairs))  11.2 us
    dot_general x16, matrix products, select_dot_t(): lax.dot_general(selector, values, (((0,), (0,)), ((), ())), preferred_ele...  9.62 us
    ppermute x1, waiting for transfers between devices, swap_add(): return value + lax.ppermute(value, axis, [(0, 1), (1, 0)])  1.85 us
    ppermute x1, waiting for transfers between devices, per_device(): sent = lax.ppermute(theirs.astype(jnp.bfloat16), 'dither', [(0, 1), (1, 0)])  1.8 us
    ppermute x1, starting transfers between devices, per_device(): sent = lax.ppermute(theirs.astype(jnp.bfloat16), 'dither', [(0, 1), (1, 0)])  1.55 us
    another operation x4, other arithmetic  1.47 us
  transfers between devices with their start and end apart: 8, of which 4 were waited for; matrix products, arithmetic and copies ran while one was open for 19% of the time, Pallas kernels for 0%

profile of v7, /device:TPU:0, one launch (start us, length us, event | category | flops | bytes accessed | tf_op | source)
XLA Modules:
  0.0 59.9 jit_solution(2005569089412716441)
XLA Ops:
  0.6 0.7 %convert.42 = bf16[1024]{0:T(1024)(128)(2,1)S(1)} convert(s32[1024]{0:T(1024)} %param.17) | non-fusion elementwise | flops 1024 | bytes 6144 | tf_op jit(solution)/shard_map/convert.13
  1.4 0.7 %iota_compare_fusion.61 = pred[1024,16]{0,1:T(8,128)(4,1)S(1)} fusion(s32[1024]{0:T(1024)} %param.17), kind=kLoop, calls=%fused_computation.127 | loop fusion | flops 16384 | bytes 20480 | tf_op jit(solution)/shard_map/eq | solution.py:28
  2.1 0.7 %broadcast_multiply_fusion = s32[1024,1]{0,1:T(1,128)S(1)} fusion(s32[1024,1]{0,1:T(1,128)} %param.15), kind=kLoop, calls=%fused_computation.190 | loop fusion | flops 1024 | bytes 8192 | tf_op jit(solution)/shard_map/mul | solution.py:73
  2.8 0.7 %fusion.121 = (bf16[1024]{0:T(1024)(128)(2,1)S(1)}, s32[1024]{0:T(1024)S(1)}) fusion(s32[1024]{0:T(1024)S(1)} %bitcast.88, s32[1024]{0:T(1024)} %param.16), kind=kLoop, calls=%fused_computation.155 | loop fusion | flops 14336 | bytes 14336 | tf_op jit(solution)/shard_map/convert.14
  3.6 1.3 %fusion.73 = f32[1024]{0:T(1024)S(1)} fusion(s32[1024]{0:T(1024)} %bitcast.102), kind=kOutput, calls=%fused_computation.69 | convolution fusion | flops 9464832 | bytes 8192 | tf_op jit(solution)/shard_map/dot_general | solution.py:14
  5.2 0.8 %fusion.41 = bf16[1024,128]{1,0:T(8,128)(2,1)S(1)} fusion(bf16[1024,128]{1,0:T(8,128)(2,1)S(1)} %reshape.255, s32[1024]{0:T(1024)S(1)} %get-tuple-element.13), kind=kOutput, calls=%fused_computation.47 | convolution fusion | flops 269615104 | bytes 528384 | tf_op jit(solution)/shard_map/dot_general | solution.py:14
  6.0 3.9 %fusion.38 = bf16[1024,128]{0,1:T(8,128)(2,1)S(1)} fusion(bf16[16,128,128]{2,1,0:T(8,128)(2,1)S(1)} %copy-done, pred[1024,16]{0,1:T(8,128)(4,1)S(1)} %iota_compare_fusion.61, bf16[1024,128]{1,0:T(8,128)(2,1)S(1)} %fusion.41), kind=kOutput, calls=%fused_computation.46 | convolution fusion | flops 539099136 | bytes 1064960 | tf_op jit(solution)/shard_map/dot_general | solution.py:14
  11.0 5.1 %collective-permute-start.2 = (bf16[520,128]{1,0:T(8,128)(2,1)S(1)}, bf16[520,128]{1,0:T(8,128)(2,1)S(1)}, u32[]{:S(2)}, u32[]{:S(2)}) collective-permute-start(bf16[520,128]{1,0:T(8,128)(2,1)S(1)} %pad_maximum_fusion.2), channel_id=1, source_target_pairs={{0,12},{4,0},{8,4},{12,8},{1,13},{5,1},{9,5},{13,9},{2,14},{6,2},{... | collective-permute-start | bytes 399368 | tf_op jit(solution)/shard_map/ppermute | solution.py:45
  17.9 1.1 %collective-permute-start = (bf16[520,128]{1,0:T(8,128)(2,1)S(1)}, bf16[520,128]{1,0:T(8,128)(2,1)S(1)}, u32[]{:S(2)}, u32[]{:S(2)}) collective-permute-start(bf16[520,128]{1,0:T(8,128)(2,1)S(1)} %pad_maximum_fusion), channel_id=1, source_target_pairs={{0,4},{4,8},{8,12},{12,0},{1,5},{5,9},{9,13},{13,1},{2,6},{6,10},{... | collective-permute-start | bytes 399368 | tf_op jit(solution)/shard_map/ppermute | solution.py:45
  19.7 0.6 fusion.74
  20.3 7.6 %collective-permute-done.1 = bf16[520,128]{1,0:T(8,128)(2,1)S(1)} collective-permute-done((bf16[520,128]{1,0:T(8,128)(2,1)S(1)}, bf16[520,128]{1,0:T(8,128)(2,1)S(1)}, u32[]{:S(2)}, u32[]{:S(2)}) %collective-permute-start.1) | collective-permute-done | bytes 133152 | tf_op jit(solution)/shard_map/ppermute | solution.py:45
  27.9 0.8 %fusion.16 = f32[1024,128]{1,0:T(8,128)S(1)} fusion(s32[512]{0:T(512)S(1)} %add_bitcast_fusion.1, bf16[520,128]{1,0:T(8,128)(2,1)S(1)} %collective-permute-done.1), kind=kOutput, calls=%fused_computation.21 | convolution fusion | flops 134742016 | bytes 657408 | tf_op jit(solution)/shard_map/dot_general | solution.py:18
  28.8 0.8 %fusion.14 = f32[1024,128]{1,0:T(8,128)S(1)} fusion(s32[512]{0:T(512)S(1)} %add_bitcast_fusion, bf16[520,128]{1,0:T(8,128)(2,1)S(1)} %collective-permute-done.2), kind=kOutput, calls=%fused_computation.17 | convolution fusion | flops 134742016 | bytes 657408 | tf_op jit(solution)/shard_map/dot_general | solution.py:18
  29.6 0.8 %fusion.37 = f32[1024,128]{1,0:T(8,128)S(1)} fusion(f32[1024,128]{1,0:T(8,128)S(1)} %fusion.14, f32[1024,128]{1,0:T(8,128)S(1)} %fusion.16, f32[1024,128]{1,0:T(8,128)S(1)} %fusion.74, s32[512]{0:T(512)S(1)} %add_bitcast_fusion.2, bf16[520,128]{1,0:T(8,128)(2,1)S(1)} %collective-permute-done), kind=kOutput, calls=%fused_computation.45 | convolution fusion | flops 135135232 | bytes 2230272 | tf_op jit(solution)/shard_map/dot_general | solution.py:18
  30.6 1.9 %collective-permute-done.3 = f32[1024,128]{1,0:T(8,128)S(1)} collective-permute-done((f32[1024,128]{1,0:T(8,128)S(1)}, f32[1024,128]{1,0:T(8,128)S(1)}, u32[]{:S(2)}, u32[]{:S(2)}) %collective-permute-start.3) | collective-permute-done | bytes 524320 | tf_op jit(solution)/shard_map/ppermute | solution.py:36
  34.6 1.2 %collective-permute-start.4 = (bf16[512,128]{1,0:T(8,128)(2,1)S(1)}, bf16[512,128]{1,0:T(8,128)(2,1)S(1)}, u32[]{:S(2)}, u32[]{:S(2)}) collective-permute-start(bf16[512,128]{1,0:T(8,128)(2,1)S(1)} %fusion.68), channel_id=1, source_target_pairs={{0,12},{4,0},{8,4},{12,8},{1,13},{5,1},{9,5},{13,9},{2,14},{6,2},{... | collective-permute-start | bytes 393224 | tf_op jit(solution)/shard_map/ppermute | solution.py:45
  35.8 1.9 %collective-permute-start.5 = (bf16[512,128]{1,0:T(8,128)(2,1)S(1)}, bf16[512,128]{1,0:T(8,128)(2,1)S(1)}, u32[]{:S(2)}, u32[]{:S(2)}) collective-permute-start(bf16[512,128]{1,0:T(8,128)(2,1)S(1)} %fusion.69), channel_id=1, source_target_pairs={{0,8},{4,12},{8,0},{12,4},{1,9},{5,13},{9,1},{13,5},{2,10},{6,14},... | collective-permute-start | bytes 393224 | tf_op jit(solution)/shard_map/ppermute | solution.py:45
  37.7 1.9 %collective-permute-start.6 = (bf16[512,128]{1,0:T(8,128)(2,1)S(1)}, bf16[512,128]{1,0:T(8,128)(2,1)S(1)}, u32[]{:S(2)}, u32[]{:S(2)}) collective-permute-start(bf16[512,128]{1,0:T(8,128)(2,1)S(1)} %fusion.70), channel_id=1, source_target_pairs={{0,4},{4,8},{8,12},{12,0},{1,5},{5,9},{9,13},{13,1},{2,6},{6,10},{... | collective-permute-start | bytes 393224 | tf_op jit(solution)/shard_map/ppermute | solution.py:45
  39.6 1.5 %fusion.64 = bf16[512,128]{1,0:T(8,128)(2,1)S(1)} fusion(pred[512,16]{0,1:T(8,128)(4,1)S(1)} %iota_compare_fusion.65, bf16[512,128]{1,0:T(8,128)(2,1)S(1)} %fusion.67, bf16[16,128,128]{2,1,0:T(8,128)(2,1)S(1)} %copy-done), kind=kOutput, calls=%fused_computation.62 | convolution fusion | flops 269549568 | bytes 794624 | tf_op jit(solution)/shard_map/dot_general | solution.py:14
  41.1 0.6 fusion.97
  41.7 0.6 fusion.96
  42.3 1.5 %fusion.61 = bf16[512,128]{1,0:T(8,128)(2,1)S(1)} fusion(pred[512,16]{0,1:T(8,128)(4,1)S(1)} %iota_compare_fusion.64, bf16[512,128]{1,0:T(8,128)(2,1)S(1)} %collective-permute-done.4, bf16[16,128,128]{2,1,0:T(8,128)(2,1)S(1)} %copy-done), kind=kOutput, calls=%fused_computation.61 | convolution fusion | flops 269549568 | bytes 794624 | tf_op jit(solution)/shard_map/dot_general | solution.py:14
  43.8 0.6 convolution_add_fusion.2
  44.3 5.5 %collective-permute-done.5 = bf16[512,128]{1,0:T(8,128)(2,1)S(1)} collective-permute-done((bf16[512,128]{1,0:T(8,128)(2,1)S(1)}, bf16[512,128]{1,0:T(8,128)(2,1)S(1)}, u32[]{:S(2)}, u32[]{:S(2)}) %collective-permute-start.5) | collective-permute-done | bytes 131104 | tf_op jit(solution)/shard_map/ppermute | solution.py:45
  49.8 1.5 %fusion.58 = bf16[512,128]{1,0:T(8,128)(2,1)S(1)} fusion(pred[512,16]{0,1:T(8,128)(4,1)S(1)} %iota_compare_fusion.63, bf16[512,128]{1,0:T(8,128)(2,1)S(1)} %collective-permute-done.5, bf16[16,128,128]{2,1,0:T(8,128)(2,1)S(1)} %copy-done), kind=kOutput, calls=%fused_computation.60 | convolution fusion | flops 269549568 | bytes 794624 | tf_op jit(solution)/shard_map/dot_general | solution.py:14
  51.3 0.6 convolution_add_fusion.1
  51.9 1.5 %fusion.55 = bf16[512,128]{1,0:T(8,128)(2,1)S(1)} fusion(pred[512,16]{0,1:T(8,128)(4,1)S(1)} %iota_compare_fusion.62, bf16[512,128]{1,0:T(8,128)(2,1)S(1)} %collective-permute-done.6, bf16[16,128,128]{2,1,0:T(8,128)(2,1)S(1)} %copy-done), kind=kOutput, calls=%fused_computation.59 | convolution fusion | flops 269549568 | bytes 794624 | tf_op jit(solution)/shard_map/dot_general | solution.py:14
  54.0 1.6 %collective-permute-start.7 = (bf16[128,512]{1,0:T(8,128)(2,1)S(1)}, bf16[128,512]{1,0:T(8,128)(2,1)S(1)}, u32[]{:S(2)}, u32[]{:S(2)}) collective-permute-start(bf16[128,512]{1,0:T(8,128)(2,1)S(1)} %convert_element_type.164), channel_id=1, source_target_pairs={{0,2},{2,0},{1,3},{3,1},{4,6},{6,4},{5,7},{7,5},{8,10},{10,8},{9,1... | collective-permute-start | bytes 393224 | tf_op jit(solution)/shard_map/ppermute | solution.py:147
  56.2 0.6 convolution_add_fusion.4
  56.7 0.6 convolution_add_fusion.3
  57.3 1.8 %collective-permute-done.7 = bf16[128,512]{1,0:T(8,128)(2,1)S(1)} collective-permute-done((bf16[128,512]{1,0:T(8,128)(2,1)S(1)}, bf16[128,512]{1,0:T(8,128)(2,1)S(1)}, u32[]{:S(2)}, u32[]{:S(2)}) %collective-permute-start.7) | collective-permute-done | bytes 131104 | tf_op jit(solution)/shard_map/ppermute | solution.py:147
  59.1 0.7 %convert_add_fusion = f32[128,512]{1,0:T(8,128)} fusion(f32[128,512]{1,0:T(8,128)S(1)} %reshape.259, bf16[128,512]{1,0:T(8,128)(2,1)S(1)} %collective-permute-done.7), kind=kLoop, calls=%fused_computation.116 | loop fusion | flops 131072 | bytes 655360 | tf_op jit(solution)/shard_map/add | solution.py:149
  (87 shorter events, 7.2 us)
Async XLA Ops:
  0.6 5.4 %copy-start = (bf16[16,128,128]{2,1,0:T(8,128)(2,1)S(1)}, bf16[16,128,128]{2,1,0:T(8,128)(2,1)}, u32[]{:S(2)}) copy-start(bf16[16,128,128]{2,1,0:T(8,128)(2,1)} %param.10) | copy-start | bytes 1572868
  3.5 1.3 %copy-start.5 = (s32[1024]{0:T(1024)S(1)}, s32[1024]{0:T(1024)}, u32[]{:S(2)}) copy-start(s32[1024]{0:T(1024)} %param.14) | copy-start | bytes 12292
  3.6 1.4 %copy-start.6 = (s32[1024,1]{0,1:T(1,128)S(1)}, s32[1024,1]{0,1:T(1,128)}, u32[]{:S(2)}) copy-start(s32[1024,1]{0,1:T(1,128)} %param.13) | copy-start | bytes 12292
  3.6 1.4 %copy-start.2 = (bf16[256,512]{1,0:T(8,128)(2,1)S(1)}, bf16[256,512]{1,0:T(8,128)(2,1)}, u32[]{:S(2)}) copy-start(bf16[256,512]{1,0:T(8,128)(2,1)} %param.9) | copy-start | bytes 786436
  11.0 9.3 %collective-permute-start.2 = (bf16[520,128]{1,0:T(8,128)(2,1)S(1)}, bf16[520,128]{1,0:T(8,128)(2,1)S(1)}, u32[]{:S(2)}, u32[]{:S(2)}) collective-permute-start(bf16[520,128]{1,0:T(8,128)(2,1)S(1)} %pad_maximum_fusion.2), channel_id=1, source_target_pairs={{0,12},{4,0},{8,4},{12,8},{1,13},{5,1},{9,5},{13,9},{2,14},{6,2},{... | collective-permute-start | bytes 399368 | tf_op jit(solution)/shard_map/ppermute | solution.py:45
  16.9 11.0 %collective-permute-start.1 = (bf16[520,128]{1,0:T(8,128)(2,1)S(1)}, bf16[520,128]{1,0:T(8,128)(2,1)S(1)}, u32[]{:S(2)}, u32[]{:S(2)}) collective-permute-start(bf16[520,128]{1,0:T(8,128)(2,1)S(1)} %pad_maximum_fusion.1), channel_id=1, source_target_pairs={{0,8},{4,12},{8,0},{12,4},{1,9},{5,13},{9,1},{13,5},{2,10},{6,14},... | collective-permute-start | bytes 399368 | tf_op jit(solution)/shard_map/ppermute | solution.py:45
  17.9 10.0 %collective-permute-start = (bf16[520,128]{1,0:T(8,128)(2,1)S(1)}, bf16[520,128]{1,0:T(8,128)(2,1)S(1)}, u32[]{:S(2)}, u32[]{:S(2)}) collective-permute-start(bf16[520,128]{1,0:T(8,128)(2,1)S(1)} %pad_maximum_fusion), channel_id=1, source_target_pairs={{0,4},{4,8},{8,12},{12,0},{1,5},{5,9},{9,13},{13,1},{2,6},{6,10},{... | collective-permute-start | bytes 399368 | tf_op jit(solution)/shard_map/ppermute | solution.py:45
  29.6 2.8 %copy-start.1 = (s32[1,1024,128]{2,1,0:T(8,128)S(1)}, s32[1,1024,128]{2,1,0:T(8,128)}, u32[]{:S(2)}) copy-start(s32[1,1024,128]{2,1,0:T(8,128)} %param.12) | copy-start | bytes 1572868
  29.6 2.8 %copy-start.3 = (bf16[1,1024,128]{2,1,0:T(8,128)(2,1)S(1)}, bf16[1,1024,128]{2,1,0:T(8,128)(2,1)}, u32[]{:S(2)}) copy-start(bf16[1,1024,128]{2,1,0:T(8,128)(2,1)} %param.11) | copy-start | bytes 786436
  30.5 2.0 %collective-permute-start.3 = (f32[1024,128]{1,0:T(8,128)S(1)}, f32[1024,128]{1,0:T(8,128)S(1)}, u32[]{:S(2)}, u32[]{:S(2)}) collective-permute-start(f32[1024,128]{1,0:T(8,128)S(1)} %fusion.37), channel_id=1, source_target_pairs={{0,1},{1,0},{2,3},{3,2},{4,5},{5,4},{6,7},{7,6},{8,9},{9,8},{10,11... | collective-permute-start | bytes 1572872 | tf_op jit(solution)/shard_map/ppermute | solution.py:36
  32.5 1.6 %copy-start.4 = (bf16[1024,128]{1,0:T(8,128)(2,1)}, bf16[1024,128]{1,0:T(8,128)(2,1)S(1)}, u32[]{:S(2)}) copy-start(bf16[1024,128]{1,0:T(8,128)(2,1)S(1)} %fusion.99) | copy-start | bytes 786436
  34.6 7.6 %collective-permute-start.4 = (bf16[512,128]{1,0:T(8,128)(2,1)S(1)}, bf16[512,128]{1,0:T(8,128)(2,1)S(1)}, u32[]{:S(2)}, u32[]{:S(2)}) collective-permute-start(bf16[512,128]{1,0:T(8,128)(2,1)S(1)} %fusion.68), channel_id=1, source_target_pairs={{0,12},{4,0},{8,4},{12,8},{1,13},{5,1},{9,5},{13,9},{2,14},{6,2},{... | collective-permute-start | bytes 393224 | tf_op jit(solution)/shard_map/ppermute | solution.py:45
  35.8 14.0 %collective-permute-start.5 = (bf16[512,128]{1,0:T(8,128)(2,1)S(1)}, bf16[512,128]{1,0:T(8,128)(2,1)S(1)}, u32[]{:S(2)}, u32[]{:S(2)}) collective-permute-start(bf16[512,128]{1,0:T(8,128)(2,1)S(1)} %fusion.69), channel_id=1, source_target_pairs={{0,8},{4,12},{8,0},{12,4},{1,9},{5,13},{9,1},{13,5},{2,10},{6,14},... | collective-permute-start | bytes 393224 | tf_op jit(solution)/shard_map/ppermute | solution.py:45
  37.7 14.2 %collective-permute-start.6 = (bf16[512,128]{1,0:T(8,128)(2,1)S(1)}, bf16[512,128]{1,0:T(8,128)(2,1)S(1)}, u32[]{:S(2)}, u32[]{:S(2)}) collective-permute-start(bf16[512,128]{1,0:T(8,128)(2,1)S(1)} %fusion.70), channel_id=1, source_target_pairs={{0,4},{4,8},{8,12},{12,0},{1,5},{5,9},{9,13},{13,1},{2,6},{6,10},{... | collective-permute-start | bytes 393224 | tf_op jit(solution)/shard_map/ppermute | solution.py:45
  54.0 5.1 %collective-permute-start.7 = (bf16[128,512]{1,0:T(8,128)(2,1)S(1)}, bf16[128,512]{1,0:T(8,128)(2,1)S(1)}, u32[]{:S(2)}, u32[]{:S(2)}) collective-permute-start(bf16[128,512]{1,0:T(8,128)(2,1)S(1)} %convert_element_type.164), channel_id=1, source_target_pairs={{0,2},{2,0},{1,3},{3,1},{4,6},{6,4},{5,7},{7,5},{8,10},{10,8},{9,1... | collective-permute-start | bytes 393224 | tf_op jit(solution)/shard_map/ppermute | solution.py:147

commit v8 on v4

--- a/solution.py
+++ b/solution.py
@@ -1,7 +1,51 @@
 import jax
 import jax.numpy as jnp
 from jax import lax
+from jax.experimental import pallas as pl
 from jax.sharding import PartitionSpec as P
+
+
+def source_kernel(rows_ref, kinds_ref, dest_ref, slots_ref, spectra_ref, psf_ref, blocks_ref, codes_ref):
+    entry_count = rows_ref.shape[0]
+    row_count = spectra_ref.shape[0]
+    table_count = psf_ref.shape[0]
+    tile_count, capacity, pixel_count = blocks_ref.shape
+    gather = rows_ref[...] == lax.broadcasted_iota(jnp.int32, (entry_count, row_count), 1)
+    spec = jnp.dot(
+        gather.astype(jnp.bfloat16), spectra_ref[...], preferred_element_type=jnp.float32
+    ).astype(jnp.bfloat16)
+    kinds = kinds_ref[...]
+    acc = jnp.zeros((entry_count, pixel_count), jnp.float32)
+    for kind in range(table_count):
+        chosen = jnp.where(kinds == kind, spec, jnp.zeros_like(spec))
+        acc = acc + jnp.dot(chosen, psf_ref[kind], preferred_element_type=jnp.float32)
+    traces = acc.astype(jnp.bfloat16)
+    dest = dest_ref[...]
+    slots = slots_ref[...]
+    for step in range(tile_count):
+        spots = lax.broadcasted_iota(jnp.int32, (capacity, entry_count), 0) + step * capacity
+        place = (dest == spots).astype(jnp.bfloat16)
+        blocks_ref[step] = jnp.dot(place, traces, preferred_element_type=jnp.float32).astype(
+            jnp.bfloat16
+        )
+        codes_ref[step] = lax.dot_general(
+            slots, place, (((1,), (1,)), ((), ())), preferred_element_type=jnp.float32
+        )
+
+
+def source_forward(spec_rows, kinds, dest, trace_slot, spectra_flat, psf_blocks, tile_count, capacity):
+    entry_count = spec_rows.shape[0]
+    pixel_count = psf_blocks.shape[2]
+    slots = jnp.zeros((8, entry_count), jnp.bfloat16)
+    slots = slots.at[0].set((trace_slot // 256).astype(jnp.bfloat16))
+    slots = slots.at[1].set((trace_slot % 256).astype(jnp.bfloat16))
+    return pl.pallas_call(
+        source_kernel,
+        out_shape=(
+            jax.ShapeDtypeStruct((tile_count, capacity, pixel_count), jnp.bfloat16),
+            jax.ShapeDtypeStruct((tile_count, 8, capacity), jnp.float32),
+        ),
+    )(spec_rows[:, None], kinds[:, None], dest[None, :], slots, spectra_flat, psf_blocks)
 
 
 def one_hot_rows(index, width):
@@ -78,18 +122,22 @@
     dest = shift * capacity + position
 
     gather_spec = one_hot_rows(spec_rows, row_count)
-    spec_values = select_dot(gather_spec, spectra.reshape(row_count, bin_count)).astype(jnp.bfloat16)
-    psf_flat = psf_blocks.reshape(table_count * bin_count, pixel_count)
-    traces = select_dot(spread_by_kind(spec_values, kinds, table_count), psf_flat).astype(jnp.bfloat16)
-    slot_parts = jnp.stack([trace_slot // 256, trace_slot % 256], axis=1).astype(jnp.bfloat16)
     code_rows = -(-2 * capacity // pixel_count)
+    placed, placed_codes = source_forward(
+        spec_rows,
+        kinds,
+        dest,
+        trace_slot,
+        spectra.reshape(row_count, bin_count),
+        psf_blocks,
+        tile_count,
+        capacity,
+    )
+    codes = placed_codes[:, :2].astype(jnp.bfloat16).reshape(tile_count, 2 * capacity)
+    codes = jnp.pad(codes, ((0, 0), (0, code_rows * pixel_count - 2 * capacity)))
+    send = jnp.concatenate([placed, codes.reshape(tile_count, code_rows, pixel_count)], axis=1)
+    send = [send[step] for step in range(tile_count)]
     places = [one_hot_rows(dest - step * capacity, capacity) for step in range(tile_count)]
-    send = []
-    for step in range(tile_count):
-        codes = select_dot_t(slot_parts, places[step]).astype(jnp.bfloat16).reshape(2 * capacity)
-        codes = jnp.pad(codes, (0, code_rows * pixel_count - 2 * capacity))
-        block = select_dot_t(places[step], traces).astype(jnp.bfloat16)
-        send.append(jnp.concatenate([block, codes.reshape(code_rows, pixel_count)], axis=0))
     got = exchange(send, "tile", 1)
     got_traces = [block[:capacity] for block in got]
     got_slots = []

time: 56.7 us -> 64.8 us (1.14)
  Pallas kernels: 0 us -> 8.34 us
  matrix products: 22.4 us -> 14.1 us
  local copies, waits for them, and re-layouts: 0.67 us -> 5.41 us
  waiting for transfers between devices: 18.3 us -> 22.5 us
  starting transfers between devices: 12.3 us -> 10.1 us
  other arithmetic: 1.76 us -> 3.12 us
    pallas_call x0 -> x1, Pallas kernels: none -> 8.34 us  [source_forward(): pl.pallas_call(source_kernel, out_shape=(jax.ShapeDtypeStruct((tile_count...]
    dot_general x13 -> x6, matrix products: 10.4 us -> 5.93 us  [select_dot_t(): lax.dot_general(selector, values, (((0,), (0,)), ((), ())), preferred_ele...]
    ppermute x6, waiting for transfers between devices: 13.9 us -> 18.1 us  [exchange(): moved.append(lax.ppermute(blocks[step], axis, pairs))]
    dot_general x11 -> x9, matrix products: 12 us -> 8.16 us  [select_dot(): jnp.dot(selector, values, preferred_element_type=jnp.float32, precision=p...]
    ppermute x6, starting transfers between devices: 10.7 us -> 8.44 us  [exchange(): moved.append(lax.ppermute(blocks[step], axis, pairs))]
    broadcast_in_dim x0 -> x2, local copies, waits for them, and re-layouts: none -> 2.06 us  [the longest x1 1.04 us: source_forward(): spec_rows[:, None]]
    unnamed x18 -> x21, local copies, waits for them, and re-layouts: 0.33 us -> 2.22 us
    another operation x2 -> x1, other arithmetic: 0.03 us -> 0.85 us  [the longest x1 0.02 us: per_device(): jnp.stack([trace_slot // 256, trace_slot % 256], axis=1)]
  transfers between devices with their start and end apart: 8 -> 8, of which waited for: 6 -> 8; matrix products, arithmetic and copies ran while one was open for 14% -> 8% of each run, Pallas kernels for 0% -> 0%
where the time goes in v8:
time: 64.8 us; the launch traced here: 64.4 us
  waiting for transfers between devices  22.5 us (35%)
  matrix products  14.1 us (22%)
  starting transfers between devices  10.1 us (16%)
  Pallas kernels  8.34 us (13%)
  local copies, waits for them, and re-layouts  5.41 us (8%)
  other arithmetic  3.12 us (5%)
  between operations  0.92 us (1%)
    ppermute x6, waiting for transfers between devices, exchange(): moved.append(lax.ppermute(blocks[step], axis, pairs))  18.1 us
    ppermute x6, starting transfers between devices, exchange(): moved.append(lax.ppermute(blocks[step], axis, pairs))  8.44 us
    pallas_call x1, Pallas kernels, source_forward(): pl.pallas_call(source_kernel, out_shape=(jax.ShapeDtypeStruct((tile_count...  8.34 us
    dot_general x9, matrix products, select_dot(): jnp.dot(selector, values, preferred_element_type=jnp.float32, precision=p...  8.16 us
    dot_general x6, matrix products, select_dot_t(): lax.dot_general(selector, values, (((0,), (0,)), ((), ())), preferred_ele...  5.93 us
    ppermute x1, waiting for transfers between devices, per_device(): sent = lax.ppermute(theirs.astype(jnp.bfloat16), 'dither', [(0, 1), (1, 0)])  2.54 us
    unnamed x21, local copies, waits for them, and re-layouts  2.22 us
    ppermute x1, waiting for transfers between devices, swap_add(): return value + lax.ppermute(value, axis, [(0, 1), (1, 0)])  1.85 us
  transfers between devices with their start and end apart: 8, of which 8 were waited for; matrix products, arithmetic and copies ran while one was open for 8% of the time, Pallas kernels for 0%

profile of v8, /device:TPU:0, one launch (start us, length us, event | category | flops | bytes accessed | tf_op | source)
XLA Modules:
  0.0 64.4 jit_solution(8365578976207758554)
XLA Ops:
  0.6 0.7 %broadcast_multiply_fusion = s32[1024,1]{0,1:T(1,128)S(1)} fusion(s32[1024,1]{0,1:T(1,128)} %param.19), kind=kLoop, calls=%fused_computation.117 | loop fusion | flops 1024 | bytes 8192 | tf_op jit(solution)/shard_map/mul | solution.py:115
  1.3 1.2 %fusion.40 = f32[1024]{0:T(1024)S(1)} fusion(s32[1024]{0:T(1024)} %bitcast.57), kind=kOutput, calls=%fused_computation.47 | convolution fusion | flops 9464832 | bytes 8192 | tf_op jit(solution)/shard_map/dot_general | solution.py:56
  2.7 0.9 %reshape.249.spectra_ref = bf16[1024,128]{1,0:T(8,128)(2,1)} reshape(bf16[256,512]{1,0:T(8,128)(2,1)S(1)} %copy-done.2) | data formatting | bytes 524288 | tf_op jit(solution)/shard_map/reshape | solution.py:131
  3.6 1.0 %copy.12.rows_ref = s32[1024,1]{1,0:T(8,128)} copy(s32[1024,1]{0,1:T(1,128)S(1)} %bitcast.51) | data formatting | bytes 8192 | tf_op jit(solution)/shard_map/broadcast_in_dim | solution.py:48
  4.6 1.0 %copy.13.kinds_ref = s32[1024,1]{1,0:T(8,128)} copy(s32[1024,1]{0,1:T(1,128)S(1)} %bitcast.54) | data formatting | bytes 8192 | tf_op jit(solution)/shard_map/broadcast_in_dim | solution.py:48
  5.6 0.6 fusion.71.dest_ref
  6.9 8.3 %shard_map.104 = (bf16[4,512,128]{2,1,0:T(8,128)(2,1)}, f32[4,8,512]{2,1,0:T(8,128)}) custom-call(s32[1024,1]{1,0:T(8,128)} %copy.12.rows_ref, s32[1024,1]{1,0:T(8,128)} %copy.13.kinds_ref, s32[1,1024]{1,0:T(1,128)} %fusion.71.dest_ref, bf16[8,1024]{1,0:T(8,128)(2,1)} %copy-done.5, bf16[1024,128]{1,0:T(8,128)(2,1)} %reshape.249.spectra_ref, ...), custom_call_target="tpu_custom_call" | custom-call | tf_op jit(solution)/shard_map/pallas_call | solution.py:42
  15.2 0.8 %convert.4 = bf16[4,8,512]{2,1,0:T(8,128)(2,1)S(1)} convert(f32[4,8,512]{2,1,0:T(8,128)} %get-tuple-element.28) | non-fusion elementwise | flops 16384 | bytes 98304 | tf_op jit(solution)/shard_map/convert.1
  16.1 1.1 %constant_dynamic-update-slice_fusion.1 = bf16[4,520,128]{2,1,0:T(8,128)(2,1)S(1)} fusion(bf16[4,512,128]{2,1,0:T(8,128)(2,1)} %get-tuple-element.29), kind=kLoop, calls=%fused_computation.86 | loop fusion | bytes 1048576
  17.2 3.1 %collective-permute-start = (bf16[520,128]{1,0:T(8,128)(2,1)S(1)}, bf16[520,128]{1,0:T(8,128)(2,1)S(1)}, u32[]{:S(2)}, u32[]{:S(2)}) collective-permute-start(bf16[520,128]{1,0:T(8,128)(2,1)S(1)} %get-tuple-element.34), channel_id=1, source_target_pairs={{0,4},{4,8},{8,12},{12,0},{1,5},{5,9},{9,13},{13,1},{2,6},{6,10},{... | collective-permute-start | bytes 399368 | tf_op jit(solution)/shard_map/ppermute | solution.py:87
  20.3 2.1 %collective-permute-start.2 = (bf16[520,128]{1,0:T(8,128)(2,1)S(1)}, bf16[520,128]{1,0:T(8,128)(2,1)S(1)}, u32[]{:S(2)}, u32[]{:S(2)}) collective-permute-start(bf16[520,128]{1,0:T(8,128)(2,1)S(1)} %get-tuple-element.35), channel_id=1, source_target_pairs={{0,12},{4,0},{8,4},{12,8},{1,13},{5,1},{9,5},{13,9},{2,14},{6,2},{... | collective-permute-start | bytes 399368 | tf_op jit(solution)/shard_map/ppermute | solution.py:87
  22.4 0.9 %collective-permute-start.1 = (bf16[520,128]{1,0:T(8,128)(2,1)S(1)}, bf16[520,128]{1,0:T(8,128)(2,1)S(1)}, u32[]{:S(2)}, u32[]{:S(2)}) collective-permute-start(bf16[520,128]{1,0:T(8,128)(2,1)S(1)} %get-tuple-element.36), channel_id=1, source_target_pairs={{0,8},{4,12},{8,0},{12,4},{1,9},{5,13},{9,1},{13,5},{2,10},{6,14},... | collective-permute-start | bytes 399368 | tf_op jit(solution)/shard_map/ppermute | solution.py:87
  23.4 1.7 %fusion.13 = f32[1024,128]{1,0:T(8,128)S(1)} fusion(s32[512]{0:T(512)S(1)} %bitcast.61, bf16[4,512,128]{2,1,0:T(8,128)(2,1)} %get-tuple-element.29), kind=kOutput, calls=%fused_computation.22 | convolution fusion | flops 134742016 | bytes 657408 | tf_op jit(solution)/shard_map/dot_general | solution.py:60
  25.1 1.6 %collective-permute-done = bf16[520,128]{1,0:T(8,128)(2,1)S(1)} collective-permute-done((bf16[520,128]{1,0:T(8,128)(2,1)S(1)}, bf16[520,128]{1,0:T(8,128)(2,1)S(1)}, u32[]{:S(2)}, u32[]{:S(2)}) %collective-permute-start) | collective-permute-done | bytes 133152 | tf_op jit(solution)/shard_map/ppermute | solution.py:87
  26.7 1.4 %collective-permute-done.2 = bf16[520,128]{1,0:T(8,128)(2,1)S(1)} collective-permute-done((bf16[520,128]{1,0:T(8,128)(2,1)S(1)}, bf16[520,128]{1,0:T(8,128)(2,1)S(1)}, u32[]{:S(2)}, u32[]{:S(2)}) %collective-permute-start.2) | collective-permute-done | bytes 133152 | tf_op jit(solution)/shard_map/ppermute | solution.py:87
  28.2 6.3 %collective-permute-done.1 = bf16[520,128]{1,0:T(8,128)(2,1)S(1)} collective-permute-done((bf16[520,128]{1,0:T(8,128)(2,1)S(1)}, bf16[520,128]{1,0:T(8,128)(2,1)S(1)}, u32[]{:S(2)}, u32[]{:S(2)}) %collective-permute-start.1) | collective-permute-done | bytes 133152 | tf_op jit(solution)/shard_map/ppermute | solution.py:87
  34.5 0.8 %fusion.9 = f32[1024,128]{1,0:T(8,128)S(1)} fusion(s32[512]{0:T(512)S(1)} %add_bitcast_fusion.1, bf16[520,128]{1,0:T(8,128)(2,1)S(1)} %collective-permute-done.1), kind=kOutput, calls=%fused_computation.16 | convolution fusion | flops 134742016 | bytes 657408 | tf_op jit(solution)/shard_map/dot_general | solution.py:60
  35.3 0.8 %fusion.7 = f32[1024,128]{1,0:T(8,128)S(1)} fusion(s32[512]{0:T(512)S(1)} %add_bitcast_fusion, bf16[520,128]{1,0:T(8,128)(2,1)S(1)} %collective-permute-done.2), kind=kOutput, calls=%fused_computation.13 | convolution fusion | flops 134742016 | bytes 657408 | tf_op jit(solution)/shard_map/dot_general | solution.py:60
  36.1 0.8 %fusion.27 = f32[1024,128]{1,0:T(8,128)S(1)} fusion(f32[1024,128]{1,0:T(8,128)S(1)} %fusion.7, f32[1024,128]{1,0:T(8,128)S(1)} %fusion.9, f32[1024,128]{1,0:T(8,128)S(1)} %fusion.13, s32[512]{0:T(512)S(1)} %add_bitcast_fusion.2, bf16[520,128]{1,0:T(8,128)(2,1)S(1)} %collective-permute-done), kind=kOutput, calls=%fused_computation.36 | convolution fusion | flops 135135232 | bytes 2230272 | tf_op jit(solution)/shard_map/dot_general | solution.py:60
  37.1 1.8 %collective-permute-done.3 = f32[1024,128]{1,0:T(8,128)S(1)} collective-permute-done((f32[1024,128]{1,0:T(8,128)S(1)}, f32[1024,128]{1,0:T(8,128)S(1)}, u32[]{:S(2)}, u32[]{:S(2)}) %collective-permute-start.3) | collective-permute-done | bytes 524320 | tf_op jit(solution)/shard_map/ppermute | solution.py:78
  40.6 1.7 %collective-permute-start.4 = (bf16[512,128]{1,0:T(8,128)(2,1)S(1)}, bf16[512,128]{1,0:T(8,128)(2,1)S(1)}, u32[]{:S(2)}, u32[]{:S(2)}) collective-permute-start(bf16[512,128]{1,0:T(8,128)(2,1)S(1)} %fusion.35), channel_id=1, source_target_pairs={{0,12},{4,0},{8,4},{12,8},{1,13},{5,1},{9,5},{13,9},{2,14},{6,2},{... | collective-permute-start | bytes 393224 | tf_op jit(solution)/shard_map/ppermute | solution.py:87
  42.3 0.6 collective-permute-start.6
  42.9 1.3 %fusion.15 = f32[1024,128]{1,0:T(8,128)S(1)} fusion(bf16[1024,128]{1,0:T(8,128)(2,1)S(1)} %fusion.57, s32[512]{0:T(512)S(1)} %bitcast.62, s32[1024]{0:T(1024)S(1)} %bitcast.58), kind=kOutput, calls=%fused_computation.26 | convolution fusion | flops 269549568 | bytes 792576 | tf_op jit(solution)/shard_map/dot_general | solution.py:56
  44.3 2.4 %collective-permute-done.4 = bf16[512,128]{1,0:T(8,128)(2,1)S(1)} collective-permute-done((bf16[512,128]{1,0:T(8,128)(2,1)S(1)}, bf16[512,128]{1,0:T(8,128)(2,1)S(1)}, u32[]{:S(2)}, u32[]{:S(2)}) %collective-permute-start.4) | collective-permute-done | bytes 131104 | tf_op jit(solution)/shard_map/ppermute | solution.py:87
  47.2 4.6 %collective-permute-done.6 = bf16[512,128]{1,0:T(8,128)(2,1)S(1)} collective-permute-done((bf16[512,128]{1,0:T(8,128)(2,1)S(1)}, bf16[512,128]{1,0:T(8,128)(2,1)S(1)}, u32[]{:S(2)}, u32[]{:S(2)}) %collective-permute-start.6) | collective-permute-done | bytes 131104 | tf_op jit(solution)/shard_map/ppermute | solution.py:87
  52.3 1.7 %collective-permute-done.5 = bf16[512,128]{1,0:T(8,128)(2,1)S(1)} collective-permute-done((bf16[512,128]{1,0:T(8,128)(2,1)S(1)}, bf16[512,128]{1,0:T(8,128)(2,1)S(1)}, u32[]{:S(2)}, u32[]{:S(2)}) %collective-permute-start.5) | collective-permute-done | bytes 131104 | tf_op jit(solution)/shard_map/ppermute | solution.py:87
  55.1 2.6 %fusion.30 = bf16[1024,128]{1,0:T(8,128)(2,1)S(1)} fusion(pred[1024,16]{0,1:T(8,128)(4,1)S(1)} %iota_compare_fusion.58, bf16[1024,128]{1,0:T(8,128)(2,1)S(1)} %fusion.29, bf16[16,128,128]{2,1,0:T(8,128)(2,1)S(1)} %copy-done), kind=kOutput, calls=%fused_computation.39 | convolution fusion | flops 539099136 | bytes 1064960 | tf_op jit(solution)/shard_map/dot_general | solution.py:56
  57.7 0.9 %fusion.33 = bf16[512,128]{1,0:T(8,128)(2,1)S(1)} fusion(bf16[1024,128]{1,0:T(8,128)(2,1)S(1)} %fusion.30, s32[1024]{0:T(1024)S(1)} %get-tuple-element.30), kind=kOutput, calls=%fused_computation.40 | convolution fusion | flops 134807552 | bytes 397312 | tf_op jit(solution)/shard_map/dot_general | solution.py:60
  58.6 1.6 %collective-permute-start.7 = (bf16[128,512]{1,0:T(8,128)(2,1)S(1)}, bf16[128,512]{1,0:T(8,128)(2,1)S(1)}, u32[]{:S(2)}, u32[]{:S(2)}) collective-permute-start(bf16[128,512]{1,0:T(8,128)(2,1)S(1)} %convert_element_type.131), channel_id=1, source_target_pairs={{0,2},{2,0},{1,3},{3,1},{4,6},{6,4},{5,7},{7,5},{8,10},{10,8},{9,1... | collective-permute-start | bytes 393224 | tf_op jit(solution)/shard_map/ppermute | solution.py:170
  60.2 0.9 %fusion.14 = f32[512,128]{1,0:T(8,128)S(1)} fusion(bf16[1024,128]{1,0:T(8,128)(2,1)S(1)} %fusion.30, s32[1024]{0:T(1024)S(1)} %broadcast_subtract_fusion.1), kind=kOutput, calls=%fused_computation.25 | convolution fusion | flops 134742016 | bytes 528384 | tf_op jit(solution)/shard_map/dot_general | solution.py:60
  61.1 2.5 %collective-permute-done.7 = bf16[128,512]{1,0:T(8,128)(2,1)S(1)} collective-permute-done((bf16[128,512]{1,0:T(8,128)(2,1)S(1)}, bf16[128,512]{1,0:T(8,128)(2,1)S(1)}, u32[]{:S(2)}, u32[]{:S(2)}) %collective-permute-start.7) | collective-permute-done | bytes 131104 | tf_op jit(solution)/shard_map/ppermute | solution.py:170
  63.7 0.7 %convert_add_fusion = f32[128,512]{1,0:T(8,128)} fusion(f32[128,512]{1,0:T(8,128)S(1)} %reshape.251, bf16[128,512]{1,0:T(8,128)(2,1)S(1)} %collective-permute-done.7), kind=kLoop, calls=%fused_computation.66 | loop fusion | flops 131072 | bytes 655360 | tf_op jit(solution)/shard_map/add | solution.py:172
  (54 shorter events, 4.8 us)
Async XLA Ops:
  1.3 1.3 %copy-start.8 = (s32[1024]{0:T(1024)S(1)}, s32[1024]{0:T(1024)}, u32[]{:S(2)}) copy-start(s32[1024]{0:T(1024)} %param.18) | copy-start | bytes 12292
  1.3 1.3 %copy-start.2 = (bf16[256,512]{1,0:T(8,128)(2,1)S(1)}, bf16[256,512]{1,0:T(8,128)(2,1)}, u32[]{:S(2)}) copy-start(bf16[256,512]{1,0:T(8,128)(2,1)} %param.13) | copy-start | bytes 786436
  2.6 1.0 %copy-start.9 = (s32[1024]{0:T(1024)S(1)}, s32[1024]{0:T(1024)}, u32[]{:S(2)}) copy-start(s32[1024]{0:T(1024)} %param.20) | copy-start | bytes 12292
  2.7 1.9 %copy-start.6 = (s32[1024]{0:T(1024)S(1)}, s32[1024]{0:T(1024)}, u32[]{:S(2)}) copy-start(s32[1024]{0:T(1024)} %param.21) | copy-start | bytes 12292
  3.6 2.1 %copy-start.7 = (s32[1024,1]{0,1:T(1,128)S(1)}, s32[1024,1]{0,1:T(1,128)}, u32[]{:S(2)}) copy-start(s32[1024,1]{0,1:T(1,128)} %param.17) | copy-start | bytes 12292
  6.3 0.6 copy-start.5
  17.2 9.5 %collective-permute-start = (bf16[520,128]{1,0:T(8,128)(2,1)S(1)}, bf16[520,128]{1,0:T(8,128)(2,1)S(1)}, u32[]{:S(2)}, u32[]{:S(2)}) collective-permute-start(bf16[520,128]{1,0:T(8,128)(2,1)S(1)} %get-tuple-element.34), channel_id=1, source_target_pairs={{0,4},{4,8},{8,12},{12,0},{1,5},{5,9},{9,13},{13,1},{2,6},{6,10},{... | collective-permute-start | bytes 399368 | tf_op jit(solution)/shard_map/ppermute | solution.py:87
  20.3 7.9 %collective-permute-start.2 = (bf16[520,128]{1,0:T(8,128)(2,1)S(1)}, bf16[520,128]{1,0:T(8,128)(2,1)S(1)}, u32[]{:S(2)}, u32[]{:S(2)}) collective-permute-start(bf16[520,128]{1,0:T(8,128)(2,1)S(1)} %get-tuple-element.35), channel_id=1, source_target_pairs={{0,12},{4,0},{8,4},{12,8},{1,13},{5,1},{9,5},{13,9},{2,14},{6,2},{... | collective-permute-start | bytes 399368 | tf_op jit(solution)/shard_map/ppermute | solution.py:87
  22.4 12.0 %collective-permute-start.1 = (bf16[520,128]{1,0:T(8,128)(2,1)S(1)}, bf16[520,128]{1,0:T(8,128)(2,1)S(1)}, u32[]{:S(2)}, u32[]{:S(2)}) collective-permute-start(bf16[520,128]{1,0:T(8,128)(2,1)S(1)} %get-tuple-element.36), channel_id=1, source_target_pairs={{0,8},{4,12},{8,0},{12,4},{1,9},{5,13},{9,1},{13,5},{2,10},{6,14},... | collective-permute-start | bytes 399368 | tf_op jit(solution)/shard_map/ppermute | solution.py:87
  36.1 2.8 %copy-start.1 = (s32[1,1024,128]{2,1,0:T(8,128)S(1)}, s32[1,1024,128]{2,1,0:T(8,128)}, u32[]{:S(2)}) copy-start(s32[1,1024,128]{2,1,0:T(8,128)} %param.16) | copy-start | bytes 1572868
  36.1 2.8 %copy-start.3 = (bf16[1,1024,128]{2,1,0:T(8,128)(2,1)S(1)}, bf16[1,1024,128]{2,1,0:T(8,128)(2,1)}, u32[]{:S(2)}) copy-start(bf16[1,1024,128]{2,1,0:T(8,128)(2,1)} %param.15) | copy-start | bytes 786436
  37.0 2.0 %collective-permute-start.3 = (f32[1024,128]{1,0:T(8,128)S(1)}, f32[1024,128]{1,0:T(8,128)S(1)}, u32[]{:S(2)}, u32[]{:S(2)}) collective-permute-start(f32[1024,128]{1,0:T(8,128)S(1)} %fusion.27), channel_id=1, source_target_pairs={{0,1},{1,0},{2,3},{3,2},{4,5},{5,4},{6,7},{7,6},{8,9},{9,8},{10,11... | collective-permute-start | bytes 1572872 | tf_op jit(solution)/shard_map/ppermute | solution.py:78
  39.1 3.9 %copy-start.4 = (bf16[1024,128]{1,0:T(8,128)(2,1)}, bf16[1024,128]{1,0:T(8,128)(2,1)S(1)}, u32[]{:S(2)}) copy-start(bf16[1024,128]{1,0:T(8,128)(2,1)S(1)} %fusion.57) | copy-start | bytes 786436
  40.6 6.1 %collective-permute-start.4 = (bf16[512,128]{1,0:T(8,128)(2,1)S(1)}, bf16[512,128]{1,0:T(8,128)(2,1)S(1)}, u32[]{:S(2)}, u32[]{:S(2)}) collective-permute-start(bf16[512,128]{1,0:T(8,128)(2,1)S(1)} %fusion.35), channel_id=1, source_target_pairs={{0,12},{4,0},{8,4},{12,8},{1,13},{5,1},{9,5},{13,9},{2,14},{6,2},{... | collective-permute-start | bytes 393224 | tf_op jit(solution)/shard_map/ppermute | solution.py:87
  42.3 11.8 %collective-permute-start.5 = (bf16[512,128]{1,0:T(8,128)(2,1)S(1)}, bf16[512,128]{1,0:T(8,128)(2,1)S(1)}, u32[]{:S(2)}, u32[]{:S(2)}) collective-permute-start(bf16[512,128]{1,0:T(8,128)(2,1)S(1)} %fusion.36), channel_id=1, source_target_pairs={{0,8},{4,12},{8,0},{12,4},{1,9},{5,13},{9,1},{13,5},{2,10},{6,14},... | collective-permute-start | bytes 393224 | tf_op jit(solution)/shard_map/ppermute | solution.py:87
  42.3 9.5 %collective-permute-start.6 = (bf16[512,128]{1,0:T(8,128)(2,1)S(1)}, bf16[512,128]{1,0:T(8,128)(2,1)S(1)}, u32[]{:S(2)}, u32[]{:S(2)}) collective-permute-start(bf16[512,128]{1,0:T(8,128)(2,1)S(1)} %fusion.37), channel_id=1, source_target_pairs={{0,4},{4,8},{8,12},{12,0},{1,5},{5,9},{9,13},{13,1},{2,6},{6,10},{... | collective-permute-start | bytes 393224 | tf_op jit(solution)/shard_map/ppermute | solution.py:87
  54.1 1.0 %copy-start = (bf16[16,128,128]{2,1,0:T(8,128)(2,1)S(1)}, bf16[16,128,128]{2,1,0:T(8,128)(2,1)}, u32[]{:S(2)}) copy-start(bf16[16,128,128]{2,1,0:T(8,128)(2,1)} %psf_ref.1) | copy-start | bytes 1572868
  58.6 5.0 %collective-permute-start.7 = (bf16[128,512]{1,0:T(8,128)(2,1)S(1)}, bf16[128,512]{1,0:T(8,128)(2,1)S(1)}, u32[]{:S(2)}, u32[]{:S(2)}) collective-permute-start(bf16[128,512]{1,0:T(8,128)(2,1)S(1)} %convert_element_type.131), channel_id=1, source_target_pairs={{0,2},{2,0},{1,3},{3,1},{4,6},{6,4},{5,7},{7,5},{8,10},{10,8},{9,1... | collective-permute-start | bytes 393224 | tf_op jit(solution)/shard_map/ppermute | solution.py:170

commit v9 on v4

--- a/solution.py
+++ b/solution.py
@@ -1,3 +1,5 @@
+import functools
+
 import jax
 import jax.numpy as jnp
 from jax import lax
@@ -91,19 +93,45 @@
         block = select_dot_t(places[step], traces).astype(jnp.bfloat16)
         send.append(jnp.concatenate([block, codes.reshape(code_rows, pixel_count)], axis=0))
     got = exchange(send, "tile", 1)
-    got_traces = [block[:capacity] for block in got]
-    got_slots = []
-    for block in got:
+    def decoded(block):
         codes = block[capacity:].reshape(code_rows * pixel_count)[: 2 * capacity]
         codes = codes.astype(jnp.int32).reshape(2, capacity)
-        got_slots.append(codes[0] * 256 + codes[1])
+        return block[:capacity], codes[0] * 256 + codes[1]
 
+    got_traces, got_slots = zip(*[decoded(block) for block in got])
     at_slot = [one_hot_rows(slots, slot_count) for slots in got_slots]
-    partial_value = sum(select_dot_t(a, b) for a, b in zip(at_slot, got_traces))
-    model_image = swap_add(partial_value, "band")
-    residual = (
-        bad_mask[0].astype(jnp.float32) * (model_image - observed[0].astype(jnp.float32))
-    ).astype(jnp.bfloat16)
+    if lax.axis_size("band") == 2:
+        band = lax.axis_index("band")
+        half = slot_count // 2
+        low = band * half
+        pairs = [(0, 1), (1, 0)]
+        partner = [decoded(lax.ppermute(block, "band", pairs)) for block in got]
+        parts = [
+            select_dot_t(one_hot_rows(slots - low, half), traces)
+            for traces, slots in list(zip(got_traces, got_slots)) + partner
+        ]
+        model_half = functools.reduce(jnp.add, parts)
+        observed_half = lax.dynamic_slice_in_dim(observed[0], low, half, axis=0)
+        mask_half = lax.dynamic_slice_in_dim(bad_mask[0], low, half, axis=0)
+        residual_half = (
+            mask_half.astype(jnp.float32) * (model_half - observed_half.astype(jnp.float32))
+        ).astype(jnp.bfloat16)
+        other_half = lax.ppermute(residual_half, "band", pairs)
+        residual = jnp.concatenate(
+            [
+                jnp.where(band == 0, residual_half, other_half),
+                jnp.where(band == 0, other_half, residual_half),
+            ],
+            axis=0,
+        )
+    else:
+        partial_value = functools.reduce(
+            jnp.add, [select_dot_t(a, b) for a, b in zip(at_slot, got_traces)]
+        )
+        model_image = lax.psum(partial_value, "band")
+        residual = (
+            bad_mask[0].astype(jnp.float32) * (model_image - observed[0].astype(jnp.float32))
+        ).astype(jnp.bfloat16)
 
     under_rows = [select_dot(a, residual).astype(jnp.bfloat16) for a in at_slot]
     returned = exchange(under_rows, "tile", -1)

time: 56.7 us -> 58.1 us (1.025)
  waiting for transfers between devices: 18.3 us -> 12.1 us
  starting transfers between devices: 12.3 us -> 17.6 us
  matrix products: 22.4 us -> 23.8 us
  other arithmetic: 1.76 us -> 2.46 us
    ppermute x6, waiting for transfers between devices: 13.9 us -> 8.61 us  [exchange(): moved.append(lax.ppermute(blocks[step], axis, pairs))]
    ppermute x6, starting transfers between devices: 10.7 us -> 14.9 us  [exchange(): moved.append(lax.ppermute(blocks[step], axis, pairs))]
    dot_general x13 -> x18, matrix products: 10.4 us -> 11.7 us  [select_dot_t(): lax.dot_general(selector, values, (((0,), (0,)), ((), ())), preferred_ele...]
    ppermute x1 -> x5, starting transfers between devices: 0.07 us -> 1.21 us  [the longest x4 0.72 us: per_device(): partner = [decoded(lax.ppermute(block, 'band', pairs)) for block in got]]
    ppermute x1 -> x5, waiting for transfers between devices: 1.89 us -> 0.99 us  [the longest x1 0.98 us: per_device(): other_half = lax.ppermute(residual_half, 'band', pairs)]
    broadcast_in_dim x0 -> x1, other arithmetic: none -> 0.72 us  [per_device(): return (gradient, residual[None])]
  transfers between devices with their start and end apart: 8 -> 12, of which waited for: 6 -> 6; matrix products, arithmetic and copies ran while one was open for 14% -> 18% of each run, Pallas kernels for 0% -> 0%
where the time goes in v9:
time: 58.1 us; the launch traced here: 57.9 us
  matrix products  23.8 us (41%)
  starting transfers between devices  17.6 us (30%)
  waiting for transfers between devices  12.1 us (21%)
  other arithmetic  2.46 us (4%)
  between operations  1.19 us (2%)
  local copies, waits for them, and re-layouts  0.65 us (1%)
    ppermute x6, starting transfers between devices, exchange(): moved.append(lax.ppermute(blocks[step], axis, pairs))  14.9 us
    dot_general x11, matrix products, select_dot(): jnp.dot(selector, values, preferred_element_type=jnp.float32, precision=p...  12 us
    dot_general x18, matrix products, select_dot_t(): lax.dot_general(selector, values, (((0,), (0,)), ((), ())), preferred_ele...  11.7 us
    ppermute x6, waiting for transfers between devices, exchange(): moved.append(lax.ppermute(blocks[step], axis, pairs))  8.61 us
    ppermute x1, waiting for transfers between devices, per_device(): sent = lax.ppermute(theirs.astype(jnp.bfloat16), 'dither', [(0, 1), (1, 0)])  2.55 us
    ppermute x1, starting transfers between devices, per_device(): sent = lax.ppermute(theirs.astype(jnp.bfloat16), 'dither', [(0, 1), (1, 0)])  1.55 us
  transfers between devices with their start and end apart: 12, of which 6 were waited for; matrix products, arithmetic and copies ran while one was open for 18% of the time, Pallas kernels for 0%

profile of v9, /device:TPU:0, one launch (start us, length us, event | category | flops | bytes accessed | tf_op | source)
XLA Modules:
  0.0 57.9 jit_solution(14149574608350315610)
XLA Ops:
  0.7 0.7 %broadcast_multiply_fusion = s32[1024,1]{0,1:T(1,128)S(1)} fusion(s32[1024,1]{0,1:T(1,128)} %param.15), kind=kLoop, calls=%fused_computation.175 | loop fusion | flops 1024 | bytes 8192 | tf_op jit(solution)/shard_map/mul | solution.py:73
  1.4 1.3 %fusion.66 = f32[1024]{0:T(1024)S(1)} fusion(s32[1024]{0:T(1024)} %bitcast.75), kind=kOutput, calls=%fused_computation.73 | convolution fusion | flops 9464832 | bytes 8192 | tf_op jit(solution)/shard_map/dot_general | solution.py:14
  3.8 0.8 %fusion.47 = bf16[1024,128]{1,0:T(8,128)(2,1)S(1)} fusion(bf16[1024,128]{1,0:T(8,128)(2,1)S(1)} %reshape.247, s32[1024]{0:T(1024)S(1)} %get-tuple-element.3), kind=kOutput, calls=%fused_computation.51 | convolution fusion | flops 269615104 | bytes 528384 | tf_op jit(solution)/shard_map/dot_general | solution.py:14
  4.7 3.0 %fusion.44 = bf16[1024,128]{1,0:T(8,128)(2,1)S(1)} fusion(bf16[16,128,128]{2,1,0:T(8,128)(2,1)S(1)} %copy-done, pred[1024,16]{0,1:T(8,128)(4,1)S(1)} %iota_compare_fusion.92, bf16[1024,128]{1,0:T(8,128)(2,1)S(1)} %fusion.47), kind=kOutput, calls=%fused_computation.50 | convolution fusion | flops 539099136 | bytes 1064960 | tf_op jit(solution)/shard_map/dot_general | solution.py:14
  7.7 0.9 %fusion.61 = bf16[512,128]{1,0:T(8,128)(2,1)S(1)} fusion(bf16[1024,128]{1,0:T(8,128)(2,1)S(1)} %fusion.44, s32[1024]{0:T(1024)S(1)} %bitcast.73), kind=kOutput, calls=%fused_computation.68 | convolution fusion | flops 134807552 | bytes 397312 | tf_op jit(solution)/shard_map/dot_general | solution.py:18
  8.6 4.1 %collective-permute-start.1 = (bf16[520,128]{1,0:T(8,128)(2,1)S(1)}, bf16[520,128]{1,0:T(8,128)(2,1)S(1)}, u32[]{:S(2)}, u32[]{:S(2)}) collective-permute-start(bf16[520,128]{1,0:T(8,128)(2,1)S(1)} %pad_maximum_fusion.2), channel_id=1, source_target_pairs={{0,8},{4,12},{8,0},{12,4},{1,9},{5,13},{9,1},{13,5},{2,10},{6,14},... | collective-permute-start | bytes 399368 | tf_op jit(solution)/shard_map/ppermute | solution.py:45
  13.2 0.9 %fusion.60 = bf16[512,128]{1,0:T(8,128)(2,1)S(1)} fusion(bf16[1024,128]{1,0:T(8,128)(2,1)S(1)} %fusion.44, s32[1024]{0:T(1024)S(1)} %bitcast.60), kind=kOutput, calls=%fused_computation.67 | convolution fusion | flops 134807552 | bytes 397312 | tf_op jit(solution)/shard_map/dot_general | solution.py:18
  14.1 1.6 %collective-permute-start = (bf16[520,128]{1,0:T(8,128)(2,1)S(1)}, bf16[520,128]{1,0:T(8,128)(2,1)S(1)}, u32[]{:S(2)}, u32[]{:S(2)}) collective-permute-start(bf16[520,128]{1,0:T(8,128)(2,1)S(1)} %pad_maximum_fusion.1), channel_id=1, source_target_pairs={{0,4},{4,8},{8,12},{12,0},{1,5},{5,9},{9,13},{13,1},{2,6},{6,10},{... | collective-permute-start | bytes 399368 | tf_op jit(solution)/shard_map/ppermute | solution.py:45
  16.2 0.9 %fusion.62 = bf16[512,128]{1,0:T(8,128)(2,1)S(1)} fusion(bf16[1024,128]{1,0:T(8,128)(2,1)S(1)} %fusion.44, s32[1024]{0:T(1024)S(1)} %bitcast.70), kind=kOutput, calls=%fused_computation.69 | convolution fusion | flops 134807552 | bytes 397312 | tf_op jit(solution)/shard_map/dot_general | solution.py:18
  17.2 2.5 %collective-permute-start.2 = (bf16[520,128]{1,0:T(8,128)(2,1)S(1)}, bf16[520,128]{1,0:T(8,128)(2,1)S(1)}, u32[]{:S(2)}, u32[]{:S(2)}) collective-permute-start(bf16[520,128]{1,0:T(8,128)(2,1)S(1)} %pad_maximum_fusion.3), channel_id=1, source_target_pairs={{0,12},{4,0},{8,4},{12,8},{1,13},{5,1},{9,5},{13,9},{2,14},{6,2},{... | collective-permute-start | bytes 399368 | tf_op jit(solution)/shard_map/ppermute | solution.py:45
  20.1 0.9 %fusion.59 = bf16[512,128]{1,0:T(8,128)(2,1)S(1)} fusion(bf16[1024,128]{1,0:T(8,128)(2,1)S(1)} %fusion.44, s32[1024]{0:T(1024)S(1)} %bitcast.63), kind=kOutput, calls=%fused_computation.66 | convolution fusion | flops 134807552 | bytes 397312 | tf_op jit(solution)/shard_map/dot_general | solution.py:18
  21.7 1.1 %collective-permute-done.1 = bf16[520,128]{1,0:T(8,128)(2,1)S(1)} collective-permute-done((bf16[520,128]{1,0:T(8,128)(2,1)S(1)}, bf16[520,128]{1,0:T(8,128)(2,1)S(1)}, u32[]{:S(2)}, u32[]{:S(2)}) %collective-permute-start.1) | collective-permute-done | bytes 133152 | tf_op jit(solution)/shard_map/ppermute | solution.py:45
  22.8 2.0 %collective-permute-done.2 = bf16[520,128]{1,0:T(8,128)(2,1)S(1)} collective-permute-done((bf16[520,128]{1,0:T(8,128)(2,1)S(1)}, bf16[520,128]{1,0:T(8,128)(2,1)S(1)}, u32[]{:S(2)}, u32[]{:S(2)}) %collective-permute-start.2) | collective-permute-done | bytes 133152 | tf_op jit(solution)/shard_map/ppermute | solution.py:45
  26.1 0.6 fusion.91
  26.6 0.6 convolution_add_fusion.2
  27.2 0.6 fusion.50
  27.9 0.6 fusion.93
  28.5 0.6 fusion.94
  29.1 0.6 %fusion.63 = bf16[512,128]{1,0:T(8,128)(2,1)S(1)} fusion(f32[512,128]{1,0:T(8,128)S(1)} %fusion.94, f32[512,128]{1,0:T(8,128)S(1)} %fusion.93, f32[512,128]{1,0:T(8,128)S(1)} %fusion.50, s32[512]{0:T(512)S(1)} %subtract_bitcast_fusion.2, s32[1,1024,128]{2,1,0:T(8,128)S(1)} %copy-done.2, s32[]{:T(128)S(6)} %select_n.47, ...), kind=kOutput, calls=%fused_computation.70 | convolution fusion | flops 67895296 | bytes 1443844 | tf_op jit(solution)/shard_map/dot_general | solution.py:18
  30.1 1.0 %collective-permute-done.7 = bf16[512,128]{1,0:T(8,128)(2,1)S(1)} collective-permute-done((bf16[512,128]{1,0:T(8,128)(2,1)S(1)}, bf16[512,128]{1,0:T(8,128)(2,1)S(1)}, u32[]{:S(2)}, u32[]{:S(2)}) %collective-permute-start.7) | collective-permute-done | bytes 131104 | tf_op jit(solution)/shard_map/ppermute | solution.py:119
  31.1 1.3 %fusion.22 = f32[1024,128]{1,0:T(8,128)S(1)} fusion(s32[512]{0:T(512)S(1)} %bitcast.68, s32[1024]{0:T(1024)S(1)} %bitcast.64, bf16[512,128]{1,0:T(8,128)(2,1)S(1)} %get-tuple-element.13, bf16[512,128]{1,0:T(8,128)(2,1)S(1)} %get-tuple-element.12), kind=kOutput, calls=%fused_computation.33 | convolution fusion | flops 270073856 | bytes 792576 | tf_op jit(solution)/shard_map/dot_general | solution.py:14
  33.5 2.8 %collective-permute-start.9 = (bf16[512,128]{1,0:T(8,128)(2,1)S(1)}, bf16[512,128]{1,0:T(8,128)(2,1)S(1)}, u32[]{:S(2)}, u32[]{:S(2)}) collective-permute-start(bf16[512,128]{1,0:T(8,128)(2,1)S(1)} %fusion.56), channel_id=1, source_target_pairs={{0,8},{4,12},{8,0},{12,4},{1,9},{5,13},{9,1},{13,5},{2,10},{6,14},... | collective-permute-start | bytes 393224 | tf_op jit(solution)/shard_map/ppermute | solution.py:45
  36.9 3.8 %collective-permute-start.8 = (bf16[512,128]{1,0:T(8,128)(2,1)S(1)}, bf16[512,128]{1,0:T(8,128)(2,1)S(1)}, u32[]{:S(2)}, u32[]{:S(2)}) collective-permute-start(bf16[512,128]{1,0:T(8,128)(2,1)S(1)} %fusion.57), channel_id=1, source_target_pairs={{0,12},{4,0},{8,4},{12,8},{1,13},{5,1},{9,5},{13,9},{2,14},{6,2},{... | collective-permute-start | bytes 393224 | tf_op jit(solution)/shard_map/ppermute | solution.py:45
  40.7 0.7 %fusion.122 = bf16[1,1024,128]{2,1,0:T(8,128)(2,1)} fusion(bf16[512,128]{1,0:T(8,128)(2,1)S(1)} %get-tuple-element.13, bf16[512,128]{1,0:T(8,128)(2,1)S(1)} %get-tuple-element.12), kind=kLoop, calls=%fused_computation.182 | loop fusion | flops 524288 | bytes 524288 | tf_op jit(solution)/shard_map/broadcast_in_dim | solution.py:157
  41.4 4.8 %collective-permute-done.9 = bf16[512,128]{1,0:T(8,128)(2,1)S(1)} collective-permute-done((bf16[512,128]{1,0:T(8,128)(2,1)S(1)}, bf16[512,128]{1,0:T(8,128)(2,1)S(1)}, u32[]{:S(2)}, u32[]{:S(2)}) %collective-permute-start.9) | collective-permute-done | bytes 131104 | tf_op jit(solution)/shard_map/ppermute | solution.py:45
  47.2 0.8 %collective-permute-done.8 = bf16[512,128]{1,0:T(8,128)(2,1)S(1)} collective-permute-done((bf16[512,128]{1,0:T(8,128)(2,1)S(1)}, bf16[512,128]{1,0:T(8,128)(2,1)S(1)}, u32[]{:S(2)}, u32[]{:S(2)}) %collective-permute-start.8) | collective-permute-done | bytes 131104 | tf_op jit(solution)/shard_map/ppermute | solution.py:45
  48.5 2.6 %fusion.41 = bf16[1024,128]{1,0:T(8,128)(2,1)S(1)} fusion(pred[1024,16]{0,1:T(8,128)(4,1)S(1)} %iota_compare_fusion.92, bf16[1024,128]{1,0:T(8,128)(2,1)S(1)} %fusion.40, bf16[16,128,128]{2,1,0:T(8,128)(2,1)S(1)} %copy-done), kind=kOutput, calls=%fused_computation.49 | convolution fusion | flops 539099136 | bytes 1064960 | tf_op jit(solution)/shard_map/dot_general | solution.py:14
  51.1 0.9 %fusion.54 = bf16[512,128]{1,0:T(8,128)(2,1)S(1)} fusion(bf16[1024,128]{1,0:T(8,128)(2,1)S(1)} %fusion.41, s32[1024]{0:T(1024)S(1)} %get-tuple-element.2), kind=kOutput, calls=%fused_computation.61 | convolution fusion | flops 134807552 | bytes 397312 | tf_op jit(solution)/shard_map/dot_general | solution.py:18
  52.1 1.6 %collective-permute-start.11 = (bf16[128,512]{1,0:T(8,128)(2,1)S(1)}, bf16[128,512]{1,0:T(8,128)(2,1)S(1)}, u32[]{:S(2)}, u32[]{:S(2)}) collective-permute-start(bf16[128,512]{1,0:T(8,128)(2,1)S(1)} %convert_element_type.181), channel_id=1, source_target_pairs={{0,2},{2,0},{1,3},{3,1},{4,6},{6,4},{5,7},{7,5},{8,10},{10,8},{9,1... | collective-permute-start | bytes 393224 | tf_op jit(solution)/shard_map/ppermute | solution.py:150
  53.6 0.9 %fusion.25 = f32[512,128]{1,0:T(8,128)S(1)} fusion(bf16[1024,128]{1,0:T(8,128)(2,1)S(1)} %fusion.41, s32[1024]{0:T(1024)S(1)} %broadcast_subtract_fusion.1), kind=kOutput, calls=%fused_computation.37 | convolution fusion | flops 134742016 | bytes 528384 | tf_op jit(solution)/shard_map/dot_general | solution.py:18
  54.6 2.5 %collective-permute-done.11 = bf16[128,512]{1,0:T(8,128)(2,1)S(1)} collective-permute-done((bf16[128,512]{1,0:T(8,128)(2,1)S(1)}, bf16[128,512]{1,0:T(8,128)(2,1)S(1)}, u32[]{:S(2)}, u32[]{:S(2)}) %collective-permute-start.11) | collective-permute-done | bytes 131104 | tf_op jit(solution)/shard_map/ppermute | solution.py:150
  57.1 0.7 %convert_add_fusion = f32[128,512]{1,0:T(8,128)} fusion(f32[128,512]{1,0:T(8,128)S(1)} %reshape.252, bf16[128,512]{1,0:T(8,128)(2,1)S(1)} %collective-permute-done.11), kind=kLoop, calls=%fused_computation.119 | loop fusion | flops 131072 | bytes 655360 | tf_op jit(solution)/shard_map/add | solution.py:152
  (78 shorter events, 8.3 us)
Async XLA Ops:
  0.6 4.0 %copy-start = (bf16[16,128,128]{2,1,0:T(8,128)(2,1)S(1)}, bf16[16,128,128]{2,1,0:T(8,128)(2,1)}, u32[]{:S(2)}) copy-start(bf16[16,128,128]{2,1,0:T(8,128)(2,1)} %param.10) | copy-start | bytes 1572868
  1.4 1.3 %copy-start.5 = (s32[1024]{0:T(1024)S(1)}, s32[1024]{0:T(1024)}, u32[]{:S(2)}) copy-start(s32[1024]{0:T(1024)} %param.14) | copy-start | bytes 12292
  1.4 1.4 %copy-start.6 = (s32[1024,1]{0,1:T(1,128)S(1)}, s32[1024,1]{0,1:T(1,128)}, u32[]{:S(2)}) copy-start(s32[1024,1]{0,1:T(1,128)} %param.13) | copy-start | bytes 12292
  2.7 0.7 %copy-start.4 = (s32[1024]{0:T(1024)S(1)}, s32[1024]{0:T(1024)}, u32[]{:S(2)}) copy-start(s32[1024]{0:T(1024)} %param.17) | copy-start | bytes 12292
  2.7 1.0 %copy-start.1 = (bf16[256,512]{1,0:T(8,128)(2,1)S(1)}, bf16[256,512]{1,0:T(8,128)(2,1)}, u32[]{:S(2)}) copy-start(bf16[256,512]{1,0:T(8,128)(2,1)} %param.9) | copy-start | bytes 786436
  2.9 1.0 %copy-start.7 = (s32[1024]{0:T(1024)S(1)}, s32[1024]{0:T(1024)}, u32[]{:S(2)}) copy-start(s32[1024]{0:T(1024)} %param.16) | copy-start | bytes 12292
  8.6 14.2 %collective-permute-start.1 = (bf16[520,128]{1,0:T(8,128)(2,1)S(1)}, bf16[520,128]{1,0:T(8,128)(2,1)S(1)}, u32[]{:S(2)}, u32[]{:S(2)}) collective-permute-start(bf16[520,128]{1,0:T(8,128)(2,1)S(1)} %pad_maximum_fusion.2), channel_id=1, source_target_pairs={{0,8},{4,12},{8,0},{12,4},{1,9},{5,13},{9,1},{13,5},{2,10},{6,14},... | collective-permute-start | bytes 399368 | tf_op jit(solution)/shard_map/ppermute | solution.py:45
  14.1 8.7 %collective-permute-start = (bf16[520,128]{1,0:T(8,128)(2,1)S(1)}, bf16[520,128]{1,0:T(8,128)(2,1)S(1)}, u32[]{:S(2)}, u32[]{:S(2)}) collective-permute-start(bf16[520,128]{1,0:T(8,128)(2,1)S(1)} %pad_maximum_fusion.1), channel_id=1, source_target_pairs={{0,4},{4,8},{8,12},{12,0},{1,5},{5,9},{9,13},{13,1},{2,6},{6,10},{... | collective-permute-start | bytes 399368 | tf_op jit(solution)/shard_map/ppermute | solution.py:45
  17.2 7.7 %collective-permute-start.2 = (bf16[520,128]{1,0:T(8,128)(2,1)S(1)}, bf16[520,128]{1,0:T(8,128)(2,1)S(1)}, u32[]{:S(2)}, u32[]{:S(2)}) collective-permute-start(bf16[520,128]{1,0:T(8,128)(2,1)S(1)} %pad_maximum_fusion.3), channel_id=1, source_target_pairs={{0,12},{4,0},{8,4},{12,8},{1,13},{5,1},{9,5},{13,9},{2,14},{6,2},{... | collective-permute-start | bytes 399368 | tf_op jit(solution)/shard_map/ppermute | solution.py:45
  21.0 3.8 %collective-permute-start.3 = (bf16[520,128]{1,0:T(8,128)(2,1)S(1)}, bf16[520,128]{1,0:T(8,128)(2,1)S(1)}, u32[]{:S(2)}, u32[]{:S(2)}) collective-permute-start(bf16[520,128]{1,0:T(8,128)(2,1)S(1)} %pad_maximum_fusion.4), channel_id=1, source_target_pairs={{0,1},{1,0},{2,3},{3,2},{4,5},{5,4},{6,7},{7,6},{8,9},{9,8},{10,11... | collective-permute-start | bytes 399368 | tf_op jit(solution)/shard_map/ppermute | solution.py:108
  24.9 2.9 %collective-permute-start.5 = (bf16[520,128]{1,0:T(8,128)(2,1)S(1)}, bf16[520,128]{1,0:T(8,128)(2,1)S(1)}, u32[]{:S(2)}, u32[]{:S(2)}) collective-permute-start(bf16[520,128]{1,0:T(8,128)(2,1)S(1)} %collective-permute-done.1), channel_id=1, source_target_pairs={{0,1},{1,0},{2,3},{3,2},{4,5},{5,4},{6,7},{7,6},{8,9},{9,8},{10,11... | collective-permute-start | bytes 399368 | tf_op jit(solution)/shard_map/ppermute | solution.py:108
  24.9 2.9 %collective-permute-start.4 = (bf16[520,128]{1,0:T(8,128)(2,1)S(1)}, bf16[520,128]{1,0:T(8,128)(2,1)S(1)}, u32[]{:S(2)}, u32[]{:S(2)}) collective-permute-start(bf16[520,128]{1,0:T(8,128)(2,1)S(1)} %collective-permute-done), channel_id=1, source_target_pairs={{0,1},{1,0},{2,3},{3,2},{4,5},{5,4},{6,7},{7,6},{8,9},{9,8},{10,11... | collective-permute-start | bytes 399368 | tf_op jit(solution)/shard_map/ppermute | solution.py:108
  25.4 2.4 %collective-permute-start.6 = (bf16[520,128]{1,0:T(8,128)(2,1)S(1)}, bf16[520,128]{1,0:T(8,128)(2,1)S(1)}, u32[]{:S(2)}, u32[]{:S(2)}) collective-permute-start(bf16[520,128]{1,0:T(8,128)(2,1)S(1)} %collective-permute-done.2), channel_id=1, source_target_pairs={{0,1},{1,0},{2,3},{3,2},{4,5},{5,4},{6,7},{7,6},{8,9},{9,8},{10,11... | collective-permute-start | bytes 399368 | tf_op jit(solution)/shard_map/ppermute | solution.py:108
  27.9 1.2 %copy-start.2 = (s32[1,1024,128]{2,1,0:T(8,128)S(1)}, s32[1,1024,128]{2,1,0:T(8,128)}, u32[]{:S(2)}) copy-start(s32[1,1024,128]{2,1,0:T(8,128)} %param.12) | copy-start | bytes 1572868
  27.9 1.2 %copy-start.3 = (bf16[1,1024,128]{2,1,0:T(8,128)(2,1)S(1)}, bf16[1,1024,128]{2,1,0:T(8,128)(2,1)}, u32[]{:S(2)}) copy-start(bf16[1,1024,128]{2,1,0:T(8,128)(2,1)} %param.11) | copy-start | bytes 786436
  29.6 1.5 %collective-permute-start.7 = (bf16[512,128]{1,0:T(8,128)(2,1)S(1)}, bf16[512,128]{1,0:T(8,128)(2,1)S(1)}, u32[]{:S(2)}, u32[]{:S(2)}) collective-permute-start(bf16[512,128]{1,0:T(8,128)(2,1)S(1)} %fusion.63), channel_id=1, source_target_pairs={{0,1},{1,0},{2,3},{3,2},{4,5},{5,4},{6,7},{7,6},{8,9},{9,8},{10,11... | collective-permute-start | bytes 393224 | tf_op jit(solution)/shard_map/ppermute | solution.py:119
  33.5 12.7 %collective-permute-start.9 = (bf16[512,128]{1,0:T(8,128)(2,1)S(1)}, bf16[512,128]{1,0:T(8,128)(2,1)S(1)}, u32[]{:S(2)}, u32[]{:S(2)}) collective-permute-start(bf16[512,128]{1,0:T(8,128)(2,1)S(1)} %fusion.56), channel_id=1, source_target_pairs={{0,8},{4,12},{8,0},{12,4},{1,9},{5,13},{9,1},{13,5},{2,10},{6,14},... | collective-permute-start | bytes 393224 | tf_op jit(solution)/shard_map/ppermute | solution.py:45
  36.8 9.9 %collective-permute-start.10 = (bf16[512,128]{1,0:T(8,128)(2,1)S(1)}, bf16[512,128]{1,0:T(8,128)(2,1)S(1)}, u32[]{:S(2)}, u32[]{:S(2)}) collective-permute-start(bf16[512,128]{1,0:T(8,128)(2,1)S(1)} %fusion.55), channel_id=1, source_target_pairs={{0,4},{4,8},{8,12},{12,0},{1,5},{5,9},{9,13},{13,1},{2,6},{6,10},{... | collective-permute-start | bytes 393224 | tf_op jit(solution)/shard_map/ppermute | solution.py:45
  36.9 11.1 %collective-permute-start.8 = (bf16[512,128]{1,0:T(8,128)(2,1)S(1)}, bf16[512,128]{1,0:T(8,128)(2,1)S(1)}, u32[]{:S(2)}, u32[]{:S(2)}) collective-permute-start(bf16[512,128]{1,0:T(8,128)(2,1)S(1)} %fusion.57), channel_id=1, source_target_pairs={{0,12},{4,0},{8,4},{12,8},{1,13},{5,1},{9,5},{13,9},{2,14},{6,2},{... | collective-permute-start | bytes 393224 | tf_op jit(solution)/shard_map/ppermute | solution.py:45
  52.1 5.0 %collective-permute-start.11 = (bf16[128,512]{1,0:T(8,128)(2,1)S(1)}, bf16[128,512]{1,0:T(8,128)(2,1)S(1)}, u32[]{:S(2)}, u32[]{:S(2)}) collective-permute-start(bf16[128,512]{1,0:T(8,128)(2,1)S(1)} %convert_element_type.181), channel_id=1, source_target_pairs={{0,2},{2,0},{1,3},{3,1},{4,6},{6,4},{5,7},{7,5},{8,10},{10,8},{9,1... | collective-permute-start | bytes 393224 | tf_op jit(solution)/shard_map/ppermute | solution.py:150

commit v10 on v4

--- a/solution.py
+++ b/solution.py
@@ -98,14 +98,20 @@
         codes = codes.astype(jnp.int32).reshape(2, capacity)
         got_slots.append(codes[0] * 256 + codes[1])
 
-    at_slot = [one_hot_rows(slots, slot_count) for slots in got_slots]
-    partial_value = sum(select_dot_t(a, b) for a, b in zip(at_slot, got_traces))
+    local_slot = one_hot_rows(got_slots[0], slot_count)
+    remote_slot = one_hot_rows(jnp.concatenate(got_slots[1:]), slot_count)
+    partial_value = select_dot_t(local_slot, got_traces[0]) + select_dot_t(
+        remote_slot, jnp.concatenate(got_traces[1:], axis=0)
+    )
     model_image = swap_add(partial_value, "band")
     residual = (
         bad_mask[0].astype(jnp.float32) * (model_image - observed[0].astype(jnp.float32))
     ).astype(jnp.bfloat16)
 
-    under_rows = [select_dot(a, residual).astype(jnp.bfloat16) for a in at_slot]
+    remote_rows = select_dot(remote_slot, residual).astype(jnp.bfloat16)
+    under_rows = [select_dot(local_slot, residual).astype(jnp.bfloat16)] + [
+        remote_rows[step * capacity : (step + 1) * capacity] for step in range(tile_count - 1)
+    ]
     returned = exchange(under_rows, "tile", -1)
     entry_rows = sum(select_dot(p, r) for p, r in zip(places, returned)).astype(jnp.bfloat16)
     back_table = psf_blocks.transpose(0, 2, 1).reshape(table_count * pixel_count, bin_count)

time: 56.7 us -> 56.6 us (level)
  matrix products: 22.4 us -> 21.7 us
    dot_general x13 -> x11, matrix products: 10.4 us -> 9.95 us  [select_dot_t(): lax.dot_general(selector, values, (((0,), (0,)), ((), ())), preferred_ele...]
    dot_general x11 -> x9, matrix products: 12 us -> 11.7 us  [select_dot(): jnp.dot(selector, values, preferred_element_type=jnp.float32, precision=p...]
  transfers between devices with their start and end apart: 8 -> 8, of which waited for: 6 -> 5; matrix products, arithmetic and copies ran while one was open for 14% -> 14% of each run, Pallas kernels for 0% -> 0%
where the time goes in v10:
time: 56.6 us; the launch traced here: 56.4 us
  matrix products  21.7 us (38%)
  waiting for transfers between devices  18.7 us (33%)
  starting transfers between devices  12.4 us (22%)
  other arithmetic  1.83 us (3%)
  between operations  1.03 us (2%)
  local copies, waits for them, and re-layouts  0.73 us (1%)
    ppermute x6, waiting for transfers between devices, exchange(): moved.append(lax.ppermute(blocks[step], axis, pairs))  14.2 us
    dot_general x9, matrix products, select_dot(): jnp.dot(selector, values, preferred_element_type=jnp.float32, precision=p...  11.7 us
    ppermute x6, starting transfers between devices, exchange(): moved.append(lax.ppermute(blocks[step], axis, pairs))  10.8 us
    dot_general x11, matrix products, select_dot_t(): lax.dot_general(selector, values, (((0,), (0,)), ((), ())), preferred_ele...  9.95 us
    ppermute x1, waiting for transfers between devices, per_device(): sent = lax.ppermute(theirs.astype(jnp.bfloat16), 'dither', [(0, 1), (1, 0)])  2.58 us
    ppermute x1, waiting for transfers between devices, swap_add(): return value + lax.ppermute(value, axis, [(0, 1), (1, 0)])  1.89 us
    ppermute x1, starting transfers between devices, per_device(): sent = lax.ppermute(theirs.astype(jnp.bfloat16), 'dither', [(0, 1), (1, 0)])  1.55 us
  transfers between devices with their start and end apart: 8, of which 5 were waited for; matrix products, arithmetic and copies ran while one was open for 14% of the time, Pallas kernels for 0%

profile of v10, /device:TPU:0, one launch (start us, length us, event | category | flops | bytes accessed | tf_op | source)
XLA Modules:
  0.0 56.4 jit_solution(2744155701497364700)
XLA Ops:
  0.7 0.7 %broadcast_multiply_fusion = s32[1024,1]{0,1:T(1,128)S(1)} fusion(s32[1024,1]{0,1:T(1,128)} %param.15), kind=kLoop, calls=%fused_computation.132 | loop fusion | flops 1024 | bytes 8192 | tf_op jit(solution)/shard_map/mul | solution.py:71
  1.4 1.3 %fusion.60 = f32[1024]{0:T(1024)S(1)} fusion(s32[1024]{0:T(1024)} %bitcast.63), kind=kOutput, calls=%fused_computation.62 | convolution fusion | flops 9464832 | bytes 8192 | tf_op jit(solution)/shard_map/dot_general | solution.py:12
  2.9 0.5 fusion.63
  3.8 0.8 %fusion.51 = bf16[1024,128]{1,0:T(8,128)(2,1)S(1)} fusion(bf16[1024,128]{1,0:T(8,128)(2,1)S(1)} %reshape.131, s32[1024]{0:T(1024)S(1)} %get-tuple-element.3), kind=kOutput, calls=%fused_computation.53 | convolution fusion | flops 269615104 | bytes 528384 | tf_op jit(solution)/shard_map/dot_general | solution.py:12
  4.7 3.0 %fusion.48 = bf16[1024,128]{1,0:T(8,128)(2,1)S(1)} fusion(bf16[16,128,128]{2,1,0:T(8,128)(2,1)S(1)} %copy-done, pred[1024,16]{0,1:T(8,128)(4,1)S(1)} %iota_compare_fusion.76, bf16[1024,128]{1,0:T(8,128)(2,1)S(1)} %fusion.51), kind=kOutput, calls=%fused_computation.52 | convolution fusion | flops 539099136 | bytes 1064960 | tf_op jit(solution)/shard_map/dot_general | solution.py:12
  7.7 0.9 %fusion.55 = bf16[512,128]{1,0:T(8,128)(2,1)S(1)} fusion(bf16[1024,128]{1,0:T(8,128)(2,1)S(1)} %fusion.48, s32[1024]{0:T(1024)S(1)} %bitcast.50), kind=kOutput, calls=%fused_computation.57 | convolution fusion | flops 134807552 | bytes 397312 | tf_op jit(solution)/shard_map/dot_general | solution.py:16
  8.6 3.1 %collective-permute-start = (bf16[520,128]{1,0:T(8,128)(2,1)S(1)}, bf16[520,128]{1,0:T(8,128)(2,1)S(1)}, u32[]{:S(2)}, u32[]{:S(2)}) collective-permute-start(bf16[520,128]{1,0:T(8,128)(2,1)S(1)} %pad_maximum_fusion), channel_id=1, source_target_pairs={{0,4},{4,8},{8,12},{12,0},{1,5},{5,9},{9,13},{13,1},{2,6},{6,10},{... | collective-permute-start | bytes 399368 | tf_op jit(solution)/shard_map/ppermute | solution.py:43
  11.7 0.5 fusion.64
  12.2 0.9 %fusion.56 = bf16[512,128]{1,0:T(8,128)(2,1)S(1)} fusion(bf16[1024,128]{1,0:T(8,128)(2,1)S(1)} %fusion.48, s32[1024]{0:T(1024)S(1)} %bitcast.61), kind=kOutput, calls=%fused_computation.58 | convolution fusion | flops 134807552 | bytes 397312 | tf_op jit(solution)/shard_map/dot_general | solution.py:16
  13.1 2.7 %collective-permute-start.1 = (bf16[520,128]{1,0:T(8,128)(2,1)S(1)}, bf16[520,128]{1,0:T(8,128)(2,1)S(1)}, u32[]{:S(2)}, u32[]{:S(2)}) collective-permute-start(bf16[520,128]{1,0:T(8,128)(2,1)S(1)} %pad_maximum_fusion.1), channel_id=1, source_target_pairs={{0,8},{4,12},{8,0},{12,4},{1,9},{5,13},{9,1},{13,5},{2,10},{6,14},... | collective-permute-start | bytes 399368 | tf_op jit(solution)/shard_map/ppermute | solution.py:43
  16.2 0.9 %fusion.57 = bf16[512,128]{1,0:T(8,128)(2,1)S(1)} fusion(bf16[1024,128]{1,0:T(8,128)(2,1)S(1)} %fusion.48, s32[1024]{0:T(1024)S(1)} %bitcast.58), kind=kOutput, calls=%fused_computation.59 | convolution fusion | flops 134807552 | bytes 397312 | tf_op jit(solution)/shard_map/dot_general | solution.py:16
  17.2 1.4 %collective-permute-start.2 = (bf16[520,128]{1,0:T(8,128)(2,1)S(1)}, bf16[520,128]{1,0:T(8,128)(2,1)S(1)}, u32[]{:S(2)}, u32[]{:S(2)}) collective-permute-start(bf16[520,128]{1,0:T(8,128)(2,1)S(1)} %pad_maximum_fusion.2), channel_id=1, source_target_pairs={{0,12},{4,0},{8,4},{12,8},{1,13},{5,1},{9,5},{13,9},{2,14},{6,2},{... | collective-permute-start | bytes 399368 | tf_op jit(solution)/shard_map/ppermute | solution.py:43
  18.6 0.5 fusion.62
  19.1 1.5 %fusion.28 = f32[1024,128]{1,0:T(8,128)S(1)} fusion(bf16[1024,128]{1,0:T(8,128)(2,1)S(1)} %fusion.48, s32[512]{0:T(512)S(1)} %bitcast.64, s32[1024]{0:T(1024)S(1)} %bitcast.53), kind=kOutput, calls=%fused_computation.36 | convolution fusion | flops 269549568 | bytes 792576 | tf_op jit(solution)/shard_map/dot_general | solution.py:16
  20.7 2.4 %collective-permute-done.1 = bf16[520,128]{1,0:T(8,128)(2,1)S(1)} collective-permute-done((bf16[520,128]{1,0:T(8,128)(2,1)S(1)}, bf16[520,128]{1,0:T(8,128)(2,1)S(1)}, u32[]{:S(2)}, u32[]{:S(2)}) %collective-permute-start.1) | collective-permute-done | bytes 133152 | tf_op jit(solution)/shard_map/ppermute | solution.py:43
  23.1 1.5 %collective-permute-done.2 = bf16[520,128]{1,0:T(8,128)(2,1)S(1)} collective-permute-done((bf16[520,128]{1,0:T(8,128)(2,1)S(1)}, bf16[520,128]{1,0:T(8,128)(2,1)S(1)}, u32[]{:S(2)}, u32[]{:S(2)}) %collective-permute-start.2) | collective-permute-done | bytes 133152 | tf_op jit(solution)/shard_map/ppermute | solution.py:43
  24.7 2.1 %fusion.41 = f32[1024,128]{1,0:T(8,128)S(1)} fusion(f32[1024,128]{1,0:T(8,128)S(1)} %fusion.28, s32[1536]{0:T(1024)S(1)} %pad_add_fusion, bf16[512,128]{1,0:T(8,128)(2,1)S(1)} %slice.91, bf16[512,128]{1,0:T(8,128)(2,1)S(1)} %slice.90, bf16[512,128]{1,0:T(8,128)(2,1)S(1)} %slice.89), kind=kOutput, calls=%fused_computation.47 | convolution fusion | flops 405536768 | bytes 1447936 | tf_op jit(solution)/shard_map/dot_general | solution.py:16
  26.9 1.9 %collective-permute-done.3 = f32[1024,128]{1,0:T(8,128)S(1)} collective-permute-done((f32[1024,128]{1,0:T(8,128)S(1)}, f32[1024,128]{1,0:T(8,128)S(1)}, u32[]{:S(2)}, u32[]{:S(2)}) %collective-permute-start.3) | collective-permute-done | bytes 524320 | tf_op jit(solution)/shard_map/ppermute | solution.py:34
  29.0 1.2 %fusion.12 = bf16[1536,128]{1,0:T(8,128)(2,1)S(1)} fusion(bf16[1024,128]{1,0:T(8,128)(2,1)S(1)} %fusion.85, s32[1536]{0:T(1024)S(1)} %pad_add_fusion), kind=kOutput, calls=%fused_computation.15 | convolution fusion | flops 404422656 | bytes 661504 | tf_op jit(solution)/shard_map/dot_general | solution.py:12
  30.2 2.9 %collective-permute-start.4 = (bf16[512,128]{1,0:T(8,128)(2,1)S(1)}, bf16[512,128]{1,0:T(8,128)(2,1)S(1)}, u32[]{:S(2)}, u32[]{:S(2)}) collective-permute-start(bf16[512,128]{1,0:T(8,128)(2,1)S(1)} %get-tuple-element.6), channel_id=1, source_target_pairs={{0,12},{4,0},{8,4},{12,8},{1,13},{5,1},{9,5},{13,9},{2,14},{6,2},{... | collective-permute-start | bytes 393224 | tf_op jit(solution)/shard_map/ppermute | solution.py:43
  33.1 0.8 %collective-permute-start.5 = (bf16[512,128]{1,0:T(8,128)(2,1)S(1)}, bf16[512,128]{1,0:T(8,128)(2,1)S(1)}, u32[]{:S(2)}, u32[]{:S(2)}) collective-permute-start(bf16[512,128]{1,0:T(8,128)(2,1)S(1)} %get-tuple-element.8), channel_id=1, source_target_pairs={{0,8},{4,12},{8,0},{12,4},{1,9},{5,13},{9,1},{13,5},{2,10},{6,14},... | collective-permute-start | bytes 393224 | tf_op jit(solution)/shard_map/ppermute | solution.py:43
  33.9 1.3 %fusion.29 = f32[1024,128]{1,0:T(8,128)S(1)} fusion(bf16[1024,128]{1,0:T(8,128)(2,1)S(1)} %fusion.85, s32[512]{0:T(512)S(1)} %bitcast.65, s32[1024]{0:T(1024)S(1)} %bitcast.54), kind=kOutput, calls=%fused_computation.38 | convolution fusion | flops 269549568 | bytes 792576 | tf_op jit(solution)/shard_map/dot_general | solution.py:12
  35.2 10.2 %collective-permute-done.5 = bf16[512,128]{1,0:T(8,128)(2,1)S(1)} collective-permute-done((bf16[512,128]{1,0:T(8,128)(2,1)S(1)}, bf16[512,128]{1,0:T(8,128)(2,1)S(1)}, u32[]{:S(2)}, u32[]{:S(2)}) %collective-permute-start.5) | collective-permute-done | bytes 131104 | tf_op jit(solution)/shard_map/ppermute | solution.py:43
  45.4 0.5 fusion.17
  46.0 0.5 fusion.14
  46.5 0.5 fusion.44
  47.0 2.6 %fusion.45 = bf16[1024,128]{1,0:T(8,128)(2,1)S(1)} fusion(pred[1024,16]{0,1:T(8,128)(4,1)S(1)} %iota_compare_fusion.76, bf16[1024,128]{1,0:T(8,128)(2,1)S(1)} %fusion.44, bf16[16,128,128]{2,1,0:T(8,128)(2,1)S(1)} %copy-done), kind=kOutput, calls=%fused_computation.51 | convolution fusion | flops 539099136 | bytes 1064960 | tf_op jit(solution)/shard_map/dot_general | solution.py:12
  49.6 0.9 %fusion.52 = bf16[512,128]{1,0:T(8,128)(2,1)S(1)} fusion(bf16[1024,128]{1,0:T(8,128)(2,1)S(1)} %fusion.45, s32[1024]{0:T(1024)S(1)} %get-tuple-element.2), kind=kOutput, calls=%fused_computation.54 | convolution fusion | flops 134807552 | bytes 397312 | tf_op jit(solution)/shard_map/dot_general | solution.py:16
  50.6 1.6 %collective-permute-start.7 = (bf16[128,512]{1,0:T(8,128)(2,1)S(1)}, bf16[128,512]{1,0:T(8,128)(2,1)S(1)}, u32[]{:S(2)}, u32[]{:S(2)}) collective-permute-start(bf16[128,512]{1,0:T(8,128)(2,1)S(1)} %convert_element_type.143), channel_id=1, source_target_pairs={{0,2},{2,0},{1,3},{3,1},{4,6},{6,4},{5,7},{7,5},{8,10},{10,8},{9,1... | collective-permute-start | bytes 393224 | tf_op jit(solution)/shard_map/ppermute | solution.py:128
  52.1 0.9 %fusion.32 = f32[512,128]{1,0:T(8,128)S(1)} fusion(bf16[1024,128]{1,0:T(8,128)(2,1)S(1)} %fusion.45, s32[1024]{0:T(1024)S(1)} %broadcast_subtract_fusion.1), kind=kOutput, calls=%fused_computation.42 | convolution fusion | flops 134742016 | bytes 528384 | tf_op jit(solution)/shard_map/dot_general | solution.py:16
  53.1 2.6 %collective-permute-done.7 = bf16[128,512]{1,0:T(8,128)(2,1)S(1)} collective-permute-done((bf16[128,512]{1,0:T(8,128)(2,1)S(1)}, bf16[128,512]{1,0:T(8,128)(2,1)S(1)}, u32[]{:S(2)}, u32[]{:S(2)}) %collective-permute-start.7) | collective-permute-done | bytes 131104 | tf_op jit(solution)/shard_map/ppermute | solution.py:128
  55.7 0.7 %convert_add_fusion = f32[128,512]{1,0:T(8,128)} fusion(f32[128,512]{1,0:T(8,128)S(1)} %reshape.135, bf16[128,512]{1,0:T(8,128)(2,1)S(1)} %collective-permute-done.7), kind=kLoop, calls=%fused_computation.93 | loop fusion | flops 131072 | bytes 655360 | tf_op jit(solution)/shard_map/add | solution.py:130
  (56 shorter events, 1.6 us)
Async XLA Ops:
  0.6 4.1 %copy-start = (bf16[16,128,128]{2,1,0:T(8,128)(2,1)S(1)}, bf16[16,128,128]{2,1,0:T(8,128)(2,1)}, u32[]{:S(2)}) copy-start(bf16[16,128,128]{2,1,0:T(8,128)(2,1)} %param.10) | copy-start | bytes 1572868
  1.4 1.3 %copy-start.6 = (s32[1024]{0:T(1024)S(1)}, s32[1024]{0:T(1024)}, u32[]{:S(2)}) copy-start(s32[1024]{0:T(1024)} %param.14) | copy-start | bytes 12292
  1.4 1.4 %copy-start.7 = (s32[1024,1]{0,1:T(1,128)S(1)}, s32[1024,1]{0,1:T(1,128)}, u32[]{:S(2)}) copy-start(s32[1024,1]{0,1:T(1,128)} %param.13) | copy-start | bytes 12292
  2.7 0.7 %copy-start.5 = (s32[1024]{0:T(1024)S(1)}, s32[1024]{0:T(1024)}, u32[]{:S(2)}) copy-start(s32[1024]{0:T(1024)} %param.17) | copy-start | bytes 12292
  2.7 1.0 %copy-start.2 = (bf16[256,512]{1,0:T(8,128)(2,1)S(1)}, bf16[256,512]{1,0:T(8,128)(2,1)}, u32[]{:S(2)}) copy-start(bf16[256,512]{1,0:T(8,128)(2,1)} %param.9) | copy-start | bytes 786436
  2.8 1.0 %copy-start.8 = (s32[1024]{0:T(1024)S(1)}, s32[1024]{0:T(1024)}, u32[]{:S(2)}) copy-start(s32[1024]{0:T(1024)} %param.16) | copy-start | bytes 12292
  8.6 12.0 %collective-permute-start = (bf16[520,128]{1,0:T(8,128)(2,1)S(1)}, bf16[520,128]{1,0:T(8,128)(2,1)S(1)}, u32[]{:S(2)}, u32[]{:S(2)}) collective-permute-start(bf16[520,128]{1,0:T(8,128)(2,1)S(1)} %pad_maximum_fusion), channel_id=1, source_target_pairs={{0,4},{4,8},{8,12},{12,0},{1,5},{5,9},{9,13},{13,1},{2,6},{6,10},{... | collective-permute-start | bytes 399368 | tf_op jit(solution)/shard_map/ppermute | solution.py:43
  13.1 10.0 %collective-permute-start.1 = (bf16[520,128]{1,0:T(8,128)(2,1)S(1)}, bf16[520,128]{1,0:T(8,128)(2,1)S(1)}, u32[]{:S(2)}, u32[]{:S(2)}) collective-permute-start(bf16[520,128]{1,0:T(8,128)(2,1)S(1)} %pad_maximum_fusion.1), channel_id=1, source_target_pairs={{0,8},{4,12},{8,0},{12,4},{1,9},{5,13},{9,1},{13,5},{2,10},{6,14},... | collective-permute-start | bytes 399368 | tf_op jit(solution)/shard_map/ppermute | solution.py:43
  17.2 7.5 %collective-permute-start.2 = (bf16[520,128]{1,0:T(8,128)(2,1)S(1)}, bf16[520,128]{1,0:T(8,128)(2,1)S(1)}, u32[]{:S(2)}, u32[]{:S(2)}) collective-permute-start(bf16[520,128]{1,0:T(8,128)(2,1)S(1)} %pad_maximum_fusion.2), channel_id=1, source_target_pairs={{0,12},{4,0},{8,4},{12,8},{1,13},{5,1},{9,5},{13,9},{2,14},{6,2},{... | collective-permute-start | bytes 399368 | tf_op jit(solution)/shard_map/ppermute | solution.py:43
  24.7 4.1 %copy-start.1 = (s32[1,1024,128]{2,1,0:T(8,128)S(1)}, s32[1,1024,128]{2,1,0:T(8,128)}, u32[]{:S(2)}) copy-start(s32[1,1024,128]{2,1,0:T(8,128)} %param.12) | copy-start | bytes 1572868
  24.7 4.1 %copy-start.3 = (bf16[1,1024,128]{2,1,0:T(8,128)(2,1)S(1)}, bf16[1,1024,128]{2,1,0:T(8,128)(2,1)}, u32[]{:S(2)}) copy-start(bf16[1,1024,128]{2,1,0:T(8,128)(2,1)} %param.11) | copy-start | bytes 786436
  26.8 2.0 %collective-permute-start.3 = (f32[1024,128]{1,0:T(8,128)S(1)}, f32[1024,128]{1,0:T(8,128)S(1)}, u32[]{:S(2)}, u32[]{:S(2)}) collective-permute-start(f32[1024,128]{1,0:T(8,128)S(1)} %fusion.41), channel_id=1, source_target_pairs={{0,1},{1,0},{2,3},{3,2},{4,5},{5,4},{6,7},{7,6},{8,9},{9,8},{10,11... | collective-permute-start | bytes 1572872 | tf_op jit(solution)/shard_map/ppermute | solution.py:34
  28.9 5.0 %copy-start.4 = (bf16[1024,128]{1,0:T(8,128)(2,1)}, bf16[1024,128]{1,0:T(8,128)(2,1)S(1)}, u32[]{:S(2)}) copy-start(bf16[1024,128]{1,0:T(8,128)(2,1)S(1)} %fusion.85) | copy-start | bytes 786436
  30.2 16.3 %collective-permute-start.4 = (bf16[512,128]{1,0:T(8,128)(2,1)S(1)}, bf16[512,128]{1,0:T(8,128)(2,1)S(1)}, u32[]{:S(2)}, u32[]{:S(2)}) collective-permute-start(bf16[512,128]{1,0:T(8,128)(2,1)S(1)} %get-tuple-element.6), channel_id=1, source_target_pairs={{0,12},{4,0},{8,4},{12,8},{1,13},{5,1},{9,5},{13,9},{2,14},{6,2},{... | collective-permute-start | bytes 393224 | tf_op jit(solution)/shard_map/ppermute | solution.py:43
  33.1 12.9 %collective-permute-start.6 = (bf16[512,128]{1,0:T(8,128)(2,1)S(1)}, bf16[512,128]{1,0:T(8,128)(2,1)S(1)}, u32[]{:S(2)}, u32[]{:S(2)}) collective-permute-start(bf16[512,128]{1,0:T(8,128)(2,1)S(1)} %get-tuple-element.7), channel_id=1, source_target_pairs={{0,4},{4,8},{8,12},{12,0},{1,5},{5,9},{9,13},{13,1},{2,6},{6,10},{... | collective-permute-start | bytes 393224 | tf_op jit(solution)/shard_map/ppermute | solution.py:43
  33.1 12.3 %collective-permute-start.5 = (bf16[512,128]{1,0:T(8,128)(2,1)S(1)}, bf16[512,128]{1,0:T(8,128)(2,1)S(1)}, u32[]{:S(2)}, u32[]{:S(2)}) collective-permute-start(bf16[512,128]{1,0:T(8,128)(2,1)S(1)} %get-tuple-element.8), channel_id=1, source_target_pairs={{0,8},{4,12},{8,0},{12,4},{1,9},{5,13},{9,1},{13,5},{2,10},{6,14},... | collective-permute-start | bytes 393224 | tf_op jit(solution)/shard_map/ppermute | solution.py:43
  50.6 5.1 %collective-permute-start.7 = (bf16[128,512]{1,0:T(8,128)(2,1)S(1)}, bf16[128,512]{1,0:T(8,128)(2,1)S(1)}, u32[]{:S(2)}, u32[]{:S(2)}) collective-permute-start(bf16[128,512]{1,0:T(8,128)(2,1)S(1)} %convert_element_type.143), channel_id=1, source_target_pairs={{0,2},{2,0},{1,3},{3,1},{4,6},{6,4},{5,7},{7,5},{8,10},{10,8},{9,1... | collective-permute-start | bytes 393224 | tf_op jit(solution)/shard_map/ppermute | solution.py:128

commit v11 on v10

--- a/solution.py
+++ b/solution.py
@@ -84,12 +84,15 @@
     slot_parts = jnp.stack([trace_slot // 256, trace_slot % 256], axis=1).astype(jnp.bfloat16)
     code_rows = -(-2 * capacity // pixel_count)
     places = [one_hot_rows(dest - step * capacity, capacity) for step in range(tile_count)]
+    with_codes = jnp.concatenate([traces, slot_parts], axis=1)
     send = []
     for step in range(tile_count):
-        codes = select_dot_t(slot_parts, places[step]).astype(jnp.bfloat16).reshape(2 * capacity)
+        placed = select_dot_t(places[step], with_codes).astype(jnp.bfloat16)
+        codes = placed[:, pixel_count:].T.reshape(2 * capacity)
         codes = jnp.pad(codes, (0, code_rows * pixel_count - 2 * capacity))
-        block = select_dot_t(places[step], traces).astype(jnp.bfloat16)
-        send.append(jnp.concatenate([block, codes.reshape(code_rows, pixel_count)], axis=0))
+        send.append(
+            jnp.concatenate([placed[:, :pixel_count], codes.reshape(code_rows, pixel_count)], axis=0)
+        )
     got = exchange(send, "tile", 1)
     got_traces = [block[:capacity] for block in got]
     got_slots = []
@@ -120,13 +123,11 @@
 
     if dither_count == 2:
         dither = lax.axis_index("dither")
-        half_rows = row_count // 2
-        own_start = dither * half_rows
-        their_rows = one_hot_rows(spec_rows - (half_rows - own_start), half_rows)
-        own_rows = one_hot_rows(spec_rows - own_start, half_rows)
-        theirs = select_dot_t(their_rows, terms).reshape(source_count // 2, block_count * bin_count)
+        local_grad = select_dot_t(gather_spec, terms).reshape(2, row_count // 2, bin_count)
+        halves = local_grad.reshape(2, source_count // 2, block_count * bin_count)
+        theirs = jnp.where(dither == 0, halves[1], halves[0])
+        mine = jnp.where(dither == 0, halves[0], halves[1])
         sent = lax.ppermute(theirs.astype(jnp.bfloat16), "dither", [(0, 1), (1, 0)])
-        mine = select_dot_t(own_rows, terms).reshape(source_count // 2, block_count * bin_count)
         gradient = mine + sent.astype(jnp.float32)
     else:
         local_grad = select_dot_t(gather_spec, terms)

time: 56.6 us -> 57.3 us (1.012)
  matrix products: 21.7 us -> 19 us
  waiting for transfers between devices: 18.7 us -> 20.6 us
  starting transfers between devices: 12.4 us -> 13.3 us
    dot_general x9 -> x8, matrix products: 11.7 us -> 10 us  [select_dot(): jnp.dot(selector, values, preferred_element_type=jnp.float32, precision=p...]
    ppermute x6, waiting for transfers between devices: 14.2 us -> 15.2 us  [exchange(): moved.append(lax.ppermute(blocks[step], axis, pairs))]
    dot_general x11 -> x7, matrix products: 9.95 us -> 8.94 us  [select_dot_t(): lax.dot_general(selector, values, (((0,), (0,)), ((), ())), preferred_ele...]
    ppermute x6, starting transfers between devices: 10.8 us -> 11.7 us  [exchange(): moved.append(lax.ppermute(blocks[step], axis, pairs))]
    ppermute x1, waiting for transfers between devices: 2.58 us -> 3.43 us  [per_device(): sent = lax.ppermute(theirs.astype(jnp.bfloat16), 'dither', [(0, 1), (1, 0)])]
  transfers between devices with their start and end apart: 8 -> 8, of which waited for: 5 -> 5; matrix products, arithmetic and copies ran while one was open for 14% -> 9% of each run, Pallas kernels for 0% -> 0%
where the time goes in v11:
time: 57.3 us; the launch traced here: 57 us
  waiting for transfers between devices  20.6 us (36%)
  matrix products  19 us (33%)
  starting transfers between devices  13.3 us (23%)
  other arithmetic  1.82 us (3%)
  local copies, waits for them, and re-layouts  1.24 us (2%)
  between operations  1.07 us (2%)
    ppermute x6, waiting for transfers between devices, exchange(): moved.append(lax.ppermute(blocks[step], axis, pairs))  15.2 us
    ppermute x6, starting transfers between devices, exchange(): moved.append(lax.ppermute(blocks[step], axis, pairs))  11.7 us
    dot_general x8, matrix products, select_dot(): jnp.dot(selector, values, preferred_element_type=jnp.float32, precision=p...  10 us
    dot_general x7, matrix products, select_dot_t(): lax.dot_general(selector, values, (((0,), (0,)), ((), ())), preferred_ele...  8.94 us
    ppermute x1, waiting for transfers between devices, per_device(): sent = lax.ppermute(theirs.astype(jnp.bfloat16), 'dither', [(0, 1), (1, 0)])  3.43 us
    ppermute x1, waiting for transfers between devices, swap_add(): return value + lax.ppermute(value, axis, [(0, 1), (1, 0)])  1.89 us
    ppermute x1, starting transfers between devices, per_device(): sent = lax.ppermute(theirs.astype(jnp.bfloat16), 'dither', [(0, 1), (1, 0)])  1.55 us
  transfers between devices with their start and end apart: 8, of which 5 were waited for; matrix products, arithmetic and copies ran while one was open for 9% of the time, Pallas kernels for 0%

profile of v11, /device:TPU:0, one launch (start us, length us, event | category | flops | bytes accessed | tf_op | source)
XLA Modules:
  0.0 57.0 jit_solution(8793014752471265882)
XLA Ops:
  0.7 0.7 %broadcast_multiply_fusion = s32[1024,1]{0,1:T(1,128)S(1)} fusion(s32[1024,1]{0,1:T(1,128)} %param.15), kind=kLoop, calls=%fused_computation.120 | loop fusion | flops 1024 | bytes 8192 | tf_op jit(solution)/shard_map/mul | solution.py:71
  1.4 1.2 %fusion.52 = f32[1024]{0:T(1024)S(1)} fusion(s32[1024]{0:T(1024)} %bitcast.60), kind=kOutput, calls=%fused_computation.55 | convolution fusion | flops 9464832 | bytes 8192 | tf_op jit(solution)/shard_map/dot_general | solution.py:12
  2.8 0.2 reshape.133
  3.0 0.4 copy-done.6
  3.4 0.8 %fusion.47 = bf16[1024,128]{1,0:T(8,128)(2,1)S(1)} fusion(bf16[1024,128]{1,0:T(8,128)(2,1)S(1)} %reshape.133, s32[1024]{0:T(1024)S(1)} %add.76), kind=kOutput, calls=%fused_computation.47 | convolution fusion | flops 269615104 | bytes 528384 | tf_op jit(solution)/shard_map/dot_general | solution.py:12
  4.2 3.9 %fusion.44 = bf16[1024,128]{0,1:T(8,128)(2,1)S(1)} fusion(bf16[16,128,128]{2,1,0:T(8,128)(2,1)S(1)} %copy-done, pred[1024,16]{0,1:T(8,128)(4,1)S(1)} %iota_compare_fusion.45, bf16[1024,128]{1,0:T(8,128)(2,1)S(1)} %fusion.47), kind=kOutput, calls=%fused_computation.46 | convolution fusion | flops 539099136 | bytes 1064960 | tf_op jit(solution)/shard_map/dot_general | solution.py:12
  8.2 0.7 %convolution_convert_fusion.2 = bf16[512,130]{1,0:T(8,128)(2,1)S(1)} fusion(s32[1024]{0:T(1024)S(1)} %bitcast.50, bf16[1024,1]{0,1:T(2,128)(2,1)S(1)} %stack.11, bf16[1024,1]{0,1:T(2,128)(2,1)S(1)} %stack.10, bf16[1024,128]{0,1:T(8,128)(2,1)S(1)} %fusion.44), kind=kOutput, calls=%fused_computation.50 | convolution fusion | flops 138228736 | bytes 403456 | tf_op jit(solution)/shard_map/dot_general | solution.py:16
  8.9 0.1 copy.22
  9.1 3.1 %collective-permute-start = (bf16[520,128]{1,0:T(8,128)(2,1)S(1)}, bf16[520,128]{1,0:T(8,128)(2,1)S(1)}, u32[]{:S(2)}, u32[]{:S(2)}) collective-permute-start(bf16[520,128]{1,0:T(8,128)(2,1)S(1)} %pad_maximum_fusion.1), channel_id=1, source_target_pairs={{0,4},{4,8},{8,12},{12,0},{1,5},{5,9},{9,13},{13,1},{2,6},{6,10},{... | collective-permute-start | bytes 399368 | tf_op jit(solution)/shard_map/ppermute | solution.py:43
  12.1 0.7 %convolution_convert_fusion.1 = bf16[512,130]{1,0:T(8,128)(2,1)S(1)} fusion(s32[1024]{0:T(1024)S(1)} %bitcast.58, bf16[1024,1]{0,1:T(2,128)(2,1)S(1)} %stack.11, bf16[1024,1]{0,1:T(2,128)(2,1)S(1)} %stack.10, bf16[1024,128]{0,1:T(8,128)(2,1)S(1)} %fusion.44), kind=kOutput, calls=%fused_computation.49 | convolution fusion | flops 138228736 | bytes 403456 | tf_op jit(solution)/shard_map/dot_general | solution.py:16
  12.9 0.1 copy.24
  13.0 2.7 %collective-permute-start.1 = (bf16[520,128]{1,0:T(8,128)(2,1)S(1)}, bf16[520,128]{1,0:T(8,128)(2,1)S(1)}, u32[]{:S(2)}, u32[]{:S(2)}) collective-permute-start(bf16[520,128]{1,0:T(8,128)(2,1)S(1)} %pad_maximum_fusion.2), channel_id=1, source_target_pairs={{0,8},{4,12},{8,0},{12,4},{1,9},{5,13},{9,1},{13,5},{2,10},{6,14},... | collective-permute-start | bytes 399368 | tf_op jit(solution)/shard_map/ppermute | solution.py:43
  15.7 0.7 %convolution_convert_fusion = bf16[512,130]{1,0:T(8,128)(2,1)S(1)} fusion(s32[1024]{0:T(1024)S(1)} %bitcast.56, bf16[1024,1]{0,1:T(2,128)(2,1)S(1)} %stack.11, bf16[1024,1]{0,1:T(2,128)(2,1)S(1)} %stack.10, bf16[1024,128]{0,1:T(8,128)(2,1)S(1)} %fusion.44), kind=kOutput, calls=%fused_computation.48 | convolution fusion | flops 138228736 | bytes 403456 | tf_op jit(solution)/shard_map/dot_general | solution.py:16
  16.6 1.4 %collective-permute-start.2 = (bf16[520,128]{1,0:T(8,128)(2,1)S(1)}, bf16[520,128]{1,0:T(8,128)(2,1)S(1)}, u32[]{:S(2)}, u32[]{:S(2)}) collective-permute-start(bf16[520,128]{1,0:T(8,128)(2,1)S(1)} %pad_maximum_fusion.3), channel_id=1, source_target_pairs={{0,12},{4,0},{8,4},{12,8},{1,13},{5,1},{9,5},{13,9},{2,14},{6,2},{... | collective-permute-start | bytes 399368 | tf_op jit(solution)/shard_map/ppermute | solution.py:43
  18.0 0.5 fusion.48
  18.6 0.6 fusion.53
  19.2 4.4 %collective-permute-done.1 = bf16[520,128]{1,0:T(8,128)(2,1)S(1)} collective-permute-done((bf16[520,128]{1,0:T(8,128)(2,1)S(1)}, bf16[520,128]{1,0:T(8,128)(2,1)S(1)}, u32[]{:S(2)}, u32[]{:S(2)}) %collective-permute-start.1) | collective-permute-done | bytes 133152 | tf_op jit(solution)/shard_map/ppermute | solution.py:43
  23.6 0.6 %collective-permute-done.2 = bf16[520,128]{1,0:T(8,128)(2,1)S(1)} collective-permute-done((bf16[520,128]{1,0:T(8,128)(2,1)S(1)}, bf16[520,128]{1,0:T(8,128)(2,1)S(1)}, u32[]{:S(2)}, u32[]{:S(2)}) %collective-permute-start.2) | collective-permute-done | bytes 133152 | tf_op jit(solution)/shard_map/ppermute | solution.py:43
  24.3 2.0 %fusion.37 = f32[1024,128]{1,0:T(8,128)S(1)} fusion(f32[1024,128]{1,0:T(8,128)S(1)} %fusion.53, s32[1536]{0:T(1024)S(1)} %pad_add_fusion, bf16[512,128]{1,0:T(8,128)(2,1)S(1)} %slice.143, bf16[512,128]{1,0:T(8,128)(2,1)S(1)} %slice.142, bf16[512,128]{1,0:T(8,128)(2,1)S(1)} %slice.141), kind=kOutput, calls=%fused_computation.41 | convolution fusion | flops 405536768 | bytes 1447936 | tf_op jit(solution)/shard_map/dot_general | solution.py:16
  26.4 1.9 %collective-permute-done.3 = f32[1024,128]{1,0:T(8,128)S(1)} collective-permute-done((f32[1024,128]{1,0:T(8,128)S(1)}, f32[1024,128]{1,0:T(8,128)S(1)}, u32[]{:S(2)}, u32[]{:S(2)}) %collective-permute-start.3) | collective-permute-done | bytes 524320 | tf_op jit(solution)/shard_map/ppermute | solution.py:34
  28.5 1.2 %fusion.13 = bf16[1536,128]{1,0:T(8,128)(2,1)S(1)} fusion(bf16[1024,128]{1,0:T(8,128)(2,1)S(1)} %fusion.72, s32[1536]{0:T(1024)S(1)} %pad_add_fusion), kind=kOutput, calls=%fused_computation.16 | convolution fusion | flops 404422656 | bytes 661504 | tf_op jit(solution)/shard_map/dot_general | solution.py:12
  29.7 3.8 %collective-permute-start.4 = (bf16[512,128]{1,0:T(8,128)(2,1)S(1)}, bf16[512,128]{1,0:T(8,128)(2,1)S(1)}, u32[]{:S(2)}, u32[]{:S(2)}) collective-permute-start(bf16[512,128]{1,0:T(8,128)(2,1)S(1)} %get-tuple-element.4), channel_id=1, source_target_pairs={{0,12},{4,0},{8,4},{12,8},{1,13},{5,1},{9,5},{13,9},{2,14},{6,2},{... | collective-permute-start | bytes 393224 | tf_op jit(solution)/shard_map/ppermute | solution.py:43
  33.5 0.8 %collective-permute-start.5 = (bf16[512,128]{1,0:T(8,128)(2,1)S(1)}, bf16[512,128]{1,0:T(8,128)(2,1)S(1)}, u32[]{:S(2)}, u32[]{:S(2)}) collective-permute-start(bf16[512,128]{1,0:T(8,128)(2,1)S(1)} %get-tuple-element.6), channel_id=1, source_target_pairs={{0,8},{4,12},{8,0},{12,4},{1,9},{5,13},{9,1},{13,5},{2,10},{6,14},... | collective-permute-start | bytes 393224 | tf_op jit(solution)/shard_map/ppermute | solution.py:43
  34.3 1.3 %fusion.26 = f32[1024,128]{1,0:T(8,128)S(1)} fusion(bf16[1024,128]{1,0:T(8,128)(2,1)S(1)} %fusion.72, s32[512]{0:T(512)S(1)} %bitcast.62, s32[1024]{0:T(1024)S(1)} %bitcast.54), kind=kOutput, calls=%fused_computation.34 | convolution fusion | flops 269549568 | bytes 792576 | tf_op jit(solution)/shard_map/dot_general | solution.py:12
  35.6 10.2 %collective-permute-done.5 = bf16[512,128]{1,0:T(8,128)(2,1)S(1)} collective-permute-done((bf16[512,128]{1,0:T(8,128)(2,1)S(1)}, bf16[512,128]{1,0:T(8,128)(2,1)S(1)}, u32[]{:S(2)}, u32[]{:S(2)}) %collective-permute-start.5) | collective-permute-done | bytes 131104 | tf_op jit(solution)/shard_map/ppermute | solution.py:43
  45.8 0.5 fusion.17
  46.3 0.5 fusion.15
  46.9 0.5 fusion.40
  47.4 3.7 %fusion.6 = f32[1024,128]{1,0:T(8,128)S(1)} fusion(s32[1024]{0:T(1024)S(1)} %add.76, pred[1024,16]{0,1:T(8,128)(4,1)S(1)} %iota_compare_fusion.45, bf16[1024,128]{1,0:T(8,128)(2,1)S(1)} %fusion.40, bf16[16,128,128]{2,1,0:T(8,128)(2,1)S(1)} %copy-done), kind=kOutput, calls=%fused_computation.9 | convolution fusion | flops 808583168 | bytes 1331200 | tf_op jit(solution)/shard_map/dot_general | solution.py:16
  51.2 1.6 %collective-permute-start.7 = (bf16[128,512]{1,0:T(8,128)(2,1)S(1)}, bf16[128,512]{1,0:T(8,128)(2,1)S(1)}, u32[]{:S(2)}, u32[]{:S(2)}) collective-permute-start(bf16[128,512]{1,0:T(8,128)(2,1)S(1)} %convert_element_type.129), channel_id=1, source_target_pairs={{0,2},{2,0},{1,3},{3,1},{4,6},{6,4},{5,7},{7,5},{8,10},{10,8},{9,1... | collective-permute-start | bytes 393224 | tf_op jit(solution)/shard_map/ppermute | solution.py:130
  52.8 3.4 %collective-permute-done.7 = bf16[128,512]{1,0:T(8,128)(2,1)S(1)} collective-permute-done((bf16[128,512]{1,0:T(8,128)(2,1)S(1)}, bf16[128,512]{1,0:T(8,128)(2,1)S(1)}, u32[]{:S(2)}, u32[]{:S(2)}) %collective-permute-start.7) | collective-permute-done | bytes 131104 | tf_op jit(solution)/shard_map/ppermute | solution.py:130
  56.3 0.7 %convert_add_fusion = f32[128,512]{1,0:T(8,128)} fusion(f32[128,512]{1,0:T(8,128)S(1)} %select_n.50, bf16[128,512]{1,0:T(8,128)(2,1)S(1)} %collective-permute-done.7), kind=kLoop, calls=%fused_computation.77 | loop fusion | flops 131072 | bytes 655360 | tf_op jit(solution)/shard_map/add | solution.py:131
  (61 shorter events, 0.9 us)
Async XLA Ops:
  0.6 3.6 %copy-start = (bf16[16,128,128]{2,1,0:T(8,128)(2,1)S(1)}, bf16[16,128,128]{2,1,0:T(8,128)(2,1)}, u32[]{:S(2)}) copy-start(bf16[16,128,128]{2,1,0:T(8,128)(2,1)} %param.10) | copy-start | bytes 1572868
  1.4 1.3 %copy-start.7 = (s32[1024]{0:T(1024)S(1)}, s32[1024]{0:T(1024)}, u32[]{:S(2)}) copy-start(s32[1024]{0:T(1024)} %param.14) | copy-start | bytes 12292
  1.4 1.3 %copy-start.5 = (s32[1024]{0:T(1024)S(1)}, s32[1024]{0:T(1024)}, u32[]{:S(2)}) copy-start(s32[1024]{0:T(1024)} %param.17) | copy-start | bytes 12292
  1.4 1.4 %copy-start.2 = (bf16[256,512]{1,0:T(8,128)(2,1)S(1)}, bf16[256,512]{1,0:T(8,128)(2,1)}, u32[]{:S(2)}) copy-start(bf16[256,512]{1,0:T(8,128)(2,1)} %param.9) | copy-start | bytes 786436
  2.7 0.7 %copy-start.6 = (s32[1024]{0:T(1024)S(1)}, s32[1024]{0:T(1024)}, u32[]{:S(2)}) copy-start(s32[1024]{0:T(1024)} %param.16) | copy-start | bytes 12292
  2.7 0.7 %copy-start.8 = (s32[1024,1]{0,1:T(1,128)S(1)}, s32[1024,1]{0,1:T(1,128)}, u32[]{:S(2)}) copy-start(s32[1024,1]{0,1:T(1,128)} %param.13) | copy-start | bytes 12292
  9.1 10.1 %collective-permute-start = (bf16[520,128]{1,0:T(8,128)(2,1)S(1)}, bf16[520,128]{1,0:T(8,128)(2,1)S(1)}, u32[]{:S(2)}, u32[]{:S(2)}) collective-permute-start(bf16[520,128]{1,0:T(8,128)(2,1)S(1)} %pad_maximum_fusion.1), channel_id=1, source_target_pairs={{0,4},{4,8},{8,12},{12,0},{1,5},{5,9},{9,13},{13,1},{2,6},{6,10},{... | collective-permute-start | bytes 399368 | tf_op jit(solution)/shard_map/ppermute | solution.py:43
  13.0 10.5 %collective-permute-start.1 = (bf16[520,128]{1,0:T(8,128)(2,1)S(1)}, bf16[520,128]{1,0:T(8,128)(2,1)S(1)}, u32[]{:S(2)}, u32[]{:S(2)}) collective-permute-start(bf16[520,128]{1,0:T(8,128)(2,1)S(1)} %pad_maximum_fusion.2), channel_id=1, source_target_pairs={{0,8},{4,12},{8,0},{12,4},{1,9},{5,13},{9,1},{13,5},{2,10},{6,14},... | collective-permute-start | bytes 399368 | tf_op jit(solution)/shard_map/ppermute | solution.py:43
  16.6 7.6 %collective-permute-start.2 = (bf16[520,128]{1,0:T(8,128)(2,1)S(1)}, bf16[520,128]{1,0:T(8,128)(2,1)S(1)}, u32[]{:S(2)}, u32[]{:S(2)}) collective-permute-start(bf16[520,128]{1,0:T(8,128)(2,1)S(1)} %pad_maximum_fusion.3), channel_id=1, source_target_pairs={{0,12},{4,0},{8,4},{12,8},{1,13},{5,1},{9,5},{13,9},{2,14},{6,2},{... | collective-permute-start | bytes 399368 | tf_op jit(solution)/shard_map/ppermute | solution.py:43
  24.3 4.0 %copy-start.1 = (s32[1,1024,128]{2,1,0:T(8,128)S(1)}, s32[1,1024,128]{2,1,0:T(8,128)}, u32[]{:S(2)}) copy-start(s32[1,1024,128]{2,1,0:T(8,128)} %param.12) | copy-start | bytes 1572868
  24.3 4.0 %copy-start.3 = (bf16[1,1024,128]{2,1,0:T(8,128)(2,1)S(1)}, bf16[1,1024,128]{2,1,0:T(8,128)(2,1)}, u32[]{:S(2)}) copy-start(bf16[1,1024,128]{2,1,0:T(8,128)(2,1)} %param.11) | copy-start | bytes 786436
  26.3 2.0 %collective-permute-start.3 = (f32[1024,128]{1,0:T(8,128)S(1)}, f32[1024,128]{1,0:T(8,128)S(1)}, u32[]{:S(2)}, u32[]{:S(2)}) collective-permute-start(f32[1024,128]{1,0:T(8,128)S(1)} %fusion.37), channel_id=1, source_target_pairs={{0,1},{1,0},{2,3},{3,2},{4,5},{5,4},{6,7},{7,6},{8,9},{9,8},{10,11... | collective-permute-start | bytes 1572872 | tf_op jit(solution)/shard_map/ppermute | solution.py:34
  28.4 5.9 %copy-start.4 = (bf16[1024,128]{1,0:T(8,128)(2,1)}, bf16[1024,128]{1,0:T(8,128)(2,1)S(1)}, u32[]{:S(2)}) copy-start(bf16[1024,128]{1,0:T(8,128)(2,1)S(1)} %fusion.72) | copy-start | bytes 786436
  29.7 17.1 %collective-permute-start.4 = (bf16[512,128]{1,0:T(8,128)(2,1)S(1)}, bf16[512,128]{1,0:T(8,128)(2,1)S(1)}, u32[]{:S(2)}, u32[]{:S(2)}) collective-permute-start(bf16[512,128]{1,0:T(8,128)(2,1)S(1)} %get-tuple-element.4), channel_id=1, source_target_pairs={{0,12},{4,0},{8,4},{12,8},{1,13},{5,1},{9,5},{13,9},{2,14},{6,2},{... | collective-permute-start | bytes 393224 | tf_op jit(solution)/shard_map/ppermute | solution.py:43
  33.5 12.9 %collective-permute-start.6 = (bf16[512,128]{1,0:T(8,128)(2,1)S(1)}, bf16[512,128]{1,0:T(8,128)(2,1)S(1)}, u32[]{:S(2)}, u32[]{:S(2)}) collective-permute-start(bf16[512,128]{1,0:T(8,128)(2,1)S(1)} %get-tuple-element.5), channel_id=1, source_target_pairs={{0,4},{4,8},{8,12},{12,0},{1,5},{5,9},{9,13},{13,1},{2,6},{6,10},{... | collective-permute-start | bytes 393224 | tf_op jit(solution)/shard_map/ppermute | solution.py:43
  33.5 12.3 %collective-permute-start.5 = (bf16[512,128]{1,0:T(8,128)(2,1)S(1)}, bf16[512,128]{1,0:T(8,128)(2,1)S(1)}, u32[]{:S(2)}, u32[]{:S(2)}) collective-permute-start(bf16[512,128]{1,0:T(8,128)(2,1)S(1)} %get-tuple-element.6), channel_id=1, source_target_pairs={{0,8},{4,12},{8,0},{12,4},{1,9},{5,13},{9,1},{13,5},{2,10},{6,14},... | collective-permute-start | bytes 393224 | tf_op jit(solution)/shard_map/ppermute | solution.py:43
  51.2 5.1 %collective-permute-start.7 = (bf16[128,512]{1,0:T(8,128)(2,1)S(1)}, bf16[128,512]{1,0:T(8,128)(2,1)S(1)}, u32[]{:S(2)}, u32[]{:S(2)}) collective-permute-start(bf16[128,512]{1,0:T(8,128)(2,1)S(1)} %convert_element_type.129), channel_id=1, source_target_pairs={{0,2},{2,0},{1,3},{3,1},{4,6},{6,4},{5,7},{7,5},{8,10},{10,8},{9,1... | collective-permute-start | bytes 393224 | tf_op jit(solution)/shard_map/ppermute | solution.py:130

commit v12 on v4

--- a/solution.py
+++ b/solution.py
@@ -84,19 +84,33 @@
     slot_parts = jnp.stack([trace_slot // 256, trace_slot % 256], axis=1).astype(jnp.bfloat16)
     code_rows = -(-2 * capacity // pixel_count)
     places = [one_hot_rows(dest - step * capacity, capacity) for step in range(tile_count)]
+    early = tile_count // 2
+    early_parts = jnp.concatenate([slot_parts, kinds[:, None].astype(jnp.bfloat16)], axis=1)
+    early_rows = -(-3 * capacity // pixel_count)
     send = []
     for step in range(tile_count):
-        codes = select_dot_t(slot_parts, places[step]).astype(jnp.bfloat16).reshape(2 * capacity)
-        codes = jnp.pad(codes, (0, code_rows * pixel_count - 2 * capacity))
-        block = select_dot_t(places[step], traces).astype(jnp.bfloat16)
-        send.append(jnp.concatenate([block, codes.reshape(code_rows, pixel_count)], axis=0))
+        if step == early and step > 0:
+            values, parts, rows = spec_values, early_parts, early_rows
+        else:
+            values, parts, rows = traces, slot_parts, code_rows
+        width = parts.shape[1]
+        codes = select_dot_t(parts, places[step]).astype(jnp.bfloat16).reshape(width * capacity)
+        codes = jnp.pad(codes, (0, rows * pixel_count - width * capacity))
+        block = select_dot_t(places[step], values).astype(jnp.bfloat16)
+        send.append(jnp.concatenate([block, codes.reshape(rows, pixel_count)], axis=0))
     got = exchange(send, "tile", 1)
-    got_traces = [block[:capacity] for block in got]
+    got_traces = []
     got_slots = []
-    for block in got:
-        codes = block[capacity:].reshape(code_rows * pixel_count)[: 2 * capacity]
-        codes = codes.astype(jnp.int32).reshape(2, capacity)
+    for step, block in enumerate(got):
+        width = 3 if step == early and step > 0 else 2
+        codes = block[capacity:].reshape(-1)[: width * capacity]
+        codes = codes.astype(jnp.int32).reshape(width, capacity)
         got_slots.append(codes[0] * 256 + codes[1])
+        if width == 3:
+            spread = spread_by_kind(block[:capacity], codes[2], table_count)
+            got_traces.append(select_dot(spread, psf_flat).astype(jnp.bfloat16))
+        else:
+            got_traces.append(block[:capacity])
 
     at_slot = [one_hot_rows(slots, slot_count) for slots in got_slots]
     partial_value = sum(select_dot_t(a, b) for a, b in zip(at_slot, got_traces))

time: 56.7 us -> 61 us (1.076)
  other arithmetic: 1.76 us -> 7.29 us
  waiting for transfers between devices: 18.3 us -> 14.1 us
  matrix products: 22.4 us -> 26 us
  starting transfers between devices: 12.3 us -> 10.7 us
  local copies, waits for them, and re-layouts: 0.67 us -> 1.35 us
    ppermute x6, waiting for transfers between devices: 13.9 us -> 9.68 us  [exchange(): moved.append(lax.ppermute(blocks[step], axis, pairs))]
    dot_general x13, matrix products: 10.4 us -> 14 us  [select_dot_t(): lax.dot_general(selector, values, (((0,), (0,)), ((), ())), preferred_ele...]
    select_n x0 -> x1, other arithmetic: none -> 2.69 us  [spread_by_kind(): spread = jnp.where(chosen, values[:, None, :], jnp.zeros((), values.dtype))]
    ppermute x6, starting transfers between devices: 10.7 us -> 9.03 us  [exchange(): moved.append(lax.ppermute(blocks[step], axis, pairs))]
    reshape x1, local copies, waits for them, and re-layouts: 0.16 us -> 1.11 us  [per_device(): spectra.reshape(row_count, bin_count)]
    convert_element_type x3 -> x4, other arithmetic: 0.02 us -> 0.71 us  [the longest x1 0.69 us: per_device(): kinds[:, None].astype(jnp.bfloat16)]
    another operation x1, other arithmetic: 0.01 us -> 0.7 us
    sub x2, other arithmetic: 0.03 us -> 0.72 us  [per_device(): dest - step * capacity]
  transfers between devices with their start and end apart: 8 -> 8, of which waited for: 6 -> 4; matrix products, arithmetic and copies ran while one was open for 14% -> 21% of each run, Pallas kernels for 0% -> 0%
where the time goes in v12:
time: 61 us; the launch traced here: 60.4 us
  matrix products  26 us (43%)
  waiting for transfers between devices  14.1 us (23%)
  starting transfers between devices  10.7 us (18%)
  other arithmetic  7.29 us (12%)
  local copies, waits for them, and re-layouts  1.35 us (2%)
  between operations  0.99 us (2%)
    dot_general x13, matrix products, select_dot_t(): lax.dot_general(selector, values, (((0,), (0,)), ((), ())), preferred_ele...  14 us
    dot_general x11, matrix products, select_dot(): jnp.dot(selector, values, preferred_element_type=jnp.float32, precision=p...  12 us
    ppermute x6, waiting for transfers between devices, exchange(): moved.append(lax.ppermute(blocks[step], axis, pairs))  9.68 us
    ppermute x6, starting transfers between devices, exchange(): moved.append(lax.ppermute(blocks[step], axis, pairs))  9.03 us
    select_n x1, other arithmetic, spread_by_kind(): spread = jnp.where(chosen, values[:, None, :], jnp.zeros((), values.dtype))  2.69 us
    ppermute x1, waiting for transfers between devices, per_device(): sent = lax.ppermute(theirs.astype(jnp.bfloat16), 'dither', [(0, 1), (1, 0)])  2.54 us
    ppermute x1, waiting for transfers between devices, swap_add(): return value + lax.ppermute(value, axis, [(0, 1), (1, 0)])  1.88 us
    ppermute x1, starting transfers between devices, per_device(): sent = lax.ppermute(theirs.astype(jnp.bfloat16), 'dither', [(0, 1), (1, 0)])  1.56 us
  transfers between devices with their start and end apart: 8, of which 4 were waited for; matrix products, arithmetic and copies ran while one was open for 21% of the time, Pallas kernels for 0%

profile of v12, /device:TPU:0, one launch (start us, length us, event | category | flops | bytes accessed | tf_op | source)
XLA Modules:
  0.0 60.4 jit_solution(17659328499002473585)
XLA Ops:
  0.7 1.2 %fusion.76 = f32[1024]{0:T(1024)S(1)} fusion(s32[1024]{0:T(1024)} %bitcast.73), kind=kOutput, calls=%fused_computation.75 | convolution fusion | flops 9464832 | bytes 8192 | tf_op jit(solution)/shard_map/dot_general | solution.py:12
  1.9 0.7 %broadcast_add_fusion.2 = (s32[1024,1]{0,1:T(1,128)S(1)}, s32[1024,1]{0,1:T(1,128)S(1)}) fusion(s32[1024,1]{0,1:T(1,128)S(1)} %bitcast.66, s32[1024,1]{0,1:T(1,128)} %param.13, s32[]{:T(128)S(6)} %axis_index.28), kind=kLoop, calls=%fused_computation.154 | loop fusion | flops 15360 | bytes 16388 | tf_op jit(solution)/shard_map/sub | solution.py:86
  2.6 0.7 %broadcast_multiply_fusion = s32[1024,1]{0,1:T(1,128)S(1)} fusion(s32[1024,1]{0,1:T(1,128)} %param.15), kind=kLoop, calls=%fused_computation.156 | loop fusion | flops 1024 | bytes 8192 | tf_op jit(solution)/shard_map/mul | solution.py:71
  3.3 1.1 %reshape.176 = bf16[1024,128]{1,0:T(8,128)(2,1)S(1)} reshape(bf16[256,512]{1,0:T(8,128)(2,1)} %param.9) | data formatting | bytes 524288 | tf_op jit(solution)/shard_map/reshape | solution.py:81
  4.5 0.7 %fusion.118 = (bf16[1024]{0:T(1024)(128)(2,1)S(1)}, bf16[1024]{0:T(1024)(128)(2,1)S(1)}) fusion(s32[1024]{0:T(1024)} %param.14), kind=kLoop, calls=%fused_computation.131 | loop fusion | flops 21504 | bytes 8192 | tf_op jit(solution)/shard_map/convert.4
  5.2 0.7 %convert_element_type.147 = bf16[1024]{0:T(1024)(128)(2,1)S(1)} convert(s32[1024]{0:T(1024)} %param.17) | non-fusion elementwise | flops 1024 | bytes 6144 | tf_op jit(solution)/shard_map/convert_element_type | solution.py:88
  5.9 0.7 %broadcast_subtract_fusion = (s32[1024]{0:T(1024)S(1)}, s32[1024]{0:T(1024)S(1)}) fusion(s32[]{:T(128)S(6)} %sub.59, s32[1024]{0:T(1024)S(1)} %bitcast.65, s32[1024]{0:T(1024)} %param.16), kind=kLoop, calls=%fused_computation.149 | loop fusion | flops 2048 | bytes 16388 | tf_op jit(solution)/shard_map/sub | solution.py:133
  6.6 0.8 %fusion.56 = bf16[1024,128]{1,0:T(8,128)(2,1)S(1)} fusion(bf16[1024,128]{1,0:T(8,128)(2,1)S(1)} %reshape.176, s32[1024]{0:T(1024)S(1)} %get-tuple-element.3), kind=kOutput, calls=%fused_computation.61 | convolution fusion | flops 269615104 | bytes 528384 | tf_op jit(solution)/shard_map/dot_general | solution.py:12
  7.4 0.9 %fusion.65 = bf16[512,128]{1,0:T(8,128)(2,1)S(1)} fusion(bf16[1024,128]{1,0:T(8,128)(2,1)S(1)} %fusion.56, s32[1024]{0:T(1024)S(1)} %bitcast.70), kind=kOutput, calls=%fused_computation.68 | convolution fusion | flops 134807552 | bytes 397312 | tf_op jit(solution)/shard_map/dot_general | solution.py:16
  8.8 4.1 %collective-permute-start.1 = (bf16[524,128]{1,0:T(8,128)(2,1)S(1)}, bf16[524,128]{1,0:T(8,128)(2,1)S(1)}, u32[]{:S(2)}, u32[]{:S(2)}) collective-permute-start(bf16[524,128]{1,0:T(8,128)(2,1)S(1)} %pad_maximum_fusion), channel_id=1, source_target_pairs={{0,8},{4,12},{8,0},{12,4},{1,9},{5,13},{9,1},{13,5},{2,10},{6,14},... | collective-permute-start | bytes 402440 | tf_op jit(solution)/shard_map/ppermute | solution.py:43
  13.0 3.0 %fusion.53 = bf16[1024,128]{1,0:T(8,128)(2,1)S(1)} fusion(bf16[16,128,128]{2,1,0:T(8,128)(2,1)S(1)} %copy-done, pred[1024,16]{0,1:T(8,128)(4,1)S(1)} %iota_compare_fusion.91, bf16[1024,128]{1,0:T(8,128)(2,1)S(1)} %fusion.56), kind=kOutput, calls=%fused_computation.60 | convolution fusion | flops 539099136 | bytes 1064960 | tf_op jit(solution)/shard_map/dot_general | solution.py:12
  16.0 0.9 %fusion.67 = bf16[512,128]{1,0:T(8,128)(2,1)S(1)} fusion(bf16[1024,128]{1,0:T(8,128)(2,1)S(1)} %fusion.53, s32[1024]{0:T(1024)S(1)} %bitcast.67), kind=kOutput, calls=%fused_computation.70 | convolution fusion | flops 134807552 | bytes 397312 | tf_op jit(solution)/shard_map/dot_general | solution.py:16
  17.4 1.4 %collective-permute-start.2 = (bf16[520,128]{1,0:T(8,128)(2,1)S(1)}, bf16[520,128]{1,0:T(8,128)(2,1)S(1)}, u32[]{:S(2)}, u32[]{:S(2)}) collective-permute-start(bf16[520,128]{1,0:T(8,128)(2,1)S(1)} %pad_maximum_fusion.2), channel_id=1, source_target_pairs={{0,12},{4,0},{8,4},{12,8},{1,13},{5,1},{9,5},{13,9},{2,14},{6,2},{... | collective-permute-start | bytes 399368 | tf_op jit(solution)/shard_map/ppermute | solution.py:43
  18.8 0.9 %fusion.63 = bf16[512,128]{1,0:T(8,128)(2,1)S(1)} fusion(bf16[1024,128]{1,0:T(8,128)(2,1)S(1)} %fusion.53, s32[1024]{0:T(1024)S(1)} %bitcast.59), kind=kOutput, calls=%fused_computation.66 | convolution fusion | flops 134807552 | bytes 397312 | tf_op jit(solution)/shard_map/dot_general | solution.py:16
  20.2 0.9 %collective-permute-start = (bf16[520,128]{1,0:T(8,128)(2,1)S(1)}, bf16[520,128]{1,0:T(8,128)(2,1)S(1)}, u32[]{:S(2)}, u32[]{:S(2)}) collective-permute-start(bf16[520,128]{1,0:T(8,128)(2,1)S(1)} %pad_maximum_fusion.1), channel_id=1, source_target_pairs={{0,4},{4,8},{8,12},{12,0},{1,5},{5,9},{9,13},{13,1},{2,6},{6,10},{... | collective-permute-start | bytes 399368 | tf_op jit(solution)/shard_map/ppermute | solution.py:43
  21.6 1.5 %fusion.31 = f32[1024,128]{1,0:T(8,128)S(1)} fusion(bf16[1024,128]{1,0:T(8,128)(2,1)S(1)} %fusion.53, s32[512]{0:T(512)S(1)} %bitcast.74, s32[1024]{0:T(1024)S(1)} %bitcast.63), kind=kOutput, calls=%fused_computation.41 | convolution fusion | flops 269549568 | bytes 792576 | tf_op jit(solution)/shard_map/dot_general | solution.py:16
  23.2 1.6 %fusion.12 = f32[1024,128]{1,0:T(8,128)} fusion(s32[512]{0:T(512)S(1)} %add_bitcast_fusion, bf16[520,128]{1,0:T(8,128)(2,1)S(1)} %collective-permute-done.2), kind=kOutput, calls=%fused_computation.16 | convolution fusion | flops 134742016 | bytes 657408 | tf_op jit(solution)/shard_map/dot_general | solution.py:16
  24.8 2.4 %collective-permute-done = bf16[520,128]{1,0:T(8,128)(2,1)S(1)} collective-permute-done((bf16[520,128]{1,0:T(8,128)(2,1)S(1)}, bf16[520,128]{1,0:T(8,128)(2,1)S(1)}, u32[]{:S(2)}, u32[]{:S(2)}) %collective-permute-start) | collective-permute-done | bytes 133152 | tf_op jit(solution)/shard_map/ppermute | solution.py:43
  27.5 2.7 %broadcast_select_fusion = bf16[512,16,128]{2,1,0:T(8,128)(2,1)S(1)} fusion(pred[512,16]{1,0:T(8,128)(4,1)S(1)} %iota_compare_fusion.90, bf16[512,128]{1,0:T(8,128)(2,1)S(1)} %slice.89), kind=kLoop, calls=%fused_computation.49 | loop fusion | flops 1048576 | bytes 2236416 | tf_op jit(solution)/shard_map/jit(_where)/select_n | solution.py:27
  30.2 2.3 %fusion.17 = f32[1024,128]{1,0:T(8,128)} fusion(bf16[16,128,128]{2,1,0:T(8,128)(2,1)S(1)} %copy-done, bf16[512,16,128]{2,1,0:T(8,128)(2,1)S(1)} %broadcast_select_fusion, s32[512]{0:T(512)S(1)} %get-tuple-element.6), kind=kOutput, calls=%fused_computation.23 | convolution fusion | flops 403243008 | bytes 3147776 | tf_op jit(solution)/shard_map/dot_general | solution.py:16
  32.5 2.1 %fusion.46 = f32[1024,128]{1,0:T(8,128)S(1)} fusion(f32[1024,128]{1,0:T(8,128)} %fusion.12, f32[1024,128]{1,0:T(8,128)} %fusion.17, f32[1024,128]{1,0:T(8,128)S(1)} %fusion.31, s32[512]{0:T(512)S(1)} %add_bitcast_fusion.1, bf16[520,128]{1,0:T(8,128)(2,1)S(1)} %collective-permute-done), kind=kOutput, calls=%fused_computation.55 | convolution fusion | flops 135135232 | bytes 2230272 | tf_op jit(solution)/shard_map/dot_general | solution.py:16
  34.7 1.9 %collective-permute-done.3 = f32[1024,128]{1,0:T(8,128)S(1)} collective-permute-done((f32[1024,128]{1,0:T(8,128)S(1)}, f32[1024,128]{1,0:T(8,128)S(1)}, u32[]{:S(2)}, u32[]{:S(2)}) %collective-permute-start.3) | collective-permute-done | bytes 524320 | tf_op jit(solution)/shard_map/ppermute | solution.py:34
  38.9 1.3 %collective-permute-start.4 = (bf16[512,128]{1,0:T(8,128)(2,1)S(1)}, bf16[512,128]{1,0:T(8,128)(2,1)S(1)}, u32[]{:S(2)}, u32[]{:S(2)}) collective-permute-start(bf16[512,128]{1,0:T(8,128)(2,1)S(1)} %fusion.64), channel_id=1, source_target_pairs={{0,12},{4,0},{8,4},{12,8},{1,13},{5,1},{9,5},{13,9},{2,14},{6,2},{... | collective-permute-start | bytes 393224 | tf_op jit(solution)/shard_map/ppermute | solution.py:43
  40.2 0.7 %collective-permute-start.6 = (bf16[512,128]{1,0:T(8,128)(2,1)S(1)}, bf16[512,128]{1,0:T(8,128)(2,1)S(1)}, u32[]{:S(2)}, u32[]{:S(2)}) collective-permute-start(bf16[512,128]{1,0:T(8,128)(2,1)S(1)} %fusion.68), channel_id=1, source_target_pairs={{0,4},{4,8},{8,12},{12,0},{1,5},{5,9},{9,13},{13,1},{2,6},{6,10},{... | collective-permute-start | bytes 393224 | tf_op jit(solution)/shard_map/ppermute | solution.py:43
  40.9 1.3 %fusion.32 = f32[1024,128]{1,0:T(8,128)S(1)} fusion(bf16[1024,128]{1,0:T(8,128)(2,1)S(1)} %fusion.107, s32[512]{0:T(512)S(1)} %bitcast.75, s32[1024]{0:T(1024)S(1)} %bitcast.64), kind=kOutput, calls=%fused_computation.43 | convolution fusion | flops 269549568 | bytes 792576 | tf_op jit(solution)/shard_map/dot_general | solution.py:12
  42.2 7.3 %collective-permute-done.5 = bf16[512,128]{1,0:T(8,128)(2,1)S(1)} collective-permute-done((bf16[512,128]{1,0:T(8,128)(2,1)S(1)}, bf16[512,128]{1,0:T(8,128)(2,1)S(1)}, u32[]{:S(2)}, u32[]{:S(2)}) %collective-permute-start.5) | collective-permute-done | bytes 131104 | tf_op jit(solution)/shard_map/ppermute | solution.py:43
  51.0 2.6 %fusion.50 = bf16[1024,128]{1,0:T(8,128)(2,1)S(1)} fusion(pred[1024,16]{0,1:T(8,128)(4,1)S(1)} %iota_compare_fusion.91, bf16[1024,128]{1,0:T(8,128)(2,1)S(1)} %fusion.49, bf16[16,128,128]{2,1,0:T(8,128)(2,1)S(1)} %copy-done), kind=kOutput, calls=%fused_computation.59 | convolution fusion | flops 539099136 | bytes 1064960 | tf_op jit(solution)/shard_map/dot_general | solution.py:12
  53.6 0.9 %fusion.60 = bf16[512,128]{1,0:T(8,128)(2,1)S(1)} fusion(bf16[1024,128]{1,0:T(8,128)(2,1)S(1)} %fusion.50, s32[1024]{0:T(1024)S(1)} %get-tuple-element.2), kind=kOutput, calls=%fused_computation.63 | convolution fusion | flops 134807552 | bytes 397312 | tf_op jit(solution)/shard_map/dot_general | solution.py:16
  54.6 1.6 %collective-permute-start.7 = (bf16[128,512]{1,0:T(8,128)(2,1)S(1)}, bf16[128,512]{1,0:T(8,128)(2,1)S(1)}, u32[]{:S(2)}, u32[]{:S(2)}) collective-permute-start(bf16[128,512]{1,0:T(8,128)(2,1)S(1)} %convert_element_type.165), channel_id=1, source_target_pairs={{0,2},{2,0},{1,3},{3,1},{4,6},{6,4},{5,7},{7,5},{8,10},{10,8},{9,1... | collective-permute-start | bytes 393224 | tf_op jit(solution)/shard_map/ppermute | solution.py:136
  56.2 0.9 %fusion.35 = f32[512,128]{1,0:T(8,128)S(1)} fusion(bf16[1024,128]{1,0:T(8,128)(2,1)S(1)} %fusion.50, s32[1024]{0:T(1024)S(1)} %broadcast_subtract_fusion.1), kind=kOutput, calls=%fused_computation.47 | convolution fusion | flops 134742016 | bytes 528384 | tf_op jit(solution)/shard_map/dot_general | solution.py:16
  57.1 2.5 %collective-permute-done.7 = bf16[128,512]{1,0:T(8,128)(2,1)S(1)} collective-permute-done((bf16[128,512]{1,0:T(8,128)(2,1)S(1)}, bf16[128,512]{1,0:T(8,128)(2,1)S(1)}, u32[]{:S(2)}, u32[]{:S(2)}) %collective-permute-start.7) | collective-permute-done | bytes 131104 | tf_op jit(solution)/shard_map/ppermute | solution.py:136
  59.6 0.7 %convert_add_fusion = f32[128,512]{1,0:T(8,128)} fusion(f32[128,512]{1,0:T(8,128)S(1)} %reshape.180, bf16[128,512]{1,0:T(8,128)(2,1)S(1)} %collective-permute-done.7), kind=kLoop, calls=%fused_computation.107 | loop fusion | flops 131072 | bytes 655360 | tf_op jit(solution)/shard_map/add | solution.py:138
  (52 shorter events, 6.3 us)
Async XLA Ops:
  0.6 12.4 %copy-start = (bf16[16,128,128]{2,1,0:T(8,128)(2,1)S(1)}, bf16[16,128,128]{2,1,0:T(8,128)(2,1)}, u32[]{:S(2)}) copy-start(bf16[16,128,128]{2,1,0:T(8,128)(2,1)} %param.10) | copy-start | bytes 1572868
  4.5 8.5 %copy-start.4 = (s32[1024]{0:T(1024)S(1)}, s32[1024]{0:T(1024)}, u32[]{:S(2)}) copy-start(s32[1024]{0:T(1024)} %param.17) | copy-start | bytes 12292
  8.8 18.4 %collective-permute-start.1 = (bf16[524,128]{1,0:T(8,128)(2,1)S(1)}, bf16[524,128]{1,0:T(8,128)(2,1)S(1)}, u32[]{:S(2)}, u32[]{:S(2)}) collective-permute-start(bf16[524,128]{1,0:T(8,128)(2,1)S(1)} %pad_maximum_fusion), channel_id=1, source_target_pairs={{0,8},{4,12},{8,0},{12,4},{1,9},{5,13},{9,1},{13,5},{2,10},{6,14},... | collective-permute-start | bytes 402440 | tf_op jit(solution)/shard_map/ppermute | solution.py:43
  17.4 5.8 %collective-permute-start.2 = (bf16[520,128]{1,0:T(8,128)(2,1)S(1)}, bf16[520,128]{1,0:T(8,128)(2,1)S(1)}, u32[]{:S(2)}, u32[]{:S(2)}) collective-permute-start(bf16[520,128]{1,0:T(8,128)(2,1)S(1)} %pad_maximum_fusion.2), channel_id=1, source_target_pairs={{0,12},{4,0},{8,4},{12,8},{1,13},{5,1},{9,5},{13,9},{2,14},{6,2},{... | collective-permute-start | bytes 399368 | tf_op jit(solution)/shard_map/ppermute | solution.py:43
  20.2 7.0 %collective-permute-start = (bf16[520,128]{1,0:T(8,128)(2,1)S(1)}, bf16[520,128]{1,0:T(8,128)(2,1)S(1)}, u32[]{:S(2)}, u32[]{:S(2)}) collective-permute-start(bf16[520,128]{1,0:T(8,128)(2,1)S(1)} %pad_maximum_fusion.1), channel_id=1, source_target_pairs={{0,4},{4,8},{8,12},{12,0},{1,5},{5,9},{9,13},{13,1},{2,6},{6,10},{... | collective-permute-start | bytes 399368 | tf_op jit(solution)/shard_map/ppermute | solution.py:43
  32.5 4.1 %copy-start.1 = (s32[1,1024,128]{2,1,0:T(8,128)S(1)}, s32[1,1024,128]{2,1,0:T(8,128)}, u32[]{:S(2)}) copy-start(s32[1,1024,128]{2,1,0:T(8,128)} %param.12) | copy-start | bytes 1572868
  32.5 4.1 %copy-start.2 = (bf16[1,1024,128]{2,1,0:T(8,128)(2,1)S(1)}, bf16[1,1024,128]{2,1,0:T(8,128)(2,1)}, u32[]{:S(2)}) copy-start(bf16[1,1024,128]{2,1,0:T(8,128)(2,1)} %param.11) | copy-start | bytes 786436
  34.6 2.0 %collective-permute-start.3 = (f32[1024,128]{1,0:T(8,128)S(1)}, f32[1024,128]{1,0:T(8,128)S(1)}, u32[]{:S(2)}, u32[]{:S(2)}) collective-permute-start(f32[1024,128]{1,0:T(8,128)S(1)} %fusion.46), channel_id=1, source_target_pairs={{0,1},{1,0},{2,3},{3,2},{4,5},{5,4},{6,7},{7,6},{8,9},{9,8},{10,11... | collective-permute-start | bytes 1572872 | tf_op jit(solution)/shard_map/ppermute | solution.py:34
  36.7 5.5 %copy-start.3 = (bf16[1024,128]{1,0:T(8,128)(2,1)}, bf16[1024,128]{1,0:T(8,128)(2,1)S(1)}, u32[]{:S(2)}) copy-start(bf16[1024,128]{1,0:T(8,128)(2,1)S(1)} %fusion.107) | copy-start | bytes 786436
  38.3 11.2 %collective-permute-start.5 = (bf16[512,128]{1,0:T(8,128)(2,1)S(1)}, bf16[512,128]{1,0:T(8,128)(2,1)S(1)}, u32[]{:S(2)}, u32[]{:S(2)}) collective-permute-start(bf16[512,128]{1,0:T(8,128)(2,1)S(1)} %fusion.66), channel_id=1, source_target_pairs={{0,8},{4,12},{8,0},{12,4},{1,9},{5,13},{9,1},{13,5},{2,10},{6,14},... | collective-permute-start | bytes 393224 | tf_op jit(solution)/shard_map/ppermute | solution.py:43
  38.9 11.6 %collective-permute-start.4 = (bf16[512,128]{1,0:T(8,128)(2,1)S(1)}, bf16[512,128]{1,0:T(8,128)(2,1)S(1)}, u32[]{:S(2)}, u32[]{:S(2)}) collective-permute-start(bf16[512,128]{1,0:T(8,128)(2,1)S(1)} %fusion.64), channel_id=1, source_target_pairs={{0,12},{4,0},{8,4},{12,8},{1,13},{5,1},{9,5},{13,9},{2,14},{6,2},{... | collective-permute-start | bytes 393224 | tf_op jit(solution)/shard_map/ppermute | solution.py:43
  40.2 9.8 %collective-permute-start.6 = (bf16[512,128]{1,0:T(8,128)(2,1)S(1)}, bf16[512,128]{1,0:T(8,128)(2,1)S(1)}, u32[]{:S(2)}, u32[]{:S(2)}) collective-permute-start(bf16[512,128]{1,0:T(8,128)(2,1)S(1)} %fusion.68), channel_id=1, source_target_pairs={{0,4},{4,8},{8,12},{12,0},{1,5},{5,9},{9,13},{13,1},{2,6},{6,10},{... | collective-permute-start | bytes 393224 | tf_op jit(solution)/shard_map/ppermute | solution.py:43
  54.6 5.0 %collective-permute-start.7 = (bf16[128,512]{1,0:T(8,128)(2,1)S(1)}, bf16[128,512]{1,0:T(8,128)(2,1)S(1)}, u32[]{:S(2)}, u32[]{:S(2)}) collective-permute-start(bf16[128,512]{1,0:T(8,128)(2,1)S(1)} %convert_element_type.165), channel_id=1, source_target_pairs={{0,2},{2,0},{1,3},{3,1},{4,6},{6,4},{5,7},{7,5},{8,10},{10,8},{9,1... | collective-permute-start | bytes 393224 | tf_op jit(solution)/shard_map/ppermute | solution.py:136

commit v13 on v4

--- a/solution.py
+++ b/solution.py
@@ -84,9 +84,11 @@
     slot_parts = jnp.stack([trace_slot // 256, trace_slot % 256], axis=1).astype(jnp.bfloat16)
     code_rows = -(-2 * capacity // pixel_count)
     places = [one_hot_rows(dest - step * capacity, capacity) for step in range(tile_count)]
+    all_codes = select_dot_t(slot_parts, one_hot_rows(dest, send_count)).astype(jnp.bfloat16)
+    all_codes = all_codes.reshape(2, tile_count, capacity)
     send = []
     for step in range(tile_count):
-        codes = select_dot_t(slot_parts, places[step]).astype(jnp.bfloat16).reshape(2 * capacity)
+        codes = all_codes[:, step].reshape(2 * capacity)
         codes = jnp.pad(codes, (0, code_rows * pixel_count - 2 * capacity))
         block = select_dot_t(places[step], traces).astype(jnp.bfloat16)
         send.append(jnp.concatenate([block, codes.reshape(code_rows, pixel_count)], axis=0))

time: 56.7 us -> 58.1 us (1.025)
  starting transfers between devices: 12.3 us -> 13.3 us
  waiting for transfers between devices: 18.3 us -> 18.9 us
    ppermute x6, starting transfers between devices: 10.7 us -> 11.7 us  [exchange(): moved.append(lax.ppermute(blocks[step], axis, pairs))]
    dot_general x13 -> x10, matrix products: 10.4 us -> 9.98 us  [select_dot_t(): lax.dot_general(selector, values, (((0,), (0,)), ((), ())), preferred_ele...]
  transfers between devices with their start and end apart: 8 -> 8, of which waited for: 6 -> 6; matrix products, arithmetic and copies ran while one was open for 14% -> 11% of each run, Pallas kernels for 0% -> 0%
where the time goes in v13:
time: 58.1 us; the launch traced here: 57.9 us
  matrix products  22 us (38%)
  waiting for transfers between devices  18.9 us (33%)
  starting transfers between devices  13.3 us (23%)
  other arithmetic  1.75 us (3%)
  between operations  1.03 us (2%)
  local copies, waits for them, and re-layouts  0.86 us (1%)
    ppermute x6, waiting for transfers between devices, exchange(): moved.append(lax.ppermute(blocks[step], axis, pairs))  14.4 us
    dot_general x11, matrix products, select_dot(): jnp.dot(selector, values, preferred_element_type=jnp.float32, precision=p...  12 us
    ppermute x6, starting transfers between devices, exchange(): moved.append(lax.ppermute(blocks[step], axis, pairs))  11.7 us
    dot_general x10, matrix products, select_dot_t(): lax.dot_general(selector, values, (((0,), (0,)), ((), ())), preferred_ele...  9.98 us
    ppermute x1, waiting for transfers between devices, per_device(): sent = lax.ppermute(theirs.astype(jnp.bfloat16), 'dither', [(0, 1), (1, 0)])  2.56 us
    ppermute x1, waiting for transfers between devices, swap_add(): return value + lax.ppermute(value, axis, [(0, 1), (1, 0)])  1.89 us
    ppermute x1, starting transfers between devices, per_device(): sent = lax.ppermute(theirs.astype(jnp.bfloat16), 'dither', [(0, 1), (1, 0)])  1.55 us
  transfers between devices with their start and end apart: 8, of which 6 were waited for; matrix products, arithmetic and copies ran while one was open for 11% of the time, Pallas kernels for 0%

profile of v13, /device:TPU:0, one launch (start us, length us, event | category | flops | bytes accessed | tf_op | source)
XLA Modules:
  0.0 57.9 jit_solution(3044632335312642408)
XLA Ops:
  0.7 0.7 %broadcast_multiply_fusion = s32[1024,1]{0,1:T(1,128)S(1)} fusion(s32[1024,1]{0,1:T(1,128)} %param.15), kind=kLoop, calls=%fused_computation.137 | loop fusion | flops 1024 | bytes 8192 | tf_op jit(solution)/shard_map/mul | solution.py:71
  1.4 1.3 %fusion.65 = f32[1024]{0:T(1024)S(1)} fusion(s32[1024]{0:T(1024)} %bitcast.68), kind=kOutput, calls=%fused_computation.70 | convolution fusion | flops 9464832 | bytes 8192 | tf_op jit(solution)/shard_map/dot_general | solution.py:12
  2.8 1.6 %fusion.10 = bf16[2,2048]{1,0:T(2,128)(2,1)S(1)} fusion(s32[1024]{0:T(1024)S(1)} %bitcast.59, bf16[1024,1]{0,1:T(2,128)(2,1)S(1)} %stack.13, bf16[1024,1]{0,1:T(2,128)(2,1)S(1)} %stack.12), kind=kOutput, calls=%fused_computation.13 | convolution fusion | flops 10498048 | bytes 16384 | tf_op jit(solution)/shard_map/dot_general | solution.py:16
  5.1 0.8 %fusion.53 = bf16[1024,128]{1,0:T(8,128)(2,1)S(1)} fusion(bf16[1024,128]{1,0:T(8,128)(2,1)S(1)} %reshape.145, s32[1024]{0:T(1024)S(1)} %get-tuple-element.3), kind=kOutput, calls=%fused_computation.58 | convolution fusion | flops 269615104 | bytes 528384 | tf_op jit(solution)/shard_map/dot_general | solution.py:12
  5.9 3.0 %fusion.50 = bf16[1024,128]{1,0:T(8,128)(2,1)S(1)} fusion(bf16[16,128,128]{2,1,0:T(8,128)(2,1)S(1)} %copy-done, pred[1024,16]{0,1:T(8,128)(4,1)S(1)} %iota_compare_fusion.80, bf16[1024,128]{1,0:T(8,128)(2,1)S(1)} %fusion.53), kind=kOutput, calls=%fused_computation.57 | convolution fusion | flops 539099136 | bytes 1064960 | tf_op jit(solution)/shard_map/dot_general | solution.py:12
  8.9 0.9 %fusion.57 = bf16[512,128]{1,0:T(8,128)(2,1)S(1)} fusion(bf16[1024,128]{1,0:T(8,128)(2,1)S(1)} %fusion.50, s32[1024]{0:T(1024)S(1)} %bitcast.57), kind=kOutput, calls=%fused_computation.62 | convolution fusion | flops 134807552 | bytes 397312 | tf_op jit(solution)/shard_map/dot_general | solution.py:16
  9.9 3.1 %collective-permute-start = (bf16[520,128]{1,0:T(8,128)(2,1)S(1)}, bf16[520,128]{1,0:T(8,128)(2,1)S(1)}, u32[]{:S(2)}, u32[]{:S(2)}) collective-permute-start(bf16[520,128]{1,0:T(8,128)(2,1)S(1)} %pad_maximum_fusion), channel_id=1, source_target_pairs={{0,4},{4,8},{8,12},{12,0},{1,5},{5,9},{9,13},{13,1},{2,6},{6,10},{... | collective-permute-start | bytes 399368 | tf_op jit(solution)/shard_map/ppermute | solution.py:43
  12.9 0.9 %fusion.59 = bf16[512,128]{1,0:T(8,128)(2,1)S(1)} fusion(bf16[1024,128]{1,0:T(8,128)(2,1)S(1)} %fusion.50, s32[1024]{0:T(1024)S(1)} %bitcast.64), kind=kOutput, calls=%fused_computation.64 | convolution fusion | flops 134807552 | bytes 397312 | tf_op jit(solution)/shard_map/dot_general | solution.py:16
  13.9 2.7 %collective-permute-start.1 = (bf16[520,128]{1,0:T(8,128)(2,1)S(1)}, bf16[520,128]{1,0:T(8,128)(2,1)S(1)}, u32[]{:S(2)}, u32[]{:S(2)}) collective-permute-start(bf16[520,128]{1,0:T(8,128)(2,1)S(1)} %pad_maximum_fusion.1), channel_id=1, source_target_pairs={{0,8},{4,12},{8,0},{12,4},{1,9},{5,13},{9,1},{13,5},{2,10},{6,14},... | collective-permute-start | bytes 399368 | tf_op jit(solution)/shard_map/ppermute | solution.py:43
  16.5 0.9 %fusion.61 = bf16[512,128]{1,0:T(8,128)(2,1)S(1)} fusion(bf16[1024,128]{1,0:T(8,128)(2,1)S(1)} %fusion.50, s32[1024]{0:T(1024)S(1)} %bitcast.66), kind=kOutput, calls=%fused_computation.66 | convolution fusion | flops 134807552 | bytes 397312 | tf_op jit(solution)/shard_map/dot_general | solution.py:16
  17.4 1.4 %collective-permute-start.2 = (bf16[520,128]{1,0:T(8,128)(2,1)S(1)}, bf16[520,128]{1,0:T(8,128)(2,1)S(1)}, u32[]{:S(2)}, u32[]{:S(2)}) collective-permute-start(bf16[520,128]{1,0:T(8,128)(2,1)S(1)} %pad_maximum_fusion.2), channel_id=1, source_target_pairs={{0,12},{4,0},{8,4},{12,8},{1,13},{5,1},{9,5},{13,9},{2,14},{6,2},{... | collective-permute-start | bytes 399368 | tf_op jit(solution)/shard_map/ppermute | solution.py:43
  18.9 1.5 %fusion.29 = f32[1024,128]{1,0:T(8,128)S(1)} fusion(bf16[1024,128]{1,0:T(8,128)(2,1)S(1)} %fusion.50, s32[512]{0:T(512)S(1)} %bitcast.69, s32[1024]{0:T(1024)S(1)} %bitcast.60), kind=kOutput, calls=%fused_computation.40 | convolution fusion | flops 269549568 | bytes 792576 | tf_op jit(solution)/shard_map/dot_general | solution.py:16
  20.5 3.9 %collective-permute-done.1 = bf16[520,128]{1,0:T(8,128)(2,1)S(1)} collective-permute-done((bf16[520,128]{1,0:T(8,128)(2,1)S(1)}, bf16[520,128]{1,0:T(8,128)(2,1)S(1)}, u32[]{:S(2)}, u32[]{:S(2)}) %collective-permute-start.1) | collective-permute-done | bytes 133152 | tf_op jit(solution)/shard_map/ppermute | solution.py:43
  24.4 0.6 %collective-permute-done.2 = bf16[520,128]{1,0:T(8,128)(2,1)S(1)} collective-permute-done((bf16[520,128]{1,0:T(8,128)(2,1)S(1)}, bf16[520,128]{1,0:T(8,128)(2,1)S(1)}, u32[]{:S(2)}, u32[]{:S(2)}) %collective-permute-start.2) | collective-permute-done | bytes 133152 | tf_op jit(solution)/shard_map/ppermute | solution.py:43
  25.0 0.8 %fusion.13 = f32[1024,128]{1,0:T(8,128)S(1)} fusion(s32[512]{0:T(512)S(1)} %add_bitcast_fusion, bf16[520,128]{1,0:T(8,128)(2,1)S(1)} %collective-permute-done.2), kind=kOutput, calls=%fused_computation.18 | convolution fusion | flops 134742016 | bytes 657408 | tf_op jit(solution)/shard_map/dot_general | solution.py:16
  25.8 0.8 %fusion.17 = f32[1024,128]{1,0:T(8,128)S(1)} fusion(s32[512]{0:T(512)S(1)} %add_bitcast_fusion.1, bf16[520,128]{1,0:T(8,128)(2,1)S(1)} %collective-permute-done.1), kind=kOutput, calls=%fused_computation.24 | convolution fusion | flops 134742016 | bytes 657408 | tf_op jit(solution)/shard_map/dot_general | solution.py:16
  26.7 0.8 %fusion.43 = f32[1024,128]{1,0:T(8,128)S(1)} fusion(f32[1024,128]{1,0:T(8,128)S(1)} %fusion.13, f32[1024,128]{1,0:T(8,128)S(1)} %fusion.17, f32[1024,128]{1,0:T(8,128)S(1)} %fusion.29, s32[512]{0:T(512)S(1)} %add_bitcast_fusion.2, bf16[520,128]{1,0:T(8,128)(2,1)S(1)} %collective-permute-done), kind=kOutput, calls=%fused_computation.52 | convolution fusion | flops 135135232 | bytes 2230272 | tf_op jit(solution)/shard_map/dot_general | solution.py:16
  27.6 1.9 %collective-permute-done.3 = f32[1024,128]{1,0:T(8,128)S(1)} collective-permute-done((f32[1024,128]{1,0:T(8,128)S(1)}, f32[1024,128]{1,0:T(8,128)S(1)}, u32[]{:S(2)}, u32[]{:S(2)}) %collective-permute-start.3) | collective-permute-done | bytes 524320 | tf_op jit(solution)/shard_map/ppermute | solution.py:34
  29.6 0.5 fusion.62
  30.1 0.5 fusion.60
  30.7 0.5 fusion.58
  31.2 3.9 %collective-permute-start.4 = (bf16[512,128]{1,0:T(8,128)(2,1)S(1)}, bf16[512,128]{1,0:T(8,128)(2,1)S(1)}, u32[]{:S(2)}, u32[]{:S(2)}) collective-permute-start(bf16[512,128]{1,0:T(8,128)(2,1)S(1)} %fusion.58), channel_id=1, source_target_pairs={{0,12},{4,0},{8,4},{12,8},{1,13},{5,1},{9,5},{13,9},{2,14},{6,2},{... | collective-permute-start | bytes 393224 | tf_op jit(solution)/shard_map/ppermute | solution.py:43
  35.8 1.3 %fusion.30 = f32[1024,128]{1,0:T(8,128)S(1)} fusion(bf16[1024,128]{1,0:T(8,128)(2,1)S(1)} %fusion.87, s32[512]{0:T(512)S(1)} %bitcast.70, s32[1024]{0:T(1024)S(1)} %bitcast.61), kind=kOutput, calls=%fused_computation.42 | convolution fusion | flops 269549568 | bytes 792576 | tf_op jit(solution)/shard_map/dot_general | solution.py:12
  37.1 7.6 %collective-permute-done.6 = bf16[512,128]{1,0:T(8,128)(2,1)S(1)} collective-permute-done((bf16[512,128]{1,0:T(8,128)(2,1)S(1)}, bf16[512,128]{1,0:T(8,128)(2,1)S(1)}, u32[]{:S(2)}, u32[]{:S(2)}) %collective-permute-start.6) | collective-permute-done | bytes 131104 | tf_op jit(solution)/shard_map/ppermute | solution.py:43
  45.1 2.3 %collective-permute-done.5 = bf16[512,128]{1,0:T(8,128)(2,1)S(1)} collective-permute-done((bf16[512,128]{1,0:T(8,128)(2,1)S(1)}, bf16[512,128]{1,0:T(8,128)(2,1)S(1)}, u32[]{:S(2)}, u32[]{:S(2)}) %collective-permute-start.5) | collective-permute-done | bytes 131104 | tf_op jit(solution)/shard_map/ppermute | solution.py:43
  48.0 0.5 fusion.46
  48.5 2.6 %fusion.47 = bf16[1024,128]{1,0:T(8,128)(2,1)S(1)} fusion(pred[1024,16]{0,1:T(8,128)(4,1)S(1)} %iota_compare_fusion.80, bf16[1024,128]{1,0:T(8,128)(2,1)S(1)} %fusion.46, bf16[16,128,128]{2,1,0:T(8,128)(2,1)S(1)} %copy-done), kind=kOutput, calls=%fused_computation.56 | convolution fusion | flops 539099136 | bytes 1064960 | tf_op jit(solution)/shard_map/dot_general | solution.py:12
  51.1 0.9 %fusion.54 = bf16[512,128]{1,0:T(8,128)(2,1)S(1)} fusion(bf16[1024,128]{1,0:T(8,128)(2,1)S(1)} %fusion.47, s32[1024]{0:T(1024)S(1)} %get-tuple-element.2), kind=kOutput, calls=%fused_computation.59 | convolution fusion | flops 134807552 | bytes 397312 | tf_op jit(solution)/shard_map/dot_general | solution.py:16
  52.1 1.6 %collective-permute-start.7 = (bf16[128,512]{1,0:T(8,128)(2,1)S(1)}, bf16[128,512]{1,0:T(8,128)(2,1)S(1)}, u32[]{:S(2)}, u32[]{:S(2)}) collective-permute-start(bf16[128,512]{1,0:T(8,128)(2,1)S(1)} %convert_element_type.142), channel_id=1, source_target_pairs={{0,2},{2,0},{1,3},{3,1},{4,6},{6,4},{5,7},{7,5},{8,10},{10,8},{9,1... | collective-permute-start | bytes 393224 | tf_op jit(solution)/shard_map/ppermute | solution.py:124
  53.6 0.9 %fusion.32 = f32[512,128]{1,0:T(8,128)S(1)} fusion(bf16[1024,128]{1,0:T(8,128)(2,1)S(1)} %fusion.47, s32[1024]{0:T(1024)S(1)} %broadcast_subtract_fusion.1), kind=kOutput, calls=%fused_computation.45 | convolution fusion | flops 134742016 | bytes 528384 | tf_op jit(solution)/shard_map/dot_general | solution.py:16
  54.6 2.6 %collective-permute-done.7 = bf16[128,512]{1,0:T(8,128)(2,1)S(1)} collective-permute-done((bf16[128,512]{1,0:T(8,128)(2,1)S(1)}, bf16[128,512]{1,0:T(8,128)(2,1)S(1)}, u32[]{:S(2)}, u32[]{:S(2)}) %collective-permute-start.7) | collective-permute-done | bytes 131104 | tf_op jit(solution)/shard_map/ppermute | solution.py:124
  57.1 0.7 %convert_add_fusion = f32[128,512]{1,0:T(8,128)} fusion(f32[128,512]{1,0:T(8,128)S(1)} %reshape.149, bf16[128,512]{1,0:T(8,128)(2,1)S(1)} %collective-permute-done.7), kind=kLoop, calls=%fused_computation.93 | loop fusion | flops 131072 | bytes 655360 | tf_op jit(solution)/shard_map/add | solution.py:126
  (54 shorter events, 2.8 us)
Async XLA Ops:
  0.6 5.3 %copy-start = (bf16[16,128,128]{2,1,0:T(8,128)(2,1)S(1)}, bf16[16,128,128]{2,1,0:T(8,128)(2,1)}, u32[]{:S(2)}) copy-start(bf16[16,128,128]{2,1,0:T(8,128)(2,1)} %param.10) | copy-start | bytes 1572868
  1.4 1.3 %copy-start.6 = (s32[1024]{0:T(1024)S(1)}, s32[1024]{0:T(1024)}, u32[]{:S(2)}) copy-start(s32[1024]{0:T(1024)} %param.14) | copy-start | bytes 12292
  1.4 1.3 %copy-start.7 = (s32[1024,1]{0,1:T(1,128)S(1)}, s32[1024,1]{0,1:T(1,128)}, u32[]{:S(2)}) copy-start(s32[1024,1]{0,1:T(1,128)} %param.13) | copy-start | bytes 12292
  2.8 1.6 %copy-start.5 = (s32[1024]{0:T(1024)S(1)}, s32[1024]{0:T(1024)}, u32[]{:S(2)}) copy-start(s32[1024]{0:T(1024)} %param.17) | copy-start | bytes 12292
  2.8 1.7 %copy-start.2 = (bf16[256,512]{1,0:T(8,128)(2,1)S(1)}, bf16[256,512]{1,0:T(8,128)(2,1)}, u32[]{:S(2)}) copy-start(bf16[256,512]{1,0:T(8,128)(2,1)} %param.9) | copy-start | bytes 786436
  4.4 0.7 %copy-start.8 = (s32[1024]{0:T(1024)S(1)}, s32[1024]{0:T(1024)}, u32[]{:S(2)}) copy-start(s32[1024]{0:T(1024)} %param.16) | copy-start | bytes 12292
  9.9 10.6 %collective-permute-start = (bf16[520,128]{1,0:T(8,128)(2,1)S(1)}, bf16[520,128]{1,0:T(8,128)(2,1)S(1)}, u32[]{:S(2)}, u32[]{:S(2)}) collective-permute-start(bf16[520,128]{1,0:T(8,128)(2,1)S(1)} %pad_maximum_fusion), channel_id=1, source_target_pairs={{0,4},{4,8},{8,12},{12,0},{1,5},{5,9},{9,13},{13,1},{2,6},{6,10},{... | collective-permute-start | bytes 399368 | tf_op jit(solution)/shard_map/ppermute | solution.py:43
  13.9 10.5 %collective-permute-start.1 = (bf16[520,128]{1,0:T(8,128)(2,1)S(1)}, bf16[520,128]{1,0:T(8,128)(2,1)S(1)}, u32[]{:S(2)}, u32[]{:S(2)}) collective-permute-start(bf16[520,128]{1,0:T(8,128)(2,1)S(1)} %pad_maximum_fusion.1), channel_id=1, source_target_pairs={{0,8},{4,12},{8,0},{12,4},{1,9},{5,13},{9,1},{13,5},{2,10},{6,14},... | collective-permute-start | bytes 399368 | tf_op jit(solution)/shard_map/ppermute | solution.py:43
  17.4 7.6 %collective-permute-start.2 = (bf16[520,128]{1,0:T(8,128)(2,1)S(1)}, bf16[520,128]{1,0:T(8,128)(2,1)S(1)}, u32[]{:S(2)}, u32[]{:S(2)}) collective-permute-start(bf16[520,128]{1,0:T(8,128)(2,1)S(1)} %pad_maximum_fusion.2), channel_id=1, source_target_pairs={{0,12},{4,0},{8,4},{12,8},{1,13},{5,1},{9,5},{13,9},{2,14},{6,2},{... | collective-permute-start | bytes 399368 | tf_op jit(solution)/shard_map/ppermute | solution.py:43
  26.7 2.8 %copy-start.1 = (s32[1,1024,128]{2,1,0:T(8,128)S(1)}, s32[1,1024,128]{2,1,0:T(8,128)}, u32[]{:S(2)}) copy-start(s32[1,1024,128]{2,1,0:T(8,128)} %param.12) | copy-start | bytes 1572868
  26.7 2.8 %copy-start.3 = (bf16[1,1024,128]{2,1,0:T(8,128)(2,1)S(1)}, bf16[1,1024,128]{2,1,0:T(8,128)(2,1)}, u32[]{:S(2)}) copy-start(bf16[1,1024,128]{2,1,0:T(8,128)(2,1)} %param.11) | copy-start | bytes 786436
  27.5 2.0 %collective-permute-start.3 = (f32[1024,128]{1,0:T(8,128)S(1)}, f32[1024,128]{1,0:T(8,128)S(1)}, u32[]{:S(2)}, u32[]{:S(2)}) collective-permute-start(f32[1024,128]{1,0:T(8,128)S(1)} %fusion.43), channel_id=1, source_target_pairs={{0,1},{1,0},{2,3},{3,2},{4,5},{5,4},{6,7},{7,6},{8,9},{9,8},{10,11... | collective-permute-start | bytes 1572872 | tf_op jit(solution)/shard_map/ppermute | solution.py:34
  29.6 6.1 %copy-start.4 = (bf16[1024,128]{1,0:T(8,128)(2,1)}, bf16[1024,128]{1,0:T(8,128)(2,1)S(1)}, u32[]{:S(2)}) copy-start(bf16[1024,128]{1,0:T(8,128)(2,1)S(1)} %fusion.87) | copy-start | bytes 786436
  31.2 16.8 %collective-permute-start.4 = (bf16[512,128]{1,0:T(8,128)(2,1)S(1)}, bf16[512,128]{1,0:T(8,128)(2,1)S(1)}, u32[]{:S(2)}, u32[]{:S(2)}) collective-permute-start(bf16[512,128]{1,0:T(8,128)(2,1)S(1)} %fusion.58), channel_id=1, source_target_pairs={{0,12},{4,0},{8,4},{12,8},{1,13},{5,1},{9,5},{13,9},{2,14},{6,2},{... | collective-permute-start | bytes 393224 | tf_op jit(solution)/shard_map/ppermute | solution.py:43
  35.1 12.4 %collective-permute-start.5 = (bf16[512,128]{1,0:T(8,128)(2,1)S(1)}, bf16[512,128]{1,0:T(8,128)(2,1)S(1)}, u32[]{:S(2)}, u32[]{:S(2)}) collective-permute-start(bf16[512,128]{1,0:T(8,128)(2,1)S(1)} %fusion.60), channel_id=1, source_target_pairs={{0,8},{4,12},{8,0},{12,4},{1,9},{5,13},{9,1},{13,5},{2,10},{6,14},... | collective-permute-start | bytes 393224 | tf_op jit(solution)/shard_map/ppermute | solution.py:43
  35.5 9.1 %collective-permute-start.6 = (bf16[512,128]{1,0:T(8,128)(2,1)S(1)}, bf16[512,128]{1,0:T(8,128)(2,1)S(1)}, u32[]{:S(2)}, u32[]{:S(2)}) collective-permute-start(bf16[512,128]{1,0:T(8,128)(2,1)S(1)} %fusion.62), channel_id=1, source_target_pairs={{0,4},{4,8},{8,12},{12,0},{1,5},{5,9},{9,13},{13,1},{2,6},{6,10},{... | collective-permute-start | bytes 393224 | tf_op jit(solution)/shard_map/ppermute | solution.py:43
  52.1 5.0 %collective-permute-start.7 = (bf16[128,512]{1,0:T(8,128)(2,1)S(1)}, bf16[128,512]{1,0:T(8,128)(2,1)S(1)}, u32[]{:S(2)}, u32[]{:S(2)}) collective-permute-start(bf16[128,512]{1,0:T(8,128)(2,1)S(1)} %convert_element_type.142), channel_id=1, source_target_pairs={{0,2},{2,0},{1,3},{3,1},{4,6},{6,4},{5,7},{7,5},{8,10},{10,8},{9,1... | collective-permute-start | bytes 393224 | tf_op jit(solution)/shard_map/ppermute | solution.py:124

commit v14 on v4

--- a/solution.py
+++ b/solution.py
@@ -6,6 +6,13 @@
 
 def one_hot_rows(index, width):
     return (index[:, None] == jnp.arange(width, dtype=jnp.int32)[None, :]).astype(jnp.bfloat16)
+
+
+def row_hot(source, block, block_count, start, width):
+    rows = start + jnp.arange(width, dtype=jnp.int32)[None, :]
+    return (
+        (rows // block_count == source[:, None]) & (rows % block_count == block[:, None])
+    ).astype(jnp.bfloat16)
 
 
 def select_dot(selector, values, precision=None):
@@ -68,7 +75,7 @@
 
     target = trace_tile[:, 0]
     kinds = psf_index
-    spec_rows = trace_source[:, 0] * block_count + trace_block
+    source_here = trace_source[:, 0]
     member = one_hot_rows(target, tile_count)
     entry_ids = jnp.arange(entry_count, dtype=jnp.int32)
     up_to = (entry_ids[None, :] <= entry_ids[:, None]).astype(jnp.bfloat16)
@@ -77,7 +84,7 @@
     shift = (target - lax.axis_index("tile")) % tile_count
     dest = shift * capacity + position
 
-    gather_spec = one_hot_rows(spec_rows, row_count)
+    gather_spec = row_hot(source_here, trace_block, block_count, 0, row_count)
     spec_values = select_dot(gather_spec, spectra.reshape(row_count, bin_count)).astype(jnp.bfloat16)
     psf_flat = psf_blocks.reshape(table_count * bin_count, pixel_count)
     traces = select_dot(spread_by_kind(spec_values, kinds, table_count), psf_flat).astype(jnp.bfloat16)
@@ -116,8 +123,8 @@
         dither = lax.axis_index("dither")
         half_rows = row_count // 2
         own_start = dither * half_rows
-        their_rows = one_hot_rows(spec_rows - (half_rows - own_start), half_rows)
-        own_rows = one_hot_rows(spec_rows - own_start, half_rows)
+        their_rows = row_hot(source_here, trace_block, block_count, half_rows - own_start, half_rows)
+        own_rows = row_hot(source_here, trace_block, block_count, own_start, half_rows)
         theirs = select_dot_t(their_rows, terms).reshape(source_count // 2, block_count * bin_count)
         sent = lax.ppermute(theirs.astype(jnp.bfloat16), "dither", [(0, 1), (1, 0)])
         mine = select_dot_t(own_rows, terms).reshape(source_count // 2, block_count * bin_count)

time: 56.7 us -> 55.5 us (0.979); the launches traced: 56.4 us -> 54.4 us
  waiting for transfers between devices: 18.3 us -> 14.9 us
  starting transfers between devices: 12.3 us -> 13.6 us
  local copies, waits for them, and re-layouts: 0.67 us -> 1.52 us
  other arithmetic: 1.76 us -> 1.03 us
    ppermute x6, waiting for transfers between devices: 13.9 us -> 10.7 us  [exchange(): moved.append(lax.ppermute(blocks[step], axis, pairs))]
    ppermute x6, starting transfers between devices: 10.7 us -> 12 us  [exchange(): moved.append(lax.ppermute(blocks[step], axis, pairs))]
    reshape x1, local copies, waits for them, and re-layouts: 0.16 us -> 1.17 us  [per_device(): spectra.reshape(row_count, bin_count)]
    mul x1 -> x0, other arithmetic: 0.75 us -> none  [per_device(): spec_rows = trace_source[:, 0] * block_count + trace_block]
  transfers between devices with their start and end apart: 8 -> 8, of which waited for: 6 -> 7; matrix products, arithmetic and copies ran while one was open for 14% -> 15% of each run, Pallas kernels for 0% -> 0%
where the time goes in v14:
time: 55.5 us; the launch traced here: 54.4 us
  matrix products  22.3 us (40%)
  waiting for transfers between devices  14.9 us (27%)
  starting transfers between devices  13.6 us (25%)
  local copies, waits for them, and re-layouts  1.52 us (3%)
  other arithmetic  1.03 us (2%)
  between operations  1.03 us (2%)
    ppermute x6, starting transfers between devices, exchange(): moved.append(lax.ppermute(blocks[step], axis, pairs))  12 us
    dot_general x11, matrix products, select_dot(): jnp.dot(selector, values, preferred_element_type=jnp.float32, precision=p...  11.7 us
    ppermute x6, waiting for transfers between devices, exchange(): moved.append(lax.ppermute(blocks[step], axis, pairs))  10.7 us
    dot_general x13, matrix products, select_dot_t(): lax.dot_general(selector, values, (((0,), (0,)), ((), ())), preferred_ele...  10.6 us
    ppermute x1, waiting for transfers between devices, per_device(): sent = lax.ppermute(theirs.astype(jnp.bfloat16), 'dither', [(0, 1), (1, 0)])  2.41 us
    ppermute x1, waiting for transfers between devices, swap_add(): return value + lax.ppermute(value, axis, [(0, 1), (1, 0)])  1.86 us
    ppermute x1, starting transfers between devices, per_device(): sent = lax.ppermute(theirs.astype(jnp.bfloat16), 'dither', [(0, 1), (1, 0)])  1.55 us
    reshape x1, local copies, waits for them, and re-layouts, per_device(): spectra.reshape(row_count, bin_count)  1.17 us
  transfers between devices with their start and end apart: 8, of which 7 were waited for; matrix products, arithmetic and copies ran while one was open for 15% of the time, Pallas kernels for 0%

profile of v14, /device:TPU:0, one launch (start us, length us, event | category | flops | bytes accessed | tf_op | source)
XLA Modules:
  0.0 54.4 jit_solution(4193506107539074817)
XLA Ops:
  0.7 1.2 %reshape.305 = bf16[1024,128]{1,0:T(8,128)(2,1)S(1)} reshape(bf16[256,512]{1,0:T(8,128)(2,1)} %param.9) | data formatting | bytes 524288 | tf_op jit(solution)/shard_map/reshape | solution.py:88
  2.6 1.3 %fusion.66 = bf16[1024,128]{1,0:T(8,128)(2,1)S(1)} fusion(bf16[1024,128]{1,0:T(8,128)(2,1)S(1)} %reshape.305, s32[1024]{0:T(1024)S(1)} %get-tuple-element.8, s32[1024]{0:T(1024)S(1)} %get-tuple-element.9, s32[1024]{0:T(1024)S(1)} %copy-done.7, s32[1024]{0:T(1024)S(1)} %bitcast.67), kind=kOutput, calls=%fused_computation.67 | convolution fusion | flops 271712256 | bytes 540672 | tf_op jit(solution)/shard_map/dot_general | solution.py:19
  3.9 3.0 %fusion.63 = bf16[1024,128]{1,0:T(8,128)(2,1)S(1)} fusion(bf16[16,128,128]{2,1,0:T(8,128)(2,1)S(1)} %copy-done, pred[1024,16]{0,1:T(8,128)(4,1)S(1)} %iota_compare_fusion.80, bf16[1024,128]{1,0:T(8,128)(2,1)S(1)} %fusion.66), kind=kOutput, calls=%fused_computation.66 | convolution fusion | flops 539099136 | bytes 1064960 | tf_op jit(solution)/shard_map/dot_general | solution.py:19
  6.9 0.9 %fusion.76 = bf16[512,128]{1,0:T(8,128)(2,1)S(1)} fusion(bf16[1024,128]{1,0:T(8,128)(2,1)S(1)} %fusion.63, s32[1024]{0:T(1024)S(1)} %bitcast.61), kind=kOutput, calls=%fused_computation.73 | convolution fusion | flops 134807552 | bytes 397312 | tf_op jit(solution)/shard_map/dot_general | solution.py:23
  8.4 4.1 %collective-permute-start.1 = (bf16[520,128]{1,0:T(8,128)(2,1)S(1)}, bf16[520,128]{1,0:T(8,128)(2,1)S(1)}, u32[]{:S(2)}, u32[]{:S(2)}) collective-permute-start(bf16[520,128]{1,0:T(8,128)(2,1)S(1)} %pad_maximum_fusion.1), channel_id=1, source_target_pairs={{0,8},{4,12},{8,0},{12,4},{1,9},{5,13},{9,1},{13,5},{2,10},{6,14},... | collective-permute-start | bytes 399368 | tf_op jit(solution)/shard_map/ppermute | solution.py:50
  12.5 0.9 %fusion.78 = bf16[512,128]{1,0:T(8,128)(2,1)S(1)} fusion(bf16[1024,128]{1,0:T(8,128)(2,1)S(1)} %fusion.63, s32[1024]{0:T(1024)S(1)} %bitcast.58), kind=kOutput, calls=%fused_computation.75 | convolution fusion | flops 134807552 | bytes 397312 | tf_op jit(solution)/shard_map/dot_general | solution.py:23
  13.9 1.4 %collective-permute-start.2 = (bf16[520,128]{1,0:T(8,128)(2,1)S(1)}, bf16[520,128]{1,0:T(8,128)(2,1)S(1)}, u32[]{:S(2)}, u32[]{:S(2)}) collective-permute-start(bf16[520,128]{1,0:T(8,128)(2,1)S(1)} %pad_maximum_fusion.2), channel_id=1, source_target_pairs={{0,12},{4,0},{8,4},{12,8},{1,13},{5,1},{9,5},{13,9},{2,14},{6,2},{... | collective-permute-start | bytes 399368 | tf_op jit(solution)/shard_map/ppermute | solution.py:50
  15.3 0.9 %fusion.74 = bf16[512,128]{1,0:T(8,128)(2,1)S(1)} fusion(bf16[1024,128]{1,0:T(8,128)(2,1)S(1)} %fusion.63, s32[1024]{0:T(1024)S(1)} %bitcast.51), kind=kOutput, calls=%fused_computation.71 | convolution fusion | flops 134807552 | bytes 397312 | tf_op jit(solution)/shard_map/dot_general | solution.py:23
  16.7 0.7 %collective-permute-start = (bf16[520,128]{1,0:T(8,128)(2,1)S(1)}, bf16[520,128]{1,0:T(8,128)(2,1)S(1)}, u32[]{:S(2)}, u32[]{:S(2)}) collective-permute-start(bf16[520,128]{1,0:T(8,128)(2,1)S(1)} %pad_maximum_fusion), channel_id=1, source_target_pairs={{0,4},{4,8},{8,12},{12,0},{1,5},{5,9},{9,13},{13,1},{2,6},{6,10},{... | collective-permute-start | bytes 399368 | tf_op jit(solution)/shard_map/ppermute | solution.py:50
  17.9 1.5 %fusion.33 = f32[1024,128]{1,0:T(8,128)S(1)} fusion(bf16[1024,128]{1,0:T(8,128)(2,1)S(1)} %fusion.63, s32[512]{0:T(512)S(1)} %bitcast.65, s32[1024]{0:T(1024)S(1)} %bitcast.55), kind=kOutput, calls=%fused_computation.41 | convolution fusion | flops 269549568 | bytes 792576 | tf_op jit(solution)/shard_map/dot_general | solution.py:23
  19.7 2.3 %collective-permute-done.2 = bf16[520,128]{1,0:T(8,128)(2,1)S(1)} collective-permute-done((bf16[520,128]{1,0:T(8,128)(2,1)S(1)}, bf16[520,128]{1,0:T(8,128)(2,1)S(1)}, u32[]{:S(2)}, u32[]{:S(2)}) %collective-permute-start.2) | collective-permute-done | bytes 133152 | tf_op jit(solution)/shard_map/ppermute | solution.py:50
  22.1 1.5 %collective-permute-done = bf16[520,128]{1,0:T(8,128)(2,1)S(1)} collective-permute-done((bf16[520,128]{1,0:T(8,128)(2,1)S(1)}, bf16[520,128]{1,0:T(8,128)(2,1)S(1)}, u32[]{:S(2)}, u32[]{:S(2)}) %collective-permute-start) | collective-permute-done | bytes 133152 | tf_op jit(solution)/shard_map/ppermute | solution.py:50
  23.6 0.8 %fusion.18 = f32[1024,128]{1,0:T(8,128)S(1)} fusion(s32[512]{0:T(512)S(1)} %add_bitcast_fusion.1, bf16[520,128]{1,0:T(8,128)(2,1)S(1)} %collective-permute-done.1), kind=kOutput, calls=%fused_computation.22 | convolution fusion | flops 134742016 | bytes 657408 | tf_op jit(solution)/shard_map/dot_general | solution.py:23
  24.4 0.8 %fusion.13 = f32[1024,128]{1,0:T(8,128)S(1)} fusion(s32[512]{0:T(512)S(1)} %add_bitcast_fusion, bf16[520,128]{1,0:T(8,128)(2,1)S(1)} %collective-permute-done.2), kind=kOutput, calls=%fused_computation.15 | convolution fusion | flops 134742016 | bytes 657408 | tf_op jit(solution)/shard_map/dot_general | solution.py:23
  25.3 0.8 %fusion.56 = f32[1024,128]{1,0:T(8,128)S(1)} fusion(f32[1024,128]{1,0:T(8,128)S(1)} %fusion.13, f32[1024,128]{1,0:T(8,128)S(1)} %fusion.18, f32[1024,128]{1,0:T(8,128)S(1)} %fusion.33, s32[512]{0:T(512)S(1)} %add_bitcast_fusion.2, bf16[520,128]{1,0:T(8,128)(2,1)S(1)} %collective-permute-done), kind=kOutput, calls=%fused_computation.61 | convolution fusion | flops 135135232 | bytes 2230272 | tf_op jit(solution)/shard_map/dot_general | solution.py:23
  26.2 1.9 %collective-permute-done.3 = f32[1024,128]{1,0:T(8,128)S(1)} collective-permute-done((f32[1024,128]{1,0:T(8,128)S(1)}, f32[1024,128]{1,0:T(8,128)S(1)}, u32[]{:S(2)}, u32[]{:S(2)}) %collective-permute-start.3) | collective-permute-done | bytes 524320 | tf_op jit(solution)/shard_map/ppermute | solution.py:41
  28.2 0.5 fusion.77
  28.7 0.5 fusion.75
  29.2 0.5 fusion.79
  29.8 3.7 %collective-permute-start.5 = (bf16[512,128]{1,0:T(8,128)(2,1)S(1)}, bf16[512,128]{1,0:T(8,128)(2,1)S(1)}, u32[]{:S(2)}, u32[]{:S(2)}) collective-permute-start(bf16[512,128]{1,0:T(8,128)(2,1)S(1)} %fusion.77), channel_id=1, source_target_pairs={{0,8},{4,12},{8,0},{12,4},{1,9},{5,13},{9,1},{13,5},{2,10},{6,14},... | collective-permute-start | bytes 393224 | tf_op jit(solution)/shard_map/ppermute | solution.py:50
  33.5 0.9 %collective-permute-start.4 = (bf16[512,128]{1,0:T(8,128)(2,1)S(1)}, bf16[512,128]{1,0:T(8,128)(2,1)S(1)}, u32[]{:S(2)}, u32[]{:S(2)}) collective-permute-start(bf16[512,128]{1,0:T(8,128)(2,1)S(1)} %fusion.75), channel_id=1, source_target_pairs={{0,12},{4,0},{8,4},{12,8},{1,13},{5,1},{9,5},{13,9},{2,14},{6,2},{... | collective-permute-start | bytes 393224 | tf_op jit(solution)/shard_map/ppermute | solution.py:50
  34.4 1.1 %collective-permute-start.6 = (bf16[512,128]{1,0:T(8,128)(2,1)S(1)}, bf16[512,128]{1,0:T(8,128)(2,1)S(1)}, u32[]{:S(2)}, u32[]{:S(2)}) collective-permute-start(bf16[512,128]{1,0:T(8,128)(2,1)S(1)} %fusion.79), channel_id=1, source_target_pairs={{0,4},{4,8},{8,12},{12,0},{1,5},{5,9},{9,13},{13,1},{2,6},{6,10},{... | collective-permute-start | bytes 393224 | tf_op jit(solution)/shard_map/ppermute | solution.py:50
  35.5 1.3 %fusion.34 = f32[1024,128]{1,0:T(8,128)S(1)} fusion(bf16[1024,128]{1,0:T(8,128)(2,1)S(1)} %fusion.119, s32[512]{0:T(512)S(1)} %bitcast.66, s32[1024]{0:T(1024)S(1)} %bitcast.56), kind=kOutput, calls=%fused_computation.43 | convolution fusion | flops 269549568 | bytes 792576 | tf_op jit(solution)/shard_map/dot_general | solution.py:19
  36.8 3.8 %collective-permute-done.5 = bf16[512,128]{1,0:T(8,128)(2,1)S(1)} collective-permute-done((bf16[512,128]{1,0:T(8,128)(2,1)S(1)}, bf16[512,128]{1,0:T(8,128)(2,1)S(1)}, u32[]{:S(2)}, u32[]{:S(2)}) %collective-permute-start.5) | collective-permute-done | bytes 131104 | tf_op jit(solution)/shard_map/ppermute | solution.py:50
  41.2 2.7 %collective-permute-done.6 = bf16[512,128]{1,0:T(8,128)(2,1)S(1)} collective-permute-done((bf16[512,128]{1,0:T(8,128)(2,1)S(1)}, bf16[512,128]{1,0:T(8,128)(2,1)S(1)}, u32[]{:S(2)}, u32[]{:S(2)}) %collective-permute-start.6) | collective-permute-done | bytes 131104 | tf_op jit(solution)/shard_map/ppermute | solution.py:50
  44.4 0.5 fusion.59
  45.0 2.6 %fusion.60 = bf16[1024,128]{1,0:T(8,128)(2,1)S(1)} fusion(pred[1024,16]{0,1:T(8,128)(4,1)S(1)} %iota_compare_fusion.80, bf16[1024,128]{1,0:T(8,128)(2,1)S(1)} %fusion.59, bf16[16,128,128]{2,1,0:T(8,128)(2,1)S(1)} %copy-done), kind=kOutput, calls=%fused_computation.65 | convolution fusion | flops 539099136 | bytes 1064960 | tf_op jit(solution)/shard_map/dot_general | solution.py:19
  47.6 1.0 %fusion.69 = bf16[512,128]{1,0:T(8,128)(2,1)S(1)} fusion(bf16[1024,128]{1,0:T(8,128)(2,1)S(1)} %fusion.60, s32[512]{0:T(512)S(1)} %get-tuple-element.12, s32[512]{0:T(512)S(1)} %get-tuple-element.13, s32[1024]{0:T(1024)S(1)} %copy-done.7, s32[1024]{0:T(1024)S(1)} %bitcast.68), kind=kOutput, calls=%fused_computation.68 | convolution fusion | flops 135856128 | bytes 405504 | tf_op jit(solution)/shard_map/dot_general | solution.py:23
  48.7 1.6 %collective-permute-start.7 = (bf16[128,512]{1,0:T(8,128)(2,1)S(1)}, bf16[128,512]{1,0:T(8,128)(2,1)S(1)}, u32[]{:S(2)}, u32[]{:S(2)}) collective-permute-start(bf16[128,512]{1,0:T(8,128)(2,1)S(1)} %convert_element_type.153), channel_id=1, source_target_pairs={{0,2},{2,0},{1,3},{3,1},{4,6},{6,4},{5,7},{7,5},{8,10},{10,8},{9,1... | collective-permute-start | bytes 393224 | tf_op jit(solution)/shard_map/ppermute | solution.py:129
  50.2 1.0 %fusion.43 = f32[512,128]{1,0:T(8,128)S(1)} fusion(bf16[1024,128]{1,0:T(8,128)(2,1)S(1)} %fusion.60, s32[512]{0:T(512)S(1)} %get-tuple-element.10, s32[512]{0:T(512)S(1)} %get-tuple-element.11, s32[1024]{0:T(1024)S(1)} %copy-done.7, s32[1024]{0:T(1024)S(1)} %bitcast.69), kind=kOutput, calls=%fused_computation.52 | convolution fusion | flops 135790592 | bytes 536576 | tf_op jit(solution)/shard_map/dot_general | solution.py:23
  51.3 2.4 %collective-permute-done.7 = bf16[128,512]{1,0:T(8,128)(2,1)S(1)} collective-permute-done((bf16[128,512]{1,0:T(8,128)(2,1)S(1)}, bf16[128,512]{1,0:T(8,128)(2,1)S(1)}, u32[]{:S(2)}, u32[]{:S(2)}) %collective-permute-start.7) | collective-permute-done | bytes 131104 | tf_op jit(solution)/shard_map/ppermute | solution.py:129
  53.7 0.7 %convert_add_fusion = f32[128,512]{1,0:T(8,128)} fusion(f32[128,512]{1,0:T(8,128)S(1)} %reshape.309, bf16[128,512]{1,0:T(8,128)(2,1)S(1)} %collective-permute-done.7), kind=kLoop, calls=%fused_computation.117 | loop fusion | flops 131072 | bytes 655360 | tf_op jit(solution)/shard_map/add | solution.py:131
  (55 shorter events, 4.4 us)
Async XLA Ops:
  0.6 3.3 %copy-start = (bf16[16,128,128]{2,1,0:T(8,128)(2,1)S(1)}, bf16[16,128,128]{2,1,0:T(8,128)(2,1)}, u32[]{:S(2)}) copy-start(bf16[16,128,128]{2,1,0:T(8,128)(2,1)} %param.10) | copy-start | bytes 1572868
  0.6 1.2 %copy-start.4 = (s32[1024]{0:T(1024)S(1)}, s32[1024]{0:T(1024)}, u32[]{:S(2)}) copy-start(s32[1024]{0:T(1024)} %param.17) | copy-start | bytes 12292
  0.7 1.2 %copy-start.6 = (s32[1024,1]{0,1:T(1,128)S(1)}, s32[1024,1]{0,1:T(1,128)}, u32[]{:S(2)}) copy-start(s32[1024,1]{0,1:T(1,128)} %param.13) | copy-start | bytes 12292
  1.9 0.7 %copy-start.5 = (s32[1024]{0:T(1024)S(1)}, s32[1024]{0:T(1024)}, u32[]{:S(2)}) copy-start(s32[1024]{0:T(1024)} %param.14) | copy-start | bytes 12292
  1.9 0.7 %copy-start.7 = (s32[1024]{0:T(1024)S(1)}, s32[1024]{0:T(1024)}, u32[]{:S(2)}) copy-start(s32[1024]{0:T(1024)} %param.16) | copy-start | bytes 12292
  1.9 0.7 %copy-start.8 = (s32[1024,1]{0,1:T(1,128)S(1)}, s32[1024,1]{0,1:T(1,128)}, u32[]{:S(2)}) copy-start(s32[1024,1]{0,1:T(1,128)} %param.15) | copy-start | bytes 12292
  8.4 11.3 %collective-permute-start.1 = (bf16[520,128]{1,0:T(8,128)(2,1)S(1)}, bf16[520,128]{1,0:T(8,128)(2,1)S(1)}, u32[]{:S(2)}, u32[]{:S(2)}) collective-permute-start(bf16[520,128]{1,0:T(8,128)(2,1)S(1)} %pad_maximum_fusion.1), channel_id=1, source_target_pairs={{0,8},{4,12},{8,0},{12,4},{1,9},{5,13},{9,1},{13,5},{2,10},{6,14},... | collective-permute-start | bytes 399368 | tf_op jit(solution)/shard_map/ppermute | solution.py:50
  13.9 8.2 %collective-permute-start.2 = (bf16[520,128]{1,0:T(8,128)(2,1)S(1)}, bf16[520,128]{1,0:T(8,128)(2,1)S(1)}, u32[]{:S(2)}, u32[]{:S(2)}) collective-permute-start(bf16[520,128]{1,0:T(8,128)(2,1)S(1)} %pad_maximum_fusion.2), channel_id=1, source_target_pairs={{0,12},{4,0},{8,4},{12,8},{1,13},{5,1},{9,5},{13,9},{2,14},{6,2},{... | collective-permute-start | bytes 399368 | tf_op jit(solution)/shard_map/ppermute | solution.py:50
  16.7 6.9 %collective-permute-start = (bf16[520,128]{1,0:T(8,128)(2,1)S(1)}, bf16[520,128]{1,0:T(8,128)(2,1)S(1)}, u32[]{:S(2)}, u32[]{:S(2)}) collective-permute-start(bf16[520,128]{1,0:T(8,128)(2,1)S(1)} %pad_maximum_fusion), channel_id=1, source_target_pairs={{0,4},{4,8},{8,12},{12,0},{1,5},{5,9},{9,13},{13,1},{2,6},{6,10},{... | collective-permute-start | bytes 399368 | tf_op jit(solution)/shard_map/ppermute | solution.py:50
  25.2 2.8 %copy-start.1 = (s32[1,1024,128]{2,1,0:T(8,128)S(1)}, s32[1,1024,128]{2,1,0:T(8,128)}, u32[]{:S(2)}) copy-start(s32[1,1024,128]{2,1,0:T(8,128)} %param.12) | copy-start | bytes 1572868
  25.3 2.8 %copy-start.2 = (bf16[1,1024,128]{2,1,0:T(8,128)(2,1)S(1)}, bf16[1,1024,128]{2,1,0:T(8,128)(2,1)}, u32[]{:S(2)}) copy-start(bf16[1,1024,128]{2,1,0:T(8,128)(2,1)} %param.11) | copy-start | bytes 786436
  26.1 2.0 %collective-permute-start.3 = (f32[1024,128]{1,0:T(8,128)S(1)}, f32[1024,128]{1,0:T(8,128)S(1)}, u32[]{:S(2)}, u32[]{:S(2)}) collective-permute-start(f32[1024,128]{1,0:T(8,128)S(1)} %fusion.56), channel_id=1, source_target_pairs={{0,1},{1,0},{2,3},{3,2},{4,5},{5,4},{6,7},{7,6},{8,9},{9,8},{10,11... | collective-permute-start | bytes 1572872 | tf_op jit(solution)/shard_map/ppermute | solution.py:41
  28.2 7.3 %copy-start.3 = (bf16[1024,128]{1,0:T(8,128)(2,1)}, bf16[1024,128]{1,0:T(8,128)(2,1)S(1)}, u32[]{:S(2)}) copy-start(bf16[1024,128]{1,0:T(8,128)(2,1)S(1)} %fusion.119) | copy-start | bytes 786436
  29.8 10.9 %collective-permute-start.5 = (bf16[512,128]{1,0:T(8,128)(2,1)S(1)}, bf16[512,128]{1,0:T(8,128)(2,1)S(1)}, u32[]{:S(2)}, u32[]{:S(2)}) collective-permute-start(bf16[512,128]{1,0:T(8,128)(2,1)S(1)} %fusion.77), channel_id=1, source_target_pairs={{0,8},{4,12},{8,0},{12,4},{1,9},{5,13},{9,1},{13,5},{2,10},{6,14},... | collective-permute-start | bytes 393224 | tf_op jit(solution)/shard_map/ppermute | solution.py:50
  33.5 10.9 %collective-permute-start.4 = (bf16[512,128]{1,0:T(8,128)(2,1)S(1)}, bf16[512,128]{1,0:T(8,128)(2,1)S(1)}, u32[]{:S(2)}, u32[]{:S(2)}) collective-permute-start(bf16[512,128]{1,0:T(8,128)(2,1)S(1)} %fusion.75), channel_id=1, source_target_pairs={{0,12},{4,0},{8,4},{12,8},{1,13},{5,1},{9,5},{13,9},{2,14},{6,2},{... | collective-permute-start | bytes 393224 | tf_op jit(solution)/shard_map/ppermute | solution.py:50
  34.4 9.5 %collective-permute-start.6 = (bf16[512,128]{1,0:T(8,128)(2,1)S(1)}, bf16[512,128]{1,0:T(8,128)(2,1)S(1)}, u32[]{:S(2)}, u32[]{:S(2)}) collective-permute-start(bf16[512,128]{1,0:T(8,128)(2,1)S(1)} %fusion.79), channel_id=1, source_target_pairs={{0,4},{4,8},{8,12},{12,0},{1,5},{5,9},{9,13},{13,1},{2,6},{6,10},{... | collective-permute-start | bytes 393224 | tf_op jit(solution)/shard_map/ppermute | solution.py:50
  48.7 5.0 %collective-permute-start.7 = (bf16[128,512]{1,0:T(8,128)(2,1)S(1)}, bf16[128,512]{1,0:T(8,128)(2,1)S(1)}, u32[]{:S(2)}, u32[]{:S(2)}) collective-permute-start(bf16[128,512]{1,0:T(8,128)(2,1)S(1)} %convert_element_type.153), channel_id=1, source_target_pairs={{0,2},{2,0},{1,3},{3,1},{4,6},{6,4},{5,7},{7,5},{8,10},{10,8},{9,1... | collective-permute-start | bytes 393224 | tf_op jit(solution)/shard_map/ppermute | solution.py:129

commit v15 on v14

--- a/solution.py
+++ b/solution.py
@@ -84,8 +84,13 @@
     shift = (target - lax.axis_index("tile")) % tile_count
     dest = shift * capacity + position
 
+    source_hot = one_hot_rows(source_here, source_count)
+    whole_rows = select_dot(source_hot, spectra).astype(jnp.bfloat16)
+    chosen_block = trace_block[:, None, None] == jnp.arange(block_count, dtype=jnp.int32)[None, :, None]
+    spec_values = jnp.sum(
+        jnp.where(chosen_block, whole_rows.reshape(entry_count, block_count, bin_count), 0.0), axis=1
+    ).astype(jnp.bfloat16)
     gather_spec = row_hot(source_here, trace_block, block_count, 0, row_count)
-    spec_values = select_dot(gather_spec, spectra.reshape(row_count, bin_count)).astype(jnp.bfloat16)
     psf_flat = psf_blocks.reshape(table_count * bin_count, pixel_count)
     traces = select_dot(spread_by_kind(spec_values, kinds, table_count), psf_flat).astype(jnp.bfloat16)
     slot_parts = jnp.stack([trace_slot // 256, trace_slot % 256], axis=1).astype(jnp.bfloat16)
@@ -123,11 +128,14 @@
         dither = lax.axis_index("dither")
         half_rows = row_count // 2
         own_start = dither * half_rows
-        their_rows = row_hot(source_here, trace_block, block_count, half_rows - own_start, half_rows)
-        own_rows = row_hot(source_here, trace_block, block_count, own_start, half_rows)
-        theirs = select_dot_t(their_rows, terms).reshape(source_count // 2, block_count * bin_count)
+        half_sources = source_count // 2
+        own_first = dither * half_sources
+        by_block = spread_by_kind(terms, trace_block, block_count)
+        their_hot = one_hot_rows(source_here - (half_sources - own_first), half_sources)
+        own_hot = one_hot_rows(source_here - own_first, half_sources)
+        theirs = select_dot_t(their_hot, by_block)
         sent = lax.ppermute(theirs.astype(jnp.bfloat16), "dither", [(0, 1), (1, 0)])
-        mine = select_dot_t(own_rows, terms).reshape(source_count // 2, block_count * bin_count)
+        mine = select_dot_t(own_hot, by_block)
         gradient = mine + sent.astype(jnp.float32)
     else:
         local_grad = select_dot_t(gather_spec, terms)

time: 55.5 us -> 57.5 us (1.036); the launches traced: 54.4 us -> 57.2 us
  waiting for transfers between devices: 14.9 us -> 18.7 us
  local copies, waits for them, and re-layouts: 1.52 us -> 0.62 us
    ppermute x6, waiting for transfers between devices: 10.7 us -> 13.4 us  [exchange(): moved.append(lax.ppermute(blocks[step], axis, pairs))]
    reshape x2 -> x0, local copies, waits for them, and re-layouts: 1.21 us -> none  [the longest x1 1.17 us: per_device(): spectra.reshape(row_count, bin_count)]
    ppermute x1, waiting for transfers between devices: 2.41 us -> 3.47 us  [per_device(): sent = lax.ppermute(theirs.astype(jnp.bfloat16), 'dither', [(0, 1), (1, 0)])]
    add x1 -> x0, other arithmetic: 0.73 us -> none  [per_device(): gradient = mine + sent.astype(jnp.float32)]
  transfers between devices with their start and end apart: 8 -> 8, of which waited for: 7 -> 6; matrix products, arithmetic and copies ran while one was open for 15% -> 13% of each run, Pallas kernels for 0% -> 0%
where the time goes in v15:
time: 57.5 us; the launch traced here: 57.2 us
  matrix products  22.6 us (39%)
  waiting for transfers between devices  18.7 us (33%)
  starting transfers between devices  13.6 us (24%)
  between operations  1.05 us (2%)
  other arithmetic  0.66 us (1%)
  local copies, waits for them, and re-layouts  0.62 us (1%)
    ppermute x6, waiting for transfers between devices, exchange(): moved.append(lax.ppermute(blocks[step], axis, pairs))  13.4 us
    ppermute x6, starting transfers between devices, exchange(): moved.append(lax.ppermute(blocks[step], axis, pairs))  12 us
    dot_general x11, matrix products, select_dot(): jnp.dot(selector, values, preferred_element_type=jnp.float32, precision=p...  11.8 us
    dot_general x13, matrix products, select_dot_t(): lax.dot_general(selector, values, (((0,), (0,)), ((), ())), preferred_ele...  10.7 us
    ppermute x1, waiting for transfers between devices, per_device(): sent = lax.ppermute(theirs.astype(jnp.bfloat16), 'dither', [(0, 1), (1, 0)])  3.47 us
    ppermute x1, waiting for transfers between devices, swap_add(): return value + lax.ppermute(value, axis, [(0, 1), (1, 0)])  1.88 us
    ppermute x1, starting transfers between devices, per_device(): sent = lax.ppermute(theirs.astype(jnp.bfloat16), 'dither', [(0, 1), (1, 0)])  1.56 us
  transfers between devices with their start and end apart: 8, of which 6 were waited for; matrix products, arithmetic and copies ran while one was open for 13% of the time, Pallas kernels for 0%

profile of v15, /device:TPU:0, one launch (start us, length us, event | category | flops | bytes accessed | tf_op | source)
XLA Modules:
  0.0 57.2 jit_solution(10974604950811485546)
XLA Ops:
  0.7 1.3 %fusion.60 = f32[1024]{0:T(1024)S(1)} fusion(s32[1024]{0:T(1024)} %bitcast.74), kind=kOutput, calls=%fused_computation.63 | convolution fusion | flops 9464832 | bytes 8192 | tf_op jit(solution)/shard_map/dot_general | solution.py:19
  2.1 0.6 %convolution_convert_fusion = bf16[1024,512]{0,1:T(8,128)(2,1)S(1)} fusion(bf16[256,512]{1,0:T(8,128)(2,1)S(1)} %copy-done.2, s32[1024]{0:T(1024)S(1)} %bitcast.58), kind=kOutput, calls=%fused_computation.40 | convolution fusion | flops 269221888 | bytes 1314816 | tf_op jit(solution)/shard_map/dot_general | solution.py:19
  3.5 3.0 %fusion.47 = bf16[1024,128]{1,0:T(8,128)(2,1)S(1)} fusion(bf16[16,128,128]{2,1,0:T(8,128)(2,1)S(1)} %copy-done, pred[1024,16]{0,1:T(8,128)(4,1)S(1)} %iota_compare_fusion.84, bf16[1024,128]{1,0:T(8,128)(2,1)S(1)} %copy.15), kind=kOutput, calls=%fused_computation.51 | convolution fusion | flops 539099136 | bytes 1064960 | tf_op jit(solution)/shard_map/dot_general | solution.py:19
  6.5 0.9 %fusion.54 = bf16[512,128]{1,0:T(8,128)(2,1)S(1)} fusion(bf16[1024,128]{1,0:T(8,128)(2,1)S(1)} %fusion.47, s32[1024]{0:T(1024)S(1)} %bitcast.71), kind=kOutput, calls=%fused_computation.56 | convolution fusion | flops 134807552 | bytes 397312 | tf_op jit(solution)/shard_map/dot_general | solution.py:23
  7.9 4.1 %collective-permute-start.1 = (bf16[520,128]{1,0:T(8,128)(2,1)S(1)}, bf16[520,128]{1,0:T(8,128)(2,1)S(1)}, u32[]{:S(2)}, u32[]{:S(2)}) collective-permute-start(bf16[520,128]{1,0:T(8,128)(2,1)S(1)} %pad_maximum_fusion.1), channel_id=1, source_target_pairs={{0,8},{4,12},{8,0},{12,4},{1,9},{5,13},{9,1},{13,5},{2,10},{6,14},... | collective-permute-start | bytes 399368 | tf_op jit(solution)/shard_map/ppermute | solution.py:50
  12.0 0.9 %fusion.56 = bf16[512,128]{1,0:T(8,128)(2,1)S(1)} fusion(bf16[1024,128]{1,0:T(8,128)(2,1)S(1)} %fusion.47, s32[1024]{0:T(1024)S(1)} %bitcast.68), kind=kOutput, calls=%fused_computation.58 | convolution fusion | flops 134807552 | bytes 397312 | tf_op jit(solution)/shard_map/dot_general | solution.py:23
  13.4 1.4 %collective-permute-start.2 = (bf16[520,128]{1,0:T(8,128)(2,1)S(1)}, bf16[520,128]{1,0:T(8,128)(2,1)S(1)}, u32[]{:S(2)}, u32[]{:S(2)}) collective-permute-start(bf16[520,128]{1,0:T(8,128)(2,1)S(1)} %pad_maximum_fusion.2), channel_id=1, source_target_pairs={{0,12},{4,0},{8,4},{12,8},{1,13},{5,1},{9,5},{13,9},{2,14},{6,2},{... | collective-permute-start | bytes 399368 | tf_op jit(solution)/shard_map/ppermute | solution.py:50
  14.8 0.9 %fusion.52 = bf16[512,128]{1,0:T(8,128)(2,1)S(1)} fusion(bf16[1024,128]{1,0:T(8,128)(2,1)S(1)} %fusion.47, s32[1024]{0:T(1024)S(1)} %bitcast.61), kind=kOutput, calls=%fused_computation.54 | convolution fusion | flops 134807552 | bytes 397312 | tf_op jit(solution)/shard_map/dot_general | solution.py:23
  16.2 0.7 %collective-permute-start = (bf16[520,128]{1,0:T(8,128)(2,1)S(1)}, bf16[520,128]{1,0:T(8,128)(2,1)S(1)}, u32[]{:S(2)}, u32[]{:S(2)}) collective-permute-start(bf16[520,128]{1,0:T(8,128)(2,1)S(1)} %pad_maximum_fusion), channel_id=1, source_target_pairs={{0,4},{4,8},{8,12},{12,0},{1,5},{5,9},{9,13},{13,1},{2,6},{6,10},{... | collective-permute-start | bytes 399368 | tf_op jit(solution)/shard_map/ppermute | solution.py:50
  17.0 0.5 fusion.62
  17.5 1.5 %fusion.27 = f32[1024,128]{1,0:T(8,128)S(1)} fusion(bf16[1024,128]{1,0:T(8,128)(2,1)S(1)} %fusion.47, s32[512]{0:T(512)S(1)} %bitcast.75, s32[1024]{0:T(1024)S(1)} %bitcast.65), kind=kOutput, calls=%fused_computation.35 | convolution fusion | flops 269549568 | bytes 792576 | tf_op jit(solution)/shard_map/dot_general | solution.py:23
  19.3 2.3 %collective-permute-done.2 = bf16[520,128]{1,0:T(8,128)(2,1)S(1)} collective-permute-done((bf16[520,128]{1,0:T(8,128)(2,1)S(1)}, bf16[520,128]{1,0:T(8,128)(2,1)S(1)}, u32[]{:S(2)}, u32[]{:S(2)}) %collective-permute-start.2) | collective-permute-done | bytes 133152 | tf_op jit(solution)/shard_map/ppermute | solution.py:50
  21.6 1.5 %collective-permute-done = bf16[520,128]{1,0:T(8,128)(2,1)S(1)} collective-permute-done((bf16[520,128]{1,0:T(8,128)(2,1)S(1)}, bf16[520,128]{1,0:T(8,128)(2,1)S(1)}, u32[]{:S(2)}, u32[]{:S(2)}) %collective-permute-start) | collective-permute-done | bytes 133152 | tf_op jit(solution)/shard_map/ppermute | solution.py:50
  23.1 0.8 %fusion.14 = f32[1024,128]{1,0:T(8,128)S(1)} fusion(s32[512]{0:T(512)S(1)} %add_bitcast_fusion.1, bf16[520,128]{1,0:T(8,128)(2,1)S(1)} %collective-permute-done.1), kind=kOutput, calls=%fused_computation.18 | convolution fusion | flops 134742016 | bytes 657408 | tf_op jit(solution)/shard_map/dot_general | solution.py:23
  24.0 0.8 %fusion.9 = f32[1024,128]{1,0:T(8,128)S(1)} fusion(s32[512]{0:T(512)S(1)} %add_bitcast_fusion, bf16[520,128]{1,0:T(8,128)(2,1)S(1)} %collective-permute-done.2), kind=kOutput, calls=%fused_computation.11 | convolution fusion | flops 134742016 | bytes 657408 | tf_op jit(solution)/shard_map/dot_general | solution.py:23
  24.8 0.8 %fusion.40 = f32[1024,128]{1,0:T(8,128)S(1)} fusion(f32[1024,128]{1,0:T(8,128)S(1)} %fusion.9, f32[1024,128]{1,0:T(8,128)S(1)} %fusion.14, f32[1024,128]{1,0:T(8,128)S(1)} %fusion.27, s32[512]{0:T(512)S(1)} %add_bitcast_fusion.2, bf16[520,128]{1,0:T(8,128)(2,1)S(1)} %collective-permute-done), kind=kOutput, calls=%fused_computation.46 | convolution fusion | flops 135135232 | bytes 2230272 | tf_op jit(solution)/shard_map/dot_general | solution.py:23
  25.7 1.9 %collective-permute-done.3 = f32[1024,128]{1,0:T(8,128)S(1)} collective-permute-done((f32[1024,128]{1,0:T(8,128)S(1)}, f32[1024,128]{1,0:T(8,128)S(1)}, u32[]{:S(2)}, u32[]{:S(2)}) %collective-permute-start.3) | collective-permute-done | bytes 524320 | tf_op jit(solution)/shard_map/ppermute | solution.py:41
  27.8 0.5 fusion.53
  28.3 0.5 fusion.55
  28.8 0.5 fusion.57
  29.3 4.6 %collective-permute-start.4 = (bf16[512,128]{1,0:T(8,128)(2,1)S(1)}, bf16[512,128]{1,0:T(8,128)(2,1)S(1)}, u32[]{:S(2)}, u32[]{:S(2)}) collective-permute-start(bf16[512,128]{1,0:T(8,128)(2,1)S(1)} %fusion.53), channel_id=1, source_target_pairs={{0,12},{4,0},{8,4},{12,8},{1,13},{5,1},{9,5},{13,9},{2,14},{6,2},{... | collective-permute-start | bytes 393224 | tf_op jit(solution)/shard_map/ppermute | solution.py:50
  33.9 1.2 %collective-permute-start.6 = (bf16[512,128]{1,0:T(8,128)(2,1)S(1)}, bf16[512,128]{1,0:T(8,128)(2,1)S(1)}, u32[]{:S(2)}, u32[]{:S(2)}) collective-permute-start(bf16[512,128]{1,0:T(8,128)(2,1)S(1)} %fusion.57), channel_id=1, source_target_pairs={{0,4},{4,8},{8,12},{12,0},{1,5},{5,9},{9,13},{13,1},{2,6},{6,10},{... | collective-permute-start | bytes 393224 | tf_op jit(solution)/shard_map/ppermute | solution.py:50
  35.0 1.3 %fusion.28 = f32[1024,128]{1,0:T(8,128)S(1)} fusion(bf16[1024,128]{1,0:T(8,128)(2,1)S(1)} %fusion.89, s32[512]{0:T(512)S(1)} %bitcast.76, s32[1024]{0:T(1024)S(1)} %bitcast.66), kind=kOutput, calls=%fused_computation.37 | convolution fusion | flops 269549568 | bytes 792576 | tf_op jit(solution)/shard_map/dot_general | solution.py:19
  36.3 9.3 %collective-permute-done.5 = bf16[512,128]{1,0:T(8,128)(2,1)S(1)} collective-permute-done((bf16[512,128]{1,0:T(8,128)(2,1)S(1)}, bf16[512,128]{1,0:T(8,128)(2,1)S(1)}, u32[]{:S(2)}, u32[]{:S(2)}) %collective-permute-start.5) | collective-permute-done | bytes 131104 | tf_op jit(solution)/shard_map/ppermute | solution.py:50
  45.6 0.5 fusion.15
  46.1 0.5 fusion.10
  46.6 0.5 fusion.43
  47.2 2.6 %fusion.44 = bf16[1024,128]{1,0:T(8,128)(2,1)S(1)} fusion(pred[1024,16]{0,1:T(8,128)(4,1)S(1)} %iota_compare_fusion.84, bf16[1024,128]{1,0:T(8,128)(2,1)S(1)} %fusion.43, bf16[16,128,128]{2,1,0:T(8,128)(2,1)S(1)} %copy-done), kind=kOutput, calls=%fused_computation.50 | convolution fusion | flops 539099136 | bytes 1064960 | tf_op jit(solution)/shard_map/dot_general | solution.py:19
  50.0 0.7 %convolution_convert_fusion.1 = bf16[128,512]{1,0:T(8,128)(2,1)S(1)} fusion(bf16[1024,512]{0,1:T(8,128)(2,1)S(1)} %bitcast.54, s32[1024]{0:T(1024)S(1)} %bitcast.60), kind=kOutput, calls=%fused_computation.60 | convolution fusion | flops 134545408 | bytes 1183744 | tf_op jit(solution)/shard_map/dot_general | solution.py:23
  50.8 1.6 %collective-permute-start.7 = (bf16[128,512]{1,0:T(8,128)(2,1)S(1)}, bf16[128,512]{1,0:T(8,128)(2,1)S(1)}, u32[]{:S(2)}, u32[]{:S(2)}) collective-permute-start(bf16[128,512]{1,0:T(8,128)(2,1)S(1)} %convolution_convert_fusion.1), channel_id=1, source_target_pairs={{0,2},{2,0},{1,3},{3,1},{4,6},{6,4},{5,7},{7,5},{8,10},{10,8},{9,1... | collective-permute-start | bytes 393224 | tf_op jit(solution)/shard_map/ppermute | solution.py:137
  52.3 3.5 %collective-permute-done.7 = bf16[128,512]{1,0:T(8,128)(2,1)S(1)} collective-permute-done((bf16[128,512]{1,0:T(8,128)(2,1)S(1)}, bf16[128,512]{1,0:T(8,128)(2,1)S(1)}, u32[]{:S(2)}, u32[]{:S(2)}) %collective-permute-start.7) | collective-permute-done | bytes 131104 | tf_op jit(solution)/shard_map/ppermute | solution.py:137
  55.8 1.4 %convert_add_fusion = f32[128,512]{1,0:T(8,128)} fusion(bf16[128,512]{1,0:T(8,128)(2,1)S(1)} %collective-permute-done.7, bf16[1024,512]{0,1:T(8,128)(2,1)S(1)} %bitcast.55, s32[1024]{0:T(1024)S(1)} %bitcast.59), kind=kOutput, calls=%fused_computation.102 | convolution fusion | flops 134610944 | bytes 1445888 | tf_op jit(solution)/shard_map/dot_general | solution.py:23
  (56 shorter events, 3.1 us)
Async XLA Ops:
  0.6 2.8 %copy-start = (bf16[16,128,128]{2,1,0:T(8,128)(2,1)S(1)}, bf16[16,128,128]{2,1,0:T(8,128)(2,1)}, u32[]{:S(2)}) copy-start(bf16[16,128,128]{2,1,0:T(8,128)(2,1)} %param.10) | copy-start | bytes 1572868
  0.6 1.3 %copy-start.9 = (s32[1024,1]{0,1:T(1,128)S(1)}, s32[1024,1]{0,1:T(1,128)}, u32[]{:S(2)}) copy-start(s32[1024,1]{0,1:T(1,128)} %param.13) | copy-start | bytes 12292
  0.7 1.4 %copy-start.7 = (s32[1024]{0:T(1024)S(1)}, s32[1024]{0:T(1024)}, u32[]{:S(2)}) copy-start(s32[1024]{0:T(1024)} %param.16) | copy-start | bytes 12292
  0.7 1.4 %copy-start.5 = (s32[1024,1]{0,1:T(1,128)S(1)}, s32[1024,1]{0,1:T(1,128)}, u32[]{:S(2)}) copy-start(s32[1024,1]{0,1:T(1,128)} %param.15) | copy-start | bytes 12292
  0.7 1.4 %copy-start.2 = (bf16[256,512]{1,0:T(8,128)(2,1)S(1)}, bf16[256,512]{1,0:T(8,128)(2,1)}, u32[]{:S(2)}) copy-start(bf16[256,512]{1,0:T(8,128)(2,1)} %param.9) | copy-start | bytes 786436
  2.7 0.7 %copy-start.6 = (s32[1024]{0:T(1024)S(1)}, s32[1024]{0:T(1024)}, u32[]{:S(2)}) copy-start(s32[1024]{0:T(1024)} %param.17) | copy-start | bytes 12292
  2.7 0.7 %copy-start.8 = (s32[1024]{0:T(1024)S(1)}, s32[1024]{0:T(1024)}, u32[]{:S(2)}) copy-start(s32[1024]{0:T(1024)} %param.14) | copy-start | bytes 12292
  7.9 11.3 %collective-permute-start.1 = (bf16[520,128]{1,0:T(8,128)(2,1)S(1)}, bf16[520,128]{1,0:T(8,128)(2,1)S(1)}, u32[]{:S(2)}, u32[]{:S(2)}) collective-permute-start(bf16[520,128]{1,0:T(8,128)(2,1)S(1)} %pad_maximum_fusion.1), channel_id=1, source_target_pairs={{0,8},{4,12},{8,0},{12,4},{1,9},{5,13},{9,1},{13,5},{2,10},{6,14},... | collective-permute-start | bytes 399368 | tf_op jit(solution)/shard_map/ppermute | solution.py:50
  13.4 8.2 %collective-permute-start.2 = (bf16[520,128]{1,0:T(8,128)(2,1)S(1)}, bf16[520,128]{1,0:T(8,128)(2,1)S(1)}, u32[]{:S(2)}, u32[]{:S(2)}) collective-permute-start(bf16[520,128]{1,0:T(8,128)(2,1)S(1)} %pad_maximum_fusion.2), channel_id=1, source_target_pairs={{0,12},{4,0},{8,4},{12,8},{1,13},{5,1},{9,5},{13,9},{2,14},{6,2},{... | collective-permute-start | bytes 399368 | tf_op jit(solution)/shard_map/ppermute | solution.py:50
  16.2 6.9 %collective-permute-start = (bf16[520,128]{1,0:T(8,128)(2,1)S(1)}, bf16[520,128]{1,0:T(8,128)(2,1)S(1)}, u32[]{:S(2)}, u32[]{:S(2)}) collective-permute-start(bf16[520,128]{1,0:T(8,128)(2,1)S(1)} %pad_maximum_fusion), channel_id=1, source_target_pairs={{0,4},{4,8},{8,12},{12,0},{1,5},{5,9},{9,13},{13,1},{2,6},{6,10},{... | collective-permute-start | bytes 399368 | tf_op jit(solution)/shard_map/ppermute | solution.py:50
  24.8 2.8 %copy-start.1 = (s32[1,1024,128]{2,1,0:T(8,128)S(1)}, s32[1,1024,128]{2,1,0:T(8,128)}, u32[]{:S(2)}) copy-start(s32[1,1024,128]{2,1,0:T(8,128)} %param.12) | copy-start | bytes 1572868
  24.8 2.8 %copy-start.3 = (bf16[1,1024,128]{2,1,0:T(8,128)(2,1)S(1)}, bf16[1,1024,128]{2,1,0:T(8,128)(2,1)}, u32[]{:S(2)}) copy-start(bf16[1,1024,128]{2,1,0:T(8,128)(2,1)} %param.11) | copy-start | bytes 786436
  25.6 2.0 %collective-permute-start.3 = (f32[1024,128]{1,0:T(8,128)S(1)}, f32[1024,128]{1,0:T(8,128)S(1)}, u32[]{:S(2)}, u32[]{:S(2)}) collective-permute-start(f32[1024,128]{1,0:T(8,128)S(1)} %fusion.40), channel_id=1, source_target_pairs={{0,1},{1,0},{2,3},{3,2},{4,5},{5,4},{6,7},{7,6},{8,9},{9,8},{10,11... | collective-permute-start | bytes 1572872 | tf_op jit(solution)/shard_map/ppermute | solution.py:41
  27.7 7.3 %copy-start.4 = (bf16[1024,128]{1,0:T(8,128)(2,1)}, bf16[1024,128]{1,0:T(8,128)(2,1)S(1)}, u32[]{:S(2)}) copy-start(bf16[1024,128]{1,0:T(8,128)(2,1)S(1)} %fusion.89) | copy-start | bytes 786436
  29.3 17.3 %collective-permute-start.4 = (bf16[512,128]{1,0:T(8,128)(2,1)S(1)}, bf16[512,128]{1,0:T(8,128)(2,1)S(1)}, u32[]{:S(2)}, u32[]{:S(2)}) collective-permute-start(bf16[512,128]{1,0:T(8,128)(2,1)S(1)} %fusion.53), channel_id=1, source_target_pairs={{0,12},{4,0},{8,4},{12,8},{1,13},{5,1},{9,5},{13,9},{2,14},{6,2},{... | collective-permute-start | bytes 393224 | tf_op jit(solution)/shard_map/ppermute | solution.py:50
  33.9 11.8 %collective-permute-start.5 = (bf16[512,128]{1,0:T(8,128)(2,1)S(1)}, bf16[512,128]{1,0:T(8,128)(2,1)S(1)}, u32[]{:S(2)}, u32[]{:S(2)}) collective-permute-start(bf16[512,128]{1,0:T(8,128)(2,1)S(1)} %fusion.55), channel_id=1, source_target_pairs={{0,8},{4,12},{8,0},{12,4},{1,9},{5,13},{9,1},{13,5},{2,10},{6,14},... | collective-permute-start | bytes 393224 | tf_op jit(solution)/shard_map/ppermute | solution.py:50
  33.9 12.3 %collective-permute-start.6 = (bf16[512,128]{1,0:T(8,128)(2,1)S(1)}, bf16[512,128]{1,0:T(8,128)(2,1)S(1)}, u32[]{:S(2)}, u32[]{:S(2)}) collective-permute-start(bf16[512,128]{1,0:T(8,128)(2,1)S(1)} %fusion.57), channel_id=1, source_target_pairs={{0,4},{4,8},{8,12},{12,0},{1,5},{5,9},{9,13},{13,1},{2,6},{6,10},{... | collective-permute-start | bytes 393224 | tf_op jit(solution)/shard_map/ppermute | solution.py:50
  50.8 5.0 %collective-permute-start.7 = (bf16[128,512]{1,0:T(8,128)(2,1)S(1)}, bf16[128,512]{1,0:T(8,128)(2,1)S(1)}, u32[]{:S(2)}, u32[]{:S(2)}) collective-permute-start(bf16[128,512]{1,0:T(8,128)(2,1)S(1)} %convolution_convert_fusion.1), channel_id=1, source_target_pairs={{0,2},{2,0},{1,3},{3,1},{4,6},{6,4},{5,7},{7,5},{8,10},{10,8},{9,1... | collective-permute-start | bytes 393224 | tf_op jit(solution)/shard_map/ppermute | solution.py:137

commit v16 on v14

--- a/solution.py
+++ b/solution.py
@@ -84,8 +84,13 @@
     shift = (target - lax.axis_index("tile")) % tile_count
     dest = shift * capacity + position
 
+    source_hot = one_hot_rows(source_here, source_count)
+    whole_rows = select_dot(source_hot, spectra).astype(jnp.bfloat16)
+    chosen_block = trace_block[:, None, None] == jnp.arange(block_count, dtype=jnp.int32)[None, :, None]
+    spec_values = jnp.sum(
+        jnp.where(chosen_block, whole_rows.reshape(entry_count, block_count, bin_count), 0.0), axis=1
+    ).astype(jnp.bfloat16)
     gather_spec = row_hot(source_here, trace_block, block_count, 0, row_count)
-    spec_values = select_dot(gather_spec, spectra.reshape(row_count, bin_count)).astype(jnp.bfloat16)
     psf_flat = psf_blocks.reshape(table_count * bin_count, pixel_count)
     traces = select_dot(spread_by_kind(spec_values, kinds, table_count), psf_flat).astype(jnp.bfloat16)
     slot_parts = jnp.stack([trace_slot // 256, trace_slot % 256], axis=1).astype(jnp.bfloat16)

time: 55.5 us -> 57.8 us (1.041); the launches traced: 54.4 us -> 57.6 us
  waiting for transfers between devices: 14.9 us -> 17.6 us
  other arithmetic: 1.03 us -> 2.07 us
  local copies, waits for them, and re-layouts: 1.52 us -> 0.6 us
    ppermute x6, waiting for transfers between devices: 10.7 us -> 13.4 us  [exchange(): moved.append(lax.ppermute(blocks[step], axis, pairs))]
    reshape x1 -> x0, local copies, waits for them, and re-layouts: 1.17 us -> none  [per_device(): spectra.reshape(row_count, bin_count)]
    eq x0 -> x1, other arithmetic: none -> 0.75 us  [per_device(): trace_block[:, None, None]]
  transfers between devices with their start and end apart: 8 -> 8, of which waited for: 7 -> 6; matrix products, arithmetic and copies ran while one was open for 15% -> 14% of each run, Pallas kernels for 0% -> 0%
where the time goes in v16:
time: 57.8 us; the launch traced here: 57.6 us
  matrix products  22.6 us (39%)
  waiting for transfers between devices  17.6 us (30%)
  starting transfers between devices  13.6 us (24%)
  other arithmetic  2.07 us (4%)
  between operations  1.03 us (2%)
  local copies, waits for them, and re-layouts  0.6 us (1%)
    ppermute x6, waiting for transfers between devices, exchange(): moved.append(lax.ppermute(blocks[step], axis, pairs))  13.4 us
    dot_general x11, matrix products, select_dot(): jnp.dot(selector, values, preferred_element_type=jnp.float32, precision=p...  12 us
    ppermute x6, starting transfers between devices, exchange(): moved.append(lax.ppermute(blocks[step], axis, pairs))  12 us
    dot_general x13, matrix products, select_dot_t(): lax.dot_general(selector, values, (((0,), (0,)), ((), ())), preferred_ele...  10.6 us
    ppermute x1, waiting for transfers between devices, per_device(): sent = lax.ppermute(theirs.astype(jnp.bfloat16), 'dither', [(0, 1), (1, 0)])  2.41 us
    ppermute x1, waiting for transfers between devices, swap_add(): return value + lax.ppermute(value, axis, [(0, 1), (1, 0)])  1.86 us
    ppermute x1, starting transfers between devices, per_device(): sent = lax.ppermute(theirs.astype(jnp.bfloat16), 'dither', [(0, 1), (1, 0)])  1.56 us
  transfers between devices with their start and end apart: 8, of which 6 were waited for; matrix products, arithmetic and copies ran while one was open for 14% of the time, Pallas kernels for 0%

profile of v16, /device:TPU:0, one launch (start us, length us, event | category | flops | bytes accessed | tf_op | source)
XLA Modules:
  0.0 57.6 jit_solution(452779715610272235)
XLA Ops:
  0.6 0.8 %iota_compare_fusion.83 = pred[1024,4]{0,1:T(4,128)(4,1)S(1)} fusion(s32[1024]{0:T(1024)} %param.16), kind=kLoop, calls=%fused_computation.122 | loop fusion | flops 4096 | bytes 8192 | tf_op jit(solution)/shard_map/eq | solution.py:89
  1.4 1.6 %convolution_convert_fusion = bf16[1024,512]{0,1:T(8,128)(2,1)S(1)} fusion(bf16[256,512]{1,0:T(8,128)(2,1)} %param.9, s32[1024]{0:T(1024)} %bitcast.60), kind=kOutput, calls=%fused_computation.48 | convolution fusion | flops 269221888 | bytes 1314816 | tf_op jit(solution)/shard_map/dot_general | solution.py:19
  4.3 3.0 %fusion.55 = bf16[1024,128]{1,0:T(8,128)(2,1)S(1)} fusion(bf16[16,128,128]{2,1,0:T(8,128)(2,1)S(1)} %copy-done, pred[1024,16]{0,1:T(8,128)(4,1)S(1)} %iota_compare_fusion.82, bf16[1024,128]{1,0:T(8,128)(2,1)S(1)} %copy.13), kind=kOutput, calls=%fused_computation.59 | convolution fusion | flops 539099136 | bytes 1064960 | tf_op jit(solution)/shard_map/dot_general | solution.py:19
  7.3 0.9 %fusion.65 = bf16[512,128]{1,0:T(8,128)(2,1)S(1)} fusion(bf16[1024,128]{1,0:T(8,128)(2,1)S(1)} %fusion.55, s32[1024]{0:T(1024)S(1)} %bitcast.66), kind=kOutput, calls=%fused_computation.65 | convolution fusion | flops 134807552 | bytes 397312 | tf_op jit(solution)/shard_map/dot_general | solution.py:23
  8.7 4.1 %collective-permute-start.1 = (bf16[520,128]{1,0:T(8,128)(2,1)S(1)}, bf16[520,128]{1,0:T(8,128)(2,1)S(1)}, u32[]{:S(2)}, u32[]{:S(2)}) collective-permute-start(bf16[520,128]{1,0:T(8,128)(2,1)S(1)} %pad_maximum_fusion.1), channel_id=1, source_target_pairs={{0,8},{4,12},{8,0},{12,4},{1,9},{5,13},{9,1},{13,5},{2,10},{6,14},... | collective-permute-start | bytes 399368 | tf_op jit(solution)/shard_map/ppermute | solution.py:50
  12.8 0.9 %fusion.67 = bf16[512,128]{1,0:T(8,128)(2,1)S(1)} fusion(bf16[1024,128]{1,0:T(8,128)(2,1)S(1)} %fusion.55, s32[1024]{0:T(1024)S(1)} %bitcast.63), kind=kOutput, calls=%fused_computation.67 | convolution fusion | flops 134807552 | bytes 397312 | tf_op jit(solution)/shard_map/dot_general | solution.py:23
  14.3 1.4 %collective-permute-start.2 = (bf16[520,128]{1,0:T(8,128)(2,1)S(1)}, bf16[520,128]{1,0:T(8,128)(2,1)S(1)}, u32[]{:S(2)}, u32[]{:S(2)}) collective-permute-start(bf16[520,128]{1,0:T(8,128)(2,1)S(1)} %pad_maximum_fusion.2), channel_id=1, source_target_pairs={{0,12},{4,0},{8,4},{12,8},{1,13},{5,1},{9,5},{13,9},{2,14},{6,2},{... | collective-permute-start | bytes 399368 | tf_op jit(solution)/shard_map/ppermute | solution.py:50
  15.7 0.9 %fusion.63 = bf16[512,128]{1,0:T(8,128)(2,1)S(1)} fusion(bf16[1024,128]{1,0:T(8,128)(2,1)S(1)} %fusion.55, s32[1024]{0:T(1024)S(1)} %bitcast.53), kind=kOutput, calls=%fused_computation.63 | convolution fusion | flops 134807552 | bytes 397312 | tf_op jit(solution)/shard_map/dot_general | solution.py:23
  17.1 0.7 %collective-permute-start = (bf16[520,128]{1,0:T(8,128)(2,1)S(1)}, bf16[520,128]{1,0:T(8,128)(2,1)S(1)}, u32[]{:S(2)}, u32[]{:S(2)}) collective-permute-start(bf16[520,128]{1,0:T(8,128)(2,1)S(1)} %pad_maximum_fusion), channel_id=1, source_target_pairs={{0,4},{4,8},{8,12},{12,0},{1,5},{5,9},{9,13},{13,1},{2,6},{6,10},{... | collective-permute-start | bytes 399368 | tf_op jit(solution)/shard_map/ppermute | solution.py:50
  18.3 1.5 %fusion.27 = f32[1024,128]{1,0:T(8,128)S(1)} fusion(bf16[1024,128]{1,0:T(8,128)(2,1)S(1)} %fusion.55, s32[512]{0:T(512)S(1)} %bitcast.70, s32[1024]{0:T(1024)S(1)} %bitcast.57), kind=kOutput, calls=%fused_computation.35 | convolution fusion | flops 269549568 | bytes 792576 | tf_op jit(solution)/shard_map/dot_general | solution.py:23
  20.1 2.3 %collective-permute-done.2 = bf16[520,128]{1,0:T(8,128)(2,1)S(1)} collective-permute-done((bf16[520,128]{1,0:T(8,128)(2,1)S(1)}, bf16[520,128]{1,0:T(8,128)(2,1)S(1)}, u32[]{:S(2)}, u32[]{:S(2)}) %collective-permute-start.2) | collective-permute-done | bytes 133152 | tf_op jit(solution)/shard_map/ppermute | solution.py:50
  22.4 1.5 %collective-permute-done = bf16[520,128]{1,0:T(8,128)(2,1)S(1)} collective-permute-done((bf16[520,128]{1,0:T(8,128)(2,1)S(1)}, bf16[520,128]{1,0:T(8,128)(2,1)S(1)}, u32[]{:S(2)}, u32[]{:S(2)}) %collective-permute-start) | collective-permute-done | bytes 133152 | tf_op jit(solution)/shard_map/ppermute | solution.py:50
  24.0 0.8 %fusion.14 = f32[1024,128]{1,0:T(8,128)S(1)} fusion(s32[512]{0:T(512)S(1)} %add_bitcast_fusion.1, bf16[520,128]{1,0:T(8,128)(2,1)S(1)} %collective-permute-done.1), kind=kOutput, calls=%fused_computation.18 | convolution fusion | flops 134742016 | bytes 657408 | tf_op jit(solution)/shard_map/dot_general | solution.py:23
  24.8 0.8 %fusion.9 = f32[1024,128]{1,0:T(8,128)S(1)} fusion(s32[512]{0:T(512)S(1)} %add_bitcast_fusion, bf16[520,128]{1,0:T(8,128)(2,1)S(1)} %collective-permute-done.2), kind=kOutput, calls=%fused_computation.11 | convolution fusion | flops 134742016 | bytes 657408 | tf_op jit(solution)/shard_map/dot_general | solution.py:23
  25.6 0.8 %fusion.48 = f32[1024,128]{1,0:T(8,128)S(1)} fusion(f32[1024,128]{1,0:T(8,128)S(1)} %fusion.9, f32[1024,128]{1,0:T(8,128)S(1)} %fusion.14, f32[1024,128]{1,0:T(8,128)S(1)} %fusion.27, s32[512]{0:T(512)S(1)} %add_bitcast_fusion.2, bf16[520,128]{1,0:T(8,128)(2,1)S(1)} %collective-permute-done), kind=kOutput, calls=%fused_computation.54 | convolution fusion | flops 135135232 | bytes 2230272 | tf_op jit(solution)/shard_map/dot_general | solution.py:23
  26.6 1.9 %collective-permute-done.3 = f32[1024,128]{1,0:T(8,128)S(1)} collective-permute-done((f32[1024,128]{1,0:T(8,128)S(1)}, f32[1024,128]{1,0:T(8,128)S(1)}, u32[]{:S(2)}, u32[]{:S(2)}) %collective-permute-start.3) | collective-permute-done | bytes 524320 | tf_op jit(solution)/shard_map/ppermute | solution.py:41
  28.6 0.5 fusion.64
  29.1 0.5 fusion.66
  29.6 0.5 fusion.68
  30.1 4.6 %collective-permute-start.4 = (bf16[512,128]{1,0:T(8,128)(2,1)S(1)}, bf16[512,128]{1,0:T(8,128)(2,1)S(1)}, u32[]{:S(2)}, u32[]{:S(2)}) collective-permute-start(bf16[512,128]{1,0:T(8,128)(2,1)S(1)} %fusion.64), channel_id=1, source_target_pairs={{0,12},{4,0},{8,4},{12,8},{1,13},{5,1},{9,5},{13,9},{2,14},{6,2},{... | collective-permute-start | bytes 393224 | tf_op jit(solution)/shard_map/ppermute | solution.py:50
  34.7 1.2 %collective-permute-start.6 = (bf16[512,128]{1,0:T(8,128)(2,1)S(1)}, bf16[512,128]{1,0:T(8,128)(2,1)S(1)}, u32[]{:S(2)}, u32[]{:S(2)}) collective-permute-start(bf16[512,128]{1,0:T(8,128)(2,1)S(1)} %fusion.68), channel_id=1, source_target_pairs={{0,4},{4,8},{8,12},{12,0},{1,5},{5,9},{9,13},{13,1},{2,6},{6,10},{... | collective-permute-start | bytes 393224 | tf_op jit(solution)/shard_map/ppermute | solution.py:50
  35.9 1.3 %fusion.28 = f32[1024,128]{1,0:T(8,128)S(1)} fusion(bf16[1024,128]{1,0:T(8,128)(2,1)S(1)} %fusion.108, s32[512]{0:T(512)S(1)} %bitcast.71, s32[1024]{0:T(1024)S(1)} %bitcast.58), kind=kOutput, calls=%fused_computation.37 | convolution fusion | flops 269549568 | bytes 792576 | tf_op jit(solution)/shard_map/dot_general | solution.py:19
  37.2 9.3 %collective-permute-done.5 = bf16[512,128]{1,0:T(8,128)(2,1)S(1)} collective-permute-done((bf16[512,128]{1,0:T(8,128)(2,1)S(1)}, bf16[512,128]{1,0:T(8,128)(2,1)S(1)}, u32[]{:S(2)}, u32[]{:S(2)}) %collective-permute-start.5) | collective-permute-done | bytes 131104 | tf_op jit(solution)/shard_map/ppermute | solution.py:50
  46.5 0.5 fusion.15
  47.0 0.5 fusion.10
  47.5 0.5 fusion.51
  48.1 2.6 %fusion.52 = bf16[1024,128]{1,0:T(8,128)(2,1)S(1)} fusion(pred[1024,16]{0,1:T(8,128)(4,1)S(1)} %iota_compare_fusion.82, bf16[1024,128]{1,0:T(8,128)(2,1)S(1)} %fusion.51, bf16[16,128,128]{2,1,0:T(8,128)(2,1)S(1)} %copy-done), kind=kOutput, calls=%fused_computation.58 | convolution fusion | flops 539099136 | bytes 1064960 | tf_op jit(solution)/shard_map/dot_general | solution.py:19
  50.7 1.0 %fusion.58 = bf16[512,128]{1,0:T(8,128)(2,1)S(1)} fusion(bf16[1024,128]{1,0:T(8,128)(2,1)S(1)} %fusion.52, s32[512]{0:T(512)S(1)} %get-tuple-element.10, s32[512]{0:T(512)S(1)} %get-tuple-element.11, s32[1024]{0:T(1024)S(1)} %copy-done.7, s32[1024]{0:T(1024)S(1)} %bitcast.61), kind=kOutput, calls=%fused_computation.60 | convolution fusion | flops 135856128 | bytes 405504 | tf_op jit(solution)/shard_map/dot_general | solution.py:23
  51.8 1.6 %collective-permute-start.7 = (bf16[128,512]{1,0:T(8,128)(2,1)S(1)}, bf16[128,512]{1,0:T(8,128)(2,1)S(1)}, u32[]{:S(2)}, u32[]{:S(2)}) collective-permute-start(bf16[128,512]{1,0:T(8,128)(2,1)S(1)} %convert_element_type.157), channel_id=1, source_target_pairs={{0,2},{2,0},{1,3},{3,1},{4,6},{6,4},{5,7},{7,5},{8,10},{10,8},{9,1... | collective-permute-start | bytes 393224 | tf_op jit(solution)/shard_map/ppermute | solution.py:134
  53.3 1.0 %fusion.35 = f32[512,128]{1,0:T(8,128)S(1)} fusion(bf16[1024,128]{1,0:T(8,128)(2,1)S(1)} %fusion.52, s32[512]{0:T(512)S(1)} %get-tuple-element.8, s32[512]{0:T(512)S(1)} %get-tuple-element.9, s32[1024]{0:T(1024)S(1)} %copy-done.7, s32[1024]{0:T(1024)S(1)} %bitcast.62), kind=kOutput, calls=%fused_computation.44 | convolution fusion | flops 135790592 | bytes 536576 | tf_op jit(solution)/shard_map/dot_general | solution.py:23
  54.4 2.4 %collective-permute-done.7 = bf16[128,512]{1,0:T(8,128)(2,1)S(1)} collective-permute-done((bf16[128,512]{1,0:T(8,128)(2,1)S(1)}, bf16[128,512]{1,0:T(8,128)(2,1)S(1)}, u32[]{:S(2)}, u32[]{:S(2)}) %collective-permute-start.7) | collective-permute-done | bytes 131104 | tf_op jit(solution)/shard_map/ppermute | solution.py:134
  56.8 0.7 %convert_add_fusion = f32[128,512]{1,0:T(8,128)} fusion(f32[128,512]{1,0:T(8,128)S(1)} %reshape.282, bf16[128,512]{1,0:T(8,128)(2,1)S(1)} %collective-permute-done.7), kind=kLoop, calls=%fused_computation.112 | loop fusion | flops 131072 | bytes 655360 | tf_op jit(solution)/shard_map/add | solution.py:136
  (56 shorter events, 3.9 us)
Async XLA Ops:
  0.6 3.7 %copy-start = (bf16[16,128,128]{2,1,0:T(8,128)(2,1)S(1)}, bf16[16,128,128]{2,1,0:T(8,128)(2,1)}, u32[]{:S(2)}) copy-start(bf16[16,128,128]{2,1,0:T(8,128)(2,1)} %param.10) | copy-start | bytes 1572868
  3.0 0.7 %copy-start.5 = (s32[1024]{0:T(1024)S(1)}, s32[1024]{0:T(1024)}, u32[]{:S(2)}) copy-start(s32[1024]{0:T(1024)} %param.17) | copy-start | bytes 12292
  3.0 0.7 %copy-start.8 = (s32[1024,1]{0,1:T(1,128)S(1)}, s32[1024,1]{0,1:T(1,128)}, u32[]{:S(2)}) copy-start(s32[1024,1]{0,1:T(1,128)} %param.13) | copy-start | bytes 12292
  3.3 1.0 %copy-start.6 = (s32[1024]{0:T(1024)S(1)}, s32[1024]{0:T(1024)}, u32[]{:S(2)}) copy-start(s32[1024]{0:T(1024)} %param.14) | copy-start | bytes 12292
  8.7 11.3 %collective-permute-start.1 = (bf16[520,128]{1,0:T(8,128)(2,1)S(1)}, bf16[520,128]{1,0:T(8,128)(2,1)S(1)}, u32[]{:S(2)}, u32[]{:S(2)}) collective-permute-start(bf16[520,128]{1,0:T(8,128)(2,1)S(1)} %pad_maximum_fusion.1), channel_id=1, source_target_pairs={{0,8},{4,12},{8,0},{12,4},{1,9},{5,13},{9,1},{13,5},{2,10},{6,14},... | collective-permute-start | bytes 399368 | tf_op jit(solution)/shard_map/ppermute | solution.py:50
  14.3 8.2 %collective-permute-start.2 = (bf16[520,128]{1,0:T(8,128)(2,1)S(1)}, bf16[520,128]{1,0:T(8,128)(2,1)S(1)}, u32[]{:S(2)}, u32[]{:S(2)}) collective-permute-start(bf16[520,128]{1,0:T(8,128)(2,1)S(1)} %pad_maximum_fusion.2), channel_id=1, source_target_pairs={{0,12},{4,0},{8,4},{12,8},{1,13},{5,1},{9,5},{13,9},{2,14},{6,2},{... | collective-permute-start | bytes 399368 | tf_op jit(solution)/shard_map/ppermute | solution.py:50
  17.1 6.9 %collective-permute-start = (bf16[520,128]{1,0:T(8,128)(2,1)S(1)}, bf16[520,128]{1,0:T(8,128)(2,1)S(1)}, u32[]{:S(2)}, u32[]{:S(2)}) collective-permute-start(bf16[520,128]{1,0:T(8,128)(2,1)S(1)} %pad_maximum_fusion), channel_id=1, source_target_pairs={{0,4},{4,8},{8,12},{12,0},{1,5},{5,9},{9,13},{13,1},{2,6},{6,10},{... | collective-permute-start | bytes 399368 | tf_op jit(solution)/shard_map/ppermute | solution.py:50
  25.6 2.8 %copy-start.1 = (s32[1,1024,128]{2,1,0:T(8,128)S(1)}, s32[1,1024,128]{2,1,0:T(8,128)}, u32[]{:S(2)}) copy-start(s32[1,1024,128]{2,1,0:T(8,128)} %param.12) | copy-start | bytes 1572868
  25.6 2.8 %copy-start.2 = (bf16[1,1024,128]{2,1,0:T(8,128)(2,1)S(1)}, bf16[1,1024,128]{2,1,0:T(8,128)(2,1)}, u32[]{:S(2)}) copy-start(bf16[1,1024,128]{2,1,0:T(8,128)(2,1)} %param.11) | copy-start | bytes 786436
  26.5 2.0 %collective-permute-start.3 = (f32[1024,128]{1,0:T(8,128)S(1)}, f32[1024,128]{1,0:T(8,128)S(1)}, u32[]{:S(2)}, u32[]{:S(2)}) collective-permute-start(f32[1024,128]{1,0:T(8,128)S(1)} %fusion.48), channel_id=1, source_target_pairs={{0,1},{1,0},{2,3},{3,2},{4,5},{5,4},{6,7},{7,6},{8,9},{9,8},{10,11... | collective-permute-start | bytes 1572872 | tf_op jit(solution)/shard_map/ppermute | solution.py:41
  28.6 7.3 %copy-start.3 = (bf16[1024,128]{1,0:T(8,128)(2,1)}, bf16[1024,128]{1,0:T(8,128)(2,1)S(1)}, u32[]{:S(2)}) copy-start(bf16[1024,128]{1,0:T(8,128)(2,1)S(1)} %fusion.108) | copy-start | bytes 786436
  30.1 17.4 %collective-permute-start.4 = (bf16[512,128]{1,0:T(8,128)(2,1)S(1)}, bf16[512,128]{1,0:T(8,128)(2,1)S(1)}, u32[]{:S(2)}, u32[]{:S(2)}) collective-permute-start(bf16[512,128]{1,0:T(8,128)(2,1)S(1)} %fusion.64), channel_id=1, source_target_pairs={{0,12},{4,0},{8,4},{12,8},{1,13},{5,1},{9,5},{13,9},{2,14},{6,2},{... | collective-permute-start | bytes 393224 | tf_op jit(solution)/shard_map/ppermute | solution.py:50
  34.7 11.8 %collective-permute-start.5 = (bf16[512,128]{1,0:T(8,128)(2,1)S(1)}, bf16[512,128]{1,0:T(8,128)(2,1)S(1)}, u32[]{:S(2)}, u32[]{:S(2)}) collective-permute-start(bf16[512,128]{1,0:T(8,128)(2,1)S(1)} %fusion.66), channel_id=1, source_target_pairs={{0,8},{4,12},{8,0},{12,4},{1,9},{5,13},{9,1},{13,5},{2,10},{6,14},... | collective-permute-start | bytes 393224 | tf_op jit(solution)/shard_map/ppermute | solution.py:50
  34.7 12.3 %collective-permute-start.6 = (bf16[512,128]{1,0:T(8,128)(2,1)S(1)}, bf16[512,128]{1,0:T(8,128)(2,1)S(1)}, u32[]{:S(2)}, u32[]{:S(2)}) collective-permute-start(bf16[512,128]{1,0:T(8,128)(2,1)S(1)} %fusion.68), channel_id=1, source_target_pairs={{0,4},{4,8},{8,12},{12,0},{1,5},{5,9},{9,13},{13,1},{2,6},{6,10},{... | collective-permute-start | bytes 393224 | tf_op jit(solution)/shard_map/ppermute | solution.py:50
  48.0 2.6 %copy-start.4 = (s32[1024,1]{0,1:T(1,128)S(1)}, s32[1024,1]{0,1:T(1,128)}, u32[]{:S(2)}) copy-start(s32[1024,1]{0,1:T(1,128)} %param.15) | copy-start | bytes 12292
  48.0 2.6 %copy-start.7 = (s32[1024]{0:T(1024)S(1)}, s32[1024]{0:T(1024)}, u32[]{:S(2)}) copy-start(s32[1024]{0:T(1024)} %param.16) | copy-start | bytes 12292
  51.8 5.0 %collective-permute-start.7 = (bf16[128,512]{1,0:T(8,128)(2,1)S(1)}, bf16[128,512]{1,0:T(8,128)(2,1)S(1)}, u32[]{:S(2)}, u32[]{:S(2)}) collective-permute-start(bf16[128,512]{1,0:T(8,128)(2,1)S(1)} %convert_element_type.157), channel_id=1, source_target_pairs={{0,2},{2,0},{1,3},{3,1},{4,6},{6,4},{5,7},{7,5},{8,10},{10,8},{9,1... | collective-permute-start | bytes 393224 | tf_op jit(solution)/shard_map/ppermute | solution.py:134

commit v17 on v14

--- a/solution.py
+++ b/solution.py
@@ -1,3 +1,5 @@
+import functools
+
 import jax
 import jax.numpy as jnp
 from jax import lax
@@ -85,7 +87,15 @@
     dest = shift * capacity + position
 
     gather_spec = row_hot(source_here, trace_block, block_count, 0, row_count)
-    spec_values = select_dot(gather_spec, spectra.reshape(row_count, bin_count)).astype(jnp.bfloat16)
+    spec_parts = [
+        select_dot(
+            ((source_here[:, None] == jnp.arange(source_count, dtype=jnp.int32)[None, :])
+             & (trace_block[:, None] == part)).astype(jnp.bfloat16),
+            spectra[:, part * bin_count : (part + 1) * bin_count],
+        )
+        for part in range(block_count)
+    ]
+    spec_values = functools.reduce(jnp.add, spec_parts).astype(jnp.bfloat16)
     psf_flat = psf_blocks.reshape(table_count * bin_count, pixel_count)
     traces = select_dot(spread_by_kind(spec_values, kinds, table_count), psf_flat).astype(jnp.bfloat16)
     slot_parts = jnp.stack([trace_slot // 256, trace_slot % 256], axis=1).astype(jnp.bfloat16)

time: 55.5 us -> 58.9 us (1.061); the launches traced: 54.4 us -> 58.6 us
  waiting for transfers between devices: 14.9 us -> 17.6 us
  other arithmetic: 1.03 us -> 2.47 us
  matrix products: 22.3 us -> 23.7 us
  local copies, waits for them, and re-layouts: 1.52 us -> 0.24 us
    ppermute x6, waiting for transfers between devices: 10.7 us -> 13.4 us  [exchange(): moved.append(lax.ppermute(blocks[step], axis, pairs))]
    dot_general x11 -> x14, matrix products: 11.7 us -> 13 us  [select_dot(): jnp.dot(selector, values, preferred_element_type=jnp.float32, precision=p...]
    reshape x1 -> x0, local copies, waits for them, and re-layouts: 1.17 us -> none  [per_device(): spectra.reshape(row_count, bin_count)]
    eq x0 -> x1, other arithmetic: none -> 0.75 us  [per_device(): trace_block[:, None] == part]
    eq x1, other arithmetic: 0.01 us -> 0.7 us  [spread_by_kind(): kinds[:, None, None]]
  transfers between devices with their start and end apart: 8 -> 8, of which waited for: 7 -> 5; matrix products, arithmetic and copies ran while one was open for 15% -> 14% of each run, Pallas kernels for 0% -> 0%
where the time goes in v17:
time: 58.9 us; the launch traced here: 58.6 us
  matrix products  23.7 us (40%)
  waiting for transfers between devices  17.6 us (30%)
  starting transfers between devices  13.6 us (23%)
  other arithmetic  2.47 us (4%)
  between operations  1.04 us (2%)
    ppermute x6, waiting for transfers between devices, exchange(): moved.append(lax.ppermute(blocks[step], axis, pairs))  13.4 us
    dot_general x14, matrix products, select_dot(): jnp.dot(selector, values, preferred_element_type=jnp.float32, precision=p...  13 us
    ppermute x6, starting transfers between devices, exchange(): moved.append(lax.ppermute(blocks[step], axis, pairs))  12 us
    dot_general x13, matrix products, select_dot_t(): lax.dot_general(selector, values, (((0,), (0,)), ((), ())), preferred_ele...  10.6 us
    ppermute x1, waiting for transfers between devices, per_device(): sent = lax.ppermute(theirs.astype(jnp.bfloat16), 'dither', [(0, 1), (1, 0)])  2.41 us
    ppermute x1, waiting for transfers between devices, swap_add(): return value + lax.ppermute(value, axis, [(0, 1), (1, 0)])  1.86 us
    ppermute x1, starting transfers between devices, per_device(): sent = lax.ppermute(theirs.astype(jnp.bfloat16), 'dither', [(0, 1), (1, 0)])  1.55 us
  transfers between devices with their start and end apart: 8, of which 5 were waited for; matrix products, arithmetic and copies ran while one was open for 14% of the time, Pallas kernels for 0%

profile of v17, /device:TPU:0, one launch (start us, length us, event | category | flops | bytes accessed | tf_op | source)
XLA Modules:
  0.0 58.6 jit_solution(14709830455964463089)
XLA Ops:
  0.6 0.8 %broadcast_compare_fusion = (pred[1024]{0:T(1024)(128)(4,1)S(1)}, pred[1024]{0:T(1024)(128)(4,1)S(1)}, pred[1024]{0:T(1024)(128)(4,1)S(1)}, pred[1024]{0:T(1024)(128)(4,1)S(1)}) fusion(s32[1024]{0:T(1024)} %param.16), kind=kLoop, calls=%fused_computation.182 | loop fusion | flops 4096 | bytes 8192 | tf_op jit(solution)/shard_map/eq | solution.py:93
  1.4 0.7 %iota_compare_fusion.81 = pred[1024,16]{0,1:T(8,128)(4,1)S(1)} fusion(s32[1024]{0:T(1024)} %param.17), kind=kLoop, calls=%fused_computation.137 | loop fusion | flops 16384 | bytes 20480 | tf_op jit(solution)/shard_map/eq | solution.py:35
  2.2 1.3 %fusion.72 = f32[1024]{0:T(1024)S(1)} fusion(s32[1024]{0:T(1024)} %bitcast.69), kind=kOutput, calls=%fused_computation.74 | convolution fusion | flops 9464832 | bytes 8192 | tf_op jit(solution)/shard_map/dot_general | solution.py:21
  5.4 3.0 %fusion.55 = bf16[1024,128]{1,0:T(8,128)(2,1)S(1)} fusion(bf16[16,128,128]{2,1,0:T(8,128)(2,1)S(1)} %copy-done, pred[1024,16]{0,1:T(8,128)(4,1)S(1)} %iota_compare_fusion.81, bf16[1024,128]{1,0:T(8,128)(2,1)S(1)} %fusion.58), kind=kOutput, calls=%fused_computation.61 | convolution fusion | flops 539099136 | bytes 1064960 | tf_op jit(solution)/shard_map/dot_general | solution.py:21
  8.4 0.9 %fusion.66 = bf16[512,128]{1,0:T(8,128)(2,1)S(1)} fusion(bf16[1024,128]{1,0:T(8,128)(2,1)S(1)} %fusion.55, s32[1024]{0:T(1024)S(1)} %bitcast.66), kind=kOutput, calls=%fused_computation.68 | convolution fusion | flops 134807552 | bytes 397312 | tf_op jit(solution)/shard_map/dot_general | solution.py:25
  9.9 4.1 %collective-permute-start.1 = (bf16[520,128]{1,0:T(8,128)(2,1)S(1)}, bf16[520,128]{1,0:T(8,128)(2,1)S(1)}, u32[]{:S(2)}, u32[]{:S(2)}) collective-permute-start(bf16[520,128]{1,0:T(8,128)(2,1)S(1)} %pad_maximum_fusion.1), channel_id=1, source_target_pairs={{0,8},{4,12},{8,0},{12,4},{1,9},{5,13},{9,1},{13,5},{2,10},{6,14},... | collective-permute-start | bytes 399368 | tf_op jit(solution)/shard_map/ppermute | solution.py:52
  14.0 0.9 %fusion.68 = bf16[512,128]{1,0:T(8,128)(2,1)S(1)} fusion(bf16[1024,128]{1,0:T(8,128)(2,1)S(1)} %fusion.55, s32[1024]{0:T(1024)S(1)} %bitcast.63), kind=kOutput, calls=%fused_computation.70 | convolution fusion | flops 134807552 | bytes 397312 | tf_op jit(solution)/shard_map/dot_general | solution.py:25
  15.4 1.4 %collective-permute-start.2 = (bf16[520,128]{1,0:T(8,128)(2,1)S(1)}, bf16[520,128]{1,0:T(8,128)(2,1)S(1)}, u32[]{:S(2)}, u32[]{:S(2)}) collective-permute-start(bf16[520,128]{1,0:T(8,128)(2,1)S(1)} %pad_maximum_fusion.2), channel_id=1, source_target_pairs={{0,12},{4,0},{8,4},{12,8},{1,13},{5,1},{9,5},{13,9},{2,14},{6,2},{... | collective-permute-start | bytes 399368 | tf_op jit(solution)/shard_map/ppermute | solution.py:52
  16.8 0.9 %fusion.64 = bf16[512,128]{1,0:T(8,128)(2,1)S(1)} fusion(bf16[1024,128]{1,0:T(8,128)(2,1)S(1)} %fusion.55, s32[1024]{0:T(1024)S(1)} %bitcast.56), kind=kOutput, calls=%fused_computation.66 | convolution fusion | flops 134807552 | bytes 397312 | tf_op jit(solution)/shard_map/dot_general | solution.py:25
  18.2 0.9 %collective-permute-start = (bf16[520,128]{1,0:T(8,128)(2,1)S(1)}, bf16[520,128]{1,0:T(8,128)(2,1)S(1)}, u32[]{:S(2)}, u32[]{:S(2)}) collective-permute-start(bf16[520,128]{1,0:T(8,128)(2,1)S(1)} %pad_maximum_fusion), channel_id=1, source_target_pairs={{0,4},{4,8},{8,12},{12,0},{1,5},{5,9},{9,13},{13,1},{2,6},{6,10},{... | collective-permute-start | bytes 399368 | tf_op jit(solution)/shard_map/ppermute | solution.py:52
  19.6 1.5 %fusion.27 = f32[1024,128]{1,0:T(8,128)S(1)} fusion(bf16[1024,128]{1,0:T(8,128)(2,1)S(1)} %fusion.55, s32[512]{0:T(512)S(1)} %bitcast.70, s32[1024]{0:T(1024)S(1)} %bitcast.60), kind=kOutput, calls=%fused_computation.35 | convolution fusion | flops 269549568 | bytes 792576 | tf_op jit(solution)/shard_map/dot_general | solution.py:25
  21.2 0.9 %collective-permute-done.2 = bf16[520,128]{1,0:T(8,128)(2,1)S(1)} collective-permute-done((bf16[520,128]{1,0:T(8,128)(2,1)S(1)}, bf16[520,128]{1,0:T(8,128)(2,1)S(1)}, u32[]{:S(2)}, u32[]{:S(2)}) %collective-permute-start.2) | collective-permute-done | bytes 133152 | tf_op jit(solution)/shard_map/ppermute | solution.py:52
  22.1 3.1 %collective-permute-done = bf16[520,128]{1,0:T(8,128)(2,1)S(1)} collective-permute-done((bf16[520,128]{1,0:T(8,128)(2,1)S(1)}, bf16[520,128]{1,0:T(8,128)(2,1)S(1)}, u32[]{:S(2)}, u32[]{:S(2)}) %collective-permute-start) | collective-permute-done | bytes 133152 | tf_op jit(solution)/shard_map/ppermute | solution.py:52
  25.3 0.8 %fusion.14 = f32[1024,128]{1,0:T(8,128)S(1)} fusion(s32[512]{0:T(512)S(1)} %add_bitcast_fusion.1, bf16[520,128]{1,0:T(8,128)(2,1)S(1)} %collective-permute-done.1), kind=kOutput, calls=%fused_computation.18 | convolution fusion | flops 134742016 | bytes 657408 | tf_op jit(solution)/shard_map/dot_general | solution.py:25
  26.1 0.8 %fusion.9 = f32[1024,128]{1,0:T(8,128)S(1)} fusion(s32[512]{0:T(512)S(1)} %add_bitcast_fusion, bf16[520,128]{1,0:T(8,128)(2,1)S(1)} %collective-permute-done.2), kind=kOutput, calls=%fused_computation.11 | convolution fusion | flops 134742016 | bytes 657408 | tf_op jit(solution)/shard_map/dot_general | solution.py:25
  26.9 0.8 %fusion.48 = f32[1024,128]{1,0:T(8,128)S(1)} fusion(f32[1024,128]{1,0:T(8,128)S(1)} %fusion.9, f32[1024,128]{1,0:T(8,128)S(1)} %fusion.14, f32[1024,128]{1,0:T(8,128)S(1)} %fusion.27, s32[512]{0:T(512)S(1)} %add_bitcast_fusion.2, bf16[520,128]{1,0:T(8,128)(2,1)S(1)} %collective-permute-done), kind=kOutput, calls=%fused_computation.56 | convolution fusion | flops 135135232 | bytes 2230272 | tf_op jit(solution)/shard_map/dot_general | solution.py:25
  27.9 1.9 %collective-permute-done.3 = f32[1024,128]{1,0:T(8,128)S(1)} collective-permute-done((f32[1024,128]{1,0:T(8,128)S(1)}, f32[1024,128]{1,0:T(8,128)S(1)}, u32[]{:S(2)}, u32[]{:S(2)}) %collective-permute-start.3) | collective-permute-done | bytes 524320 | tf_op jit(solution)/shard_map/ppermute | solution.py:43
  29.9 0.5 fusion.65
  30.4 0.5 fusion.67
  30.9 0.5 fusion.69
  31.4 4.4 %collective-permute-start.4 = (bf16[512,128]{1,0:T(8,128)(2,1)S(1)}, bf16[512,128]{1,0:T(8,128)(2,1)S(1)}, u32[]{:S(2)}, u32[]{:S(2)}) collective-permute-start(bf16[512,128]{1,0:T(8,128)(2,1)S(1)} %fusion.65), channel_id=1, source_target_pairs={{0,12},{4,0},{8,4},{12,8},{1,13},{5,1},{9,5},{13,9},{2,14},{6,2},{... | collective-permute-start | bytes 393224 | tf_op jit(solution)/shard_map/ppermute | solution.py:52
  35.8 1.2 %collective-permute-start.6 = (bf16[512,128]{1,0:T(8,128)(2,1)S(1)}, bf16[512,128]{1,0:T(8,128)(2,1)S(1)}, u32[]{:S(2)}, u32[]{:S(2)}) collective-permute-start(bf16[512,128]{1,0:T(8,128)(2,1)S(1)} %fusion.69), channel_id=1, source_target_pairs={{0,4},{4,8},{8,12},{12,0},{1,5},{5,9},{9,13},{13,1},{2,6},{6,10},{... | collective-permute-start | bytes 393224 | tf_op jit(solution)/shard_map/ppermute | solution.py:52
  37.0 1.3 %fusion.28 = f32[1024,128]{1,0:T(8,128)S(1)} fusion(bf16[1024,128]{1,0:T(8,128)(2,1)S(1)} %fusion.118, s32[512]{0:T(512)S(1)} %bitcast.71, s32[1024]{0:T(1024)S(1)} %bitcast.61), kind=kOutput, calls=%fused_computation.37 | convolution fusion | flops 269549568 | bytes 792576 | tf_op jit(solution)/shard_map/dot_general | solution.py:21
  38.3 9.3 %collective-permute-done.5 = bf16[512,128]{1,0:T(8,128)(2,1)S(1)} collective-permute-done((bf16[512,128]{1,0:T(8,128)(2,1)S(1)}, bf16[512,128]{1,0:T(8,128)(2,1)S(1)}, u32[]{:S(2)}, u32[]{:S(2)}) %collective-permute-start.5) | collective-permute-done | bytes 131104 | tf_op jit(solution)/shard_map/ppermute | solution.py:52
  47.6 0.5 fusion.15
  48.6 0.5 fusion.51
  49.2 2.6 %fusion.52 = bf16[1024,128]{1,0:T(8,128)(2,1)S(1)} fusion(pred[1024,16]{0,1:T(8,128)(4,1)S(1)} %iota_compare_fusion.81, bf16[1024,128]{1,0:T(8,128)(2,1)S(1)} %fusion.51, bf16[16,128,128]{2,1,0:T(8,128)(2,1)S(1)} %copy-done), kind=kOutput, calls=%fused_computation.60 | convolution fusion | flops 539099136 | bytes 1064960 | tf_op jit(solution)/shard_map/dot_general | solution.py:21
  51.8 1.0 %fusion.59 = bf16[512,128]{1,0:T(8,128)(2,1)S(1)} fusion(bf16[1024,128]{1,0:T(8,128)(2,1)S(1)} %fusion.52, s32[512]{0:T(512)S(1)} %get-tuple-element.14, s32[512]{0:T(512)S(1)} %get-tuple-element.15, s32[1024]{0:T(1024)S(1)} %copy-done.7, s32[1024]{0:T(1024)S(1)} %bitcast.54), kind=kOutput, calls=%fused_computation.63 | convolution fusion | flops 135856128 | bytes 405504 | tf_op jit(solution)/shard_map/dot_general | solution.py:25
  52.9 1.6 %collective-permute-start.7 = (bf16[128,512]{1,0:T(8,128)(2,1)S(1)}, bf16[128,512]{1,0:T(8,128)(2,1)S(1)}, u32[]{:S(2)}, u32[]{:S(2)}) collective-permute-start(bf16[128,512]{1,0:T(8,128)(2,1)S(1)} %convert_element_type.156), channel_id=1, source_target_pairs={{0,2},{2,0},{1,3},{3,1},{4,6},{6,4},{5,7},{7,5},{8,10},{10,8},{9,1... | collective-permute-start | bytes 393224 | tf_op jit(solution)/shard_map/ppermute | solution.py:139
  54.4 1.0 %fusion.35 = f32[512,128]{1,0:T(8,128)S(1)} fusion(bf16[1024,128]{1,0:T(8,128)(2,1)S(1)} %fusion.52, s32[512]{0:T(512)S(1)} %get-tuple-element.12, s32[512]{0:T(512)S(1)} %get-tuple-element.13, s32[1024]{0:T(1024)S(1)} %copy-done.7, s32[1024]{0:T(1024)S(1)} %bitcast.55), kind=kOutput, calls=%fused_computation.44 | convolution fusion | flops 135790592 | bytes 536576 | tf_op jit(solution)/shard_map/dot_general | solution.py:25
  55.5 2.4 %collective-permute-done.7 = bf16[128,512]{1,0:T(8,128)(2,1)S(1)} collective-permute-done((bf16[128,512]{1,0:T(8,128)(2,1)S(1)}, bf16[128,512]{1,0:T(8,128)(2,1)S(1)}, u32[]{:S(2)}, u32[]{:S(2)}) %collective-permute-start.7) | collective-permute-done | bytes 131104 | tf_op jit(solution)/shard_map/ppermute | solution.py:139
  57.9 0.7 %convert_add_fusion = f32[128,512]{1,0:T(8,128)} fusion(f32[128,512]{1,0:T(8,128)S(1)} %reshape.261, bf16[128,512]{1,0:T(8,128)(2,1)S(1)} %collective-permute-done.7), kind=kLoop, calls=%fused_computation.126 | loop fusion | flops 131072 | bytes 655360 | tf_op jit(solution)/shard_map/add | solution.py:141
  (57 shorter events, 4.9 us)
Async XLA Ops:
  0.6 4.8 %copy-start = (bf16[16,128,128]{2,1,0:T(8,128)(2,1)S(1)}, bf16[16,128,128]{2,1,0:T(8,128)(2,1)}, u32[]{:S(2)}) copy-start(bf16[16,128,128]{2,1,0:T(8,128)(2,1)} %param.10) | copy-start | bytes 1572868
  2.1 1.3 %copy-start.8 = (s32[1024,1]{0,1:T(1,128)S(1)}, s32[1024,1]{0,1:T(1,128)}, u32[]{:S(2)}) copy-start(s32[1024,1]{0,1:T(1,128)} %param.13) | copy-start | bytes 12292
  2.1 1.4 %copy-start.6 = (s32[1024]{0:T(1024)S(1)}, s32[1024]{0:T(1024)}, u32[]{:S(2)}) copy-start(s32[1024]{0:T(1024)} %param.14) | copy-start | bytes 12292
  2.1 1.4 %copy-start.4 = (bf16[256,512]{1,0:T(8,128)(2,1)S(1)}, bf16[256,512]{1,0:T(8,128)(2,1)}, u32[]{:S(2)}) copy-start(bf16[256,512]{1,0:T(8,128)(2,1)} %param.9) | copy-start | bytes 786436
  2.1 1.4 %copy-start.5 = (s32[1024,1]{0,1:T(1,128)S(1)}, s32[1024,1]{0,1:T(1,128)}, u32[]{:S(2)}) copy-start(s32[1024,1]{0,1:T(1,128)} %param.15) | copy-start | bytes 12292
  9.9 11.3 %collective-permute-start.1 = (bf16[520,128]{1,0:T(8,128)(2,1)S(1)}, bf16[520,128]{1,0:T(8,128)(2,1)S(1)}, u32[]{:S(2)}, u32[]{:S(2)}) collective-permute-start(bf16[520,128]{1,0:T(8,128)(2,1)S(1)} %pad_maximum_fusion.1), channel_id=1, source_target_pairs={{0,8},{4,12},{8,0},{12,4},{1,9},{5,13},{9,1},{13,5},{2,10},{6,14},... | collective-permute-start | bytes 399368 | tf_op jit(solution)/shard_map/ppermute | solution.py:52
  15.4 6.8 %collective-permute-start.2 = (bf16[520,128]{1,0:T(8,128)(2,1)S(1)}, bf16[520,128]{1,0:T(8,128)(2,1)S(1)}, u32[]{:S(2)}, u32[]{:S(2)}) collective-permute-start(bf16[520,128]{1,0:T(8,128)(2,1)S(1)} %pad_maximum_fusion.2), channel_id=1, source_target_pairs={{0,12},{4,0},{8,4},{12,8},{1,13},{5,1},{9,5},{13,9},{2,14},{6,2},{... | collective-permute-start | bytes 399368 | tf_op jit(solution)/shard_map/ppermute | solution.py:52
  18.2 7.1 %collective-permute-start = (bf16[520,128]{1,0:T(8,128)(2,1)S(1)}, bf16[520,128]{1,0:T(8,128)(2,1)S(1)}, u32[]{:S(2)}, u32[]{:S(2)}) collective-permute-start(bf16[520,128]{1,0:T(8,128)(2,1)S(1)} %pad_maximum_fusion), channel_id=1, source_target_pairs={{0,4},{4,8},{8,12},{12,0},{1,5},{5,9},{9,13},{13,1},{2,6},{6,10},{... | collective-permute-start | bytes 399368 | tf_op jit(solution)/shard_map/ppermute | solution.py:52
  26.9 2.8 %copy-start.1 = (s32[1,1024,128]{2,1,0:T(8,128)S(1)}, s32[1,1024,128]{2,1,0:T(8,128)}, u32[]{:S(2)}) copy-start(s32[1,1024,128]{2,1,0:T(8,128)} %param.12) | copy-start | bytes 1572868
  26.9 2.8 %copy-start.2 = (bf16[1,1024,128]{2,1,0:T(8,128)(2,1)S(1)}, bf16[1,1024,128]{2,1,0:T(8,128)(2,1)}, u32[]{:S(2)}) copy-start(bf16[1,1024,128]{2,1,0:T(8,128)(2,1)} %param.11) | copy-start | bytes 786436
  27.8 2.0 %collective-permute-start.3 = (f32[1024,128]{1,0:T(8,128)S(1)}, f32[1024,128]{1,0:T(8,128)S(1)}, u32[]{:S(2)}, u32[]{:S(2)}) collective-permute-start(f32[1024,128]{1,0:T(8,128)S(1)} %fusion.48), channel_id=1, source_target_pairs={{0,1},{1,0},{2,3},{3,2},{4,5},{5,4},{6,7},{7,6},{8,9},{9,8},{10,11... | collective-permute-start | bytes 1572872 | tf_op jit(solution)/shard_map/ppermute | solution.py:43
  29.9 7.1 %copy-start.3 = (bf16[1024,128]{1,0:T(8,128)(2,1)}, bf16[1024,128]{1,0:T(8,128)(2,1)S(1)}, u32[]{:S(2)}) copy-start(bf16[1024,128]{1,0:T(8,128)(2,1)S(1)} %fusion.118) | copy-start | bytes 786436
  31.4 17.2 %collective-permute-start.4 = (bf16[512,128]{1,0:T(8,128)(2,1)S(1)}, bf16[512,128]{1,0:T(8,128)(2,1)S(1)}, u32[]{:S(2)}, u32[]{:S(2)}) collective-permute-start(bf16[512,128]{1,0:T(8,128)(2,1)S(1)} %fusion.65), channel_id=1, source_target_pairs={{0,12},{4,0},{8,4},{12,8},{1,13},{5,1},{9,5},{13,9},{2,14},{6,2},{... | collective-permute-start | bytes 393224 | tf_op jit(solution)/shard_map/ppermute | solution.py:52
  35.8 11.8 %collective-permute-start.5 = (bf16[512,128]{1,0:T(8,128)(2,1)S(1)}, bf16[512,128]{1,0:T(8,128)(2,1)S(1)}, u32[]{:S(2)}, u32[]{:S(2)}) collective-permute-start(bf16[512,128]{1,0:T(8,128)(2,1)S(1)} %fusion.67), channel_id=1, source_target_pairs={{0,8},{4,12},{8,0},{12,4},{1,9},{5,13},{9,1},{13,5},{2,10},{6,14},... | collective-permute-start | bytes 393224 | tf_op jit(solution)/shard_map/ppermute | solution.py:52
  35.8 12.3 %collective-permute-start.6 = (bf16[512,128]{1,0:T(8,128)(2,1)S(1)}, bf16[512,128]{1,0:T(8,128)(2,1)S(1)}, u32[]{:S(2)}, u32[]{:S(2)}) collective-permute-start(bf16[512,128]{1,0:T(8,128)(2,1)S(1)} %fusion.69), channel_id=1, source_target_pairs={{0,4},{4,8},{8,12},{12,0},{1,5},{5,9},{9,13},{13,1},{2,6},{6,10},{... | collective-permute-start | bytes 393224 | tf_op jit(solution)/shard_map/ppermute | solution.py:52
  49.1 2.6 %copy-start.7 = (s32[1024]{0:T(1024)S(1)}, s32[1024]{0:T(1024)}, u32[]{:S(2)}) copy-start(s32[1024]{0:T(1024)} %param.16) | copy-start | bytes 12292
  52.9 5.0 %collective-permute-start.7 = (bf16[128,512]{1,0:T(8,128)(2,1)S(1)}, bf16[128,512]{1,0:T(8,128)(2,1)S(1)}, u32[]{:S(2)}, u32[]{:S(2)}) collective-permute-start(bf16[128,512]{1,0:T(8,128)(2,1)S(1)} %convert_element_type.156), channel_id=1, source_target_pairs={{0,2},{2,0},{1,3},{3,1},{4,6},{6,4},{5,7},{7,5},{8,10},{10,8},{9,1... | collective-permute-start | bytes 393224 | tf_op jit(solution)/shard_map/ppermute | solution.py:139

commit v18 on v14

--- a/solution.py
+++ b/solution.py
@@ -99,13 +99,12 @@
         send.append(jnp.concatenate([block, codes.reshape(code_rows, pixel_count)], axis=0))
     got = exchange(send, "tile", 1)
     got_traces = [block[:capacity] for block in got]
-    got_slots = []
+    at_slot = []
     for block in got:
         codes = block[capacity:].reshape(code_rows * pixel_count)[: 2 * capacity]
         codes = codes.astype(jnp.int32).reshape(2, capacity)
-        got_slots.append(codes[0] * 256 + codes[1])
+        at_slot.append(row_hot(codes[0], codes[1], 256, 0, slot_count))
 
-    at_slot = [one_hot_rows(slots, slot_count) for slots in got_slots]
     partial_value = sum(select_dot_t(a, b) for a, b in zip(at_slot, got_traces))
     model_image = swap_add(partial_value, "band")
     residual = (

time: 55.5 us -> 58.5 us (1.054); the launches traced: 54.4 us -> 58.2 us
  waiting for transfers between devices: 14.9 us -> 19.9 us
  starting transfers between devices: 13.6 us -> 11.1 us
  matrix products: 22.3 us -> 23.6 us
  other arithmetic: 1.03 us -> 1.75 us
  local copies, waits for them, and re-layouts: 1.52 us -> 0.88 us
    ppermute x6, waiting for transfers between devices: 10.7 us -> 15.6 us  [exchange(): moved.append(lax.ppermute(blocks[step], axis, pairs))]
    ppermute x6, starting transfers between devices: 12 us -> 9.45 us  [exchange(): moved.append(lax.ppermute(blocks[step], axis, pairs))]
    dot_general x11, matrix products: 11.7 us -> 12.7 us  [select_dot(): jnp.dot(selector, values, preferred_element_type=jnp.float32, precision=p...]
    reshape x1, local copies, waits for them, and re-layouts: 1.17 us -> 0.16 us  [per_device(): spectra.reshape(row_count, bin_count)]
    another operation x1, other arithmetic: 0.01 us -> 0.75 us
  transfers between devices with their start and end apart: 8 -> 8, of which waited for: 7 -> 5; matrix products, arithmetic and copies ran while one was open for 15% -> 14% of each run, Pallas kernels for 0% -> 0%
where the time goes in v18:
time: 58.5 us; the launch traced here: 58.2 us
  matrix products  23.6 us (40%)
  waiting for transfers between devices  19.9 us (34%)
  starting transfers between devices  11.1 us (19%)
  other arithmetic  1.75 us (3%)
  between operations  1.04 us (2%)
  local copies, waits for them, and re-layouts  0.88 us (2%)
    ppermute x6, waiting for transfers between devices, exchange(): moved.append(lax.ppermute(blocks[step], axis, pairs))  15.6 us
    dot_general x11, matrix products, select_dot(): jnp.dot(selector, values, preferred_element_type=jnp.float32, precision=p...  12.7 us
    dot_general x13, matrix products, select_dot_t(): lax.dot_general(selector, values, (((0,), (0,)), ((), ())), preferred_ele...  10.9 us
    ppermute x6, starting transfers between devices, exchange(): moved.append(lax.ppermute(blocks[step], axis, pairs))  9.45 us
    ppermute x1, waiting for transfers between devices, per_device(): sent = lax.ppermute(theirs.astype(jnp.bfloat16), 'dither', [(0, 1), (1, 0)])  2.4 us
    ppermute x1, waiting for transfers between devices, swap_add(): return value + lax.ppermute(value, axis, [(0, 1), (1, 0)])  1.86 us
    ppermute x1, starting transfers between devices, per_device(): sent = lax.ppermute(theirs.astype(jnp.bfloat16), 'dither', [(0, 1), (1, 0)])  1.56 us
  transfers between devices with their start and end apart: 8, of which 5 were waited for; matrix products, arithmetic and copies ran while one was open for 14% of the time, Pallas kernels for 0%

profile of v18, /device:TPU:0, one launch (start us, length us, event | category | flops | bytes accessed | tf_op | source)
XLA Modules:
  0.0 58.2 jit_solution(924874793039664045)
XLA Ops:
  0.7 0.8 %fusion.163 = (bf16[1024]{0:T(1024)(128)(2,1)S(1)}, bf16[1024]{0:T(1024)(128)(2,1)S(1)}) fusion(s32[1024]{0:T(1024)} %param.14), kind=kLoop, calls=%fused_computation.178 | loop fusion | flops 21504 | bytes 8192 | tf_op jit(solution)/shard_map/convert.4
  1.4 1.2 %fusion.82 = f32[1024]{0:T(1024)S(1)} fusion(s32[1024]{0:T(1024)} %bitcast.68), kind=kOutput, calls=%fused_computation.79 | convolution fusion | flops 9464832 | bytes 8192 | tf_op jit(solution)/shard_map/dot_general | solution.py:19
  3.5 1.3 %fusion.66 = bf16[1024,128]{1,0:T(8,128)(2,1)S(1)} fusion(bf16[1024,128]{1,0:T(8,128)(2,1)S(1)} %reshape.328, s32[1024]{0:T(1024)S(1)} %get-tuple-element.16, s32[1024]{0:T(1024)S(1)} %get-tuple-element.17, s32[1024]{0:T(1024)S(1)} %copy-done.7, s32[1024]{0:T(1024)S(1)} %bitcast.76), kind=kOutput, calls=%fused_computation.67 | convolution fusion | flops 271712256 | bytes 540672 | tf_op jit(solution)/shard_map/dot_general | solution.py:19
  4.8 3.0 %fusion.63 = bf16[1024,128]{1,0:T(8,128)(2,1)S(1)} fusion(bf16[16,128,128]{2,1,0:T(8,128)(2,1)S(1)} %copy-done, pred[1024,16]{0,1:T(8,128)(4,1)S(1)} %iota_compare_fusion.52, bf16[1024,128]{1,0:T(8,128)(2,1)S(1)} %fusion.66), kind=kOutput, calls=%fused_computation.66 | convolution fusion | flops 539099136 | bytes 1064960 | tf_op jit(solution)/shard_map/dot_general | solution.py:19
  7.8 0.9 %fusion.77 = bf16[512,128]{1,0:T(8,128)(2,1)S(1)} fusion(bf16[1024,128]{1,0:T(8,128)(2,1)S(1)} %fusion.63, s32[1024]{0:T(1024)S(1)} %bitcast.58), kind=kOutput, calls=%fused_computation.74 | convolution fusion | flops 134807552 | bytes 397312 | tf_op jit(solution)/shard_map/dot_general | solution.py:23
  9.2 3.1 %collective-permute-start = (bf16[520,128]{1,0:T(8,128)(2,1)S(1)}, bf16[520,128]{1,0:T(8,128)(2,1)S(1)}, u32[]{:S(2)}, u32[]{:S(2)}) collective-permute-start(bf16[520,128]{1,0:T(8,128)(2,1)S(1)} %pad_maximum_fusion), channel_id=1, source_target_pairs={{0,4},{4,8},{8,12},{12,0},{1,5},{5,9},{9,13},{13,1},{2,6},{6,10},{... | collective-permute-start | bytes 399368 | tf_op jit(solution)/shard_map/ppermute | solution.py:50
  12.3 0.9 %fusion.79 = bf16[512,128]{1,0:T(8,128)(2,1)S(1)} fusion(bf16[1024,128]{1,0:T(8,128)(2,1)S(1)} %fusion.63, s32[1024]{0:T(1024)S(1)} %bitcast.65), kind=kOutput, calls=%fused_computation.76 | convolution fusion | flops 134807552 | bytes 397312 | tf_op jit(solution)/shard_map/dot_general | solution.py:23
  13.7 2.3 %collective-permute-start.2 = (bf16[520,128]{1,0:T(8,128)(2,1)S(1)}, bf16[520,128]{1,0:T(8,128)(2,1)S(1)}, u32[]{:S(2)}, u32[]{:S(2)}) collective-permute-start(bf16[520,128]{1,0:T(8,128)(2,1)S(1)} %pad_maximum_fusion.2), channel_id=1, source_target_pairs={{0,12},{4,0},{8,4},{12,8},{1,13},{5,1},{9,5},{13,9},{2,14},{6,2},{... | collective-permute-start | bytes 399368 | tf_op jit(solution)/shard_map/ppermute | solution.py:50
  16.0 0.9 %fusion.78 = bf16[512,128]{1,0:T(8,128)(2,1)S(1)} fusion(bf16[1024,128]{1,0:T(8,128)(2,1)S(1)} %fusion.63, s32[1024]{0:T(1024)S(1)} %bitcast.69), kind=kOutput, calls=%fused_computation.75 | convolution fusion | flops 134807552 | bytes 397312 | tf_op jit(solution)/shard_map/dot_general | solution.py:23
  17.4 1.1 %collective-permute-start.1 = (bf16[520,128]{1,0:T(8,128)(2,1)S(1)}, bf16[520,128]{1,0:T(8,128)(2,1)S(1)}, u32[]{:S(2)}, u32[]{:S(2)}) collective-permute-start(bf16[520,128]{1,0:T(8,128)(2,1)S(1)} %pad_maximum_fusion.1), channel_id=1, source_target_pairs={{0,8},{4,12},{8,0},{12,4},{1,9},{5,13},{9,1},{13,5},{2,10},{6,14},... | collective-permute-start | bytes 399368 | tf_op jit(solution)/shard_map/ppermute | solution.py:50
  18.9 1.6 %fusion.40 = f32[1024,128]{1,0:T(8,128)S(1)} fusion(bf16[1024,128]{1,0:T(8,128)(2,1)S(1)} %fusion.63, s32[1024]{0:T(1024)S(1)} %get-tuple-element.18, s32[1024]{0:T(1024)S(1)} %get-tuple-element.19, s32[1024]{0:T(1024)S(1)} %bitcast.62, s32[512]{0:T(512)S(1)} %bitcast.74, s32[512]{0:T(512)S(1)} %bitcast.72), kind=kOutput, calls=%fused_computation.49 | convolution fusion | flops 270598144 | bytes 802816 | tf_op jit(solution)/shard_map/dot_general | solution.py:23
  20.7 5.7 %collective-permute-done.1 = bf16[520,128]{1,0:T(8,128)(2,1)S(1)} collective-permute-done((bf16[520,128]{1,0:T(8,128)(2,1)S(1)}, bf16[520,128]{1,0:T(8,128)(2,1)S(1)}, u32[]{:S(2)}, u32[]{:S(2)}) %collective-permute-start.1) | collective-permute-done | bytes 133152 | tf_op jit(solution)/shard_map/ppermute | solution.py:50
  26.4 0.9 %fusion.46 = f32[1024,128]{1,0:T(8,128)S(1)} fusion(s32[1024]{0:T(1024)S(1)} %get-tuple-element.18, s32[1024]{0:T(1024)S(1)} %get-tuple-element.19, s32[512]{0:T(512)S(1)} %get-tuple-element.13, s32[512]{0:T(512)S(1)} %get-tuple-element.12, bf16[520,128]{1,0:T(8,128)(2,1)S(1)} %collective-permute-done.2), kind=kOutput, calls=%fused_computation.55 | convolution fusion | flops 135790592 | bytes 667648 | tf_op jit(solution)/shard_map/dot_general | solution.py:23
  27.3 0.9 %fusion.58 = f32[1024,128]{1,0:T(8,128)S(1)} fusion(f32[1024,128]{1,0:T(8,128)S(1)} %fusion.40, s32[1024]{0:T(1024)S(1)} %get-tuple-element.18, s32[1024]{0:T(1024)S(1)} %get-tuple-element.19, s32[512]{0:T(512)S(1)} %get-tuple-element.7, s32[512]{0:T(512)S(1)} %get-tuple-element.6, bf16[520,128]{1,0:T(8,128)(2,1)S(1)} %collective-permute-done), kind=kOutput, calls=%fused_computation.63 | convolution fusion | flops 135921664 | bytes 1191936 | tf_op jit(solution)/shard_map/dot_general | solution.py:23
  28.2 0.9 %fusion.57 = f32[1024,128]{1,0:T(8,128)S(1)} fusion(f32[1024,128]{1,0:T(8,128)S(1)} %fusion.46, f32[1024,128]{1,0:T(8,128)S(1)} %fusion.58, s32[1024]{0:T(1024)S(1)} %get-tuple-element.18, s32[1024]{0:T(1024)S(1)} %get-tuple-element.19, s32[512]{0:T(512)S(1)} %get-tuple-element.5, s32[512]{0:T(512)S(1)} %get-tuple-element.4, ...), kind=kOutput, calls=%fused_computation.62 | convolution fusion | flops 136052736 | bytes 1716224 | tf_op jit(solution)/shard_map/dot_general | solution.py:23
  29.2 1.9 %collective-permute-done.3 = f32[1024,128]{1,0:T(8,128)S(1)} collective-permute-done((f32[1024,128]{1,0:T(8,128)S(1)}, f32[1024,128]{1,0:T(8,128)S(1)}, u32[]{:S(2)}, u32[]{:S(2)}) %collective-permute-start.3) | collective-permute-done | bytes 524320 | tf_op jit(solution)/shard_map/ppermute | solution.py:41
  31.2 0.6 %fusion.71 = bf16[512,128]{1,0:T(8,128)(2,1)S(1)} fusion(bf16[1024,128]{1,0:T(8,128)(2,1)S(1)} %fusion.146, s32[1024]{0:T(1024)S(1)} %get-tuple-element.18, s32[1024]{0:T(1024)S(1)} %get-tuple-element.19, s32[512]{0:T(512)S(1)} %get-tuple-element.7, s32[512]{0:T(512)S(1)} %get-tuple-element.6), kind=kOutput, calls=%fused_computation.70 | convolution fusion | flops 135856128 | bytes 405504 | tf_op jit(solution)/shard_map/dot_general | solution.py:19
  31.8 0.6 %fusion.70 = bf16[512,128]{1,0:T(8,128)(2,1)S(1)} fusion(bf16[1024,128]{1,0:T(8,128)(2,1)S(1)} %fusion.146, s32[1024]{0:T(1024)S(1)} %get-tuple-element.18, s32[1024]{0:T(1024)S(1)} %get-tuple-element.19, s32[512]{0:T(512)S(1)} %get-tuple-element.5, s32[512]{0:T(512)S(1)} %get-tuple-element.4), kind=kOutput, calls=%fused_computation.69 | convolution fusion | flops 135856128 | bytes 405504 | tf_op jit(solution)/shard_map/dot_general | solution.py:19
  32.4 0.6 %fusion.69 = bf16[512,128]{1,0:T(8,128)(2,1)S(1)} fusion(bf16[1024,128]{1,0:T(8,128)(2,1)S(1)} %fusion.146, s32[1024]{0:T(1024)S(1)} %get-tuple-element.18, s32[1024]{0:T(1024)S(1)} %get-tuple-element.19, s32[512]{0:T(512)S(1)} %get-tuple-element.13, s32[512]{0:T(512)S(1)} %get-tuple-element.12), kind=kOutput, calls=%fused_computation.68 | convolution fusion | flops 135856128 | bytes 405504 | tf_op jit(solution)/shard_map/dot_general | solution.py:19
  33.0 2.4 %collective-permute-start.4 = (bf16[512,128]{1,0:T(8,128)(2,1)S(1)}, bf16[512,128]{1,0:T(8,128)(2,1)S(1)}, u32[]{:S(2)}, u32[]{:S(2)}) collective-permute-start(bf16[512,128]{1,0:T(8,128)(2,1)S(1)} %fusion.71), channel_id=1, source_target_pairs={{0,12},{4,0},{8,4},{12,8},{1,13},{5,1},{9,5},{13,9},{2,14},{6,2},{... | collective-permute-start | bytes 393224 | tf_op jit(solution)/shard_map/ppermute | solution.py:50
  35.4 0.6 %collective-permute-start.6 = (bf16[512,128]{1,0:T(8,128)(2,1)S(1)}, bf16[512,128]{1,0:T(8,128)(2,1)S(1)}, u32[]{:S(2)}, u32[]{:S(2)}) collective-permute-start(bf16[512,128]{1,0:T(8,128)(2,1)S(1)} %fusion.69), channel_id=1, source_target_pairs={{0,4},{4,8},{8,12},{12,0},{1,5},{5,9},{9,13},{13,1},{2,6},{6,10},{... | collective-permute-start | bytes 393224 | tf_op jit(solution)/shard_map/ppermute | solution.py:50
  36.1 1.3 %fusion.26 = f32[1024,128]{1,0:T(8,128)S(1)} fusion(bf16[1024,128]{1,0:T(8,128)(2,1)S(1)} %fusion.146, s32[1024]{0:T(1024)S(1)} %get-tuple-element.18, s32[1024]{0:T(1024)S(1)} %get-tuple-element.19, s32[1024]{0:T(1024)S(1)} %bitcast.63, s32[512]{0:T(512)S(1)} %bitcast.75, s32[512]{0:T(512)S(1)} %bitcast.73), kind=kOutput, calls=%fused_computation.31 | convolution fusion | flops 270598144 | bytes 802816 | tf_op jit(solution)/shard_map/dot_general | solution.py:19
  37.4 9.8 %collective-permute-done.5 = bf16[512,128]{1,0:T(8,128)(2,1)S(1)} collective-permute-done((bf16[512,128]{1,0:T(8,128)(2,1)S(1)}, bf16[512,128]{1,0:T(8,128)(2,1)S(1)}, u32[]{:S(2)}, u32[]{:S(2)}) %collective-permute-start.5) | collective-permute-done | bytes 131104 | tf_op jit(solution)/shard_map/ppermute | solution.py:50
  47.2 0.5 fusion.15
  47.7 0.5 fusion.12
  48.2 0.5 fusion.59
  48.8 2.6 %fusion.60 = bf16[1024,128]{1,0:T(8,128)(2,1)S(1)} fusion(pred[1024,16]{0,1:T(8,128)(4,1)S(1)} %iota_compare_fusion.52, bf16[1024,128]{1,0:T(8,128)(2,1)S(1)} %fusion.59, bf16[16,128,128]{2,1,0:T(8,128)(2,1)S(1)} %copy-done), kind=kOutput, calls=%fused_computation.65 | convolution fusion | flops 539099136 | bytes 1064960 | tf_op jit(solution)/shard_map/dot_general | solution.py:19
  51.3 1.0 %fusion.73 = bf16[512,128]{1,0:T(8,128)(2,1)S(1)} fusion(bf16[1024,128]{1,0:T(8,128)(2,1)S(1)} %fusion.60, s32[512]{0:T(512)S(1)} %get-tuple-element.22, s32[512]{0:T(512)S(1)} %get-tuple-element.23, s32[1024]{0:T(1024)S(1)} %copy-done.7, s32[1024]{0:T(1024)S(1)} %bitcast.77), kind=kOutput, calls=%fused_computation.72 | convolution fusion | flops 135856128 | bytes 405504 | tf_op jit(solution)/shard_map/dot_general | solution.py:23
  52.5 1.6 %collective-permute-start.7 = (bf16[128,512]{1,0:T(8,128)(2,1)S(1)}, bf16[128,512]{1,0:T(8,128)(2,1)S(1)}, u32[]{:S(2)}, u32[]{:S(2)}) collective-permute-start(bf16[128,512]{1,0:T(8,128)(2,1)S(1)} %convert_element_type.153), channel_id=1, source_target_pairs={{0,2},{2,0},{1,3},{3,1},{4,6},{6,4},{5,7},{7,5},{8,10},{10,8},{9,1... | collective-permute-start | bytes 393224 | tf_op jit(solution)/shard_map/ppermute | solution.py:128
  54.0 1.0 %fusion.35 = f32[512,128]{1,0:T(8,128)S(1)} fusion(bf16[1024,128]{1,0:T(8,128)(2,1)S(1)} %fusion.60, s32[512]{0:T(512)S(1)} %get-tuple-element.20, s32[512]{0:T(512)S(1)} %get-tuple-element.21, s32[1024]{0:T(1024)S(1)} %copy-done.7, s32[1024]{0:T(1024)S(1)} %bitcast.78), kind=kOutput, calls=%fused_computation.44 | convolution fusion | flops 135790592 | bytes 536576 | tf_op jit(solution)/shard_map/dot_general | solution.py:23
  55.1 2.4 %collective-permute-done.7 = bf16[128,512]{1,0:T(8,128)(2,1)S(1)} collective-permute-done((bf16[128,512]{1,0:T(8,128)(2,1)S(1)}, bf16[128,512]{1,0:T(8,128)(2,1)S(1)}, u32[]{:S(2)}, u32[]{:S(2)}) %collective-permute-start.7) | collective-permute-done | bytes 131104 | tf_op jit(solution)/shard_map/ppermute | solution.py:128
  57.5 0.7 %convert_add_fusion = f32[128,512]{1,0:T(8,128)} fusion(f32[128,512]{1,0:T(8,128)S(1)} %reshape.332, bf16[128,512]{1,0:T(8,128)(2,1)S(1)} %collective-permute-done.7), kind=kLoop, calls=%fused_computation.141 | loop fusion | flops 131072 | bytes 655360 | tf_op jit(solution)/shard_map/add | solution.py:130
  (56 shorter events, 3.3 us)
Async XLA Ops:
  0.6 4.2 %copy-start = (bf16[16,128,128]{2,1,0:T(8,128)(2,1)S(1)}, bf16[16,128,128]{2,1,0:T(8,128)(2,1)}, u32[]{:S(2)}) copy-start(bf16[16,128,128]{2,1,0:T(8,128)(2,1)} %param.10) | copy-start | bytes 1572868
  1.4 1.3 %copy-start.2 = (bf16[256,512]{1,0:T(8,128)(2,1)S(1)}, bf16[256,512]{1,0:T(8,128)(2,1)}, u32[]{:S(2)}) copy-start(bf16[256,512]{1,0:T(8,128)(2,1)} %param.9) | copy-start | bytes 786436
  2.7 0.7 %copy-start.5 = (s32[1024]{0:T(1024)S(1)}, s32[1024]{0:T(1024)}, u32[]{:S(2)}) copy-start(s32[1024]{0:T(1024)} %param.17) | copy-start | bytes 12292
  2.7 0.7 %copy-start.6 = (s32[1024,1]{0,1:T(1,128)S(1)}, s32[1024,1]{0,1:T(1,128)}, u32[]{:S(2)}) copy-start(s32[1024,1]{0,1:T(1,128)} %param.13) | copy-start | bytes 12292
  2.7 0.8 %copy-start.7 = (s32[1024]{0:T(1024)S(1)}, s32[1024]{0:T(1024)}, u32[]{:S(2)}) copy-start(s32[1024]{0:T(1024)} %param.16) | copy-start | bytes 12292
  2.7 0.8 %copy-start.8 = (s32[1024,1]{0,1:T(1,128)S(1)}, s32[1024,1]{0,1:T(1,128)}, u32[]{:S(2)}) copy-start(s32[1024,1]{0,1:T(1,128)} %param.15) | copy-start | bytes 12292
  9.2 11.3 %collective-permute-start = (bf16[520,128]{1,0:T(8,128)(2,1)S(1)}, bf16[520,128]{1,0:T(8,128)(2,1)S(1)}, u32[]{:S(2)}, u32[]{:S(2)}) collective-permute-start(bf16[520,128]{1,0:T(8,128)(2,1)S(1)} %pad_maximum_fusion), channel_id=1, source_target_pairs={{0,4},{4,8},{8,12},{12,0},{1,5},{5,9},{9,13},{13,1},{2,6},{6,10},{... | collective-permute-start | bytes 399368 | tf_op jit(solution)/shard_map/ppermute | solution.py:50
  13.7 7.0 %collective-permute-start.2 = (bf16[520,128]{1,0:T(8,128)(2,1)S(1)}, bf16[520,128]{1,0:T(8,128)(2,1)S(1)}, u32[]{:S(2)}, u32[]{:S(2)}) collective-permute-start(bf16[520,128]{1,0:T(8,128)(2,1)S(1)} %pad_maximum_fusion.2), channel_id=1, source_target_pairs={{0,12},{4,0},{8,4},{12,8},{1,13},{5,1},{9,5},{13,9},{2,14},{6,2},{... | collective-permute-start | bytes 399368 | tf_op jit(solution)/shard_map/ppermute | solution.py:50
  17.4 9.0 %collective-permute-start.1 = (bf16[520,128]{1,0:T(8,128)(2,1)S(1)}, bf16[520,128]{1,0:T(8,128)(2,1)S(1)}, u32[]{:S(2)}, u32[]{:S(2)}) collective-permute-start(bf16[520,128]{1,0:T(8,128)(2,1)S(1)} %pad_maximum_fusion.1), channel_id=1, source_target_pairs={{0,8},{4,12},{8,0},{12,4},{1,9},{5,13},{9,1},{13,5},{2,10},{6,14},... | collective-permute-start | bytes 399368 | tf_op jit(solution)/shard_map/ppermute | solution.py:50
  28.2 2.9 %copy-start.1 = (s32[1,1024,128]{2,1,0:T(8,128)S(1)}, s32[1,1024,128]{2,1,0:T(8,128)}, u32[]{:S(2)}) copy-start(s32[1,1024,128]{2,1,0:T(8,128)} %param.12) | copy-start | bytes 1572868
  28.2 2.9 %copy-start.3 = (bf16[1,1024,128]{2,1,0:T(8,128)(2,1)S(1)}, bf16[1,1024,128]{2,1,0:T(8,128)(2,1)}, u32[]{:S(2)}) copy-start(bf16[1,1024,128]{2,1,0:T(8,128)(2,1)} %param.11) | copy-start | bytes 786436
  29.1 2.0 %collective-permute-start.3 = (f32[1024,128]{1,0:T(8,128)S(1)}, f32[1024,128]{1,0:T(8,128)S(1)}, u32[]{:S(2)}, u32[]{:S(2)}) collective-permute-start(f32[1024,128]{1,0:T(8,128)S(1)} %fusion.57), channel_id=1, source_target_pairs={{0,1},{1,0},{2,3},{3,2},{4,5},{5,4},{6,7},{7,6},{8,9},{9,8},{10,11... | collective-permute-start | bytes 1572872 | tf_op jit(solution)/shard_map/ppermute | solution.py:41
  31.2 4.9 %copy-start.4 = (bf16[1024,128]{1,0:T(8,128)(2,1)}, bf16[1024,128]{1,0:T(8,128)(2,1)S(1)}, u32[]{:S(2)}) copy-start(bf16[1024,128]{1,0:T(8,128)(2,1)S(1)} %fusion.146) | copy-start | bytes 786436
  33.0 15.2 %collective-permute-start.4 = (bf16[512,128]{1,0:T(8,128)(2,1)S(1)}, bf16[512,128]{1,0:T(8,128)(2,1)S(1)}, u32[]{:S(2)}, u32[]{:S(2)}) collective-permute-start(bf16[512,128]{1,0:T(8,128)(2,1)S(1)} %fusion.71), channel_id=1, source_target_pairs={{0,12},{4,0},{8,4},{12,8},{1,13},{5,1},{9,5},{13,9},{2,14},{6,2},{... | collective-permute-start | bytes 393224 | tf_op jit(solution)/shard_map/ppermute | solution.py:50
  35.4 11.8 %collective-permute-start.5 = (bf16[512,128]{1,0:T(8,128)(2,1)S(1)}, bf16[512,128]{1,0:T(8,128)(2,1)S(1)}, u32[]{:S(2)}, u32[]{:S(2)}) collective-permute-start(bf16[512,128]{1,0:T(8,128)(2,1)S(1)} %fusion.70), channel_id=1, source_target_pairs={{0,8},{4,12},{8,0},{12,4},{1,9},{5,13},{9,1},{13,5},{2,10},{6,14},... | collective-permute-start | bytes 393224 | tf_op jit(solution)/shard_map/ppermute | solution.py:50
  35.4 12.3 %collective-permute-start.6 = (bf16[512,128]{1,0:T(8,128)(2,1)S(1)}, bf16[512,128]{1,0:T(8,128)(2,1)S(1)}, u32[]{:S(2)}, u32[]{:S(2)}) collective-permute-start(bf16[512,128]{1,0:T(8,128)(2,1)S(1)} %fusion.69), channel_id=1, source_target_pairs={{0,4},{4,8},{8,12},{12,0},{1,5},{5,9},{9,13},{13,1},{2,6},{6,10},{... | collective-permute-start | bytes 393224 | tf_op jit(solution)/shard_map/ppermute | solution.py:50
  52.5 5.0 %collective-permute-start.7 = (bf16[128,512]{1,0:T(8,128)(2,1)S(1)}, bf16[128,512]{1,0:T(8,128)(2,1)S(1)}, u32[]{:S(2)}, u32[]{:S(2)}) collective-permute-start(bf16[128,512]{1,0:T(8,128)(2,1)S(1)} %convert_element_type.153), channel_id=1, source_target_pairs={{0,2},{2,0},{1,3},{3,1},{4,6},{6,4},{5,7},{7,5},{8,10},{10,8},{9,1... | collective-permute-start | bytes 393224 | tf_op jit(solution)/shard_map/ppermute | solution.py:128
